TPU v7x, 32 devices: a whole 2x2x4 slice. The times are simulated.
32 devices in a mesh: section: 4 (over y, x), tp: 4 (over z), mirror: 2 (over core).
Axes of the slice: x: 2, y: 2, z: 4, core: 2. Of those that a mesh axis runs over, the one named last changes fastest.
Arguments:
- feats: bfloat16 [2, 2, 128, 5120], P('mirror', None, 'tp'), may hold values from -16 to 16
- types: int32 [2, 2, 128], P('mirror', None, 'tp'), may hold values from 0 to 63
- segs: int32 [2, 2, 5, 128], P('mirror'), may hold values from 0 to 3, never falling along the last dimension, each value on 1 to 64 neighbouring positions
- type_table: bfloat16 [64, 5120], replicated, may hold values from -3 to 3
- gains: float32 [2, 4, 5120], P('mirror', 'section'), may hold values from 0.25 to 1.75, as said below
- w_qkv: bfloat16 [2, 4, 3, 5120, 512], P('mirror', 'section', None, None, 'tp'), may hold values from -8 to 8, as said below
- w_out: bfloat16 [2, 4, 512, 5120], P('mirror', 'section', 'tp'), as said below
- carry_acts: bfloat16 [2, 4, 128, 5120], P('mirror', 'section', 'tp'), may hold values from -16 to 16
- grad_in: bfloat16 [2, 4, 128, 5120], P('mirror', 'section', 'tp'), may hold values from -6 to 6
- saved: bfloat16 [2, 4, 2, 128, 5120], P('mirror', 'section', None, 'tp'), may hold values from -16 to 16
- cotangent: bfloat16 [2, 2, 128, 5120], P('mirror', None, 'tp'), may hold values from -6 to 6
Outputs:
- acts: bfloat16 [2, 4, 2, 128, 5120], P('mirror', 'section', None, 'tp')
- grad_acts: bfloat16 [2, 4, 2, 128, 5120], P('mirror', 'section', None, 'tp')
- grad_qkv: bfloat16 [2, 4, 3, 5120, 512], P('mirror', 'section', None, None, 'tp')
- grad_out: bfloat16 [2, 4, 512, 5120], P('mirror', 'section', 'tp')
Inputs may be any that keep to these rules, and one draw needn't show every extreme that they name: w_qkv[1, k] equals w_qkv[0, 3 - k]. w_out[1, k] equals w_out[0, 3 - k]. gains[1, k] equals gains[0, 3 - k]. `segs`: segment numbers never fall along a micro-batch; each segment holds at most half of 128 tokens, and one holds exactly that many.
All inputs are finite; a program needn't handle non-finite values.
Results may differ from a plain program's by a relative error of at most 0.015.
Values may be sent and summed in bfloat16 or wider, within the bound.
No kernel may reach another device: no remote copies, remote signals or barrier semaphores. Data moves between devices by JAX's collectives and lax.ppermute only.
A program may use at most 128 MiB of HBM per device.

v0:
```python
import math

import jax
import jax.numpy as jnp
from jax import lax
from jax.sharding import PartitionSpec as P

HD = 128


def passed_along(block, axis, distance):
    devices = range(lax.axis_size(axis))
    route = [(i - distance, i) for i in devices if i - distance in devices]
    return lax.ppermute(block, axis, route)


def swapped(value, axis, apart):
    return lax.ppermute(value, axis, [(i, i ^ 1 << apart) for i in range(lax.axis_size(axis))])


def normalize(values, gain_row):
    mean_square = jnp.mean(values * values, axis=-1, keepdims=True)
    return values * lax.rsqrt(mean_square + 1e-05) * gain_row


def segment_mask(segment_ids):
    position = jnp.arange(segment_ids.shape[0], dtype=jnp.int32)
    causal = position[None, :] <= position[:, None]
    return causal & (segment_ids[:, None] == segment_ids[None, :])


def attend(queries, keys_all, values_all, seg_mask):
    scores = jnp.einsum(
        "ihd,jhd->hij", queries, keys_all, preferred_element_type=jnp.float32
    ) / math.sqrt(queries.shape[-1])
    scores = jnp.where(seg_mask[None], scores, -1e30)
    highest = lax.stop_gradient(jnp.max(scores, axis=-1, keepdims=True))
    expo = jnp.exp(scores - highest)
    probs = (expo / jnp.sum(expo, axis=-1, keepdims=True)).astype(values_all.dtype)
    return jnp.einsum("hij,jhd->ihd", probs, values_all, preferred_element_type=jnp.float32)


def embedding(feat_rows, type_rows, type_table):
    onehot = (
        type_rows[:, None] == jnp.arange(type_table.shape[0], dtype=jnp.int32)[None, :]
    ).astype(jnp.bfloat16)
    looked = jnp.dot(onehot, type_table, preferred_element_type=jnp.float32)
    return (feat_rows.astype(jnp.float32) + looked).astype(jnp.bfloat16)


def shards(
    feats, types, segs, type_table, gains, w_qkv, w_out, carry_acts, grad_in, saved, cotangent
):
    sections = lax.axis_size("section")
    section_index = lax.axis_index("section")
    on_first_pipe = lax.axis_index("mirror") == 0
    position = jnp.where(on_first_pipe, section_index, sections - 1 - section_index)
    gain_row = gains[0, 0]
    qkv_weight = w_qkv[0, 0]
    out_weight = w_out[0, 0]
    window_steps = feats.shape[1]
    seq_len = segs.shape[3]
    model_width = qkv_weight.shape[1]
    inner_here = qkv_weight.shape[-1]
    heads_here = inner_here // HD

    def mask_for(which, index):
        return segment_mask(lax.dynamic_index_in_dim(segs[0, which], index, 0, keepdims=False))

    def backward_layer(layer_in, upstream, seg_mask):
        normed = normalize(layer_in.astype(jnp.float32), gain_row).astype(jnp.bfloat16)
        normed_full, upstream_full = (
            lax.all_gather(normed, "tp", axis=0, tiled=True),
            lax.all_gather(upstream, "tp", axis=0, tiled=True),
        )
        projected = jnp.einsum(
            "sd,cdn->csn", normed_full, qkv_weight, preferred_element_type=jnp.float32
        ).astype(jnp.bfloat16)
        heads_view = projected.reshape(3, seq_len, heads_here, HD)
        primal, pull_attend = jax.vjp(
            lambda query_part, key_part, value_part: attend(
                query_part, key_part, value_part, seg_mask
            ),
            heads_view[0],
            heads_view[1],
            heads_view[2],
        )
        mixed = primal.reshape(seq_len, inner_here).astype(jnp.bfloat16)
        d_mixed = jnp.einsum(
            "sd,nd->sn", upstream_full, out_weight, preferred_element_type=jnp.float32
        ).astype(jnp.bfloat16)
        pulled = pull_attend(d_mixed.astype(jnp.float32).reshape(seq_len, heads_here, HD))
        d_projected = jnp.stack(pulled).reshape(3, seq_len, inner_here)
        d_normed = lax.psum_scatter(
            jnp.einsum(
                "csn,cdn->sd", d_projected, qkv_weight, preferred_element_type=jnp.float32
            ).astype(jnp.bfloat16),
            "tp",
            scatter_dimension=0,
            tiled=True,
        )
        unused_norm, pull_norm = jax.vjp(
            lambda inputs: normalize(inputs, gain_row), layer_in.astype(jnp.float32)
        )
        d_input = pull_norm(d_normed.astype(jnp.float32))[0]
        result = (upstream.astype(jnp.float32) + d_input).astype(jnp.bfloat16)
        qkv_term = jnp.einsum(
            "sd,csn->cdn", normed_full, d_projected, preferred_element_type=jnp.float32
        )
        out_term = jnp.einsum("sn,sd->nd", mixed, upstream_full, preferred_element_type=jnp.float32)
        return (result, qkv_term, out_term)

    forward_in = carry_acts[0, 0]
    backward_in = grad_in[0, 0]
    forward_outs = []
    backward_outs = []
    qkv_total = jnp.zeros(qkv_weight.shape, jnp.float32)
    out_total = jnp.zeros(out_weight.shape, jnp.float32)
    for step_index in range(window_steps):
        embedded = embedding(feats[0, step_index], types[0, step_index], type_table)
        current = jnp.where(position == 0, embedded, forward_in)
        forward_normed = normalize(current.astype(jnp.float32), gain_row).astype(jnp.bfloat16)
        forward_normed_full = lax.all_gather(forward_normed, "tp", axis=0, tiled=True)
        forward_projected = jnp.einsum(
            "sd,cdn->csn", forward_normed_full, qkv_weight, preferred_element_type=jnp.float32
        ).astype(jnp.bfloat16)
        forward_heads_view = forward_projected.reshape(3, seq_len, heads_here, HD)
        forward_mixed = (
            attend(
                forward_heads_view[0],
                forward_heads_view[1],
                forward_heads_view[2],
                mask_for(0, step_index - position + sections - 1),
            )
            .reshape(seq_len, inner_here)
            .astype(jnp.bfloat16)
        )
        attn_rows = lax.psum_scatter(
            jnp.dot(forward_mixed, out_weight, preferred_element_type=jnp.float32).astype(
                jnp.bfloat16
            ),
            "tp",
            scatter_dimension=0,
            tiled=True,
        ).astype(jnp.float32)
        forward_out = (current.astype(jnp.float32) + attn_rows).astype(jnp.bfloat16)
        upstream = jnp.where(position == sections - 1, cotangent[0, step_index], backward_in)
        backward_out, qkv_term, out_term = backward_layer(
            saved[0, 0, step_index], upstream, mask_for(1, step_index + position)
        )
        qkv_total = qkv_total + qkv_term
        out_total = out_total + out_term
        forward_outs.append(forward_out)
        backward_outs.append(backward_out)
        if step_index + 1 < window_steps:
            toward_higher = jnp.where(on_first_pipe, forward_out, backward_out)
            toward_lower = jnp.where(on_first_pipe, backward_out, forward_out)
            from_lower = passed_along(toward_higher, "section", 1)
            from_upper = passed_along(toward_lower, "section", -1)
            forward_in = jnp.where(on_first_pipe, from_lower, from_upper)
            backward_in = jnp.where(on_first_pipe, from_upper, from_lower)
    qkv_size = qkv_total.size
    own_terms = jnp.concatenate(
        [qkv_total.astype(jnp.bfloat16).reshape(-1), out_total.astype(jnp.bfloat16).reshape(-1)]
    )
    bit_count = lax.axis_size(("section", "mirror")).bit_length() - 1
    partner = own_terms
    for bit_number in range(bit_count):
        partner = swapped(partner, ("section", "mirror"), bit_number)
    summed = (own_terms.astype(jnp.float32) + partner.astype(jnp.float32)).astype(jnp.bfloat16)
    grad_qkv = summed[:qkv_size].reshape(3, model_width, inner_here)
    grad_out = summed[qkv_size:].reshape(inner_here, model_width)
    acts_block = jnp.stack(forward_outs)[None, None]
    grads_block = jnp.stack(backward_outs)[None, None]
    return (acts_block, grads_block, grad_qkv[None, None], grad_out[None, None])


def solution(mesh):
    in_specs = (
        P("mirror", None, "tp", None),
        P("mirror", None, "tp"),
        P("mirror", None, None, None),
        P(),
        P("mirror", "section", None),
        P("mirror", "section", None, None, "tp"),
        P("mirror", "section", "tp", None),
        P("mirror", "section", "tp", None),
        P("mirror", "section", "tp", None),
        P("mirror", "section", None, "tp", None),
        P("mirror", None, "tp", None),
    )
    out_specs = (
        P("mirror", "section", None, "tp", None),
        P("mirror", "section", None, "tp", None),
        P("mirror", "section", None, None, "tp"),
        P("mirror", "section", "tp", None),
    )
    return jax.shard_map(shards, mesh=mesh, in_specs=in_specs, out_specs=out_specs, check_vma=False)
```

profile of v0, /device:TPU:0, one launch (start us, length us, event | category | flops | bytes accessed | tf_op | source)
XLA Modules:
  0.0 553.4 jit_solution(733608073758702413)
XLA Ops:
  11.4 34.4 %all-gather.10.cloned.1.call-done = bf16[128,5120]{1,0:T(8,128)(2,1)} async-done(((bf16[32,5120]{1,0:T(8,128)(2,1)}), bf16[128,5120]{1,0:T(8,128)(2,1)}) %all-gather.10.cloned.1.call-update) | async-done | bytes 1310736 | tf_op jit(solution)/shard_map/all_gather | solution.py:73
  45.8 3.4 fusion.65
  49.4 30.3 %all-gather.18.cloned.1.call-done = bf16[1,1,128,5120]{3,2,1,0:T(8,128)(2,1)} async-done(((bf16[1,1,32,5120]{3,2,1,0:T(8,128)(2,1)}), bf16[1,1,128,5120]{3,2,1,0:T(8,128)(2,1)}) %all-gather.18.cloned.1.call-update) | async-done | bytes 1310736 | tf_op jit(solution)/shard_map/all_gather | solution.py:74
  82.3 4.5 fusion.2
  90.1 27.4 %reduce-scatter.7.cloned.1.call-done = bf16[32,5120]{1,0:T(8,128)(2,1)} async-done(((bf16[128,5120]{1,0:T(8,128)(2,1)}), bf16[32,5120]{1,0:T(8,128)(2,1)}) %reduce-scatter.7.cloned.1.call-update) | async-done | bytes 327696 | tf_op jit(solution)/shard_map/reduce_scatter | solution.py:94
  121.6 30.7 %all-gather.8.cloned.1.call-done = bf16[128,5120]{1,0:T(8,128)(2,1)} async-done(((bf16[32,5120]{1,0:T(8,128)(2,1)}), bf16[128,5120]{1,0:T(8,128)(2,1)}) %all-gather.8.cloned.1.call-update) | async-done | bytes 1310736 | tf_op jit(solution)/shard_map/all_gather | solution.py:123
  159.5 28.8 %reduce-scatter.5.cloned.1.call-done = bf16[32,5120]{1,0:T(8,128)(2,1)} async-done(((bf16[128,5120]{1,0:T(8,128)(2,1)}), bf16[32,5120]{1,0:T(8,128)(2,1)}) %reduce-scatter.5.cloned.1.call-update) | async-done | bytes 327696 | tf_op jit(solution)/shard_map/reduce_scatter | solution.py:138
  190.6 3.5 collective-permute-start
  195.4 5.2 collective-permute-done
  200.6 9.0 %collective-permute-done.1 = bf16[32,5120]{1,0:T(8,128)(2,1)S(1)} collective-permute-done((bf16[32,5120]{1,0:T(8,128)(2,1)S(1)}, bf16[32,5120]{1,0:T(8,128)(2,1)S(1)}, u32[]{:S(2)}, u32[]{:S(2)}) %collective-permute-start.1) | collective-permute-done | bytes 327712 | tf_op jit(solution)/shard_map/ppermute | solution.py:14
  213.5 5.6 %fusion.22 = f32[3,128,5120]{2,1,0:T(8,128)} fusion(bf16[128,5120]{1,0:T(8,128)(2,1)} %all-gather.10.cloned.1.call-done, bf16[1,128,1,128]{3,1,2,0:T(8,128)(2,1)} %copy-done.19, bf16[1,128,1,128]{3,1,2,0:T(8,128)(2,1)S(1)} %fusion.91, bf16[1,128,1,128]{3,1,2,0:T(8,128)(2,1)S(1)} %fusion.90), kind=kOutput, calls=%fused_computation.32 | convolution fusion | flops 503414784 | bytes 9273344 | tf_op jit(solution)/shard_map/sd,csn->cdn/dot_general | solution.py:107
  221.6 3.4 fusion.55
  225.2 30.3 %all-gather.14.cloned.1.call-done = bf16[128,5120]{1,0:T(8,128)(2,1)} async-done(((bf16[32,5120]{1,0:T(8,128)(2,1)}), bf16[128,5120]{1,0:T(8,128)(2,1)}) %all-gather.14.cloned.1.call-update) | async-done | bytes 1310736 | tf_op jit(solution)/shard_map/all_gather | solution.py:74
  258.7 3.5 fusion.18
  263.9 6.4 %fusion = bf16[3,5120,128]{1,2,0:T(8,128)(2,1)} fusion(f32[3,128,5120]{2,1,0:T(8,128)} %fusion.22, bf16[128,5120]{1,0:T(8,128)(2,1)S(1)} %copy-done.4, bf16[1,128,1,128]{3,1,2,0:T(8,128)(2,1)S(1)} %copy-done.20, bf16[1,128,1,128]{3,1,2,0:T(8,128)(2,1)S(1)} %fusion.94, bf16[1,128,1,128]{3,1,2,0:T(8,128)(2,1)S(1)} %fusion.93), kind=kOutput, calls=%fused_computation.2 | convolution fusion | flops 507346944 | bytes 13205504 | tf_op jit(solution)/shard_map/sd,csn->cdn/dot_general | solution.py:107
  270.3 6.3 %copy.23 = bf16[3,5120,128]{2,1,0:T(8,128)(2,1)} copy(bf16[3,5120,128]{1,2,0:T(8,128)(2,1)} %fusion) | data formatting | bytes 7864320 | tf_op jit(solution)/shard_map/convert_element_type | solution.py:164
  276.6 14.2 %pad_maximum_fusion = bf16[2621440]{0:T(1024)(128)(2,1)} fusion(bf16[655360]{0:T(1024)(128)(2,1)S(1)} %bitcast.314, bf16[1966080]{0:T(1024)(128)(2,1)} %bitcast.312), kind=kLoop, calls=%fused_computation.17 | loop fusion | flops 10485760 | bytes 10485760 | tf_op jit(solution)/shard_map/concatenate | solution.py:163
  293.2 6.5 %collective-permute-done.2 = bf16[2621440]{0:T(1024)(128)(2,1)} collective-permute-done((bf16[2621440]{0:T(1024)(128)(2,1)}, bf16[2621440]{0:T(1024)(128)(2,1)}, u32[]{:S(2)}, u32[]{:S(2)}) %collective-permute-start.2) | collective-permute-done | bytes 5242912 | tf_op jit(solution)/shard_map/ppermute | solution.py:18
  303.6 20.3 %reduce-scatter.11.cloned.1.call-done = bf16[32,5120]{1,0:T(8,128)(2,1)} async-done(((bf16[128,5120]{1,0:T(8,128)(2,1)}), bf16[32,5120]{1,0:T(8,128)(2,1)}) %reduce-scatter.11.cloned.1.call-update) | async-done | bytes 327696 | tf_op jit(solution)/shard_map/reduce_scatter | solution.py:94
  327.8 87.3 %collective-permute-done.3 = bf16[2621440]{0:T(1024)(128)(2,1)} collective-permute-done((bf16[2621440]{0:T(1024)(128)(2,1)}, bf16[2621440]{0:T(1024)(128)(2,1)}, u32[]{:S(2)}, u32[]{:S(2)}) %collective-permute-start.3) | collective-permute-done | bytes 5242912 | tf_op jit(solution)/shard_map/ppermute | solution.py:18
  416.6 3.4 fusion.60
  424.8 26.9 %reduce-scatter.9.cloned.1.call-done = bf16[32,5120]{1,0:T(8,128)(2,1)} async-done(((bf16[128,5120]{1,0:T(8,128)(2,1)}), bf16[32,5120]{1,0:T(8,128)(2,1)}) %reduce-scatter.9.cloned.1.call-update) | async-done | bytes 327696 | tf_op jit(solution)/shard_map/reduce_scatter | solution.py:138
  453.8 75.9 %collective-permute-done.4 = bf16[2621440]{0:T(1024)(128)(2,1)} collective-permute-done((bf16[2621440]{0:T(1024)(128)(2,1)}, bf16[2621440]{0:T(1024)(128)(2,1)}, u32[]{:S(2)}, u32[]{:S(2)}) %collective-permute-start.4) | collective-permute-done | bytes 5242912 | tf_op jit(solution)/shard_map/ppermute | solution.py:18
  529.7 13.3 %add_convert_fusion = bf16[2621440]{0:T(1024)(128)(2,1)S(1)} fusion(bf16[2621440]{0:T(1024)(128)(2,1)} %collective-permute-done.4, bf16[655360]{0:T(1024)(128)(2,1)S(1)} %bitcast.315, bf16[1966080]{0:T(1024)(128)(2,1)} %bitcast.313), kind=kLoop, calls=%fused_computation | loop fusion | flops 18350080 | bytes 15728640 | tf_op jit(solution)/shard_map/convert_element_type | solution.py:170
  (137 shorter events, 58.5 us)
Async XLA Ops:
  7.2 72.5 %copy-start = (bf16[1,1,128,5120]{3,2,1,0:T(8,128)(2,1)S(1)}, bf16[1,1,128,5120]{3,2,1,0:T(8,128)(2,1)}, u32[]{:S(2)}) copy-start(bf16[1,1,128,5120]{3,2,1,0:T(8,128)(2,1)} %param.17) | copy-start | bytes 3932164
  7.2 38.6 %all-gather.10.cloned.1.call-start = ((), (), s32[]{:S(2)}) async-start(), calls=%async_computation.6 | async-start | bytes 1638400 | tf_op jit(solution)/shard_map/all_gather | solution.py:73
  10.5 69.3 %all-gather.18.cloned.1.call-start = ((), (), s32[]{:S(2)}) async-start(), calls=%async_computation.13 | async-start | bytes 1638400 | tf_op jit(solution)/shard_map/all_gather | solution.py:74
  11.3 106.1 %reduce-scatter.7.cloned.1.call-start = ((), (), s32[]{:S(2)}) async-start(), calls=%async_computation.7 | async-start | bytes 1638400 | tf_op jit(solution)/shard_map/reduce_scatter | solution.py:94
  86.9 30.6 %copy-start.2 = (bf16[1,1,2,32,5120]{4,3,2,1,0:T(8,128)(2,1)S(1)}, bf16[1,1,2,32,5120]{4,3,2,1,0:T(8,128)(2,1)}, u32[]{:S(2)}) copy-start(bf16[1,1,2,32,5120]{4,3,2,1,0:T(8,128)(2,1)} %param.20) | copy-start | bytes 1966084
  86.9 30.6 %copy-start.12 = (f32[1,1,5120]{2,1,0:T(1,128)S(1)}, f32[1,1,5120]{2,1,0:T(1,128)}, u32[]{:S(2)}) copy-start(f32[1,1,5120]{2,1,0:T(1,128)} %param.15) | copy-start | bytes 61444
  86.9 65.4 %all-gather.8.cloned.1.call-start = ((), (), s32[]{:S(2)}) async-start(), calls=%async_computation.4 | async-start | bytes 1638400 | tf_op jit(solution)/shard_map/all_gather | solution.py:123
  121.0 67.4 %reduce-scatter.5.cloned.1.call-start = ((), (), s32[]{:S(2)}) async-start(), calls=%async_computation.5 | async-start | bytes 1638400 | tf_op jit(solution)/shard_map/reduce_scatter | solution.py:138
  157.7 30.6 %copy-start.10 = (bf16[1,1,32,5120]{3,2,1,0:T(8,128)(2,1)S(1)}, bf16[1,1,32,5120]{3,2,1,0:T(8,128)(2,1)}, u32[]{:S(2)}) copy-start(bf16[1,1,32,5120]{3,2,1,0:T(8,128)(2,1)} %slice_select_fusion) | copy-start | bytes 983044
  157.7 30.6 %copy-start.11 = (bf16[32,5120]{1,0:T(8,128)(2,1)S(1)}, bf16[32,5120]{1,0:T(8,128)(2,1)}, u32[]{:S(2)}) copy-start(bf16[32,5120]{1,0:T(8,128)(2,1)} %reduce-scatter.7.cloned.1.call-done) | copy-start | bytes 983044
  157.7 63.9 %all-gather.16.cloned.1.call-start = ((), (), s32[]{:S(2)}) async-start(), calls=%async_computation.11 | async-start | bytes 1638400 | tf_op jit(solution)/shard_map/all_gather | solution.py:73
  159.5 95.9 %all-gather.14.cloned.1.call-start = ((), (), s32[]{:S(2)}) async-start(), calls=%async_computation.10 | async-start | bytes 1638400 | tf_op jit(solution)/shard_map/all_gather | solution.py:74
  188.3 22.0 %copy-start.14 = (bf16[1,2,32,5120]{3,2,1,0:T(8,128)(2,1)S(1)}, bf16[1,2,32,5120]{3,2,1,0:T(8,128)(2,1)}, u32[]{:S(2)}) copy-start(bf16[1,2,32,5120]{3,2,1,0:T(8,128)(2,1)} %param.21) | copy-start | bytes 1966084
  190.4 20.9 %copy-start.3 = (bf16[1,1,128,5120]{3,2,1,0:T(8,128)(2,1)S(1)}, bf16[1,1,128,5120]{3,2,1,0:T(8,128)(2,1)}, u32[]{:S(2)}) copy-start(bf16[1,1,128,5120]{3,2,1,0:T(8,128)(2,1)} %all-gather.18.cloned.1.call-done) | copy-start | bytes 3932164
  190.6 10.1 %collective-permute-start = (bf16[32,5120]{1,0:T(8,128)(2,1)S(1)}, bf16[32,5120]{1,0:T(8,128)(2,1)S(1)}, u32[]{:S(2)}, u32[]{:S(2)}) collective-permute-start(bf16[32,5120]{1,0:T(8,128)(2,1)S(1)} %broadcast_select_fusion.1), channel_id=1, source_target_pairs={{0,8},{8,16},{16,24},{1,9},{9,17},{17,25},{2,10},{10,18},{18,26},{... | collective-permute-start | bytes 983048 | tf_op jit(solution)/shard_map/ppermute | solution.py:14
  194.1 15.5 %collective-permute-start.1 = (bf16[32,5120]{1,0:T(8,128)(2,1)S(1)}, bf16[32,5120]{1,0:T(8,128)(2,1)S(1)}, u32[]{:S(2)}, u32[]{:S(2)}) collective-permute-start(bf16[32,5120]{1,0:T(8,128)(2,1)S(1)} %get-tuple-element.6), channel_id=1, source_target_pairs={{8,0},{16,8},{24,16},{9,1},{17,9},{25,17},{10,2},{18,10},{26,18},{... | collective-permute-start | bytes 983048 | tf_op jit(solution)/shard_map/ppermute | solution.py:14
  211.1 112.8 %reduce-scatter.11.cloned.1.call-start = ((), (), s32[]{:S(2)}) async-start(), calls=%async_computation.12 | async-start | bytes 1638400 | tf_op jit(solution)/shard_map/reduce_scatter | solution.py:94
  290.7 9.0 %collective-permute-start.2 = (bf16[2621440]{0:T(1024)(128)(2,1)}, bf16[2621440]{0:T(1024)(128)(2,1)}, u32[]{:S(2)}, u32[]{:S(2)}) collective-permute-start(bf16[2621440]{0:T(1024)(128)(2,1)} %pad_maximum_fusion), channel_id=1, source_target_pairs={{0,1},{1,0},{8,9},{9,8},{16,17},{17,16},{24,25},{25,24},{2,3},{3,2... | collective-permute-start | bytes 15728648 | tf_op jit(solution)/shard_map/ppermute | solution.py:18
  293.1 123.4 %all-gather.12.cloned.1.call-start = ((), (), s32[]{:S(2)}) async-start(), calls=%async_computation.8 | async-start | bytes 1638400 | tf_op jit(solution)/shard_map/all_gather | solution.py:123
  299.7 115.4 %collective-permute-start.3 = (bf16[2621440]{0:T(1024)(128)(2,1)}, bf16[2621440]{0:T(1024)(128)(2,1)}, u32[]{:S(2)}, u32[]{:S(2)}) collective-permute-start(bf16[2621440]{0:T(1024)(128)(2,1)} %collective-permute-done.2), channel_id=1, source_target_pairs={{0,8},{1,9},{8,0},{9,1},{16,24},{17,25},{24,16},{25,17},{2,10},{3,... | collective-permute-start | bytes 15728648 | tf_op jit(solution)/shard_map/ppermute | solution.py:18
  327.5 92.5 %copy-start.26 = (s32[128]{0:T(128)S(1)}, s32[128]{0:T(128)}, u32[]{:S(2)}) copy-start(s32[128]{0:T(128)} %get-tuple-element.17) | copy-start | bytes 1540
  327.5 124.2 %reduce-scatter.9.cloned.1.call-start = ((), (), s32[]{:S(2)}) async-start(), calls=%async_computation.9 | async-start | bytes 1638400 | tf_op jit(solution)/shard_map/reduce_scatter | solution.py:138
  415.1 114.5 %collective-permute-start.4 = (bf16[2621440]{0:T(1024)(128)(2,1)}, bf16[2621440]{0:T(1024)(128)(2,1)}, u32[]{:S(2)}, u32[]{:S(2)}) collective-permute-start(bf16[2621440]{0:T(1024)(128)(2,1)} %collective-permute-done.3), channel_id=1, source_target_pairs={{0,16},{1,17},{8,24},{9,25},{16,0},{17,1},{24,8},{25,9},{2,18},{3,... | collective-permute-start | bytes 15728648 | tf_op jit(solution)/shard_map/ppermute | solution.py:18
  422.0 30.9 %copy-start.7 = (bf16[32,5120]{1,0:T(8,128)(2,1)S(1)}, bf16[32,5120]{1,0:T(8,128)(2,1)}, u32[]{:S(2)}) copy-start(bf16[32,5120]{1,0:T(8,128)(2,1)} %copy-done.6) | copy-start | bytes 983044
  (18 other events, 58.0 us)
Sparse Core Ops, SparseCore 0:
  10.6 35.2 all-gather.9
  48.0 31.6 all-gather.17
  87.0 30.4 reduce-scatter.6
  121.1 31.1 all-gather.7
  157.8 30.4 reduce-scatter.4
  190.3 31.1 all-gather.15
  223.7 31.6 all-gather.13
  293.3 30.6 reduce-scatter.10
  327.6 31.1 all-gather.11
  422.1 29.5 reduce-scatter.8
where the time goes:
time: 554 us; the launch traced here: 553 us
  waiting for transfers between devices  416 us (75%)
  matrix products  52.3 us (9%)
  other arithmetic  46.1 us (8%)
  local copies, waits for them, and re-layouts  16.3 us (3%)
  between operations  14.5 us (3%)
  starting transfers between devices  8.56 us (2%)
    ppermute x3, waiting for transfers between devices, swapped(): lax.ppermute(value, axis, [(i, i ^ 1 << apart) for i in range(lax.axis_si...  170 us
    all_gather x2, waiting for transfers between devices, backward_layer(): lax.all_gather(upstream, 'tp', axis=0, tiled=True)  60.5 us
    reduce_scatter x2, waiting for transfers between devices, shards(): lax.psum_scatter(jnp.dot(forward_mixed, out_weight, preferred_element_typ...  55.7 us
    reduce_scatter x2, waiting for transfers between devices, backward_layer(): lax.psum_scatter(jnp.einsum('csn,cdn->sd', d_projected, qkv_weight, prefe...  47.7 us
    all_gather x2, waiting for transfers between devices, backward_layer(): lax.all_gather(normed, 'tp', axis=0, tiled=True)  36.8 us
    all_gather x2, waiting for transfers between devices, shards(): lax.all_gather(forward_normed, 'tp', axis=0, tiled=True)  30.7 us
    ppermute x2, waiting for transfers between devices, passed_along(): return lax.ppermute(block, axis, route)  14.2 us
    concatenate x1, other arithmetic, shards(): jnp.concatenate([qkv_total.astype(jnp.bfloat16).reshape(-1), out_total.as...  14.2 us
  transfers between devices with their start and end apart: 15, of which 14 were waited for; matrix products, arithmetic and copies ran while one was open for 7% of the time, Pallas kernels for 0%

commit v1 on v0

--- a/solution.py
+++ b/solution.py
@@ -1,4 +1,6 @@
 import math
+
+import numpy as np
 
 import jax
 import jax.numpy as jnp
@@ -14,8 +16,8 @@
     return lax.ppermute(block, axis, route)
 
 
-def swapped(value, axis, apart):
-    return lax.ppermute(value, axis, [(i, i ^ 1 << apart) for i in range(lax.axis_size(axis))])
+def flipped(value, axis, mask):
+    return lax.ppermute(value, axis, [(i, i ^ mask) for i in range(lax.axis_size(axis))])
 
 
 def normalize(values, gain_row):
@@ -46,6 +48,16 @@
     ).astype(jnp.bfloat16)
     looked = jnp.dot(onehot, type_table, preferred_element_type=jnp.float32)
     return (feat_rows.astype(jnp.float32) + looked).astype(jnp.bfloat16)
+
+
+def gathered(blocks):
+    full = lax.all_gather(jnp.stack(blocks), "tp", axis=1, tiled=True)
+    return [full[i] for i in range(len(blocks))]
+
+
+def scattered(blocks):
+    part = lax.psum_scatter(jnp.stack(blocks), "tp", scatter_dimension=1, tiled=True)
+    return [part[i] for i in range(len(blocks))]
 
 
 def shards(
@@ -67,16 +79,26 @@
     def mask_for(which, index):
         return segment_mask(lax.dynamic_index_in_dim(segs[0, which], index, 0, keepdims=False))
 
-    def backward_layer(layer_in, upstream, seg_mask):
-        normed = normalize(layer_in.astype(jnp.float32), gain_row).astype(jnp.bfloat16)
-        normed_full, upstream_full = (
-            lax.all_gather(normed, "tp", axis=0, tiled=True),
-            lax.all_gather(upstream, "tp", axis=0, tiled=True),
-        )
+    def normed_rows(rows):
+        return normalize(rows.astype(jnp.float32), gain_row).astype(jnp.bfloat16)
+
+    def heads_of(normed_full):
         projected = jnp.einsum(
             "sd,cdn->csn", normed_full, qkv_weight, preferred_element_type=jnp.float32
         ).astype(jnp.bfloat16)
-        heads_view = projected.reshape(3, seq_len, heads_here, HD)
+        return projected.reshape(3, seq_len, heads_here, HD)
+
+    def forward_part(normed_full, seg_mask):
+        heads_view = heads_of(normed_full)
+        mixed = (
+            attend(heads_view[0], heads_view[1], heads_view[2], seg_mask)
+            .reshape(seq_len, inner_here)
+            .astype(jnp.bfloat16)
+        )
+        return jnp.dot(mixed, out_weight, preferred_element_type=jnp.float32).astype(jnp.bfloat16)
+
+    def backward_part(normed_full, upstream_full, seg_mask):
+        heads_view = heads_of(normed_full)
         primal, pull_attend = jax.vjp(
             lambda query_part, key_part, value_part: attend(
                 query_part, key_part, value_part, seg_mask
@@ -91,24 +113,24 @@
         ).astype(jnp.bfloat16)
         pulled = pull_attend(d_mixed.astype(jnp.float32).reshape(seq_len, heads_here, HD))
         d_projected = jnp.stack(pulled).reshape(3, seq_len, inner_here)
-        d_normed = lax.psum_scatter(
-            jnp.einsum(
-                "csn,cdn->sd", d_projected, qkv_weight, preferred_element_type=jnp.float32
-            ).astype(jnp.bfloat16),
-            "tp",
-            scatter_dimension=0,
-            tiled=True,
-        )
+        d_normed_part = jnp.einsum(
+            "csn,cdn->sd", d_projected, qkv_weight, preferred_element_type=jnp.float32
+        ).astype(jnp.bfloat16)
+        qkv_term = jnp.einsum(
+            "sd,csn->cdn", normed_full, d_projected, preferred_element_type=jnp.float32
+        )
+        out_term = jnp.einsum("sn,sd->nd", mixed, upstream_full, preferred_element_type=jnp.float32)
+        return d_normed_part, qkv_term, out_term
+
+    def input_grad(layer_in, upstream, d_normed):
         unused_norm, pull_norm = jax.vjp(
             lambda inputs: normalize(inputs, gain_row), layer_in.astype(jnp.float32)
         )
         d_input = pull_norm(d_normed.astype(jnp.float32))[0]
-        result = (upstream.astype(jnp.float32) + d_input).astype(jnp.bfloat16)
-        qkv_term = jnp.einsum(
-            "sd,csn->cdn", normed_full, d_projected, preferred_element_type=jnp.float32
-        )
-        out_term = jnp.einsum("sn,sd->nd", mixed, upstream_full, preferred_element_type=jnp.float32)
-        return (result, qkv_term, out_term)
+        return (upstream.astype(jnp.float32) + d_input).astype(jnp.bfloat16)
+
+    saved_normed = [normed_rows(saved[0, 0, t]) for t in range(window_steps)]
+    saved_full = [None] + [gathered([saved_normed[t]])[0] for t in range(1, window_steps)]
 
     forward_in = carry_acts[0, 0]
     backward_in = grad_in[0, 0]
@@ -119,35 +141,24 @@
     for step_index in range(window_steps):
         embedded = embedding(feats[0, step_index], types[0, step_index], type_table)
         current = jnp.where(position == 0, embedded, forward_in)
-        forward_normed = normalize(current.astype(jnp.float32), gain_row).astype(jnp.bfloat16)
-        forward_normed_full = lax.all_gather(forward_normed, "tp", axis=0, tiled=True)
-        forward_projected = jnp.einsum(
-            "sd,cdn->csn", forward_normed_full, qkv_weight, preferred_element_type=jnp.float32
-        ).astype(jnp.bfloat16)
-        forward_heads_view = forward_projected.reshape(3, seq_len, heads_here, HD)
-        forward_mixed = (
-            attend(
-                forward_heads_view[0],
-                forward_heads_view[1],
-                forward_heads_view[2],
-                mask_for(0, step_index - position + sections - 1),
-            )
-            .reshape(seq_len, inner_here)
-            .astype(jnp.bfloat16)
-        )
-        attn_rows = lax.psum_scatter(
-            jnp.dot(forward_mixed, out_weight, preferred_element_type=jnp.float32).astype(
-                jnp.bfloat16
-            ),
-            "tp",
-            scatter_dimension=0,
-            tiled=True,
-        ).astype(jnp.float32)
-        forward_out = (current.astype(jnp.float32) + attn_rows).astype(jnp.bfloat16)
         upstream = jnp.where(position == sections - 1, cotangent[0, step_index], backward_in)
-        backward_out, qkv_term, out_term = backward_layer(
-            saved[0, 0, step_index], upstream, mask_for(1, step_index + position)
-        )
+        to_gather = [normed_rows(current), upstream]
+        if step_index == 0:
+            to_gather.append(saved_normed[0])
+        gathered_rows = gathered(to_gather)
+        forward_normed_full, upstream_full = gathered_rows[0], gathered_rows[1]
+        backward_normed_full = gathered_rows[2] if step_index == 0 else saved_full[step_index]
+        attn_part = forward_part(
+            forward_normed_full, mask_for(0, step_index - position + sections - 1)
+        )
+        d_normed_part, qkv_term, out_term = backward_part(
+            backward_normed_full, upstream_full, mask_for(1, step_index + position)
+        )
+        attn_rows, d_normed = scattered([attn_part, d_normed_part])
+        forward_out = (current.astype(jnp.float32) + attn_rows.astype(jnp.float32)).astype(
+            jnp.bfloat16
+        )
+        backward_out = input_grad(saved[0, 0, step_index], upstream, d_normed)
         qkv_total = qkv_total + qkv_term
         out_total = out_total + out_term
         forward_outs.append(forward_out)
@@ -159,17 +170,39 @@
             from_upper = passed_along(toward_lower, "section", -1)
             forward_in = jnp.where(on_first_pipe, from_lower, from_upper)
             backward_in = jnp.where(on_first_pipe, from_upper, from_lower)
-    qkv_size = qkv_total.size
-    own_terms = jnp.concatenate(
-        [qkv_total.astype(jnp.bfloat16).reshape(-1), out_total.astype(jnp.bfloat16).reshape(-1)]
-    )
-    bit_count = lax.axis_size(("section", "mirror")).bit_length() - 1
-    partner = own_terms
-    for bit_number in range(bit_count):
-        partner = swapped(partner, ("section", "mirror"), bit_number)
-    summed = (own_terms.astype(jnp.float32) + partner.astype(jnp.float32)).astype(jnp.bfloat16)
-    grad_qkv = summed[:qkv_size].reshape(3, model_width, inner_here)
-    grad_out = summed[qkv_size:].reshape(inner_here, model_width)
+
+    own_qkv = qkv_total.astype(jnp.bfloat16)
+    own_out = out_total.astype(jnp.bfloat16)
+    pair_axes = ("section", "mirror")
+    bit_count = lax.axis_size(pair_axes).bit_length() - 1
+    section_bits = list(range(1, bit_count))
+    if section_bits:
+        routes = []
+        for start in range(len(section_bits)):
+            order = section_bits[start:] + section_bits[:start]
+            routes.append([1 | (1 << order[0])] + [1 << bit for bit in order[1:]])
+    else:
+        routes = [[1]]
+    cuts = np.linspace(0, model_width, len(routes) + 1).astype(int)
+    qkv_sums = []
+    out_sums = []
+    for route_index, hops in enumerate(routes):
+        low, high = int(cuts[route_index]), int(cuts[route_index + 1])
+        piece = (own_qkv[:, low:high, :], own_out[:, low:high])
+        for mask in hops:
+            piece = flipped(piece, pair_axes, mask)
+        qkv_sums.append(
+            (own_qkv[:, low:high, :].astype(jnp.float32) + piece[0].astype(jnp.float32)).astype(
+                jnp.bfloat16
+            )
+        )
+        out_sums.append(
+            (own_out[:, low:high].astype(jnp.float32) + piece[1].astype(jnp.float32)).astype(
+                jnp.bfloat16
+            )
+        )
+    grad_qkv = jnp.concatenate(qkv_sums, axis=1)
+    grad_out = jnp.concatenate(out_sums, axis=1)
     acts_block = jnp.stack(forward_outs)[None, None]
     grads_block = jnp.stack(backward_outs)[None, None]
     return (acts_block, grads_block, grad_qkv[None, None], grad_out[None, None])

time: 554 us -> 422 us (0.76)
  waiting for transfers between devices: 416 us -> 307 us
  other arithmetic: 46.1 us -> 22.9 us
    ppermute x3 -> x8, waiting for transfers between devices: 170 us -> 106 us  [flipped(): lax.ppermute(value, axis, [(i, i ^ mask) for i in range(lax.axis_size(axi...]
    reduce_scatter x4 -> x2, waiting for transfers between devices: 103 us -> 50.9 us  [scattered(): lax.psum_scatter(jnp.stack(blocks), 'tp', scatter_dimension=1, tiled=True)]
    concatenate x1 -> x0, other arithmetic: 14.2 us -> none  [shards(): jnp.concatenate([qkv_total.astype(jnp.bfloat16).reshape(-1), out_total.as...]
    convert_element_type x3 -> x4, other arithmetic: 16.2 us -> 2.77 us  [the longest x1 1.16 us: shards(): (own_qkv[:, low:high, :].astype(jnp.float32) + piece[0].astype(jnp.float3...]
    all_gather x6 -> x3, waiting for transfers between devices: 128 us -> 138 us  [gathered(): full = lax.all_gather(jnp.stack(blocks), 'tp', axis=1, tiled=True)]
    convert_element_type x1 -> x0, local copies, waits for them, and re-layouts: 6.28 us -> none  [shards(): qkv_total.astype(jnp.bfloat16).reshape(-1)]
  transfers between devices with their start and end apart: 15 -> 15, of which waited for: 14 -> 11; matrix products, arithmetic and copies ran while one was open for 7% -> 8% of each run, Pallas kernels for 0% -> 0%
where the time goes in v1:
time: 422 us; the launch traced here: 421 us
  waiting for transfers between devices  307 us (73%)
  matrix products  49.4 us (12%)
  other arithmetic  22.9 us (5%)
  local copies, waits for them, and re-layouts  14.3 us (3%)
  between operations  14.3 us (3%)
  starting transfers between devices  13.5 us (3%)
    all_gather x3, waiting for transfers between devices, gathered(): full = lax.all_gather(jnp.stack(blocks), 'tp', axis=1, tiled=True)  138 us
    ppermute x8, waiting for transfers between devices, flipped(): lax.ppermute(value, axis, [(i, i ^ mask) for i in range(lax.axis_size(axi...  106 us
    reduce_scatter x2, waiting for transfers between devices, scattered(): lax.psum_scatter(jnp.stack(blocks), 'tp', scatter_dimension=1, tiled=True)  50.9 us
    ppermute x2, waiting for transfers between devices, passed_along(): return lax.ppermute(block, axis, route)  12.3 us
    dot_general x4, matrix products, heads_of(): jnp.einsum('sd,cdn->csn', normed_full, qkv_weight, preferred_element_type...  12 us
    dot_general x2, matrix products, backward_part(): jnp.einsum('sd,csn->cdn', normed_full, d_projected, preferred_element_typ...  10 us
    unnamed x63, local copies, waits for them, and re-layouts  9.89 us
  transfers between devices with their start and end apart: 15, of which 11 were waited for; matrix products, arithmetic and copies ran while one was open for 8% of the time, Pallas kernels for 0%

profile of v1, /device:TPU:0, one launch (start us, length us, event | category | flops | bytes accessed | tf_op | source)
XLA Modules:
  0.0 421.5 jit_solution(4740273681099519742)
XLA Ops:
  13.8 78.7 %all-gather.4.cloned.1.call-done = bf16[3,128,5120]{2,1,0:T(8,128)(2,1)} async-done(((bf16[3,32,5120]{2,1,0:T(8,128)(2,1)}), bf16[3,128,5120]{2,1,0:T(8,128)(2,1)}) %all-gather.4.cloned.1.call-update) | async-done | bytes 3932176 | tf_op jit(solution)/shard_map/all_gather | solution.py:54
  92.5 3.5 fusion.54
  101.9 2.5 fusion.6
  104.4 3.6 fusion.5
  109.8 50.9 %reduce-scatter.3.cloned.1.call-done = bf16[2,32,5120]{2,1,0:T(8,128)(2,1)} async-done(((bf16[2,128,5120]{2,1,0:T(8,128)(2,1)}), bf16[2,32,5120]{2,1,0:T(8,128)(2,1)}) %reduce-scatter.3.cloned.1.call-update) | async-done | bytes 655376 | tf_op jit(solution)/shard_map/reduce_scatter | solution.py:59
  162.0 2.3 broadcast_select_fusion
  165.0 4.3 %collective-permute-start = (bf16[32,5120]{1,0:T(8,128)(2,1)S(1)}, bf16[32,5120]{1,0:T(8,128)(2,1)}, u32[]{:S(2)}, u32[]{:S(2)}) collective-permute-start(bf16[32,5120]{1,0:T(8,128)(2,1)S(1)} %broadcast_select_fusion.1), channel_id=1, source_target_pairs={{0,8},{8,16},{16,24},{1,9},{9,17},{17,25},{2,10},{10,18},{18,26},{... | collective-permute-start | bytes 983048 | tf_op jit(solution)/shard_map/ppermute | solution.py:16
  171.8 3.3 collective-permute-done
  175.1 9.1 %collective-permute-done.1 = bf16[32,5120]{1,0:T(8,128)(2,1)} collective-permute-done((bf16[32,5120]{1,0:T(8,128)(2,1)}, bf16[32,5120]{1,0:T(8,128)(2,1)}, u32[]{:S(2)}, u32[]{:S(2)}) %collective-permute-start.1) | collective-permute-done | bytes 327712 | tf_op jit(solution)/shard_map/ppermute | solution.py:16
  189.0 3.4 fusion.30
  192.4 5.6 %fusion.31 = f32[3,128,5120]{2,1,0:T(8,128)} fusion(bf16[3,128,5120]{2,1,0:T(8,128)(2,1)} %all-gather.4.cloned.1.call-done, bf16[1,128,1,128]{3,1,2,0:T(8,128)(2,1)S(1)} %fusion.80, bf16[1,128,1,128]{3,1,2,0:T(8,128)(2,1)S(1)} %fusion.74, bf16[1,128,1,128]{3,1,2,0:T(8,128)(2,1)S(1)} %fusion.73), kind=kOutput, calls=%fused_computation.52 | convolution fusion | flops 503414784 | bytes 9273344 | tf_op jit(solution)/shard_map/sd,csn->cdn/dot_general | solution.py:119
  198.0 7.1 %all-gather.8.cloned.1.call-done = bf16[1,128,5120]{2,1,0:T(8,128)(2,1)} async-done(((bf16[1,32,5120]{2,1,0:T(8,128)(2,1)}), bf16[1,128,5120]{2,1,0:T(8,128)(2,1)}) %all-gather.8.cloned.1.call-update) | async-done | bytes 1310736 | tf_op jit(solution)/shard_map/all_gather | solution.py:54
  205.1 3.4 fusion.46
  208.7 52.3 %all-gather.6.cloned.1.call-done = bf16[2,128,5120]{2,1,0:T(8,128)(2,1)} async-done(((bf16[2,32,5120]{2,1,0:T(8,128)(2,1)}), bf16[2,128,5120]{2,1,0:T(8,128)(2,1)}) %all-gather.6.cloned.1.call-update) | async-done | bytes 2621456 | tf_op jit(solution)/shard_map/all_gather | solution.py:54
  264.4 3.0 fusion.51
  269.8 3.6 fusion.4
  273.4 4.4 %fusion = bf16[3,5120,128]{1,2,0:T(8,128)(2,1)S(1)} fusion(f32[3,128,5120]{2,1,0:T(8,128)} %fusion.31, bf16[1,128,5120]{2,1,0:T(8,128)(2,1)S(1)} %copy-done.7, bf16[1,128,1,128]{3,1,2,0:T(8,128)(2,1)S(1)} %copy-done.22, bf16[1,128,1,128]{3,1,2,0:T(8,128)(2,1)S(1)} %fusion.77, bf16[1,128,1,128]{3,1,2,0:T(8,128)(2,1)S(1)} %fusion.76), kind=kOutput, calls=%fused_computation.1 | convolution fusion | flops 507346944 | bytes 13205504 | tf_op jit(solution)/shard_map/sd,csn->cdn/dot_general | solution.py:119
  277.9 2.4 fusion.155
  285.5 2.8 fusion.1
  289.3 51.1 %collective-permute-done.6 = bf16[128,2560]{1,0:T(8,128)(2,1)S(1)} collective-permute-done((bf16[128,2560]{1,0:T(8,128)(2,1)S(1)}, bf16[128,2560]{1,0:T(8,128)(2,1)S(1)}, u32[]{:S(2)}, u32[]{:S(2)}) %collective-permute-start.6) | collective-permute-done | bytes 655392 | tf_op jit(solution)/shard_map/ppermute | solution.py:20
  344.5 13.5 %collective-permute-done.7 = bf16[128,2560]{1,0:T(8,128)(2,1)S(1)} collective-permute-done((bf16[128,2560]{1,0:T(8,128)(2,1)S(1)}, bf16[128,2560]{1,0:T(8,128)(2,1)S(1)}, u32[]{:S(2)}, u32[]{:S(2)}) %collective-permute-start.7) | collective-permute-done | bytes 655392 | tf_op jit(solution)/shard_map/ppermute | solution.py:20
  361.0 38.3 %collective-permute-done.3 = bf16[3,2560,128]{1,2,0:T(8,128)(2,1)S(1)} collective-permute-done((bf16[3,2560,128]{1,2,0:T(8,128)(2,1)}, bf16[3,2560,128]{1,2,0:T(8,128)(2,1)S(1)}, u32[]{:S(2)}, u32[]{:S(2)}) %collective-permute-start.3) | collective-permute-done | bytes 1966112 | tf_op jit(solution)/shard_map/ppermute | solution.py:20
  401.7 2.3 maximum_bitcast_fusion
  404.0 6.3 %copy.19 = bf16[1,1,3,5120,128]{4,3,2,1,0:T(8,128)(2,1)} copy(bf16[1,1,3,5120,128]{3,4,2,1,0:T(8,128)(2,1)} %maximum_bitcast_fusion) | data formatting | bytes 7864320
  (145 shorter events, 49.5 us)
Async XLA Ops:
  7.2 89.0 %copy-start = (bf16[1,1,128,5120]{3,2,1,0:T(8,128)(2,1)S(1)}, bf16[1,1,128,5120]{3,2,1,0:T(8,128)(2,1)}, u32[]{:S(2)}) copy-start(bf16[1,1,128,5120]{3,2,1,0:T(8,128)(2,1)} %param.17) | copy-start | bytes 3932164
  7.2 85.2 %all-gather.4.cloned.1.call-start = ((), (), s32[]{:S(2)}) async-start(), calls=%async_computation.2 | async-start | bytes 4915200 | tf_op jit(solution)/shard_map/all_gather | solution.py:54
  13.2 147.5 %reduce-scatter.3.cloned.1.call-start = ((), (), s32[]{:S(2)}) async-start(), calls=%async_computation.3 | async-start | bytes 3276800 | tf_op jit(solution)/shard_map/reduce_scatter | solution.py:59
  92.4 6.3 %copy-start.2 = (bf16[1,1,3,5120,128]{4,3,2,1,0:T(8,128)(2,1)S(1)}, bf16[1,1,3,5120,128]{4,3,2,1,0:T(8,128)(2,1)}, u32[]{:S(2)}) copy-start(bf16[1,1,3,5120,128]{4,3,2,1,0:T(8,128)(2,1)} %param.16) | copy-start | bytes 11796484
  109.7 52.2 %copy-start.27 = (f32[32]{0:T(128)S(1)}, f32[32]{0:T(128)}, u32[]{:S(2)}) copy-start(f32[32]{0:T(128)} %copy-done.26) | copy-start | bytes 388
  109.8 95.4 %all-gather.8.cloned.1.call-start = ((), (), s32[]{:S(2)}) async-start(), calls=%async_computation.5 | async-start | bytes 1638400 | tf_op jit(solution)/shard_map/all_gather | solution.py:54
  160.7 9.9 %copy-start.12 = (bf16[2,32,5120]{2,1,0:T(8,128)(2,1)S(1)}, bf16[2,32,5120]{2,1,0:T(8,128)(2,1)}, u32[]{:S(2)}) copy-start(bf16[2,32,5120]{2,1,0:T(8,128)(2,1)} %reduce-scatter.3.cloned.1.call-done) | copy-start | bytes 1966084
  162.0 22.2 %copy-start.30 = (s32[32]{0:T(128)S(1)}, s32[32]{0:T(128)}, u32[]{:S(2)}) copy-start(s32[32]{0:T(128)} %get-tuple-element.31) | copy-start | bytes 388
  165.0 21.0 %copy-start.14 = (bf16[1,2,32,5120]{3,2,1,0:T(8,128)(2,1)S(1)}, bf16[1,2,32,5120]{3,2,1,0:T(8,128)(2,1)}, u32[]{:S(2)}) copy-start(bf16[1,2,32,5120]{3,2,1,0:T(8,128)(2,1)} %param.21) | copy-start | bytes 1966084
  165.0 10.1 %collective-permute-start = (bf16[32,5120]{1,0:T(8,128)(2,1)S(1)}, bf16[32,5120]{1,0:T(8,128)(2,1)}, u32[]{:S(2)}, u32[]{:S(2)}) collective-permute-start(bf16[32,5120]{1,0:T(8,128)(2,1)S(1)} %broadcast_select_fusion.1), channel_id=1, source_target_pairs={{0,8},{8,16},{16,24},{1,9},{9,17},{17,25},{2,10},{10,18},{18,26},{... | collective-permute-start | bytes 983048 | tf_op jit(solution)/shard_map/ppermute | solution.py:16
  169.3 14.9 %collective-permute-start.1 = (bf16[32,5120]{1,0:T(8,128)(2,1)}, bf16[32,5120]{1,0:T(8,128)(2,1)}, u32[]{:S(2)}, u32[]{:S(2)}) collective-permute-start(bf16[32,5120]{1,0:T(8,128)(2,1)} %get-tuple-element.10), channel_id=1, source_target_pairs={{8,0},{16,8},{24,16},{9,1},{17,9},{25,17},{10,2},{18,10},{26,18},{... | collective-permute-start | bytes 983048 | tf_op jit(solution)/shard_map/ppermute | solution.py:16
  171.7 89.2 %all-gather.6.cloned.1.call-start = ((), (), s32[]{:S(2)}) async-start(), calls=%async_computation.4 | async-start | bytes 3276800 | tf_op jit(solution)/shard_map/all_gather | solution.py:54
  185.9 6.5 %copy-start.18 = (bf16[32,5120]{1,0:T(8,128)(2,1)}, bf16[32,5120]{1,0:T(8,128)(2,1)S(1)}, u32[]{:S(2)}) copy-start(bf16[32,5120]{1,0:T(8,128)(2,1)S(1)} %get-tuple-element.42) | copy-start | bytes 983044
  188.7 221.6 %reduce-scatter.5.cloned.1.call-start = ((), (), s32[]{:S(2)}) async-start(), calls=%async_computation.6 | async-start | bytes 3276800 | tf_op jit(solution)/shard_map/reduce_scatter | solution.py:59
  281.1 62.2 %collective-permute-start.2 = (bf16[3,2560,128]{1,2,0:T(8,128)(2,1)}, bf16[3,2560,128]{1,2,0:T(8,128)(2,1)}, u32[]{:S(2)}, u32[]{:S(2)}) collective-permute-start(bf16[3,2560,128]{1,2,0:T(8,128)(2,1)} %get-tuple-element.15), channel_id=1, source_target_pairs={{0,9},{1,8},{8,1},{9,0},{16,25},{17,24},{24,17},{25,16},{2,11},{3,... | collective-permute-start | bytes 5898248 | tf_op jit(solution)/shard_map/ppermute | solution.py:20
  281.8 62.0 %collective-permute-start.4 = (bf16[3,2560,128]{1,2,0:T(8,128)(2,1)}, bf16[3,2560,128]{1,2,0:T(8,128)(2,1)}, u32[]{:S(2)}, u32[]{:S(2)}) collective-permute-start(bf16[3,2560,128]{1,2,0:T(8,128)(2,1)} %get-tuple-element.16), channel_id=1, source_target_pairs={{0,17},{1,16},{8,25},{9,24},{16,1},{17,0},{24,9},{25,8},{2,19},{3,... | collective-permute-start | bytes 5898248 | tf_op jit(solution)/shard_map/ppermute | solution.py:20
  288.4 52.0 %collective-permute-start.6 = (bf16[128,2560]{1,0:T(8,128)(2,1)S(1)}, bf16[128,2560]{1,0:T(8,128)(2,1)S(1)}, u32[]{:S(2)}, u32[]{:S(2)}) collective-permute-start(bf16[128,2560]{1,0:T(8,128)(2,1)S(1)} %get-tuple-element.19), channel_id=1, source_target_pairs={{0,9},{1,8},{8,1},{9,0},{16,25},{17,24},{24,17},{25,16},{2,11},{3,... | collective-permute-start | bytes 1966088 | tf_op jit(solution)/shard_map/ppermute | solution.py:20
  288.5 112.0 %copy-start.4 = (bf16[3,5120,128]{1,2,0:T(8,128)(2,1)S(1)}, bf16[3,5120,128]{1,2,0:T(8,128)(2,1)}, u32[]{:S(2)}) copy-start(bf16[3,5120,128]{1,2,0:T(8,128)(2,1)} %copy-done.3) | copy-start | bytes 11796484
  288.5 53.4 %collective-permute-start.8 = (bf16[128,2560]{1,0:T(8,128)(2,1)S(1)}, bf16[128,2560]{1,0:T(8,128)(2,1)S(1)}, u32[]{:S(2)}, u32[]{:S(2)}) collective-permute-start(bf16[128,2560]{1,0:T(8,128)(2,1)S(1)} %get-tuple-element.20), channel_id=1, source_target_pairs={{0,17},{1,16},{8,25},{9,24},{16,1},{17,0},{24,9},{25,8},{2,19},{3,... | collective-permute-start | bytes 1966088 | tf_op jit(solution)/shard_map/ppermute | solution.py:20
  340.4 17.6 %collective-permute-start.7 = (bf16[128,2560]{1,0:T(8,128)(2,1)S(1)}, bf16[128,2560]{1,0:T(8,128)(2,1)S(1)}, u32[]{:S(2)}, u32[]{:S(2)}) collective-permute-start(bf16[128,2560]{1,0:T(8,128)(2,1)S(1)} %collective-permute-done.6), channel_id=1, source_target_pairs={{0,16},{1,17},{8,24},{9,25},{16,0},{17,1},{24,8},{25,9},{2,18},{3,... | collective-permute-start | bytes 1966088 | tf_op jit(solution)/shard_map/ppermute | solution.py:20
  341.9 17.6 %collective-permute-start.9 = (bf16[128,2560]{1,0:T(8,128)(2,1)S(1)}, bf16[128,2560]{1,0:T(8,128)(2,1)S(1)}, u32[]{:S(2)}, u32[]{:S(2)}) collective-permute-start(bf16[128,2560]{1,0:T(8,128)(2,1)S(1)} %collective-permute-done.8), channel_id=1, source_target_pairs={{0,8},{1,9},{8,0},{9,1},{16,24},{17,25},{24,16},{25,17},{2,10},{3,... | collective-permute-start | bytes 1966088 | tf_op jit(solution)/shard_map/ppermute | solution.py:20
  343.2 56.1 %collective-permute-start.3 = (bf16[3,2560,128]{1,2,0:T(8,128)(2,1)}, bf16[3,2560,128]{1,2,0:T(8,128)(2,1)S(1)}, u32[]{:S(2)}, u32[]{:S(2)}) collective-permute-start(bf16[3,2560,128]{1,2,0:T(8,128)(2,1)} %collective-permute-done.2), channel_id=1, source_target_pairs={{0,16},{1,17},{8,24},{9,25},{16,0},{17,1},{24,8},{25,9},{2,18},{3,... | collective-permute-start | bytes 5898248 | tf_op jit(solution)/shard_map/ppermute | solution.py:20
  343.8 56.7 %collective-permute-start.5 = (bf16[3,2560,128]{1,2,0:T(8,128)(2,1)}, bf16[3,2560,128]{1,2,0:T(8,128)(2,1)S(1)}, u32[]{:S(2)}, u32[]{:S(2)}) collective-permute-start(bf16[3,2560,128]{1,2,0:T(8,128)(2,1)} %collective-permute-done.4), channel_id=1, source_target_pairs={{0,8},{1,9},{8,0},{9,1},{16,24},{17,25},{24,16},{25,17},{2,10},{3,... | collective-permute-start | bytes 5898248 | tf_op jit(solution)/shard_map/ppermute | solution.py:20
  404.0 7.7 %copy-start.11 = (bf16[32,5120]{1,0:T(8,128)(2,1)S(1)}, bf16[32,5120]{1,0:T(8,128)(2,1)}, u32[]{:S(2)}) copy-start(bf16[32,5120]{1,0:T(8,128)(2,1)} %copy-done.10) | copy-start | bytes 983044
  (22 other events, 65.9 us)
Sparse Core Ops, SparseCore 0:
  13.3 79.1 all-gather.3
  109.9 50.7 reduce-scatter.2
  171.9 33.1 all-gather.7
  207.1 53.8 all-gather.5
  285.6 49.1 reduce-scatter.4

commit v2 on v1

--- a/solution.py
+++ b/solution.py
@@ -129,9 +129,19 @@
         d_input = pull_norm(d_normed.astype(jnp.float32))[0]
         return (upstream.astype(jnp.float32) + d_input).astype(jnp.bfloat16)
 
+    pair_axes = ("section", "mirror")
+    mirror_size = lax.axis_size("mirror")
+    up_pairs = []
+    down_pairs = []
+    for section in range(sections):
+        for mirror in range(mirror_size):
+            ahead = 1 if mirror == 0 else -1
+            if 0 <= section + ahead < sections:
+                up_pairs.append((section * mirror_size + mirror, (section + ahead) * mirror_size + mirror))
+            if 0 <= section - ahead < sections:
+                down_pairs.append((section * mirror_size + mirror, (section - ahead) * mirror_size + mirror))
+
     saved_normed = [normed_rows(saved[0, 0, t]) for t in range(window_steps)]
-    saved_full = [None] + [gathered([saved_normed[t]])[0] for t in range(1, window_steps)]
-
     forward_in = carry_acts[0, 0]
     backward_in = grad_in[0, 0]
     forward_outs = []
@@ -142,38 +152,38 @@
         embedded = embedding(feats[0, step_index], types[0, step_index], type_table)
         current = jnp.where(position == 0, embedded, forward_in)
         upstream = jnp.where(position == sections - 1, cotangent[0, step_index], backward_in)
-        to_gather = [normed_rows(current), upstream]
         if step_index == 0:
-            to_gather.append(saved_normed[0])
-        gathered_rows = gathered(to_gather)
-        forward_normed_full, upstream_full = gathered_rows[0], gathered_rows[1]
-        backward_normed_full = gathered_rows[2] if step_index == 0 else saved_full[step_index]
+            upstream_full, backward_normed_full, forward_normed_full = gathered(
+                [upstream, saved_normed[0], normed_rows(current)]
+            )
+        else:
+            upstream_full, backward_normed_full = gathered([upstream, saved_normed[step_index]])
+        if step_index > 0:
+            forward_normed, backward_normed_full = lax.optimization_barrier(
+                (normed_rows(current), backward_normed_full)
+            )
+            forward_normed_full = gathered([forward_normed])[0]
+        d_normed_part, qkv_term, out_term = backward_part(
+            backward_normed_full, upstream_full, mask_for(1, step_index + position)
+        )
+        qkv_total = qkv_total + qkv_term
+        out_total = out_total + out_term
         attn_part = forward_part(
             forward_normed_full, mask_for(0, step_index - position + sections - 1)
         )
-        d_normed_part, qkv_term, out_term = backward_part(
-            backward_normed_full, upstream_full, mask_for(1, step_index + position)
-        )
-        attn_rows, d_normed = scattered([attn_part, d_normed_part])
+        d_normed, attn_rows = scattered([d_normed_part, attn_part])
         forward_out = (current.astype(jnp.float32) + attn_rows.astype(jnp.float32)).astype(
             jnp.bfloat16
         )
         backward_out = input_grad(saved[0, 0, step_index], upstream, d_normed)
-        qkv_total = qkv_total + qkv_term
-        out_total = out_total + out_term
         forward_outs.append(forward_out)
         backward_outs.append(backward_out)
         if step_index + 1 < window_steps:
-            toward_higher = jnp.where(on_first_pipe, forward_out, backward_out)
-            toward_lower = jnp.where(on_first_pipe, backward_out, forward_out)
-            from_lower = passed_along(toward_higher, "section", 1)
-            from_upper = passed_along(toward_lower, "section", -1)
-            forward_in = jnp.where(on_first_pipe, from_lower, from_upper)
-            backward_in = jnp.where(on_first_pipe, from_upper, from_lower)
+            forward_in = lax.ppermute(forward_out, pair_axes, up_pairs)
+            backward_in = lax.ppermute(backward_out, pair_axes, down_pairs)
 
     own_qkv = qkv_total.astype(jnp.bfloat16)
     own_out = out_total.astype(jnp.bfloat16)
-    pair_axes = ("section", "mirror")
     bit_count = lax.axis_size(pair_axes).bit_length() - 1
     section_bits = list(range(1, bit_count))
     if section_bits:

time: 422 us -> 387 us (0.917)
  waiting for transfers between devices: 307 us -> 271 us
    ppermute x8, waiting for transfers between devices: 106 us -> 81.9 us  [flipped(): lax.ppermute(value, axis, [(i, i ^ mask) for i in range(lax.axis_size(axi...]
    all_gather x3, waiting for transfers between devices: 138 us -> 129 us  [gathered(): full = lax.all_gather(jnp.stack(blocks), 'tp', axis=1, tiled=True)]
    unnamed x63 -> x59, local copies, waits for them, and re-layouts: 9.89 us -> 10 us
  transfers between devices with their start and end apart: 15 -> 15, of which waited for: 11 -> 10; matrix products, arithmetic and copies ran while one was open for 8% -> 13% of each run, Pallas kernels for 0% -> 0%
where the time goes in v2:
time: 387 us; the launch traced here: 386 us
  waiting for transfers between devices  271 us (70%)
  matrix products  46.2 us (12%)
  other arithmetic  23.9 us (6%)
  starting transfers between devices  15.2 us (4%)
  local copies, waits for them, and re-layouts  15.1 us (4%)
  between operations  14.3 us (4%)
    all_gather x3, waiting for transfers between devices, gathered(): full = lax.all_gather(jnp.stack(blocks), 'tp', axis=1, tiled=True)  129 us
    ppermute x8, waiting for transfers between devices, flipped(): lax.ppermute(value, axis, [(i, i ^ mask) for i in range(lax.axis_size(axi...  81.9 us
    reduce_scatter x2, waiting for transfers between devices, scattered(): lax.psum_scatter(jnp.stack(blocks), 'tp', scatter_dimension=1, tiled=True)  50.9 us
    dot_general x4, matrix products, heads_of(): jnp.einsum('sd,cdn->csn', normed_full, qkv_weight, preferred_element_type...  12.1 us
    dot_general x2, matrix products, backward_part(): jnp.einsum('sd,csn->cdn', normed_full, d_projected, preferred_element_typ...  10.3 us
    unnamed x59, local copies, waits for them, and re-layouts  10 us
    ppermute x1, waiting for transfers between devices, shards(): backward_in = lax.ppermute(backward_out, pair_axes, down_pairs)  9.48 us
    ppermute x8, starting transfers between devices, flipped(): lax.ppermute(value, axis, [(i, i ^ mask) for i in range(lax.axis_size(axi...  9.47 us
  transfers between devices with their start and end apart: 15, of which 10 were waited for; matrix products, arithmetic and copies ran while one was open for 13% of the time, Pallas kernels for 0%

profile of v2, /device:TPU:0, one launch (start us, length us, event | category | flops | bytes accessed | tf_op | source)
XLA Modules:
  0.0 386.0 jit_solution(7261278978023303913)
XLA Ops:
  13.1 78.7 %all-gather.5.cloned.1.call-done = bf16[3,128,5120]{2,1,0:T(8,128)(2,1)} async-done(((bf16[3,32,5120]{2,1,0:T(8,128)(2,1)}), bf16[3,128,5120]{2,1,0:T(8,128)(2,1)}) %all-gather.5.cloned.1.call-update) | async-done | bytes 3932176 | tf_op jit(solution)/shard_map/all_gather | solution.py:54
  91.8 3.5 fusion.64
  101.3 2.5 fusion.6
  103.8 3.6 fusion.5
  109.2 50.9 %reduce-scatter.3.cloned.1.call-done = bf16[2,32,5120]{2,1,0:T(8,128)(2,1)} async-done(((bf16[2,128,5120]{2,1,0:T(8,128)(2,1)}), bf16[2,32,5120]{2,1,0:T(8,128)(2,1)}) %reduce-scatter.3.cloned.1.call-update) | async-done | bytes 655376 | tf_op jit(solution)/shard_map/reduce_scatter | solution.py:59
  161.4 2.3 fusion.116
  166.1 9.5 %collective-permute-done.1 = bf16[32,5120]{1,0:T(8,128)(2,1)S(1)} collective-permute-done((bf16[32,5120]{1,0:T(8,128)(2,1)S(1)}, bf16[32,5120]{1,0:T(8,128)(2,1)S(1)}, u32[]{:S(2)}, u32[]{:S(2)}) %collective-permute-start.1) | collective-permute-done | bytes 327712 | tf_op jit(solution)/shard_map/ppermute | solution.py:183
  176.6 4.1 %collective-permute-start = (bf16[32,5120]{1,0:T(8,128)(2,1)S(1)}, bf16[32,5120]{1,0:T(8,128)(2,1)}, u32[]{:S(2)}, u32[]{:S(2)}) collective-permute-start(bf16[32,5120]{1,0:T(8,128)(2,1)S(1)} %copy-done.17), channel_id=1, source_target_pairs={{0,8},{8,16},{9,1},{16,24},{17,9},{25,17},{2,10},{10,18},{11,3},{1... | collective-permute-start | bytes 983048 | tf_op jit(solution)/shard_map/ppermute | solution.py:182
  180.7 5.6 %fusion.34 = f32[3,128,5120]{2,1,0:T(8,128)} fusion(bf16[3,128,5120]{2,1,0:T(8,128)(2,1)} %all-gather.5.cloned.1.call-done, bf16[1,128,1,128]{3,1,2,0:T(8,128)(2,1)S(1)} %fusion.87, bf16[1,128,1,128]{3,1,2,0:T(8,128)(2,1)S(1)} %fusion.80, bf16[1,128,1,128]{3,1,2,0:T(8,128)(2,1)S(1)} %fusion.79), kind=kOutput, calls=%fused_computation.55 | convolution fusion | flops 503414784 | bytes 9273344 | tf_op jit(solution)/shard_map/sd,csn->cdn/dot_general | solution.py:119
  186.3 3.5 fusion.33
  192.9 37.5 %all-gather.7.cloned.1.call-done = bf16[2,128,5120]{2,1,0:T(8,128)(2,1)} async-done(((bf16[2,32,5120]{2,1,0:T(8,128)(2,1)}), bf16[2,128,5120]{2,1,0:T(8,128)(2,1)}) %all-gather.7.cloned.1.call-update) | async-done | bytes 2621456 | tf_op jit(solution)/shard_map/all_gather | solution.py:54
  232.1 3.1 fusion.56
  236.7 4.7 %fusion = bf16[3,5120,128]{1,2,0:T(8,128)(2,1)S(1)} fusion(f32[3,128,5120]{2,1,0:T(8,128)} %fusion.34, bf16[128,5120]{1,0:T(8,128)(2,1)S(1)} %slice_bitcast_fusion, bf16[1,128,1,128]{3,1,2,0:T(8,128)(2,1)S(1)} %fusion.88, bf16[1,128,1,128]{3,1,2,0:T(8,128)(2,1)S(1)} %fusion.83, bf16[1,128,1,128]{3,1,2,0:T(8,128)(2,1)S(1)} %fusion.82), kind=kOutput, calls=%fused_computation.1 | convolution fusion | flops 507346944 | bytes 13205504 | tf_op jit(solution)/shard_map/sd,csn->cdn/dot_general | solution.py:119
  248.1 2.4 fusion.4
  250.5 12.8 %all-gather.9.cloned.1.call-done = bf16[128,5120]{1,0:T(8,128)(2,1)} async-done(((bf16[32,5120]{1,0:T(8,128)(2,1)}), bf16[128,5120]{1,0:T(8,128)(2,1)}) %all-gather.9.cloned.1.call-update) | async-done | bytes 1310736 | tf_op jit(solution)/shard_map/all_gather | solution.py:54
  263.3 3.4 fusion.51
  268.9 3.1 pad_maximum_fusion.1
  272.0 2.8 fusion.1
  275.1 2.4 collective-permute-start.8
  277.6 27.1 %collective-permute-done.6 = bf16[128,2560]{1,0:T(8,128)(2,1)S(1)} collective-permute-done((bf16[128,2560]{1,0:T(8,128)(2,1)S(1)}, bf16[128,2560]{1,0:T(8,128)(2,1)S(1)}, u32[]{:S(2)}, u32[]{:S(2)}) %collective-permute-start.6) | collective-permute-done | bytes 655392 | tf_op jit(solution)/shard_map/ppermute | solution.py:20
  308.8 13.5 %collective-permute-done.7 = bf16[128,2560]{1,0:T(8,128)(2,1)S(1)} collective-permute-done((bf16[128,2560]{1,0:T(8,128)(2,1)S(1)}, bf16[128,2560]{1,0:T(8,128)(2,1)S(1)}, u32[]{:S(2)}, u32[]{:S(2)}) %collective-permute-start.7) | collective-permute-done | bytes 655392 | tf_op jit(solution)/shard_map/ppermute | solution.py:20
  325.4 38.4 %collective-permute-done.3 = bf16[3,2560,128]{1,2,0:T(8,128)(2,1)S(1)} collective-permute-done((bf16[3,2560,128]{1,2,0:T(8,128)(2,1)}, bf16[3,2560,128]{1,2,0:T(8,128)(2,1)S(1)}, u32[]{:S(2)}, u32[]{:S(2)}) %collective-permute-start.3) | collective-permute-done | bytes 1966112 | tf_op jit(solution)/shard_map/ppermute | solution.py:20
  366.2 2.3 maximum_bitcast_fusion
  368.5 6.4 %copy.19 = bf16[1,1,3,5120,128]{4,3,2,1,0:T(8,128)(2,1)} copy(bf16[1,1,3,5120,128]{3,4,2,1,0:T(8,128)(2,1)} %maximum_bitcast_fusion) | data formatting | bytes 7864320
  (141 shorter events, 47.6 us)
Async XLA Ops:
  7.2 88.4 %copy-start = (bf16[1,1,128,5120]{3,2,1,0:T(8,128)(2,1)S(1)}, bf16[1,1,128,5120]{3,2,1,0:T(8,128)(2,1)}, u32[]{:S(2)}) copy-start(bf16[1,1,128,5120]{3,2,1,0:T(8,128)(2,1)} %param.17) | copy-start | bytes 3932164
  7.2 84.6 %all-gather.5.cloned.1.call-start = ((), (), s32[]{:S(2)}) async-start(), calls=%async_computation.2 | async-start | bytes 4915200 | tf_op jit(solution)/shard_map/all_gather | solution.py:54
  12.5 147.5 %reduce-scatter.3.cloned.1.call-start = ((), (), s32[]{:S(2)}) async-start(), calls=%async_computation.3 | async-start | bytes 3276800 | tf_op jit(solution)/shard_map/reduce_scatter | solution.py:59
  109.1 52.3 %copy-start.26 = (f32[32]{0:T(128)S(1)}, f32[32]{0:T(128)}, u32[]{:S(2)}) copy-start(f32[32]{0:T(128)} %copy-done.25) | copy-start | bytes 388
  109.2 121.3 %all-gather.7.cloned.1.call-start = ((), (), s32[]{:S(2)}) async-start(), calls=%async_computation.4 | async-start | bytes 3276800 | tf_op jit(solution)/shard_map/all_gather | solution.py:54
  161.4 14.1 %copy-start.10 = (bf16[1,2,32,5120]{3,2,1,0:T(8,128)(2,1)S(1)}, bf16[1,2,32,5120]{3,2,1,0:T(8,128)(2,1)}, u32[]{:S(2)}) copy-start(bf16[1,2,32,5120]{3,2,1,0:T(8,128)(2,1)} %param.21) | copy-start | bytes 1966084
  163.7 11.8 %collective-permute-start.1 = (bf16[32,5120]{1,0:T(8,128)(2,1)S(1)}, bf16[32,5120]{1,0:T(8,128)(2,1)S(1)}, u32[]{:S(2)}, u32[]{:S(2)}) collective-permute-start(bf16[32,5120]{1,0:T(8,128)(2,1)S(1)} %get-tuple-element.26), channel_id=1, source_target_pairs={{1,9},{8,0},{9,17},{16,8},{17,25},{24,16},{3,11},{10,2},{11,19},{1... | collective-permute-start | bytes 983048 | tf_op jit(solution)/shard_map/ppermute | solution.py:183
  166.1 10.5 %copy-start.17 = (bf16[32,5120]{1,0:T(8,128)(2,1)S(1)}, bf16[32,5120]{1,0:T(8,128)(2,1)}, u32[]{:S(2)}) copy-start(bf16[32,5120]{1,0:T(8,128)(2,1)} %get-tuple-element.27) | copy-start | bytes 983044
  175.6 10.7 %copy-start.20 = (bf16[32,5120]{1,0:T(8,128)(2,1)}, bf16[32,5120]{1,0:T(8,128)(2,1)S(1)}, u32[]{:S(2)}) copy-start(bf16[32,5120]{1,0:T(8,128)(2,1)S(1)} %collective-permute-done.1) | copy-start | bytes 983044
  176.5 86.8 %all-gather.9.cloned.1.call-start = ((), (), s32[]{:S(2)}) async-start(), calls=%async_computation.6 | async-start | bytes 1638400 | tf_op jit(solution)/shard_map/all_gather | solution.py:54
  176.6 13.2 %collective-permute-start = (bf16[32,5120]{1,0:T(8,128)(2,1)S(1)}, bf16[32,5120]{1,0:T(8,128)(2,1)}, u32[]{:S(2)}, u32[]{:S(2)}) collective-permute-start(bf16[32,5120]{1,0:T(8,128)(2,1)S(1)} %copy-done.17), channel_id=1, source_target_pairs={{0,8},{8,16},{9,1},{16,24},{17,9},{25,17},{2,10},{10,18},{11,3},{1... | collective-permute-start | bytes 983048 | tf_op jit(solution)/shard_map/ppermute | solution.py:182
  231.9 143.0 %reduce-scatter.5.cloned.1.call-start = ((), (), s32[]{:S(2)}) async-start(), calls=%async_computation.5 | async-start | bytes 3276800 | tf_op jit(solution)/shard_map/reduce_scatter | solution.py:59
  245.4 62.1 %collective-permute-start.2 = (bf16[3,2560,128]{1,2,0:T(8,128)(2,1)}, bf16[3,2560,128]{1,2,0:T(8,128)(2,1)}, u32[]{:S(2)}, u32[]{:S(2)}) collective-permute-start(bf16[3,2560,128]{1,2,0:T(8,128)(2,1)} %get-tuple-element.16), channel_id=1, source_target_pairs={{0,9},{1,8},{8,1},{9,0},{16,25},{17,24},{24,17},{25,16},{2,11},{3,... | collective-permute-start | bytes 5898248 | tf_op jit(solution)/shard_map/ppermute | solution.py:20
  246.1 62.0 %collective-permute-start.4 = (bf16[3,2560,128]{1,2,0:T(8,128)(2,1)}, bf16[3,2560,128]{1,2,0:T(8,128)(2,1)}, u32[]{:S(2)}, u32[]{:S(2)}) collective-permute-start(bf16[3,2560,128]{1,2,0:T(8,128)(2,1)} %get-tuple-element.17), channel_id=1, source_target_pairs={{0,17},{1,16},{8,25},{9,24},{16,1},{17,0},{24,9},{25,8},{2,19},{3,... | collective-permute-start | bytes 5898248 | tf_op jit(solution)/shard_map/ppermute | solution.py:20
  250.5 16.2 %copy-start.27 = (s32[128]{0:T(128)S(1)}, s32[128]{0:T(128)}, u32[]{:S(2)}) copy-start(s32[128]{0:T(128)} %get-tuple-element.53) | copy-start | bytes 1540
  274.9 29.8 %collective-permute-start.6 = (bf16[128,2560]{1,0:T(8,128)(2,1)S(1)}, bf16[128,2560]{1,0:T(8,128)(2,1)S(1)}, u32[]{:S(2)}, u32[]{:S(2)}) collective-permute-start(bf16[128,2560]{1,0:T(8,128)(2,1)S(1)} %get-tuple-element.20), channel_id=1, source_target_pairs={{0,9},{1,8},{8,1},{9,0},{16,25},{17,24},{24,17},{25,16},{2,11},{3,... | collective-permute-start | bytes 1966088 | tf_op jit(solution)/shard_map/ppermute | solution.py:20
  275.1 31.2 %collective-permute-start.8 = (bf16[128,2560]{1,0:T(8,128)(2,1)S(1)}, bf16[128,2560]{1,0:T(8,128)(2,1)S(1)}, u32[]{:S(2)}, u32[]{:S(2)}) collective-permute-start(bf16[128,2560]{1,0:T(8,128)(2,1)S(1)} %get-tuple-element.21), channel_id=1, source_target_pairs={{0,17},{1,16},{8,25},{9,24},{16,1},{17,0},{24,9},{25,8},{2,19},{3,... | collective-permute-start | bytes 1966088 | tf_op jit(solution)/shard_map/ppermute | solution.py:20
  304.7 17.6 %collective-permute-start.7 = (bf16[128,2560]{1,0:T(8,128)(2,1)S(1)}, bf16[128,2560]{1,0:T(8,128)(2,1)S(1)}, u32[]{:S(2)}, u32[]{:S(2)}) collective-permute-start(bf16[128,2560]{1,0:T(8,128)(2,1)S(1)} %collective-permute-done.6), channel_id=1, source_target_pairs={{0,16},{1,17},{8,24},{9,25},{16,0},{17,1},{24,8},{25,9},{2,18},{3,... | collective-permute-start | bytes 1966088 | tf_op jit(solution)/shard_map/ppermute | solution.py:20
  306.3 17.6 %collective-permute-start.9 = (bf16[128,2560]{1,0:T(8,128)(2,1)S(1)}, bf16[128,2560]{1,0:T(8,128)(2,1)S(1)}, u32[]{:S(2)}, u32[]{:S(2)}) collective-permute-start(bf16[128,2560]{1,0:T(8,128)(2,1)S(1)} %collective-permute-done.8), channel_id=1, source_target_pairs={{0,8},{1,9},{8,0},{9,1},{16,24},{17,25},{24,16},{25,17},{2,10},{3,... | collective-permute-start | bytes 1966088 | tf_op jit(solution)/shard_map/ppermute | solution.py:20
  307.5 56.2 %collective-permute-start.3 = (bf16[3,2560,128]{1,2,0:T(8,128)(2,1)}, bf16[3,2560,128]{1,2,0:T(8,128)(2,1)S(1)}, u32[]{:S(2)}, u32[]{:S(2)}) collective-permute-start(bf16[3,2560,128]{1,2,0:T(8,128)(2,1)} %collective-permute-done.2), channel_id=1, source_target_pairs={{0,16},{1,17},{8,24},{9,25},{16,0},{17,1},{24,8},{25,9},{2,18},{3,... | collective-permute-start | bytes 5898248 | tf_op jit(solution)/shard_map/ppermute | solution.py:20
  308.1 56.9 %collective-permute-start.5 = (bf16[3,2560,128]{1,2,0:T(8,128)(2,1)}, bf16[3,2560,128]{1,2,0:T(8,128)(2,1)S(1)}, u32[]{:S(2)}, u32[]{:S(2)}) collective-permute-start(bf16[3,2560,128]{1,2,0:T(8,128)(2,1)} %collective-permute-done.4), channel_id=1, source_target_pairs={{0,8},{1,9},{8,0},{9,1},{16,24},{17,25},{24,16},{25,17},{2,10},{3,... | collective-permute-start | bytes 5898248 | tf_op jit(solution)/shard_map/ppermute | solution.py:20
  323.9 41.1 %copy-start.4 = (bf16[3,5120,128]{1,2,0:T(8,128)(2,1)S(1)}, bf16[3,5120,128]{1,2,0:T(8,128)(2,1)}, u32[]{:S(2)}) copy-start(bf16[3,5120,128]{1,2,0:T(8,128)(2,1)} %copy-done.3) | copy-start | bytes 11796484
  368.5 7.6 %copy-start.7 = (f32[32,5120]{1,0:T(8,128)S(1)}, f32[32,5120]{1,0:T(8,128)}, u32[]{:S(2)}) copy-start(f32[32,5120]{1,0:T(8,128)} %copy-done.6) | copy-start | bytes 1966084
  368.5 7.6 %copy-start.11 = (bf16[1,2,32,5120]{3,2,1,0:T(8,128)(2,1)S(1)}, bf16[1,2,32,5120]{3,2,1,0:T(8,128)(2,1)}, u32[]{:S(2)}) copy-start(bf16[1,2,32,5120]{3,2,1,0:T(8,128)(2,1)} %param.21) | copy-start | bytes 1966084
  (20 other events, 67.6 us)
Sparse Core Ops, SparseCore 0:
  12.7 79.1 all-gather.4
  109.3 50.7 reduce-scatter.2
  176.7 53.7 all-gather.6
  232.0 31.3 all-gather.8
  272.1 51.3 reduce-scatter.4

commit v3 on v2

--- a/solution.py
+++ b/solution.py
@@ -141,46 +141,72 @@
             if 0 <= section - ahead < sections:
                 down_pairs.append((section * mirror_size + mirror, (section - ahead) * mirror_size + mirror))
 
+    last_step = window_steps - 1
     saved_normed = [normed_rows(saved[0, 0, t]) for t in range(window_steps)]
-    forward_in = carry_acts[0, 0]
-    backward_in = grad_in[0, 0]
-    forward_outs = []
-    backward_outs = []
     qkv_total = jnp.zeros(qkv_weight.shape, jnp.float32)
     out_total = jnp.zeros(out_weight.shape, jnp.float32)
+
+    backward_outs = []
+    backward_in = grad_in[0, 0]
+    backward_normed_full = [None] * window_steps
+    forward_normed_first = None
+    for step_index in range(window_steps):
+        upstream = jnp.where(position == sections - 1, cotangent[0, step_index], backward_in)
+        if step_index == 0:
+            upstream_full, backward_normed_full[0] = gathered([upstream, saved_normed[0]])
+        else:
+            upstream, ready = lax.optimization_barrier((upstream, ready))
+            upstream_full = gathered([upstream])[0]
+        d_normed_part, qkv_term, out_term = backward_part(
+            backward_normed_full[step_index], upstream_full, mask_for(1, step_index + position)
+        )
+        qkv_total = qkv_total + qkv_term
+        out_total = out_total + out_term
+        if step_index == last_step:
+            last_d_normed_part = d_normed_part
+            last_upstream = upstream
+            last_upstream_full = upstream_full
+            break
+        d_normed = scattered([d_normed_part])[0]
+        if step_index == 0:
+            first_forward_in = jnp.where(
+                position == 0, embedding(feats[0, 0], types[0, 0], type_table), carry_acts[0, 0]
+            )
+            rest, d_normed = lax.optimization_barrier(
+                (saved_normed[1:] + [normed_rows(first_forward_in)], d_normed)
+            )
+            ready = gathered(rest)
+            backward_normed_full[1:] = ready[:-1]
+            forward_normed_first = ready[-1]
+        backward_out = input_grad(saved[0, 0, step_index], upstream, d_normed)
+        backward_outs.append(backward_out)
+        backward_in = lax.ppermute(backward_out, pair_axes, down_pairs)
+
+    forward_outs = []
+    forward_in = carry_acts[0, 0]
     for step_index in range(window_steps):
         embedded = embedding(feats[0, step_index], types[0, step_index], type_table)
         current = jnp.where(position == 0, embedded, forward_in)
-        upstream = jnp.where(position == sections - 1, cotangent[0, step_index], backward_in)
         if step_index == 0:
-            upstream_full, backward_normed_full, forward_normed_full = gathered(
-                [upstream, saved_normed[0], normed_rows(current)]
+            forward_normed_full, last_upstream_full = lax.optimization_barrier(
+                (forward_normed_first, last_upstream_full)
             )
         else:
-            upstream_full, backward_normed_full = gathered([upstream, saved_normed[step_index]])
-        if step_index > 0:
-            forward_normed, backward_normed_full = lax.optimization_barrier(
-                (normed_rows(current), backward_normed_full)
-            )
-            forward_normed_full = gathered([forward_normed])[0]
-        d_normed_part, qkv_term, out_term = backward_part(
-            backward_normed_full, upstream_full, mask_for(1, step_index + position)
-        )
-        qkv_total = qkv_total + qkv_term
-        out_total = out_total + out_term
+            forward_normed_full = gathered([normed_rows(current)])[0]
         attn_part = forward_part(
             forward_normed_full, mask_for(0, step_index - position + sections - 1)
         )
-        d_normed, attn_rows = scattered([d_normed_part, attn_part])
+        if step_index == last_step:
+            attn_rows, d_normed = scattered([attn_part, last_d_normed_part])
+            backward_outs.append(input_grad(saved[0, 0, last_step], last_upstream, d_normed))
+        else:
+            attn_rows = scattered([attn_part])[0]
         forward_out = (current.astype(jnp.float32) + attn_rows.astype(jnp.float32)).astype(
             jnp.bfloat16
         )
-        backward_out = input_grad(saved[0, 0, step_index], upstream, d_normed)
         forward_outs.append(forward_out)
-        backward_outs.append(backward_out)
-        if step_index + 1 < window_steps:
+        if step_index < last_step:
             forward_in = lax.ppermute(forward_out, pair_axes, up_pairs)
-            backward_in = lax.ppermute(backward_out, pair_axes, down_pairs)
 
     own_qkv = qkv_total.astype(jnp.bfloat16)
     own_out = out_total.astype(jnp.bfloat16)

time: 387 us -> 402 us (1.039)
  waiting for transfers between devices: 271 us -> 281 us
    all_gather x3 -> x4, waiting for transfers between devices: 129 us -> 143 us  [gathered(): full = lax.all_gather(jnp.stack(blocks), 'tp', axis=1, tiled=True)]
    ppermute x8, waiting for transfers between devices: 81.9 us -> 76.2 us  [flipped(): lax.ppermute(value, axis, [(i, i ^ mask) for i in range(lax.axis_size(axi...]
    ppermute x8, starting transfers between devices: 9.47 us -> 13.8 us  [flipped(): lax.ppermute(value, axis, [(i, i ^ mask) for i in range(lax.axis_size(axi...]
    reduce_scatter x2 -> x3, waiting for transfers between devices: 50.9 us -> 46.6 us  [scattered(): lax.psum_scatter(jnp.stack(blocks), 'tp', scatter_dimension=1, tiled=True)]
    ppermute x1, waiting for transfers between devices: 0.01 us -> 4.27 us  [shards(): forward_in = lax.ppermute(forward_out, pair_axes, up_pairs)]
    unnamed x59 -> x53, local copies, waits for them, and re-layouts: 10 us -> 11 us
  transfers between devices with their start and end apart: 15 -> 17, of which waited for: 10 -> 13; matrix products, arithmetic and copies ran while one was open for 13% -> 13% of each run, Pallas kernels for 0% -> 0%
where the time goes in v3:
time: 402 us; the launch traced here: 401 us
  waiting for transfers between devices  281 us (70%)
  matrix products  44 us (11%)
  other arithmetic  25.9 us (6%)
  starting transfers between devices  19 us (5%)
  local copies, waits for them, and re-layouts  16.9 us (4%)
  between operations  14.6 us (4%)
    all_gather x4, waiting for transfers between devices, gathered(): full = lax.all_gather(jnp.stack(blocks), 'tp', axis=1, tiled=True)  143 us
    ppermute x8, waiting for transfers between devices, flipped(): lax.ppermute(value, axis, [(i, i ^ mask) for i in range(lax.axis_size(axi...  76.2 us
    reduce_scatter x3, waiting for transfers between devices, scattered(): lax.psum_scatter(jnp.stack(blocks), 'tp', scatter_dimension=1, tiled=True)  46.6 us
    ppermute x8, starting transfers between devices, flipped(): lax.ppermute(value, axis, [(i, i ^ mask) for i in range(lax.axis_size(axi...  13.8 us
    dot_general x4, matrix products, heads_of(): jnp.einsum('sd,cdn->csn', normed_full, qkv_weight, preferred_element_type...  11 us
    unnamed x53, local copies, waits for them, and re-layouts  11 us
    dot_general x2, matrix products, backward_part(): jnp.einsum('sd,csn->cdn', normed_full, d_projected, preferred_element_typ...  10.6 us
    ppermute x1, waiting for transfers between devices, shards(): backward_in = lax.ppermute(backward_out, pair_axes, down_pairs)  10.6 us
  transfers between devices with their start and end apart: 17, of which 13 were waited for; matrix products, arithmetic and copies ran while one was open for 13% of the time, Pallas kernels for 0%

profile of v3, /device:TPU:0, one launch (start us, length us, event | category | flops | bytes accessed | tf_op | source)
XLA Modules:
  0.0 400.8 jit_solution(17342441569960381355)
XLA Ops:
  11.9 57.4 %all-gather.7.cloned.1.call-done = bf16[2,128,5120]{2,1,0:T(8,128)(2,1)} async-done(((bf16[2,32,5120]{2,1,0:T(8,128)(2,1)}), bf16[2,128,5120]{2,1,0:T(8,128)(2,1)}) %all-gather.7.cloned.1.call-update) | async-done | bytes 2621456 | tf_op jit(solution)/shard_map/all_gather | solution.py:54
  69.4 3.5 fusion.63
  81.3 27.1 %reduce-scatter.4.cloned.1.call-done = bf16[1,32,5120]{2,1,0:T(8,128)(2,1)} async-done(((bf16[1,128,5120]{2,1,0:T(8,128)(2,1)}), bf16[1,32,5120]{2,1,0:T(8,128)(2,1)}) %reduce-scatter.4.cloned.1.call-update) | async-done | bytes 327696 | tf_op jit(solution)/shard_map/reduce_scatter | solution.py:59
  115.2 10.6 %collective-permute-done = bf16[32,5120]{1,0:T(8,128)(2,1)S(1)} collective-permute-done((bf16[32,5120]{1,0:T(8,128)(2,1)S(1)}, bf16[32,5120]{1,0:T(8,128)(2,1)S(1)}, u32[]{:S(2)}, u32[]{:S(2)}) %collective-permute-start) | collective-permute-done | bytes 327712 | tf_op jit(solution)/shard_map/ppermute | solution.py:183
  126.6 37.5 %all-gather.9.cloned.1.call-done = bf16[2,128,5120]{2,1,0:T(8,128)(2,1)} async-done(((bf16[2,32,5120]{2,1,0:T(8,128)(2,1)}), bf16[2,128,5120]{2,1,0:T(8,128)(2,1)}) %all-gather.9.cloned.1.call-update) | async-done | bytes 2621456 | tf_op jit(solution)/shard_map/all_gather | solution.py:54
  167.2 30.8 %all-gather.11.cloned.1.call-done = bf16[128,5120]{1,0:T(8,128)(2,1)} async-done(((bf16[32,5120]{1,0:T(8,128)(2,1)}), bf16[128,5120]{1,0:T(8,128)(2,1)}) %all-gather.11.cloned.1.call-update) | async-done | bytes 1310736 | tf_op jit(solution)/shard_map/all_gather | solution.py:54
  198.0 3.4 fusion.58
  202.2 2.5 fusion.6
  204.8 3.6 fusion.32
  208.4 5.7 %fusion.33 = f32[3,128,5120]{2,1,0:T(8,128)} fusion(bf16[2,128,5120]{2,1,0:T(8,128)(2,1)} %all-gather.7.cloned.1.call-done, bf16[1,128,1,128]{3,1,2,0:T(8,128)(2,1)S(1)} %fusion.86, bf16[1,128,1,128]{3,1,2,0:T(8,128)(2,1)S(1)} %fusion.79, bf16[1,128,1,128]{3,1,2,0:T(8,128)(2,1)S(1)} %fusion.78), kind=kOutput, calls=%fused_computation.52 | convolution fusion | flops 503414784 | bytes 9273344 | tf_op jit(solution)/shard_map/sd,csn->cdn/dot_general | solution.py:119
  216.0 19.4 %reduce-scatter.6.cloned.1.call-done = bf16[1,32,5120]{2,1,0:T(8,128)(2,1)} async-done(((bf16[1,128,5120]{2,1,0:T(8,128)(2,1)}), bf16[1,32,5120]{2,1,0:T(8,128)(2,1)}) %reduce-scatter.6.cloned.1.call-update) | async-done | bytes 327696 | tf_op jit(solution)/shard_map/reduce_scatter | solution.py:59
  236.4 3.4 collective-permute-start.1
  240.1 4.3 %collective-permute-done.1 = bf16[32,5120]{1,0:T(8,128)(2,1)S(1)} collective-permute-done((bf16[32,5120]{1,0:T(8,128)(2,1)S(1)}, bf16[32,5120]{1,0:T(8,128)(2,1)S(1)}, u32[]{:S(2)}, u32[]{:S(2)}) %collective-permute-start.1) | collective-permute-done | bytes 327712 | tf_op jit(solution)/shard_map/ppermute | solution.py:209
  248.3 4.9 %fusion = bf16[3,5120,128]{1,2,0:T(8,128)(2,1)S(1)} fusion(f32[3,128,5120]{2,1,0:T(8,128)} %fusion.33, bf16[2,128,5120]{2,1,0:T(8,128)(2,1)} %all-gather.9.cloned.1.call-done, bf16[1,128,1,128]{3,1,2,0:T(8,128)(2,1)S(1)} %fusion.87, bf16[1,128,1,128]{3,1,2,0:T(8,128)(2,1)S(1)} %fusion.83, bf16[1,128,1,128]{3,1,2,0:T(8,128)(2,1)S(1)} %fusion.82), kind=kOutput, calls=%fused_computation.1 | convolution fusion | flops 507346944 | bytes 13205504 | tf_op jit(solution)/shard_map/sd,csn->cdn/dot_general | solution.py:119
  257.1 3.3 collective-permute-start.2
  265.1 17.1 %all-gather.13.cloned.1.call-done = bf16[128,5120]{1,0:T(8,128)(2,1)} async-done(((bf16[32,5120]{1,0:T(8,128)(2,1)}), bf16[128,5120]{1,0:T(8,128)(2,1)}) %all-gather.13.cloned.1.call-update) | async-done | bytes 1310736 | tf_op jit(solution)/shard_map/all_gather | solution.py:54
  282.2 3.4 fusion.53
  287.8 3.1 pad_maximum_fusion
  290.9 2.8 fusion.1
  296.5 21.1 %collective-permute-done.6 = bf16[128,2560]{1,0:T(8,128)(2,1)S(1)} collective-permute-done((bf16[128,2560]{1,0:T(8,128)(2,1)S(1)}, bf16[128,2560]{1,0:T(8,128)(2,1)S(1)}, u32[]{:S(2)}, u32[]{:S(2)}) %collective-permute-start.6) | collective-permute-done | bytes 655392 | tf_op jit(solution)/shard_map/ppermute | solution.py:20
  317.6 3.3 collective-permute-start.7
  323.0 13.5 %collective-permute-done.7 = bf16[128,2560]{1,0:T(8,128)(2,1)S(1)} collective-permute-done((bf16[128,2560]{1,0:T(8,128)(2,1)S(1)}, bf16[128,2560]{1,0:T(8,128)(2,1)S(1)}, u32[]{:S(2)}, u32[]{:S(2)}) %collective-permute-start.7) | collective-permute-done | bytes 655392 | tf_op jit(solution)/shard_map/ppermute | solution.py:20
  340.0 38.1 %collective-permute-done.3 = bf16[3,2560,128]{1,2,0:T(8,128)(2,1)S(1)} collective-permute-done((bf16[3,2560,128]{1,2,0:T(8,128)(2,1)}, bf16[3,2560,128]{1,2,0:T(8,128)(2,1)S(1)}, u32[]{:S(2)}, u32[]{:S(2)}) %collective-permute-start.3) | collective-permute-done | bytes 1966112 | tf_op jit(solution)/shard_map/ppermute | solution.py:20
  383.2 6.3 %copy.19 = bf16[1,1,3,5120,128]{4,3,2,1,0:T(8,128)(2,1)} copy(bf16[1,1,3,5120,128]{3,4,2,1,0:T(8,128)(2,1)} %maximum_bitcast_fusion) | data formatting | bytes 7864320
  (140 shorter events, 60.2 us)
Async XLA Ops:
  7.2 66.0 %copy-start = (bf16[1,1,128,5120]{3,2,1,0:T(8,128)(2,1)S(1)}, bf16[1,1,128,5120]{3,2,1,0:T(8,128)(2,1)}, u32[]{:S(2)}) copy-start(bf16[1,1,128,5120]{3,2,1,0:T(8,128)(2,1)} %param.17) | copy-start | bytes 3932164
  7.2 62.2 %all-gather.7.cloned.1.call-start = ((), (), s32[]{:S(2)}) async-start(), calls=%async_computation.3 | async-start | bytes 3276800 | tf_op jit(solution)/shard_map/all_gather | solution.py:54
  11.8 96.6 %reduce-scatter.4.cloned.1.call-start = ((), (), s32[]{:S(2)}) async-start(), calls=%async_computation.4 | async-start | bytes 1638400 | tf_op jit(solution)/shard_map/reduce_scatter | solution.py:59
  78.2 85.9 %all-gather.9.cloned.1.call-start = ((), (), s32[]{:S(2)}) async-start(), calls=%async_computation.5 | async-start | bytes 3276800 | tf_op jit(solution)/shard_map/all_gather | solution.py:54
  110.5 87.5 %all-gather.11.cloned.1.call-start = ((), (), s32[]{:S(2)}) async-start(), calls=%async_computation.8 | async-start | bytes 1638400 | tf_op jit(solution)/shard_map/all_gather | solution.py:54
  110.5 15.3 %copy-start.13 = (bf16[1,2,32,5120]{3,2,1,0:T(8,128)(2,1)S(1)}, bf16[1,2,32,5120]{3,2,1,0:T(8,128)(2,1)}, u32[]{:S(2)}) copy-start(bf16[1,2,32,5120]{3,2,1,0:T(8,128)(2,1)} %param.21) | copy-start | bytes 1966084
  114.0 11.9 %collective-permute-start = (bf16[32,5120]{1,0:T(8,128)(2,1)S(1)}, bf16[32,5120]{1,0:T(8,128)(2,1)S(1)}, u32[]{:S(2)}, u32[]{:S(2)}) collective-permute-start(bf16[32,5120]{1,0:T(8,128)(2,1)S(1)} %fusion.103), channel_id=1, source_target_pairs={{1,9},{8,0},{9,17},{16,8},{17,25},{24,16},{3,11},{10,2},{11,19},{1... | collective-permute-start | bytes 983048 | tf_op jit(solution)/shard_map/ppermute | solution.py:183
  166.6 68.8 %reduce-scatter.6.cloned.1.call-start = ((), (), s32[]{:S(2)}) async-start(), calls=%async_computation.6 | async-start | bytes 1638400 | tf_op jit(solution)/shard_map/reduce_scatter | solution.py:59
  204.8 77.5 %all-gather.13.cloned.1.call-start = ((), (), s32[]{:S(2)}) async-start(), calls=%async_computation.9 | async-start | bytes 1638400 | tf_op jit(solution)/shard_map/all_gather | solution.py:54
  215.5 28.9 %copy-start.23 = (s32[32]{0:T(128)S(1)}, s32[32]{0:T(128)}, u32[]{:S(2)}) copy-start(s32[32]{0:T(128)} %get-tuple-element.38) | copy-start | bytes 388
  236.4 9.4 %copy-start.14 = (bf16[32,5120]{1,0:T(8,128)(2,1)}, bf16[32,5120]{1,0:T(8,128)(2,1)S(1)}, u32[]{:S(2)}) copy-start(bf16[32,5120]{1,0:T(8,128)(2,1)S(1)} %fusion.112) | copy-start | bytes 983044
  236.4 8.0 %collective-permute-start.1 = (bf16[32,5120]{1,0:T(8,128)(2,1)S(1)}, bf16[32,5120]{1,0:T(8,128)(2,1)S(1)}, u32[]{:S(2)}, u32[]{:S(2)}) collective-permute-start(bf16[32,5120]{1,0:T(8,128)(2,1)S(1)} %fusion.112), channel_id=1, source_target_pairs={{0,8},{8,16},{9,1},{16,24},{17,9},{25,17},{2,10},{10,18},{11,3},{1... | collective-permute-start | bytes 983048 | tf_op jit(solution)/shard_map/ppermute | solution.py:209
  247.6 141.9 %reduce-scatter.8.cloned.1.call-start = ((), (), s32[]{:S(2)}) async-start(), calls=%async_computation.7 | async-start | bytes 3276800 | tf_op jit(solution)/shard_map/reduce_scatter | solution.py:59
  253.1 9.6 %copy-start.3 = (bf16[1,1,3,5120,128]{4,3,2,1,0:T(8,128)(2,1)S(1)}, bf16[1,1,3,5120,128]{4,3,2,1,0:T(8,128)(2,1)}, u32[]{:S(2)}) copy-start(bf16[1,1,3,5120,128]{4,3,2,1,0:T(8,128)(2,1)} %param.16) | copy-start | bytes 11796484
  257.1 64.4 %collective-permute-start.2 = (bf16[3,2560,128]{1,2,0:T(8,128)(2,1)}, bf16[3,2560,128]{1,2,0:T(8,128)(2,1)}, u32[]{:S(2)}, u32[]{:S(2)}) collective-permute-start(bf16[3,2560,128]{1,2,0:T(8,128)(2,1)} %get-tuple-element.22), channel_id=1, source_target_pairs={{0,9},{1,8},{8,1},{9,0},{16,25},{17,24},{24,17},{25,16},{2,11},{3,... | collective-permute-start | bytes 5898248 | tf_op jit(solution)/shard_map/ppermute | solution.py:20
  260.3 61.2 %collective-permute-start.4 = (bf16[3,2560,128]{1,2,0:T(8,128)(2,1)}, bf16[3,2560,128]{1,2,0:T(8,128)(2,1)}, u32[]{:S(2)}, u32[]{:S(2)}) collective-permute-start(bf16[3,2560,128]{1,2,0:T(8,128)(2,1)} %get-tuple-element.23), channel_id=1, source_target_pairs={{0,17},{1,16},{8,25},{9,24},{16,1},{17,0},{24,9},{25,8},{2,19},{3,... | collective-permute-start | bytes 5898248 | tf_op jit(solution)/shard_map/ppermute | solution.py:20
  265.1 20.5 %copy-start.25 = (s32[128]{0:T(128)S(1)}, s32[128]{0:T(128)}, u32[]{:S(2)}) copy-start(s32[128]{0:T(128)} %get-tuple-element.34) | copy-start | bytes 1540
  293.8 23.8 %collective-permute-start.6 = (bf16[128,2560]{1,0:T(8,128)(2,1)S(1)}, bf16[128,2560]{1,0:T(8,128)(2,1)S(1)}, u32[]{:S(2)}, u32[]{:S(2)}) collective-permute-start(bf16[128,2560]{1,0:T(8,128)(2,1)S(1)} %get-tuple-element.26), channel_id=1, source_target_pairs={{0,9},{1,8},{8,1},{9,0},{16,25},{17,24},{24,17},{25,16},{2,11},{3,... | collective-permute-start | bytes 1966088 | tf_op jit(solution)/shard_map/ppermute | solution.py:20
  294.0 26.9 %collective-permute-start.8 = (bf16[128,2560]{1,0:T(8,128)(2,1)S(1)}, bf16[128,2560]{1,0:T(8,128)(2,1)S(1)}, u32[]{:S(2)}, u32[]{:S(2)}) collective-permute-start(bf16[128,2560]{1,0:T(8,128)(2,1)S(1)} %get-tuple-element.27), channel_id=1, source_target_pairs={{0,17},{1,16},{8,25},{9,24},{16,1},{17,0},{24,9},{25,8},{2,19},{3,... | collective-permute-start | bytes 1966088 | tf_op jit(solution)/shard_map/ppermute | solution.py:20
  317.6 18.9 %collective-permute-start.7 = (bf16[128,2560]{1,0:T(8,128)(2,1)S(1)}, bf16[128,2560]{1,0:T(8,128)(2,1)S(1)}, u32[]{:S(2)}, u32[]{:S(2)}) collective-permute-start(bf16[128,2560]{1,0:T(8,128)(2,1)S(1)} %collective-permute-done.6), channel_id=1, source_target_pairs={{0,16},{1,17},{8,24},{9,25},{16,0},{17,1},{24,8},{25,9},{2,18},{3,... | collective-permute-start | bytes 1966088 | tf_op jit(solution)/shard_map/ppermute | solution.py:20
  320.9 17.6 %collective-permute-start.9 = (bf16[128,2560]{1,0:T(8,128)(2,1)S(1)}, bf16[128,2560]{1,0:T(8,128)(2,1)S(1)}, u32[]{:S(2)}, u32[]{:S(2)}) collective-permute-start(bf16[128,2560]{1,0:T(8,128)(2,1)S(1)} %collective-permute-done.8), channel_id=1, source_target_pairs={{0,8},{1,9},{8,0},{9,1},{16,24},{17,25},{24,16},{25,17},{2,10},{3,... | collective-permute-start | bytes 1966088 | tf_op jit(solution)/shard_map/ppermute | solution.py:20
  321.5 56.7 %collective-permute-start.3 = (bf16[3,2560,128]{1,2,0:T(8,128)(2,1)}, bf16[3,2560,128]{1,2,0:T(8,128)(2,1)S(1)}, u32[]{:S(2)}, u32[]{:S(2)}) collective-permute-start(bf16[3,2560,128]{1,2,0:T(8,128)(2,1)} %collective-permute-done.2), channel_id=1, source_target_pairs={{0,16},{1,17},{8,24},{9,25},{16,0},{17,1},{24,8},{25,9},{2,18},{3,... | collective-permute-start | bytes 5898248 | tf_op jit(solution)/shard_map/ppermute | solution.py:20
  321.5 58.1 %collective-permute-start.5 = (bf16[3,2560,128]{1,2,0:T(8,128)(2,1)}, bf16[3,2560,128]{1,2,0:T(8,128)(2,1)S(1)}, u32[]{:S(2)}, u32[]{:S(2)}) collective-permute-start(bf16[3,2560,128]{1,2,0:T(8,128)(2,1)} %collective-permute-done.4), channel_id=1, source_target_pairs={{0,8},{1,9},{8,0},{9,1},{16,24},{17,25},{24,16},{25,17},{2,10},{3,... | collective-permute-start | bytes 5898248 | tf_op jit(solution)/shard_map/ppermute | solution.py:20
  338.5 41.1 %copy-start.5 = (bf16[3,5120,128]{1,2,0:T(8,128)(2,1)S(1)}, bf16[3,5120,128]{1,2,0:T(8,128)(2,1)}, u32[]{:S(2)}) copy-start(bf16[3,5120,128]{1,2,0:T(8,128)(2,1)} %copy-done.4) | copy-start | bytes 11796484
  (19 other events, 61.9 us)
Sparse Core Ops, SparseCore 0:
  12.0 57.3 all-gather.6
  78.3 30.1 reduce-scatter.3
  110.6 53.4 all-gather.8
  166.7 31.2 all-gather.10
  204.9 30.4 reduce-scatter.5
  247.7 34.5 all-gather.12
  291.0 51.3 reduce-scatter.7

commit v4 on v3

--- a/solution.py
+++ b/solution.py
@@ -141,6 +141,18 @@
             if 0 <= section - ahead < sections:
                 down_pairs.append((section * mirror_size + mirror, (section - ahead) * mirror_size + mirror))
 
+    bit_count = lax.axis_size(pair_axes).bit_length() - 1
+    section_bits = list(range(1, bit_count))
+    if section_bits:
+        routes = []
+        for start in range(len(section_bits)):
+            order = section_bits[start:] + section_bits[:start]
+            routes.append([1 | (1 << order[0])] + [1 << bit for bit in order[1:]])
+    else:
+        routes = [[1]]
+    cuts = np.linspace(0, model_width, len(routes) + 1).astype(int)
+    spans = [(int(cuts[i]), int(cuts[i + 1])) for i in range(len(routes))]
+
     last_step = window_steps - 1
     saved_normed = [normed_rows(saved[0, 0, t]) for t in range(window_steps)]
     qkv_total = jnp.zeros(qkv_weight.shape, jnp.float32)
@@ -148,14 +160,14 @@
 
     backward_outs = []
     backward_in = grad_in[0, 0]
-    backward_normed_full = [None] * window_steps
-    forward_normed_first = None
     for step_index in range(window_steps):
         upstream = jnp.where(position == sections - 1, cotangent[0, step_index], backward_in)
         if step_index == 0:
-            upstream_full, backward_normed_full[0] = gathered([upstream, saved_normed[0]])
+            upstream_full, *backward_normed_full = gathered([upstream] + saved_normed)
         else:
-            upstream, ready = lax.optimization_barrier((upstream, ready))
+            upstream, forward_normed_full = lax.optimization_barrier(
+                (upstream, forward_normed_full)
+            )
             upstream_full = gathered([upstream])[0]
         d_normed_part, qkv_term, out_term = backward_part(
             backward_normed_full[step_index], upstream_full, mask_for(1, step_index + position)
@@ -172,15 +184,21 @@
             first_forward_in = jnp.where(
                 position == 0, embedding(feats[0, 0], types[0, 0], type_table), carry_acts[0, 0]
             )
-            rest, d_normed = lax.optimization_barrier(
-                (saved_normed[1:] + [normed_rows(first_forward_in)], d_normed)
-            )
-            ready = gathered(rest)
-            backward_normed_full[1:] = ready[:-1]
-            forward_normed_first = ready[-1]
+            first_normed, d_normed = lax.optimization_barrier(
+                (normed_rows(first_forward_in), d_normed)
+            )
+            forward_normed_full = gathered([first_normed])[0]
         backward_out = input_grad(saved[0, 0, step_index], upstream, d_normed)
         backward_outs.append(backward_out)
         backward_in = lax.ppermute(backward_out, pair_axes, down_pairs)
+
+    own_qkv = qkv_total.astype(jnp.bfloat16)
+    own_out = out_total.astype(jnp.bfloat16)
+    in_flight = []
+    for (low, high), hops in zip(spans, routes):
+        in_flight.append(
+            flipped((own_qkv[:, low:high, :], own_out[:, low:high]), pair_axes, hops[0])
+        )
 
     forward_outs = []
     forward_in = carry_acts[0, 0]
@@ -189,10 +207,11 @@
         current = jnp.where(position == 0, embedded, forward_in)
         if step_index == 0:
             forward_normed_full, last_upstream_full = lax.optimization_barrier(
-                (forward_normed_first, last_upstream_full)
+                (forward_normed_full, last_upstream_full)
             )
         else:
-            forward_normed_full = gathered([normed_rows(current)])[0]
+            forward_normed, in_flight = lax.optimization_barrier((normed_rows(current), in_flight))
+            forward_normed_full = gathered([forward_normed])[0]
         attn_part = forward_part(
             forward_normed_full, mask_for(0, step_index - position + sections - 1)
         )
@@ -208,24 +227,10 @@
         if step_index < last_step:
             forward_in = lax.ppermute(forward_out, pair_axes, up_pairs)
 
-    own_qkv = qkv_total.astype(jnp.bfloat16)
-    own_out = out_total.astype(jnp.bfloat16)
-    bit_count = lax.axis_size(pair_axes).bit_length() - 1
-    section_bits = list(range(1, bit_count))
-    if section_bits:
-        routes = []
-        for start in range(len(section_bits)):
-            order = section_bits[start:] + section_bits[:start]
-            routes.append([1 | (1 << order[0])] + [1 << bit for bit in order[1:]])
-    else:
-        routes = [[1]]
-    cuts = np.linspace(0, model_width, len(routes) + 1).astype(int)
     qkv_sums = []
     out_sums = []
-    for route_index, hops in enumerate(routes):
-        low, high = int(cuts[route_index]), int(cuts[route_index + 1])
-        piece = (own_qkv[:, low:high, :], own_out[:, low:high])
-        for mask in hops:
+    for (low, high), hops, piece in zip(spans, routes, in_flight):
+        for mask in hops[1:]:
             piece = flipped(piece, pair_axes, mask)
         qkv_sums.append(
             (own_qkv[:, low:high, :].astype(jnp.float32) + piece[0].astype(jnp.float32)).astype(

time: 402 us -> 399 us (level)
  starting transfers between devices: 19 us -> 12.5 us
  waiting for transfers between devices: 281 us -> 286 us
    ppermute x1, waiting for transfers between devices: 4.27 us -> 22.5 us  [shards(): forward_in = lax.ppermute(forward_out, pair_axes, up_pairs)]
    ppermute x8, waiting for transfers between devices: 76.2 us -> 68.2 us  [flipped(): lax.ppermute(value, axis, [(i, i ^ mask) for i in range(lax.axis_size(axi...]
    ppermute x8, starting transfers between devices: 13.8 us -> 7.31 us  [flipped(): lax.ppermute(value, axis, [(i, i ^ mask) for i in range(lax.axis_size(axi...]
    reduce_scatter x3, waiting for transfers between devices: 46.6 us -> 41.7 us  [scattered(): lax.psum_scatter(jnp.stack(blocks), 'tp', scatter_dimension=1, tiled=True)]
    unnamed x53 -> x67, local copies, waits for them, and re-layouts: 11 us -> 9.02 us
where the time goes in v4:
time: 399 us; the launch traced here: 398 us
  waiting for transfers between devices  286 us (72%)
  matrix products  46.8 us (12%)
  other arithmetic  24 us (6%)
  between operations  14.6 us (4%)
  local copies, waits for them, and re-layouts  13.8 us (3%)
  starting transfers between devices  12.5 us (3%)
    all_gather x4, waiting for transfers between devices, gathered(): full = lax.all_gather(jnp.stack(blocks), 'tp', axis=1, tiled=True)  143 us
    ppermute x8, waiting for transfers between devices, flipped(): lax.ppermute(value, axis, [(i, i ^ mask) for i in range(lax.axis_size(axi...  68.2 us
    reduce_scatter x3, waiting for transfers between devices, scattered(): lax.psum_scatter(jnp.stack(blocks), 'tp', scatter_dimension=1, tiled=True)  41.7 us
    ppermute x1, waiting for transfers between devices, shards(): forward_in = lax.ppermute(forward_out, pair_axes, up_pairs)  22.5 us
    dot_general x4, matrix products, heads_of(): jnp.einsum('sd,cdn->csn', normed_full, qkv_weight, preferred_element_type...  13.2 us
    dot_general x2, matrix products, backward_part(): jnp.einsum('sd,csn->cdn', normed_full, d_projected, preferred_element_typ...  10.6 us
    ppermute x1, waiting for transfers between devices, shards(): backward_in = lax.ppermute(backward_out, pair_axes, down_pairs)  10.6 us
    unnamed x67, local copies, waits for them, and re-layouts  9.02 us
  transfers between devices with their start and end apart: 17, of which 13 were waited for; matrix products, arithmetic and copies ran while one was open for 13% of the time, Pallas kernels for 0%

profile of v4, /device:TPU:0, one launch (start us, length us, event | category | flops | bytes accessed | tf_op | source)
XLA Modules:
  0.0 398.1 jit_solution(6817102470376816915)
XLA Ops:
  11.3 79.2 %all-gather.8.cloned.1.call-done = bf16[3,128,5120]{2,1,0:T(8,128)(2,1)} async-done(((bf16[3,32,5120]{2,1,0:T(8,128)(2,1)}), bf16[3,128,5120]{2,1,0:T(8,128)(2,1)}) %all-gather.8.cloned.1.call-update) | async-done | bytes 3932176 | tf_op jit(solution)/shard_map/all_gather | solution.py:54
  90.5 3.5 fusion.63
  103.1 26.2 %reduce-scatter.4.cloned.1.call-done = bf16[1,32,5120]{2,1,0:T(8,128)(2,1)} async-done(((bf16[1,128,5120]{2,1,0:T(8,128)(2,1)}), bf16[1,32,5120]{2,1,0:T(8,128)(2,1)}) %reduce-scatter.4.cloned.1.call-update) | async-done | bytes 327696 | tf_op jit(solution)/shard_map/reduce_scatter | solution.py:59
  133.2 10.6 %collective-permute-done = bf16[32,5120]{1,0:T(8,128)(2,1)S(1)} collective-permute-done((bf16[32,5120]{1,0:T(8,128)(2,1)S(1)}, bf16[32,5120]{1,0:T(8,128)(2,1)S(1)}, u32[]{:S(2)}, u32[]{:S(2)}) %collective-permute-start) | collective-permute-done | bytes 327712 | tf_op jit(solution)/shard_map/ppermute | solution.py:193
  144.6 18.2 %all-gather.10.cloned.1.call-done = bf16[128,5120]{1,0:T(8,128)(2,1)} async-done(((bf16[32,5120]{1,0:T(8,128)(2,1)}), bf16[128,5120]{1,0:T(8,128)(2,1)}) %all-gather.10.cloned.1.call-update) | async-done | bytes 1310736 | tf_op jit(solution)/shard_map/all_gather | solution.py:54
  163.4 3.4 fusion.55
  167.6 3.5 fusion.32
  171.1 5.7 %fusion.33 = f32[3,128,5120]{2,1,0:T(8,128)} fusion(bf16[3,128,5120]{2,1,0:T(8,128)(2,1)} %all-gather.8.cloned.1.call-done, bf16[1,128,1,128]{3,1,2,0:T(8,128)(2,1)S(1)} %fusion.86, bf16[1,128,1,128]{3,1,2,0:T(8,128)(2,1)S(1)} %fusion.79, bf16[1,128,1,128]{3,1,2,0:T(8,128)(2,1)S(1)} %fusion.78), kind=kOutput, calls=%fused_computation.51 | convolution fusion | flops 503414784 | bytes 9273344 | tf_op jit(solution)/shard_map/sd,csn->cdn/dot_general | solution.py:119
  176.8 19.0 %all-gather.12.cloned.1.call-done = bf16[128,5120]{1,0:T(8,128)(2,1)} async-done(((bf16[32,5120]{1,0:T(8,128)(2,1)}), bf16[128,5120]{1,0:T(8,128)(2,1)}) %all-gather.12.cloned.1.call-update) | async-done | bytes 1310736 | tf_op jit(solution)/shard_map/all_gather | solution.py:54
  195.8 3.0 fusion.58
  202.4 4.9 %fusion = bf16[3,5120,128]{1,2,0:T(8,128)(2,1)S(1)} fusion(f32[3,128,5120]{2,1,0:T(8,128)} %fusion.33, bf16[3,128,5120]{2,1,0:T(8,128)(2,1)} %all-gather.8.cloned.1.call-done, bf16[1,128,1,128]{3,1,2,0:T(8,128)(2,1)S(1)} %fusion.87, bf16[1,128,1,128]{3,1,2,0:T(8,128)(2,1)S(1)} %fusion.82, bf16[1,128,1,128]{3,1,2,0:T(8,128)(2,1)S(1)} %fusion.81), kind=kOutput, calls=%fused_computation.1 | convolution fusion | flops 507346944 | bytes 13205504 | tf_op jit(solution)/shard_map/sd,csn->cdn/dot_general | solution.py:119
  207.3 2.5 fusion.148
  213.1 2.8 fusion.1
  216.0 15.5 %reduce-scatter.6.cloned.1.call-done = bf16[1,32,5120]{2,1,0:T(8,128)(2,1)} async-done(((bf16[1,128,5120]{2,1,0:T(8,128)(2,1)}), bf16[1,32,5120]{2,1,0:T(8,128)(2,1)}) %reduce-scatter.6.cloned.1.call-update) | async-done | bytes 327696 | tf_op jit(solution)/shard_map/reduce_scatter | solution.py:59
  232.8 3.4 collective-permute-start.1
  237.9 22.5 %collective-permute-done.1 = bf16[32,5120]{1,0:T(8,128)(2,1)S(1)} collective-permute-done((bf16[32,5120]{1,0:T(8,128)(2,1)S(1)}, bf16[32,5120]{1,0:T(8,128)(2,1)S(1)}, u32[]{:S(2)}, u32[]{:S(2)}) %collective-permute-start.1) | collective-permute-done | bytes 327712 | tf_op jit(solution)/shard_map/ppermute | solution.py:228
  262.6 14.4 %collective-permute-done.3 = bf16[128,2560]{1,0:T(8,128)(2,1)} collective-permute-done((bf16[128,2560]{1,0:T(8,128)(2,1)}, bf16[128,2560]{1,0:T(8,128)(2,1)}, u32[]{:S(2)}, u32[]{:S(2)}) %collective-permute-start.3) | collective-permute-done | bytes 655392 | tf_op jit(solution)/shard_map/ppermute | solution.py:20
  277.3 4.5 %fusion.4 = bf16[1,128,5120]{2,1,0:T(8,128)(2,1)} fusion(bf16[1,1,3,5120,128]{4,3,2,1,0:T(8,128)(2,1)} %param.16, bf16[1,128,1,128]{3,1,2,0:T(8,128)(2,1)S(1)} %copy-done.26, bf16[1,128,1,128]{3,1,2,0:T(8,128)(2,1)S(1)} %fusion.82, bf16[1,128,1,128]{3,1,2,0:T(8,128)(2,1)S(1)} %fusion.81), kind=kOutput, calls=%fused_computation.10 | convolution fusion | flops 504070144 | bytes 5341184 | tf_op jit(solution)/shard_map/csn,cdn->sd/dot_general | solution.py:116
  281.8 26.9 %all-gather.14.cloned.1.call-done = bf16[128,5120]{1,0:T(8,128)(2,1)} async-done(((bf16[32,5120]{1,0:T(8,128)(2,1)}), bf16[128,5120]{1,0:T(8,128)(2,1)}) %all-gather.14.cloned.1.call-update) | async-done | bytes 1310736 | tf_op jit(solution)/shard_map/all_gather | solution.py:54
  308.7 3.4 fusion.50
  314.1 3.5 pad_maximum_fusion
  321.7 13.8 %collective-permute-done.8 = bf16[128,2560]{1,0:T(8,128)(2,1)S(1)} collective-permute-done((bf16[128,2560]{1,0:T(8,128)(2,1)}, bf16[128,2560]{1,0:T(8,128)(2,1)S(1)}, u32[]{:S(2)}, u32[]{:S(2)}) %collective-permute-start.8) | collective-permute-done | bytes 655392 | tf_op jit(solution)/shard_map/ppermute | solution.py:20
  338.4 37.3 %collective-permute-done.6 = bf16[3,2560,128]{1,2,0:T(8,128)(2,1)S(1)} collective-permute-done((bf16[3,2560,128]{1,2,0:T(8,128)(2,1)}, bf16[3,2560,128]{1,2,0:T(8,128)(2,1)S(1)}, u32[]{:S(2)}, u32[]{:S(2)}) %collective-permute-start.6) | collective-permute-done | bytes 1966112 | tf_op jit(solution)/shard_map/ppermute | solution.py:20
  380.5 6.3 %copy.19 = bf16[1,1,3,5120,128]{4,3,2,1,0:T(8,128)(2,1)} copy(bf16[1,1,3,5120,128]{3,4,2,1,0:T(8,128)(2,1)} %maximum_bitcast_fusion) | data formatting | bytes 7864320
  (152 shorter events, 49.6 us)
Async XLA Ops:
  7.2 87.1 %copy-start = (bf16[1,1,128,5120]{3,2,1,0:T(8,128)(2,1)S(1)}, bf16[1,1,128,5120]{3,2,1,0:T(8,128)(2,1)}, u32[]{:S(2)}) copy-start(bf16[1,1,128,5120]{3,2,1,0:T(8,128)(2,1)} %param.17) | copy-start | bytes 3932164
  7.2 83.3 %all-gather.8.cloned.1.call-start = ((), (), s32[]{:S(2)}) async-start(), calls=%async_computation.3 | async-start | bytes 4915200 | tf_op jit(solution)/shard_map/all_gather | solution.py:54
  11.2 118.1 %reduce-scatter.4.cloned.1.call-start = ((), (), s32[]{:S(2)}) async-start(), calls=%async_computation.4 | async-start | bytes 1638400 | tf_op jit(solution)/shard_map/reduce_scatter | solution.py:59
  99.3 30.1 %copy-start.4 = (bf16[1,1,2,32,5120]{4,3,2,1,0:T(8,128)(2,1)S(1)}, bf16[1,1,2,32,5120]{4,3,2,1,0:T(8,128)(2,1)}, u32[]{:S(2)}) copy-start(bf16[1,1,2,32,5120]{4,3,2,1,0:T(8,128)(2,1)} %param.20) | copy-start | bytes 1966084
  99.3 63.4 %all-gather.10.cloned.1.call-start = ((), (), s32[]{:S(2)}) async-start(), calls=%async_computation.7 | async-start | bytes 1638400 | tf_op jit(solution)/shard_map/all_gather | solution.py:54
  130.6 65.2 %all-gather.12.cloned.1.call-start = ((), (), s32[]{:S(2)}) async-start(), calls=%async_computation.8 | async-start | bytes 1638400 | tf_op jit(solution)/shard_map/all_gather | solution.py:54
  131.9 34.9 %copy-start.17 = (bf16[32,5120]{1,0:T(8,128)(2,1)}, bf16[32,5120]{1,0:T(8,128)(2,1)S(1)}, u32[]{:S(2)}) copy-start(bf16[32,5120]{1,0:T(8,128)(2,1)S(1)} %fusion.111) | copy-start | bytes 983044
  131.9 11.9 %collective-permute-start = (bf16[32,5120]{1,0:T(8,128)(2,1)S(1)}, bf16[32,5120]{1,0:T(8,128)(2,1)S(1)}, u32[]{:S(2)}, u32[]{:S(2)}) collective-permute-start(bf16[32,5120]{1,0:T(8,128)(2,1)S(1)} %fusion.111), channel_id=1, source_target_pairs={{1,9},{8,0},{9,17},{16,8},{17,25},{24,16},{3,11},{10,2},{11,19},{1... | collective-permute-start | bytes 983048 | tf_op jit(solution)/shard_map/ppermute | solution.py:193
  162.8 68.7 %reduce-scatter.6.cloned.1.call-start = ((), (), s32[]{:S(2)}) async-start(), calls=%async_computation.5 | async-start | bytes 1638400 | tf_op jit(solution)/shard_map/reduce_scatter | solution.py:59
  200.8 107.9 %all-gather.14.cloned.1.call-start = ((), (), s32[]{:S(2)}) async-start(), calls=%async_computation.9 | async-start | bytes 1638400 | tf_op jit(solution)/shard_map/all_gather | solution.py:54
  210.5 66.5 %collective-permute-start.2 = (bf16[3,2560,128]{1,2,0:T(8,128)(2,1)}, bf16[3,2560,128]{1,2,0:T(8,128)(2,1)}, u32[]{:S(2)}, u32[]{:S(2)}) collective-permute-start(bf16[3,2560,128]{1,2,0:T(8,128)(2,1)} %get-tuple-element.33), channel_id=1, source_target_pairs={{0,9},{1,8},{8,1},{9,0},{16,25},{17,24},{24,17},{25,16},{2,11},{3,... | collective-permute-start | bytes 5898248 | tf_op jit(solution)/shard_map/ppermute | solution.py:20
  210.7 66.3 %collective-permute-start.4 = (bf16[3,2560,128]{1,2,0:T(8,128)(2,1)}, bf16[3,2560,128]{1,2,0:T(8,128)(2,1)}, u32[]{:S(2)}, u32[]{:S(2)}) collective-permute-start(bf16[3,2560,128]{1,2,0:T(8,128)(2,1)} %get-tuple-element.32), channel_id=1, source_target_pairs={{0,17},{1,16},{8,25},{9,24},{16,1},{17,0},{24,9},{25,8},{2,19},{3,... | collective-permute-start | bytes 5898248 | tf_op jit(solution)/shard_map/ppermute | solution.py:20
  216.0 44.5 %copy-start.28 = (s32[32]{0:T(128)S(1)}, s32[32]{0:T(128)}, u32[]{:S(2)}) copy-start(s32[32]{0:T(128)} %get-tuple-element.48) | copy-start | bytes 388
  232.8 27.6 %collective-permute-start.1 = (bf16[32,5120]{1,0:T(8,128)(2,1)S(1)}, bf16[32,5120]{1,0:T(8,128)(2,1)S(1)}, u32[]{:S(2)}, u32[]{:S(2)}) collective-permute-start(bf16[32,5120]{1,0:T(8,128)(2,1)S(1)} %fusion.116), channel_id=1, source_target_pairs={{0,8},{8,16},{9,1},{16,24},{17,9},{25,17},{2,10},{10,18},{11,3},{1... | collective-permute-start | bytes 983048 | tf_op jit(solution)/shard_map/ppermute | solution.py:228
  237.3 39.9 %copy-start.26 = (bf16[1,128,1,128]{3,1,2,0:T(8,128)(2,1)S(1)}, bf16[1,128,1,128]{3,1,2,0:T(8,128)(2,1)}, u32[]{:S(2)}) copy-start(bf16[1,128,1,128]{3,1,2,0:T(8,128)(2,1)} %copy-done.25) | copy-start | bytes 98308
  237.3 39.7 %collective-permute-start.3 = (bf16[128,2560]{1,0:T(8,128)(2,1)}, bf16[128,2560]{1,0:T(8,128)(2,1)}, u32[]{:S(2)}, u32[]{:S(2)}) collective-permute-start(bf16[128,2560]{1,0:T(8,128)(2,1)} %get-tuple-element.37), channel_id=1, source_target_pairs={{0,9},{1,8},{8,1},{9,0},{16,25},{17,24},{24,17},{25,16},{2,11},{3,... | collective-permute-start | bytes 1966088 | tf_op jit(solution)/shard_map/ppermute | solution.py:20
  237.3 39.7 %collective-permute-start.5 = (bf16[128,2560]{1,0:T(8,128)(2,1)}, bf16[128,2560]{1,0:T(8,128)(2,1)}, u32[]{:S(2)}, u32[]{:S(2)}) collective-permute-start(bf16[128,2560]{1,0:T(8,128)(2,1)} %get-tuple-element.36), channel_id=1, source_target_pairs={{0,17},{1,16},{8,25},{9,24},{16,1},{17,0},{24,9},{25,8},{2,19},{3,... | collective-permute-start | bytes 1966088 | tf_op jit(solution)/shard_map/ppermute | solution.py:20
  277.0 109.8 %reduce-scatter.8.cloned.1.call-start = ((), (), s32[]{:S(2)}) async-start(), calls=%async_computation.6 | async-start | bytes 3276800 | tf_op jit(solution)/shard_map/reduce_scatter | solution.py:59
  281.8 30.3 %copy-start.31 = (s32[128]{0:T(128)S(1)}, s32[128]{0:T(128)}, u32[]{:S(2)}) copy-start(s32[128]{0:T(128)} %get-tuple-element.44) | copy-start | bytes 1540
  317.6 17.9 %collective-permute-start.8 = (bf16[128,2560]{1,0:T(8,128)(2,1)}, bf16[128,2560]{1,0:T(8,128)(2,1)S(1)}, u32[]{:S(2)}, u32[]{:S(2)}) collective-permute-start(bf16[128,2560]{1,0:T(8,128)(2,1)} %collective-permute-done.3), channel_id=1, source_target_pairs={{0,16},{1,17},{8,24},{9,25},{16,0},{17,1},{24,8},{25,9},{2,18},{3,... | collective-permute-start | bytes 1966088 | tf_op jit(solution)/shard_map/ppermute | solution.py:20
  319.1 17.8 %collective-permute-start.9 = (bf16[128,2560]{1,0:T(8,128)(2,1)}, bf16[128,2560]{1,0:T(8,128)(2,1)S(1)}, u32[]{:S(2)}, u32[]{:S(2)}) collective-permute-start(bf16[128,2560]{1,0:T(8,128)(2,1)} %collective-permute-done.5), channel_id=1, source_target_pairs={{0,8},{1,9},{8,0},{9,1},{16,24},{17,25},{24,16},{25,17},{2,10},{3,... | collective-permute-start | bytes 1966088 | tf_op jit(solution)/shard_map/ppermute | solution.py:20
  320.6 55.1 %collective-permute-start.6 = (bf16[3,2560,128]{1,2,0:T(8,128)(2,1)}, bf16[3,2560,128]{1,2,0:T(8,128)(2,1)S(1)}, u32[]{:S(2)}, u32[]{:S(2)}) collective-permute-start(bf16[3,2560,128]{1,2,0:T(8,128)(2,1)} %collective-permute-done.2), channel_id=1, source_target_pairs={{0,16},{1,17},{8,24},{9,25},{16,0},{17,1},{24,8},{25,9},{2,18},{3,... | collective-permute-start | bytes 5898248 | tf_op jit(solution)/shard_map/ppermute | solution.py:20
  321.1 55.8 %collective-permute-start.7 = (bf16[3,2560,128]{1,2,0:T(8,128)(2,1)}, bf16[3,2560,128]{1,2,0:T(8,128)(2,1)S(1)}, u32[]{:S(2)}, u32[]{:S(2)}) collective-permute-start(bf16[3,2560,128]{1,2,0:T(8,128)(2,1)} %collective-permute-done.4), channel_id=1, source_target_pairs={{0,8},{1,9},{8,0},{9,1},{16,24},{17,25},{24,16},{25,17},{2,10},{3,... | collective-permute-start | bytes 5898248 | tf_op jit(solution)/shard_map/ppermute | solution.py:20
  336.9 40.0 %copy-start.3 = (bf16[3,5120,128]{1,2,0:T(8,128)(2,1)S(1)}, bf16[3,5120,128]{1,2,0:T(8,128)(2,1)}, u32[]{:S(2)}) copy-start(bf16[3,5120,128]{1,2,0:T(8,128)(2,1)} %copy-done.2) | copy-start | bytes 11796484
  (26 other events, 223.5 us)
Sparse Core Ops, SparseCore 0:
  11.3 79.1 all-gather.7
  99.4 29.8 reduce-scatter.3
  131.5 31.1 all-gather.9
  164.2 31.6 all-gather.11
  200.9 30.4 reduce-scatter.5
  277.1 31.4 all-gather.13
  317.7 51.3 reduce-scatter.7

commit v5 on v4

--- a/solution.py
+++ b/solution.py
@@ -116,11 +116,23 @@
         d_normed_part = jnp.einsum(
             "csn,cdn->sd", d_projected, qkv_weight, preferred_element_type=jnp.float32
         ).astype(jnp.bfloat16)
-        qkv_term = jnp.einsum(
-            "sd,csn->cdn", normed_full, d_projected, preferred_element_type=jnp.float32
-        )
-        out_term = jnp.einsum("sn,sd->nd", mixed, upstream_full, preferred_element_type=jnp.float32)
-        return d_normed_part, qkv_term, out_term
+        return d_normed_part, d_projected, mixed
+
+    def weight_terms(normed_fulls, d_projecteds, mixeds, upstream_fulls):
+        qkv_sum = None
+        out_sum = None
+        for normed_full, d_projected, mixed, upstream_full in zip(
+            normed_fulls, d_projecteds, mixeds, upstream_fulls
+        ):
+            qkv_term = jnp.einsum(
+                "sd,csn->cdn", normed_full, d_projected, preferred_element_type=jnp.float32
+            )
+            out_term = jnp.einsum(
+                "sn,sd->nd", mixed, upstream_full, preferred_element_type=jnp.float32
+            )
+            qkv_sum = qkv_term if qkv_sum is None else qkv_sum + qkv_term
+            out_sum = out_term if out_sum is None else out_sum + out_term
+        return qkv_sum.astype(jnp.bfloat16), out_sum.astype(jnp.bfloat16)
 
     def input_grad(layer_in, upstream, d_normed):
         unused_norm, pull_norm = jax.vjp(
@@ -150,100 +162,93 @@
             routes.append([1 | (1 << order[0])] + [1 << bit for bit in order[1:]])
     else:
         routes = [[1]]
-    cuts = np.linspace(0, model_width, len(routes) + 1).astype(int)
-    spans = [(int(cuts[i]), int(cuts[i + 1])) for i in range(len(routes))]
+
+    def to_partner(value, axis):
+        cuts = np.linspace(0, value.shape[axis], len(routes) + 1).astype(int)
+        pieces = []
+        for index, hops in enumerate(routes):
+            piece = lax.slice_in_dim(value, int(cuts[index]), int(cuts[index + 1]), axis=axis)
+            for mask in hops:
+                piece = flipped(piece, pair_axes, mask)
+            pieces.append(piece)
+        return jnp.concatenate(pieces, axis=axis) if len(pieces) > 1 else pieces[0]
 
     last_step = window_steps - 1
     saved_normed = [normed_rows(saved[0, 0, t]) for t in range(window_steps)]
-    qkv_total = jnp.zeros(qkv_weight.shape, jnp.float32)
-    out_total = jnp.zeros(out_weight.shape, jnp.float32)
-
+    backward_normed_full = [None] * window_steps
+    upstream_fulls = []
+    d_projecteds = []
+    mixeds = []
+    partner_normed = [None] * window_steps
+    partner_upstream = []
+    partner_d_projected = []
+    partner_mixed = []
+    forward_outs = []
     backward_outs = []
+    forward_in = carry_acts[0, 0]
     backward_in = grad_in[0, 0]
-    for step_index in range(window_steps):
-        upstream = jnp.where(position == sections - 1, cotangent[0, step_index], backward_in)
-        if step_index == 0:
-            upstream_full, *backward_normed_full = gathered([upstream] + saved_normed)
-        else:
-            upstream, forward_normed_full = lax.optimization_barrier(
-                (upstream, forward_normed_full)
-            )
-            upstream_full = gathered([upstream])[0]
-        d_normed_part, qkv_term, out_term = backward_part(
-            backward_normed_full[step_index], upstream_full, mask_for(1, step_index + position)
-        )
-        qkv_total = qkv_total + qkv_term
-        out_total = out_total + out_term
-        if step_index == last_step:
-            last_d_normed_part = d_normed_part
-            last_upstream = upstream
-            last_upstream_full = upstream_full
-            break
-        d_normed = scattered([d_normed_part])[0]
-        if step_index == 0:
-            first_forward_in = jnp.where(
-                position == 0, embedding(feats[0, 0], types[0, 0], type_table), carry_acts[0, 0]
-            )
-            first_normed, d_normed = lax.optimization_barrier(
-                (normed_rows(first_forward_in), d_normed)
-            )
-            forward_normed_full = gathered([first_normed])[0]
-        backward_out = input_grad(saved[0, 0, step_index], upstream, d_normed)
-        backward_outs.append(backward_out)
-        backward_in = lax.ppermute(backward_out, pair_axes, down_pairs)
-
-    own_qkv = qkv_total.astype(jnp.bfloat16)
-    own_out = out_total.astype(jnp.bfloat16)
-    in_flight = []
-    for (low, high), hops in zip(spans, routes):
-        in_flight.append(
-            flipped((own_qkv[:, low:high, :], own_out[:, low:high]), pair_axes, hops[0])
-        )
-
-    forward_outs = []
-    forward_in = carry_acts[0, 0]
     for step_index in range(window_steps):
         embedded = embedding(feats[0, step_index], types[0, step_index], type_table)
         current = jnp.where(position == 0, embedded, forward_in)
+        upstream = jnp.where(position == sections - 1, cotangent[0, step_index], backward_in)
         if step_index == 0:
-            forward_normed_full, last_upstream_full = lax.optimization_barrier(
-                (forward_normed_full, last_upstream_full)
-            )
+            upstream_full, backward_normed_full[0] = gathered([upstream, saved_normed[0]])
+            sent = to_partner(jnp.stack([upstream_full, backward_normed_full[0]]), 1)
+            partner_upstream.append(sent[0])
+            partner_normed[0] = sent[1]
+            forward_rows, upstream_full = lax.optimization_barrier(
+                ([normed_rows(current)] + saved_normed[1:], upstream_full)
+            )
+            forward_normed_full, *later = gathered(forward_rows)
+            backward_normed_full[1:] = later
+            for later_index, later_full in enumerate(later):
+                partner_normed[later_index + 1] = to_partner(later_full, 0)
         else:
-            forward_normed, in_flight = lax.optimization_barrier((normed_rows(current), in_flight))
+            upstream, last_result, held = lax.optimization_barrier(
+                (upstream, last_result, (partner_upstream, partner_normed[:step_index], partner_d_projected, partner_mixed))
+            )
+            partner_upstream, normed_done, partner_d_projected, partner_mixed = held
+            partner_normed[:step_index] = normed_done
+            upstream_full = gathered([upstream])[0]
+            partner_upstream.append(to_partner(upstream_full, 0))
+            forward_normed, upstream_full = lax.optimization_barrier(
+                (normed_rows(current), upstream_full)
+            )
             forward_normed_full = gathered([forward_normed])[0]
+        d_normed_part, d_projected, mixed = backward_part(
+            backward_normed_full[step_index], upstream_full, mask_for(1, step_index + position)
+        )
+        upstream_fulls.append(upstream_full)
+        d_projecteds.append(d_projected)
+        mixeds.append(mixed)
+        partner_d_projected.append(to_partner(d_projected, 1))
+        partner_mixed.append(to_partner(mixed, 0))
+        d_normed_part, forward_normed_full = lax.optimization_barrier(
+            (d_normed_part, forward_normed_full)
+        )
+        d_normed = scattered([d_normed_part])[0]
         attn_part = forward_part(
             forward_normed_full, mask_for(0, step_index - position + sections - 1)
         )
-        if step_index == last_step:
-            attn_rows, d_normed = scattered([attn_part, last_d_normed_part])
-            backward_outs.append(input_grad(saved[0, 0, last_step], last_upstream, d_normed))
-        else:
-            attn_rows = scattered([attn_part])[0]
+        attn_part, d_normed = lax.optimization_barrier((attn_part, d_normed))
+        attn_rows = scattered([attn_part])[0]
+        last_result = attn_rows
+        backward_out = input_grad(saved[0, 0, step_index], upstream, d_normed)
         forward_out = (current.astype(jnp.float32) + attn_rows.astype(jnp.float32)).astype(
             jnp.bfloat16
         )
         forward_outs.append(forward_out)
+        backward_outs.append(backward_out)
         if step_index < last_step:
+            backward_in = lax.ppermute(backward_out, pair_axes, down_pairs)
             forward_in = lax.ppermute(forward_out, pair_axes, up_pairs)
 
-    qkv_sums = []
-    out_sums = []
-    for (low, high), hops, piece in zip(spans, routes, in_flight):
-        for mask in hops[1:]:
-            piece = flipped(piece, pair_axes, mask)
-        qkv_sums.append(
-            (own_qkv[:, low:high, :].astype(jnp.float32) + piece[0].astype(jnp.float32)).astype(
-                jnp.bfloat16
-            )
-        )
-        out_sums.append(
-            (own_out[:, low:high].astype(jnp.float32) + piece[1].astype(jnp.float32)).astype(
-                jnp.bfloat16
-            )
-        )
-    grad_qkv = jnp.concatenate(qkv_sums, axis=1)
-    grad_out = jnp.concatenate(out_sums, axis=1)
+    own_qkv, own_out = weight_terms(backward_normed_full, d_projecteds, mixeds, upstream_fulls)
+    other_qkv, other_out = weight_terms(
+        partner_normed, partner_d_projected, partner_mixed, partner_upstream
+    )
+    grad_qkv = (own_qkv.astype(jnp.float32) + other_qkv.astype(jnp.float32)).astype(jnp.bfloat16)
+    grad_out = (own_out.astype(jnp.float32) + other_out.astype(jnp.float32)).astype(jnp.bfloat16)
     acts_block = jnp.stack(forward_outs)[None, None]
     grads_block = jnp.stack(backward_outs)[None, None]
     return (acts_block, grads_block, grad_qkv[None, None], grad_out[None, None])

time: 399 us -> 368 us (0.922)
  waiting for transfers between devices: 286 us -> 222 us
  starting transfers between devices: 12.5 us -> 34 us
  matrix products: 46.8 us -> 58.6 us
  local copies, waits for them, and re-layouts: 13.8 us -> 25.2 us
  other arithmetic: 24 us -> 12.9 us
    ppermute x8 -> x28, waiting for transfers between devices: 68.2 us -> 44.7 us  [flipped(): lax.ppermute(value, axis, [(i, i ^ mask) for i in range(lax.axis_size(axi...]
    ppermute x8 -> x28, starting transfers between devices: 7.31 us -> 29.3 us  [flipped(): lax.ppermute(value, axis, [(i, i ^ mask) for i in range(lax.axis_size(axi...]
    dot_general x4 -> x8, matrix products: 16.9 us -> 35.3 us  [the longest x4 24.8 us: weight_terms(): jnp.einsum('sd,csn->cdn', normed_full, d_projected, preferred_element_typ...]
    ppermute x1, waiting for transfers between devices: 22.5 us -> 4.3 us  [shards(): forward_in = lax.ppermute(forward_out, pair_axes, up_pairs)]
    all_gather x4, waiting for transfers between devices: 143 us -> 134 us  [gathered(): full = lax.all_gather(jnp.stack(blocks), 'tp', axis=1, tiled=True)]
    reduce_scatter x3 -> x4, waiting for transfers between devices: 41.7 us -> 32.2 us  [scattered(): lax.psum_scatter(jnp.stack(blocks), 'tp', scatter_dimension=1, tiled=True)]
    squeeze x0 -> x3, local copies, waits for them, and re-layouts: none -> 6.86 us  [the longest x2 3.92 us: gathered(): return [full[i] for i in range(len(blocks))]]
    dot_general x4, matrix products: 13.2 us -> 8.17 us  [heads_of(): jnp.einsum('sd,cdn->csn', normed_full, qkv_weight, preferred_element_type...]
  transfers between devices with their start and end apart: 17 -> 38, of which waited for: 13 -> 17; matrix products, arithmetic and copies ran while one was open for 13% -> 22% of each run, Pallas kernels for 0% -> 0%
where the time goes in v5:
time: 368 us; the launch traced here: 367 us
  waiting for transfers between devices  222 us (60%)
  matrix products  58.6 us (16%)
  starting transfers between devices  34 us (9%)
  local copies, waits for them, and re-layouts  25.2 us (7%)
  between operations  14.9 us (4%)
  other arithmetic  12.9 us (4%)
    all_gather x4, waiting for transfers between devices, gathered(): full = lax.all_gather(jnp.stack(blocks), 'tp', axis=1, tiled=True)  134 us
    ppermute x28, waiting for transfers between devices, flipped(): lax.ppermute(value, axis, [(i, i ^ mask) for i in range(lax.axis_size(axi...  44.7 us
    reduce_scatter x4, waiting for transfers between devices, scattered(): lax.psum_scatter(jnp.stack(blocks), 'tp', scatter_dimension=1, tiled=True)  32.2 us
    ppermute x28, starting transfers between devices, flipped(): lax.ppermute(value, axis, [(i, i ^ mask) for i in range(lax.axis_size(axi...  29.3 us
    dot_general x4, matrix products, weight_terms(): jnp.einsum('sd,csn->cdn', normed_full, d_projected, preferred_element_typ...  24.8 us
    unnamed x96, local copies, waits for them, and re-layouts  10.7 us
    dot_general x4, matrix products, weight_terms(): jnp.einsum('sn,sd->nd', mixed, upstream_full, preferred_element_type=jnp....  10.6 us
    dot_general x4, matrix products, heads_of(): jnp.einsum('sd,cdn->csn', normed_full, qkv_weight, preferred_element_type...  8.17 us
  transfers between devices with their start and end apart: 38, of which 17 were waited for; matrix products, arithmetic and copies ran while one was open for 22% of the time, Pallas kernels for 0%

profile of v5, /device:TPU:0, one launch (start us, length us, event | category | flops | bytes accessed | tf_op | source)
XLA Modules:
  0.0 367.4 jit_solution(16262063002748887817)
XLA Ops:
  14.7 53.8 %all-gather.7.cloned.1.call-done = bf16[2,128,5120]{2,1,0:T(8,128)(2,1)} async-done(((bf16[2,32,5120]{2,1,0:T(8,128)(2,1)}), bf16[2,128,5120]{2,1,0:T(8,128)(2,1)}) %all-gather.7.cloned.1.call-update) | async-done | bytes 2621456 | tf_op jit(solution)/shard_map/all_gather | solution.py:54
  71.1 3.5 fusion.71
  78.5 46.1 %all-gather.9.cloned.1.call-done = bf16[2,128,5120]{2,1,0:T(8,128)(2,1)} async-done(((bf16[2,32,5120]{2,1,0:T(8,128)(2,1)}), bf16[2,128,5120]{2,1,0:T(8,128)(2,1)}) %all-gather.9.cloned.1.call-update) | async-done | bytes 2621456 | tf_op jit(solution)/shard_map/all_gather | solution.py:54
  127.8 3.6 fusion.155
  139.3 18.3 %reduce-scatter.5.cloned.1.call-done = bf16[1,32,5120]{2,1,0:T(8,128)(2,1)} async-done(((bf16[1,128,5120]{2,1,0:T(8,128)(2,1)}), bf16[1,32,5120]{2,1,0:T(8,128)(2,1)}) %reduce-scatter.5.cloned.1.call-update) | async-done | bytes 327696 | tf_op jit(solution)/shard_map/reduce_scatter | solution.py:59
  158.3 4.4 %collective-permute-done.2 = bf16[2,64,5120]{2,1,0:T(8,128)(2,1)} collective-permute-done((bf16[2,64,5120]{2,1,0:T(8,128)(2,1)}, bf16[2,64,5120]{2,1,0:T(8,128)(2,1)}, u32[]{:S(2)}, u32[]{:S(2)}) %collective-permute-start.2) | collective-permute-done | bytes 1310752 | tf_op jit(solution)/shard_map/ppermute | solution.py:20
  168.1 5.6 %fusion.41 = f32[3,128,5120]{2,1,0:T(8,128)} fusion(bf16[2,128,5120]{2,1,0:T(8,128)(2,1)} %all-gather.7.cloned.1.call-done, bf16[1,128,1,128]{3,1,2,0:T(8,128)(2,1)S(1)} %fusion.92, bf16[1,128,1,128]{3,1,2,0:T(8,128)(2,1)S(1)} %fusion.87, bf16[1,128,1,128]{3,1,2,0:T(8,128)(2,1)S(1)} %fusion.86), kind=kOutput, calls=%fused_computation.59 | convolution fusion | flops 503414784 | bytes 9273344 | tf_op jit(solution)/shard_map/sd,csn->cdn/dot_general | solution.py:127
  173.8 19.6 %collective-permute-done.12 = bf16[64,128]{1,0:T(8,128)(2,1)S(1)} collective-permute-done((bf16[64,128]{1,0:T(8,128)(2,1)S(1)}, bf16[64,128]{1,0:T(8,128)(2,1)S(1)}, u32[]{:S(2)}, u32[]{:S(2)}) %collective-permute-start.12) | collective-permute-done | bytes 16416 | tf_op jit(solution)/shard_map/ppermute | solution.py:20
  207.0 2.9 collective-permute-start
  210.2 4.3 %collective-permute-done = bf16[32,5120]{1,0:T(8,128)(2,1)S(1)} collective-permute-done((bf16[32,5120]{1,0:T(8,128)(2,1)S(1)}, bf16[32,5120]{1,0:T(8,128)(2,1)S(1)}, u32[]{:S(2)}, u32[]{:S(2)}) %collective-permute-start) | collective-permute-done | bytes 327712 | tf_op jit(solution)/shard_map/ppermute | solution.py:244
  217.3 2.9 slice_bitcast_fusion.1
  220.3 6.6 %collective-permute-done.1 = bf16[32,5120]{1,0:T(8,128)(2,1)S(1)} collective-permute-done((bf16[32,5120]{1,0:T(8,128)(2,1)S(1)}, bf16[32,5120]{1,0:T(8,128)(2,1)S(1)}, u32[]{:S(2)}, u32[]{:S(2)}) %collective-permute-start.1) | collective-permute-done | bytes 327712 | tf_op jit(solution)/shard_map/ppermute | solution.py:243
  230.7 3.0 fusion.63
  235.7 10.6 %collective-permute-done.18 = bf16[64,5120]{1,0:T(8,128)(2,1)} collective-permute-done((bf16[64,5120]{1,0:T(8,128)(2,1)S(1)}, bf16[64,5120]{1,0:T(8,128)(2,1)}, u32[]{:S(2)}, u32[]{:S(2)}) %collective-permute-start.18) | collective-permute-done | bytes 655392 | tf_op jit(solution)/shard_map/ppermute | solution.py:20
  248.4 10.8 %all-gather.11.cloned.1.call-done = bf16[128,5120]{1,0:T(8,128)(2,1)} async-done(((bf16[32,5120]{1,0:T(8,128)(2,1)}), bf16[128,5120]{1,0:T(8,128)(2,1)}) %all-gather.11.cloned.1.call-update) | async-done | bytes 1310736 | tf_op jit(solution)/shard_map/all_gather | solution.py:54
  261.5 4.3 %fusion.31 = f32[3,128,5120]{2,1,0:T(8,128)} fusion(bf16[3,128,128]{2,1,0:T(8,128)(2,1)S(1)} %pad_maximum_fusion.2, bf16[128,5120]{1,0:T(8,128)(2,1)S(1)} %copy-done.14), kind=kOutput, calls=%fused_computation.49 | convolution fusion | flops 503316480 | bytes 9273344 | tf_op jit(solution)/shard_map/sd,csn->cdn/dot_general | solution.py:127
  269.8 23.0 %all-gather.13.cloned.1.call-done = bf16[128,5120]{1,0:T(8,128)(2,1)} async-done(((bf16[32,5120]{1,0:T(8,128)(2,1)}), bf16[128,5120]{1,0:T(8,128)(2,1)}) %all-gather.13.cloned.1.call-update) | async-done | bytes 1310736 | tf_op jit(solution)/shard_map/all_gather | solution.py:54
  298.1 6.8 %add_convert_fusion.2 = bf16[3,128,5120]{2,1,0:T(8,128)(2,1)} fusion(f32[3,128,5120]{2,1,0:T(8,128)} %fusion.41, bf16[2,128,5120]{2,1,0:T(8,128)(2,1)S(1)} %copy-done.9, bf16[1,128,1,128]{3,1,2,0:T(8,128)(2,1)S(1)} %fusion.93, bf16[1,128,1,128]{3,1,2,0:T(8,128)(2,1)S(1)} %fusion.90, bf16[1,128,1,128]{3,1,2,0:T(8,128)(2,1)S(1)} %fusion.89), kind=kOutput, calls=%fused_computation.2 | convolution fusion | flops 507346944 | bytes 13205504 | tf_op jit(solution)/shard_map/sd,csn->cdn/dot_general | solution.py:127
  306.0 4.6 %collective-permute-done.24 = bf16[64,128]{1,0:T(8,128)(2,1)S(1)} collective-permute-done((bf16[64,128]{1,0:T(8,128)(2,1)S(1)}, bf16[64,128]{1,0:T(8,128)(2,1)S(1)}, u32[]{:S(2)}, u32[]{:S(2)}) %collective-permute-start.24) | collective-permute-done | bytes 16416 | tf_op jit(solution)/shard_map/ppermute | solution.py:20
  320.9 5.3 %reduce-scatter.9.cloned.1.call-done = bf16[1,32,5120]{2,1,0:T(8,128)(2,1)} async-done(((bf16[1,128,5120]{2,1,0:T(8,128)(2,1)}), bf16[1,32,5120]{2,1,0:T(8,128)(2,1)}) %reduce-scatter.9.cloned.1.call-update) | async-done | bytes 327696 | tf_op jit(solution)/shard_map/reduce_scatter | solution.py:59
  329.3 8.1 %fusion = bf16[1,1,3,5120,128]{3,4,2,1,0:T(8,128)(2,1)} fusion(f32[3,128,5120]{2,1,0:T(8,128)} %fusion.31, bf16[3,128,5120]{2,1,0:T(8,128)(2,1)} %add_convert_fusion.2, bf16[64,5120]{1,0:T(8,128)(2,1)} %collective-permute-done.21, bf16[64,5120]{1,0:T(8,128)(2,1)} %collective-permute-done.19, bf16[3,64,128]{2,1,0:T(8,128)(2,1)S(1)} %collective-permute-done.17, ...), kind=kOutput, calls=%fused_computation.3 | convolution fusion | flops 517931008 | bytes 17137664 | tf_op jit(solution)/shard_map/sd,csn->cdn/dot_general | solution.py:127
  337.4 6.3 %copy.19 = bf16[1,1,3,5120,128]{4,3,2,1,0:T(8,128)(2,1)} copy(bf16[1,1,3,5120,128]{3,4,2,1,0:T(8,128)(2,1)} %fusion) | data formatting | bytes 7864320
  343.7 4.4 %fusion.9 = bf16[1,1,128,5120]{3,2,1,0:T(8,128)(2,1)} fusion(f32[128,5120]{1,0:T(8,128)} %fusion.6, f32[128,5120]{1,0:T(8,128)} %fusion.163, bf16[64,5120]{1,0:T(8,128)(2,1)} %collective-permute-done.29, bf16[64,5120]{1,0:T(8,128)(2,1)S(1)} %collective-permute-done.27, bf16[64,128]{1,0:T(8,128)(2,1)S(1)} %collective-permute-done.25, ...), kind=kOutput, calls=%fused_computation.18 | convolution fusion | flops 173735936 | bytes 7897088 | tf_op jit(solution)/shard_map/sn,sd->nd/dot_general | solution.py:130
  350.0 8.6 %reduce-scatter.11.cloned.1.call-done = bf16[1,32,5120]{2,1,0:T(8,128)(2,1)} async-done(((bf16[1,128,5120]{2,1,0:T(8,128)(2,1)}), bf16[1,32,5120]{2,1,0:T(8,128)(2,1)}) %reduce-scatter.11.cloned.1.call-update) | async-done | bytes 327696 | tf_op jit(solution)/shard_map/reduce_scatter | solution.py:59
  (239 shorter events, 85.0 us)
Async XLA Ops:
  7.2 61.3 %all-gather.7.cloned.1.call-start = ((), (), s32[]{:S(2)}) async-start(), calls=%async_computation.4 | async-start | bytes 3276800 | tf_op jit(solution)/shard_map/all_gather | solution.py:54
  10.9 113.7 %all-gather.9.cloned.1.call-start = ((), (), s32[]{:S(2)}) async-start(), calls=%async_computation.5 | async-start | bytes 3276800 | tf_op jit(solution)/shard_map/all_gather | solution.py:54
  71.0 86.7 %reduce-scatter.5.cloned.1.call-start = ((), (), s32[]{:S(2)}) async-start(), calls=%async_computation.6 | async-start | bytes 1638400 | tf_op jit(solution)/shard_map/reduce_scatter | solution.py:59
  127.1 78.6 %reduce-scatter.7.cloned.1.call-start = ((), (), s32[]{:S(2)}) async-start(), calls=%async_computation.7 | async-start | bytes 1638400 | tf_op jit(solution)/shard_map/reduce_scatter | solution.py:59
  131.4 31.4 %collective-permute-start.2 = (bf16[2,64,5120]{2,1,0:T(8,128)(2,1)}, bf16[2,64,5120]{2,1,0:T(8,128)(2,1)}, u32[]{:S(2)}, u32[]{:S(2)}) collective-permute-start(bf16[2,64,5120]{2,1,0:T(8,128)(2,1)} %get-tuple-element.51), channel_id=1, source_target_pairs={{0,9},{1,8},{8,1},{9,0},{16,25},{17,24},{24,17},{25,16},{2,11},{3,... | collective-permute-start | bytes 3932168 | tf_op jit(solution)/shard_map/ppermute | solution.py:20
  133.1 34.5 %collective-permute-start.4 = (bf16[2,64,5120]{2,1,0:T(8,128)(2,1)}, bf16[2,64,5120]{2,1,0:T(8,128)(2,1)}, u32[]{:S(2)}, u32[]{:S(2)}) collective-permute-start(bf16[2,64,5120]{2,1,0:T(8,128)(2,1)} %get-tuple-element.50), channel_id=1, source_target_pairs={{0,17},{1,16},{8,25},{9,24},{16,1},{17,0},{24,9},{25,8},{2,19},{3,... | collective-permute-start | bytes 3932168 | tf_op jit(solution)/shard_map/ppermute | solution.py:20
  157.7 101.5 %all-gather.11.cloned.1.call-start = ((), (), s32[]{:S(2)}) async-start(), calls=%async_computation.10 | async-start | bytes 1638400 | tf_op jit(solution)/shard_map/all_gather | solution.py:54
  162.7 40.6 %collective-permute-start.3 = (bf16[2,64,5120]{2,1,0:T(8,128)(2,1)}, bf16[2,64,5120]{2,1,0:T(8,128)(2,1)S(1)}, u32[]{:S(2)}, u32[]{:S(2)}) collective-permute-start(bf16[2,64,5120]{2,1,0:T(8,128)(2,1)} %collective-permute-done.2), channel_id=1, source_target_pairs={{0,16},{1,17},{8,24},{9,25},{16,0},{17,1},{24,8},{25,9},{2,18},{3,... | collective-permute-start | bytes 3932168 | tf_op jit(solution)/shard_map/ppermute | solution.py:20
  164.3 34.5 %collective-permute-start.6 = (bf16[3,64,128]{2,1,0:T(8,128)(2,1)S(1)}, bf16[3,64,128]{2,1,0:T(8,128)(2,1)S(1)}, u32[]{:S(2)}, u32[]{:S(2)}) collective-permute-start(bf16[3,64,128]{2,1,0:T(8,128)(2,1)S(1)} %get-tuple-element.56), channel_id=1, source_target_pairs={{0,9},{1,8},{8,1},{9,0},{16,25},{17,24},{24,17},{25,16},{2,11},{3,... | collective-permute-start | bytes 147464 | tf_op jit(solution)/shard_map/ppermute | solution.py:20
  164.9 28.4 %collective-permute-start.12 = (bf16[64,128]{1,0:T(8,128)(2,1)S(1)}, bf16[64,128]{1,0:T(8,128)(2,1)S(1)}, u32[]{:S(2)}, u32[]{:S(2)}) collective-permute-start(bf16[64,128]{1,0:T(8,128)(2,1)S(1)} %get-tuple-element.61), channel_id=1, source_target_pairs={{0,17},{1,16},{8,25},{9,24},{16,1},{17,0},{24,9},{25,8},{2,19},{3,... | collective-permute-start | bytes 49160 | tf_op jit(solution)/shard_map/ppermute | solution.py:20
  166.1 29.4 %collective-permute-start.11 = (bf16[64,128]{1,0:T(8,128)(2,1)S(1)}, bf16[64,128]{1,0:T(8,128)(2,1)S(1)}, u32[]{:S(2)}, u32[]{:S(2)}) collective-permute-start(bf16[64,128]{1,0:T(8,128)(2,1)S(1)} %collective-permute-done.10), channel_id=1, source_target_pairs={{0,16},{1,17},{8,24},{9,25},{16,0},{17,1},{24,8},{25,9},{2,18},{3,... | collective-permute-start | bytes 49160 | tf_op jit(solution)/shard_map/ppermute | solution.py:20
  167.6 37.0 %collective-permute-start.5 = (bf16[2,64,5120]{2,1,0:T(8,128)(2,1)}, bf16[2,64,5120]{2,1,0:T(8,128)(2,1)S(1)}, u32[]{:S(2)}, u32[]{:S(2)}) collective-permute-start(bf16[2,64,5120]{2,1,0:T(8,128)(2,1)} %collective-permute-done.4), channel_id=1, source_target_pairs={{0,8},{1,9},{8,0},{9,1},{16,24},{17,25},{24,16},{25,17},{2,10},{3,... | collective-permute-start | bytes 3932168 | tf_op jit(solution)/shard_map/ppermute | solution.py:20
  227.6 65.3 %all-gather.13.cloned.1.call-start = ((), (), s32[]{:S(2)}) async-start(), calls=%async_computation.11 | async-start | bytes 1638400 | tf_op jit(solution)/shard_map/all_gather | solution.py:54
  229.3 17.5 %collective-permute-start.20 = (bf16[64,5120]{1,0:T(8,128)(2,1)S(1)}, bf16[64,5120]{1,0:T(8,128)(2,1)}, u32[]{:S(2)}, u32[]{:S(2)}) collective-permute-start(bf16[64,5120]{1,0:T(8,128)(2,1)S(1)} %get-tuple-element.47), channel_id=1, source_target_pairs={{0,17},{1,16},{8,25},{9,24},{16,1},{17,0},{24,9},{25,8},{2,19},{3,... | collective-permute-start | bytes 1966088 | tf_op jit(solution)/shard_map/ppermute | solution.py:20
  234.7 71.0 %collective-permute-start.22 = (bf16[64,128]{1,0:T(8,128)(2,1)}, bf16[64,128]{1,0:T(8,128)(2,1)}, u32[]{:S(2)}, u32[]{:S(2)}) collective-permute-start(bf16[64,128]{1,0:T(8,128)(2,1)} %get-tuple-element.58), channel_id=1, source_target_pairs={{0,9},{1,8},{8,1},{9,0},{16,25},{17,24},{24,17},{25,16},{2,11},{3,... | collective-permute-start | bytes 49160 | tf_op jit(solution)/shard_map/ppermute | solution.py:20
  246.2 65.6 %collective-permute-start.19 = (bf16[64,5120]{1,0:T(8,128)(2,1)}, bf16[64,5120]{1,0:T(8,128)(2,1)}, u32[]{:S(2)}, u32[]{:S(2)}) collective-permute-start(bf16[64,5120]{1,0:T(8,128)(2,1)} %collective-permute-done.18), channel_id=1, source_target_pairs={{0,16},{1,17},{8,24},{9,25},{16,0},{17,1},{24,8},{25,9},{2,18},{3,... | collective-permute-start | bytes 1966088 | tf_op jit(solution)/shard_map/ppermute | solution.py:20
  246.8 79.4 %collective-permute-start.21 = (bf16[64,5120]{1,0:T(8,128)(2,1)}, bf16[64,5120]{1,0:T(8,128)(2,1)}, u32[]{:S(2)}, u32[]{:S(2)}) collective-permute-start(bf16[64,5120]{1,0:T(8,128)(2,1)} %collective-permute-done.20), channel_id=1, source_target_pairs={{0,8},{1,9},{8,0},{9,1},{16,24},{17,25},{24,16},{25,17},{2,10},{3,... | collective-permute-start | bytes 1966088 | tf_op jit(solution)/shard_map/ppermute | solution.py:20
  259.2 67.0 %reduce-scatter.9.cloned.1.call-start = ((), (), s32[]{:S(2)}) async-start(), calls=%async_computation.8 | async-start | bytes 1638400 | tf_op jit(solution)/shard_map/reduce_scatter | solution.py:59
  292.9 65.7 %reduce-scatter.11.cloned.1.call-start = ((), (), s32[]{:S(2)}) async-start(), calls=%async_computation.9 | async-start | bytes 1638400 | tf_op jit(solution)/shard_map/reduce_scatter | solution.py:59
  293.0 23.9 %collective-permute-start.26 = (bf16[64,5120]{1,0:T(8,128)(2,1)S(1)}, bf16[64,5120]{1,0:T(8,128)(2,1)}, u32[]{:S(2)}, u32[]{:S(2)}) collective-permute-start(bf16[64,5120]{1,0:T(8,128)(2,1)S(1)} %get-tuple-element.52), channel_id=1, source_target_pairs={{0,9},{1,8},{8,1},{9,0},{16,25},{17,24},{24,17},{25,16},{2,11},{3,... | collective-permute-start | bytes 1966088 | tf_op jit(solution)/shard_map/ppermute | solution.py:20
  293.2 24.8 %collective-permute-start.28 = (bf16[64,5120]{1,0:T(8,128)(2,1)S(1)}, bf16[64,5120]{1,0:T(8,128)(2,1)}, u32[]{:S(2)}, u32[]{:S(2)}) collective-permute-start(bf16[64,5120]{1,0:T(8,128)(2,1)S(1)} %get-tuple-element.53), channel_id=1, source_target_pairs={{0,17},{1,16},{8,25},{9,24},{16,1},{17,0},{24,9},{25,8},{2,19},{3,... | collective-permute-start | bytes 1966088 | tf_op jit(solution)/shard_map/ppermute | solution.py:20
  317.0 26.7 %collective-permute-start.27 = (bf16[64,5120]{1,0:T(8,128)(2,1)}, bf16[64,5120]{1,0:T(8,128)(2,1)S(1)}, u32[]{:S(2)}, u32[]{:S(2)}) collective-permute-start(bf16[64,5120]{1,0:T(8,128)(2,1)} %collective-permute-done.26), channel_id=1, source_target_pairs={{0,16},{1,17},{8,24},{9,25},{16,0},{17,1},{24,8},{25,9},{2,18},{3,... | collective-permute-start | bytes 1966088 | tf_op jit(solution)/shard_map/ppermute | solution.py:20
  318.0 25.7 %collective-permute-start.29 = (bf16[64,5120]{1,0:T(8,128)(2,1)}, bf16[64,5120]{1,0:T(8,128)(2,1)}, u32[]{:S(2)}, u32[]{:S(2)}) collective-permute-start(bf16[64,5120]{1,0:T(8,128)(2,1)} %collective-permute-done.28), channel_id=1, source_target_pairs={{0,8},{1,9},{8,0},{9,1},{16,24},{17,25},{24,16},{25,17},{2,10},{3,... | collective-permute-start | bytes 1966088 | tf_op jit(solution)/shard_map/ppermute | solution.py:20
  326.2 17.4 %collective-permute-start.23 = (bf16[64,128]{1,0:T(8,128)(2,1)}, bf16[64,128]{1,0:T(8,128)(2,1)S(1)}, u32[]{:S(2)}, u32[]{:S(2)}) collective-permute-start(bf16[64,128]{1,0:T(8,128)(2,1)} %collective-permute-done.22), channel_id=1, source_target_pairs={{0,16},{1,17},{8,24},{9,25},{16,0},{17,1},{24,8},{25,9},{2,18},{3,... | collective-permute-start | bytes 49160 | tf_op jit(solution)/shard_map/ppermute | solution.py:20
  (61 other events, 380.4 us)
Sparse Core Ops, SparseCore 0:
  11.0 57.4 all-gather.6
  71.1 53.5 all-gather.8
  127.5 30.1 reduce-scatter.4
  160.4 30.0 reduce-scatter.6
  227.7 31.4 all-gather.10
  261.2 31.6 all-gather.12
  295.7 30.4 reduce-scatter.8
  328.5 30.0 reduce-scatter.10

commit v6 on v5

--- a/solution.py
+++ b/solution.py
@@ -193,46 +193,23 @@
         upstream = jnp.where(position == sections - 1, cotangent[0, step_index], backward_in)
         if step_index == 0:
             upstream_full, backward_normed_full[0] = gathered([upstream, saved_normed[0]])
-            sent = to_partner(jnp.stack([upstream_full, backward_normed_full[0]]), 1)
-            partner_upstream.append(sent[0])
-            partner_normed[0] = sent[1]
             forward_rows, upstream_full = lax.optimization_barrier(
                 ([normed_rows(current)] + saved_normed[1:], upstream_full)
             )
             forward_normed_full, *later = gathered(forward_rows)
             backward_normed_full[1:] = later
-            for later_index, later_full in enumerate(later):
-                partner_normed[later_index + 1] = to_partner(later_full, 0)
         else:
-            upstream, last_result, held = lax.optimization_barrier(
-                (upstream, last_result, (partner_upstream, partner_normed[:step_index], partner_d_projected, partner_mixed))
-            )
-            partner_upstream, normed_done, partner_d_projected, partner_mixed = held
-            partner_normed[:step_index] = normed_done
-            upstream_full = gathered([upstream])[0]
-            partner_upstream.append(to_partner(upstream_full, 0))
-            forward_normed, upstream_full = lax.optimization_barrier(
-                (normed_rows(current), upstream_full)
-            )
-            forward_normed_full = gathered([forward_normed])[0]
+            upstream_full, forward_normed_full = gathered([upstream, normed_rows(current)])
         d_normed_part, d_projected, mixed = backward_part(
             backward_normed_full[step_index], upstream_full, mask_for(1, step_index + position)
         )
         upstream_fulls.append(upstream_full)
         d_projecteds.append(d_projected)
         mixeds.append(mixed)
-        partner_d_projected.append(to_partner(d_projected, 1))
-        partner_mixed.append(to_partner(mixed, 0))
-        d_normed_part, forward_normed_full = lax.optimization_barrier(
-            (d_normed_part, forward_normed_full)
-        )
-        d_normed = scattered([d_normed_part])[0]
         attn_part = forward_part(
             forward_normed_full, mask_for(0, step_index - position + sections - 1)
         )
-        attn_part, d_normed = lax.optimization_barrier((attn_part, d_normed))
-        attn_rows = scattered([attn_part])[0]
-        last_result = attn_rows
+        d_normed, attn_rows = scattered([d_normed_part, attn_part])
         backward_out = input_grad(saved[0, 0, step_index], upstream, d_normed)
         forward_out = (current.astype(jnp.float32) + attn_rows.astype(jnp.float32)).astype(
             jnp.bfloat16
@@ -242,6 +219,17 @@
         if step_index < last_step:
             backward_in = lax.ppermute(backward_out, pair_axes, down_pairs)
             forward_in = lax.ppermute(forward_out, pair_axes, up_pairs)
+            held = (upstream_fulls, backward_normed_full, d_projecteds, mixeds)
+            held, backward_in, forward_in = lax.optimization_barrier(
+                (held, backward_in, forward_in)
+            )
+            upstream_fulls, backward_normed_full, d_projecteds, mixeds = held
+            if step_index == 0:
+                for later_index in range(window_steps):
+                    partner_normed[later_index] = to_partner(backward_normed_full[later_index], 0)
+        partner_upstream.append(to_partner(upstream_fulls[step_index], 0))
+        partner_d_projected.append(to_partner(d_projecteds[step_index], 1))
+        partner_mixed.append(to_partner(mixeds[step_index], 0))
 
     own_qkv, own_out = weight_terms(backward_normed_full, d_projecteds, mixeds, upstream_fulls)
     other_qkv, other_out = weight_terms(

time: 368 us -> 441 us (1.20)
  waiting for transfers between devices: 222 us -> 292 us
  matrix products: 58.6 us -> 46.6 us
  other arithmetic: 12.9 us -> 23.2 us
  starting transfers between devices: 34 us -> 41.2 us
    ppermute x28 -> x32, waiting for transfers between devices: 44.7 us -> 100 us  [flipped(): lax.ppermute(value, axis, [(i, i ^ mask) for i in range(lax.axis_size(axi...]
    dot_general x4, matrix products: 24.8 us -> 6.76 us  [weight_terms(): jnp.einsum('sd,csn->cdn', normed_full, d_projected, preferred_element_typ...]
    reduce_scatter x4 -> x2, waiting for transfers between devices: 32.2 us -> 44 us  [scattered(): lax.psum_scatter(jnp.stack(blocks), 'tp', scatter_dimension=1, tiled=True)]
    all_gather x4 -> x3, waiting for transfers between devices: 134 us -> 142 us  [gathered(): full = lax.all_gather(jnp.stack(blocks), 'tp', axis=1, tiled=True)]
    dot_general x4, matrix products: 10.6 us -> 4.79 us  [weight_terms(): jnp.einsum('sn,sd->nd', mixed, upstream_full, preferred_element_type=jnp....]
    ppermute x28 -> x32, starting transfers between devices: 29.3 us -> 35 us  [flipped(): lax.ppermute(value, axis, [(i, i ^ mask) for i in range(lax.axis_size(axi...]
    dot_general x4, matrix products: 8.17 us -> 13.3 us  [heads_of(): jnp.einsum('sd,cdn->csn', normed_full, qkv_weight, preferred_element_type...]
    unnamed x96 -> x107, local copies, waits for them, and re-layouts: 10.7 us -> 9.6 us
  transfers between devices with their start and end apart: 38 -> 39, of which waited for: 17 -> 15; matrix products, arithmetic and copies ran while one was open for 22% -> 14% of each run, Pallas kernels for 0% -> 0%
where the time goes in v6:
time: 441 us
  waiting for transfers between devices  292 us (66%)
  matrix products  46.6 us (11%)
  starting transfers between devices  41.2 us (9%)
  other arithmetic  23.2 us (5%)
  local copies, waits for them, and re-layouts  23.1 us (5%)
  between operations  14.6 us (3%)
    all_gather x3, waiting for transfers between devices, gathered(): full = lax.all_gather(jnp.stack(blocks), 'tp', axis=1, tiled=True)  142 us
    ppermute x32, waiting for transfers between devices, flipped(): lax.ppermute(value, axis, [(i, i ^ mask) for i in range(lax.axis_size(axi...  100 us
    reduce_scatter x2, waiting for transfers between devices, scattered(): lax.psum_scatter(jnp.stack(blocks), 'tp', scatter_dimension=1, tiled=True)  44 us
    ppermute x32, starting transfers between devices, flipped(): lax.ppermute(value, axis, [(i, i ^ mask) for i in range(lax.axis_size(axi...  35 us
    dot_general x4, matrix products, heads_of(): jnp.einsum('sd,cdn->csn', normed_full, qkv_weight, preferred_element_type...  13.3 us
    unnamed x107, local copies, waits for them, and re-layouts  9.6 us
  transfers between devices with their start and end apart: 39, of which 15 were waited for; matrix products, arithmetic and copies ran while one was open for 14% of the time, Pallas kernels for 0%

profile of v6, /device:TPU:0, one launch (start us, length us, event | category | flops | bytes accessed | tf_op | source)
XLA Modules:
  0.0 440.6 jit_solution(331276155219573588)
XLA Ops:
  15.2 54.3 %all-gather.4.cloned.1.call-done = bf16[2,128,5120]{2,1,0:T(8,128)(2,1)} async-done(((bf16[2,32,5120]{2,1,0:T(8,128)(2,1)}), bf16[2,128,5120]{2,1,0:T(8,128)(2,1)}) %all-gather.4.cloned.1.call-update) | async-done | bytes 2621456 | tf_op jit(solution)/shard_map/all_gather | solution.py:54
  69.6 3.1 slice_bitcast_fusion.9
  74.3 3.5 fusion.80
  81.8 45.5 %all-gather.6.cloned.1.call-done = bf16[2,128,5120]{2,1,0:T(8,128)(2,1)} async-done(((bf16[2,32,5120]{2,1,0:T(8,128)(2,1)}), bf16[2,128,5120]{2,1,0:T(8,128)(2,1)}) %all-gather.6.cloned.1.call-update) | async-done | bytes 2621456 | tf_op jit(solution)/shard_map/all_gather | solution.py:54
  127.3 3.4 fusion.77
  134.0 3.4 pad_maximum_fusion
  144.7 44.0 %reduce-scatter.3.cloned.1.call-done = bf16[2,32,5120]{2,1,0:T(8,128)(2,1)} async-done(((bf16[2,128,5120]{2,1,0:T(8,128)(2,1)}), bf16[2,32,5120]{2,1,0:T(8,128)(2,1)}) %reduce-scatter.3.cloned.1.call-update) | async-done | bytes 655376 | tf_op jit(solution)/shard_map/reduce_scatter | solution.py:59
  193.2 4.6 %collective-permute-start.1 = (bf16[32,5120]{1,0:T(8,128)(2,1)S(1)}, bf16[32,5120]{1,0:T(8,128)(2,1)S(1)}, u32[]{:S(2)}, u32[]{:S(2)}) collective-permute-start(bf16[32,5120]{1,0:T(8,128)(2,1)S(1)} %get-tuple-element.44), channel_id=1, source_target_pairs={{0,8},{8,16},{9,1},{16,24},{17,9},{25,17},{2,10},{10,18},{11,3},{1... | collective-permute-start | bytes 983048 | tf_op jit(solution)/shard_map/ppermute | solution.py:221
  198.8 5.6 %collective-permute-done = bf16[32,5120]{1,0:T(8,128)(2,1)S(1)} collective-permute-done((bf16[32,5120]{1,0:T(8,128)(2,1)S(1)}, bf16[32,5120]{1,0:T(8,128)(2,1)S(1)}, u32[]{:S(2)}, u32[]{:S(2)}) %collective-permute-start) | collective-permute-done | bytes 327712 | tf_op jit(solution)/shard_map/ppermute | solution.py:220
  206.7 3.5 fusion.72
  211.3 5.8 %collective-permute-start.26 = (bf16[64,128]{1,0:T(8,128)(2,1)}, bf16[64,128]{1,0:T(8,128)(2,1)}, u32[]{:S(2)}, u32[]{:S(2)}) collective-permute-start(bf16[64,128]{1,0:T(8,128)(2,1)} %get-tuple-element.52), channel_id=1, source_target_pairs={{0,9},{1,8},{8,1},{9,0},{16,25},{17,24},{24,17},{25,16},{2,11},{3,... | collective-permute-start | bytes 49160 | tf_op jit(solution)/shard_map/ppermute | solution.py:20
  224.2 42.5 %all-gather.8.cloned.1.call-done = bf16[2,128,5120]{2,1,0:T(8,128)(2,1)} async-done(((bf16[2,32,5120]{2,1,0:T(8,128)(2,1)}), bf16[2,128,5120]{2,1,0:T(8,128)(2,1)}) %all-gather.8.cloned.1.call-update) | async-done | bytes 2621456 | tf_op jit(solution)/shard_map/all_gather | solution.py:54
  270.8 3.0 fusion.69
  277.9 3.6 fusion.9
  295.1 12.8 %collective-permute-done.3 = bf16[3,64,128]{2,1,0:T(8,128)(2,1)S(1)} collective-permute-done((bf16[3,64,128]{2,1,0:T(8,128)(2,1)S(1)}, bf16[3,64,128]{2,1,0:T(8,128)(2,1)S(1)}, u32[]{:S(2)}, u32[]{:S(2)}) %collective-permute-start.3) | collective-permute-done | bytes 49184 | tf_op jit(solution)/shard_map/ppermute | solution.py:20
  310.0 11.8 %collective-permute-done.5 = bf16[3,64,128]{2,1,0:T(8,128)(2,1)S(1)} collective-permute-done((bf16[3,64,128]{2,1,0:T(8,128)(2,1)S(1)}, bf16[3,64,128]{2,1,0:T(8,128)(2,1)S(1)}, u32[]{:S(2)}, u32[]{:S(2)}) %collective-permute-start.5) | collective-permute-done | bytes 49184 | tf_op jit(solution)/shard_map/ppermute | solution.py:20
  327.9 10.6 %collective-permute-done.8 = bf16[64,5120]{1,0:T(8,128)(2,1)S(1)} collective-permute-done((bf16[64,5120]{1,0:T(8,128)(2,1)S(1)}, bf16[64,5120]{1,0:T(8,128)(2,1)S(1)}, u32[]{:S(2)}, u32[]{:S(2)}) %collective-permute-start.8) | collective-permute-done | bytes 655392 | tf_op jit(solution)/shard_map/ppermute | solution.py:20
  339.4 13.8 %collective-permute-done.15 = bf16[64,5120]{1,0:T(8,128)(2,1)S(1)} collective-permute-done((bf16[64,5120]{1,0:T(8,128)(2,1)}, bf16[64,5120]{1,0:T(8,128)(2,1)S(1)}, u32[]{:S(2)}, u32[]{:S(2)}) %collective-permute-start.15) | collective-permute-done | bytes 655392 | tf_op jit(solution)/shard_map/ppermute | solution.py:20
  356.9 13.8 %collective-permute-done.11 = bf16[3,64,128]{2,1,0:T(8,128)(2,1)S(1)} collective-permute-done((bf16[3,64,128]{2,1,0:T(8,128)(2,1)S(1)}, bf16[3,64,128]{2,1,0:T(8,128)(2,1)S(1)}, u32[]{:S(2)}, u32[]{:S(2)}) %collective-permute-start.11) | collective-permute-done | bytes 49184 | tf_op jit(solution)/shard_map/ppermute | solution.py:20
  378.1 7.3 %collective-permute-done.24 = bf16[64,5120]{1,0:T(8,128)(2,1)} collective-permute-done((bf16[64,5120]{1,0:T(8,128)(2,1)S(1)}, bf16[64,5120]{1,0:T(8,128)(2,1)}, u32[]{:S(2)}, u32[]{:S(2)}) %collective-permute-start.24) | collective-permute-done | bytes 655392 | tf_op jit(solution)/shard_map/ppermute | solution.py:20
  386.0 12.8 %collective-permute-done.7 = bf16[64,5120]{1,0:T(8,128)(2,1)S(1)} collective-permute-done((bf16[64,5120]{1,0:T(8,128)(2,1)S(1)}, bf16[64,5120]{1,0:T(8,128)(2,1)S(1)}, u32[]{:S(2)}, u32[]{:S(2)}) %collective-permute-start.7) | collective-permute-done | bytes 655392 | tf_op jit(solution)/shard_map/ppermute | solution.py:20
  401.2 3.1 fusion
  404.3 6.3 %copy.20 = bf16[1,1,3,5120,128]{4,3,2,1,0:T(8,128)(2,1)} copy(bf16[1,1,3,5120,128]{3,4,2,1,0:T(8,128)(2,1)} %fusion) | data formatting | bytes 7864320
  414.3 13.3 %collective-permute-done.19 = bf16[64,128]{0,1:T(8,128)(2,1)S(1)} collective-permute-done((bf16[64,128]{0,1:T(8,128)(2,1)}, bf16[64,128]{0,1:T(8,128)(2,1)S(1)}, u32[]{:S(2)}, u32[]{:S(2)}) %collective-permute-start.19) | collective-permute-done | bytes 16416 | tf_op jit(solution)/shard_map/ppermute | solution.py:20
  (250 shorter events, 94.7 us)
Async XLA Ops:
  7.2 62.4 %all-gather.4.cloned.1.call-start = ((), (), s32[]{:S(2)}) async-start(), calls=%async_computation.2 | async-start | bytes 3276800 | tf_op jit(solution)/shard_map/all_gather | solution.py:54
  12.0 115.2 %all-gather.6.cloned.1.call-start = ((), (), s32[]{:S(2)}) async-start(), calls=%async_computation.3 | async-start | bytes 3276800 | tf_op jit(solution)/shard_map/all_gather | solution.py:54
  73.6 115.1 %reduce-scatter.3.cloned.1.call-start = ((), (), s32[]{:S(2)}) async-start(), calls=%async_computation.4 | async-start | bytes 3276800 | tf_op jit(solution)/shard_map/reduce_scatter | solution.py:59
  137.5 129.3 %all-gather.8.cloned.1.call-start = ((), (), s32[]{:S(2)}) async-start(), calls=%async_computation.5 | async-start | bytes 3276800 | tf_op jit(solution)/shard_map/all_gather | solution.py:54
  206.5 222.9 %reduce-scatter.5.cloned.1.call-start = ((), (), s32[]{:S(2)}) async-start(), calls=%async_computation.6 | async-start | bytes 3276800 | tf_op jit(solution)/shard_map/reduce_scatter | solution.py:59
  211.3 73.6 %collective-permute-start.26 = (bf16[64,128]{1,0:T(8,128)(2,1)}, bf16[64,128]{1,0:T(8,128)(2,1)}, u32[]{:S(2)}, u32[]{:S(2)}) collective-permute-start(bf16[64,128]{1,0:T(8,128)(2,1)} %get-tuple-element.52), channel_id=1, source_target_pairs={{0,9},{1,8},{8,1},{9,0},{16,25},{17,24},{24,17},{25,16},{2,11},{3,... | collective-permute-start | bytes 49160 | tf_op jit(solution)/shard_map/ppermute | solution.py:20
  217.0 68.6 %collective-permute-start.28 = (bf16[64,128]{1,0:T(8,128)(2,1)S(1)}, bf16[64,128]{1,0:T(8,128)(2,1)}, u32[]{:S(2)}, u32[]{:S(2)}) collective-permute-start(bf16[64,128]{1,0:T(8,128)(2,1)S(1)} %get-tuple-element.53), channel_id=1, source_target_pairs={{0,17},{1,16},{8,25},{9,24},{16,1},{17,0},{24,9},{25,8},{2,19},{3,... | collective-permute-start | bytes 49160 | tf_op jit(solution)/shard_map/ppermute | solution.py:20
  220.1 67.5 %collective-permute-start.18 = (bf16[64,128]{0,1:T(8,128)(2,1)}, bf16[64,128]{0,1:T(8,128)(2,1)}, u32[]{:S(2)}, u32[]{:S(2)}) collective-permute-start(bf16[64,128]{0,1:T(8,128)(2,1)} %get-tuple-element.50), channel_id=1, source_target_pairs={{0,9},{1,8},{8,1},{9,0},{16,25},{17,24},{24,17},{25,16},{2,11},{3,... | collective-permute-start | bytes 49160 | tf_op jit(solution)/shard_map/ppermute | solution.py:20
  220.1 69.4 %collective-permute-start.20 = (bf16[64,128]{0,1:T(8,128)(2,1)}, bf16[64,128]{0,1:T(8,128)(2,1)}, u32[]{:S(2)}, u32[]{:S(2)}) collective-permute-start(bf16[64,128]{0,1:T(8,128)(2,1)} %get-tuple-element.51), channel_id=1, source_target_pairs={{0,17},{1,16},{8,25},{9,24},{16,1},{17,0},{24,9},{25,8},{2,19},{3,... | collective-permute-start | bytes 49160 | tf_op jit(solution)/shard_map/ppermute | solution.py:20
  221.3 101.5 %collective-permute-start.14 = (bf16[64,5120]{1,0:T(8,128)(2,1)}, bf16[64,5120]{1,0:T(8,128)(2,1)}, u32[]{:S(2)}, u32[]{:S(2)}) collective-permute-start(bf16[64,5120]{1,0:T(8,128)(2,1)} %get-tuple-element.40), channel_id=1, source_target_pairs={{0,9},{1,8},{8,1},{9,0},{16,25},{17,24},{24,17},{25,16},{2,11},{3,... | collective-permute-start | bytes 1966088 | tf_op jit(solution)/shard_map/ppermute | solution.py:20
  289.6 34.6 %collective-permute-start.22 = (bf16[64,5120]{1,0:T(8,128)(2,1)S(1)}, bf16[64,5120]{1,0:T(8,128)(2,1)}, u32[]{:S(2)}, u32[]{:S(2)}) collective-permute-start(bf16[64,5120]{1,0:T(8,128)(2,1)S(1)} %copy-done.29), channel_id=1, source_target_pairs={{0,9},{1,8},{8,1},{9,0},{16,25},{17,24},{24,17},{25,16},{2,11},{3,... | collective-permute-start | bytes 1966088 | tf_op jit(solution)/shard_map/ppermute | solution.py:20
  291.5 32.1 %collective-permute-start.16 = (bf16[64,5120]{1,0:T(8,128)(2,1)S(1)}, bf16[64,5120]{1,0:T(8,128)(2,1)S(1)}, u32[]{:S(2)}, u32[]{:S(2)}) collective-permute-start(bf16[64,5120]{1,0:T(8,128)(2,1)S(1)} %copy-done.30), channel_id=1, source_target_pairs={{0,17},{1,16},{8,25},{9,24},{16,1},{17,0},{24,9},{25,8},{2,19},{3,... | collective-permute-start | bytes 1966088 | tf_op jit(solution)/shard_map/ppermute | solution.py:20
  291.6 33.5 %collective-permute-start.6 = (bf16[64,5120]{1,0:T(8,128)(2,1)S(1)}, bf16[64,5120]{1,0:T(8,128)(2,1)S(1)}, u32[]{:S(2)}, u32[]{:S(2)}) collective-permute-start(bf16[64,5120]{1,0:T(8,128)(2,1)S(1)} %get-tuple-element.38), channel_id=1, source_target_pairs={{0,9},{1,8},{8,1},{9,0},{16,25},{17,24},{24,17},{25,16},{2,11},{3,... | collective-permute-start | bytes 1966088 | tf_op jit(solution)/shard_map/ppermute | solution.py:20
  322.8 30.4 %collective-permute-start.15 = (bf16[64,5120]{1,0:T(8,128)(2,1)}, bf16[64,5120]{1,0:T(8,128)(2,1)S(1)}, u32[]{:S(2)}, u32[]{:S(2)}) collective-permute-start(bf16[64,5120]{1,0:T(8,128)(2,1)} %collective-permute-done.14), channel_id=1, source_target_pairs={{0,16},{1,17},{8,24},{9,25},{16,0},{17,1},{24,8},{25,9},{2,18},{3,... | collective-permute-start | bytes 1966088 | tf_op jit(solution)/shard_map/ppermute | solution.py:20
  323.6 32.0 %collective-permute-start.17 = (bf16[64,5120]{1,0:T(8,128)(2,1)S(1)}, bf16[64,5120]{1,0:T(8,128)(2,1)S(1)}, u32[]{:S(2)}, u32[]{:S(2)}) collective-permute-start(bf16[64,5120]{1,0:T(8,128)(2,1)S(1)} %collective-permute-done.16), channel_id=1, source_target_pairs={{0,8},{1,9},{8,0},{9,1},{16,24},{17,25},{24,16},{25,17},{2,10},{3,... | collective-permute-start | bytes 1966088 | tf_op jit(solution)/shard_map/ppermute | solution.py:20
  324.2 29.0 %collective-permute-start.10 = (bf16[3,64,128]{2,1,0:T(8,128)(2,1)S(1)}, bf16[3,64,128]{2,1,0:T(8,128)(2,1)S(1)}, u32[]{:S(2)}, u32[]{:S(2)}) collective-permute-start(bf16[3,64,128]{2,1,0:T(8,128)(2,1)S(1)} %get-tuple-element.48), channel_id=1, source_target_pairs={{0,9},{1,8},{8,1},{9,0},{16,25},{17,24},{24,17},{25,16},{2,11},{3,... | collective-permute-start | bytes 147464 | tf_op jit(solution)/shard_map/ppermute | solution.py:20
  325.1 29.3 %collective-permute-start.12 = (bf16[3,64,128]{2,1,0:T(8,128)(2,1)S(1)}, bf16[3,64,128]{2,1,0:T(8,128)(2,1)S(1)}, u32[]{:S(2)}, u32[]{:S(2)}) collective-permute-start(bf16[3,64,128]{2,1,0:T(8,128)(2,1)S(1)} %get-tuple-element.49), channel_id=1, source_target_pairs={{0,17},{1,16},{8,25},{9,24},{16,1},{17,0},{24,9},{25,8},{2,19},{3,... | collective-permute-start | bytes 147464 | tf_op jit(solution)/shard_map/ppermute | solution.py:20
  338.5 36.7 %collective-permute-start.30 = (bf16[64,5120]{1,0:T(8,128)(2,1)S(1)}, bf16[64,5120]{1,0:T(8,128)(2,1)}, u32[]{:S(2)}, u32[]{:S(2)}) collective-permute-start(bf16[64,5120]{1,0:T(8,128)(2,1)S(1)} %get-tuple-element.32), channel_id=1, source_target_pairs={{0,9},{1,8},{8,1},{9,0},{16,25},{17,24},{24,17},{25,16},{2,11},{3,... | collective-permute-start | bytes 1966088 | tf_op jit(solution)/shard_map/ppermute | solution.py:20
  355.7 29.8 %collective-permute-start.24 = (bf16[64,5120]{1,0:T(8,128)(2,1)S(1)}, bf16[64,5120]{1,0:T(8,128)(2,1)}, u32[]{:S(2)}, u32[]{:S(2)}) collective-permute-start(bf16[64,5120]{1,0:T(8,128)(2,1)S(1)} %copy-done.28), channel_id=1, source_target_pairs={{0,17},{1,16},{8,25},{9,24},{16,1},{17,0},{24,9},{25,8},{2,19},{3,... | collective-permute-start | bytes 1966088 | tf_op jit(solution)/shard_map/ppermute | solution.py:20
  370.7 28.1 %collective-permute-start.7 = (bf16[64,5120]{1,0:T(8,128)(2,1)S(1)}, bf16[64,5120]{1,0:T(8,128)(2,1)S(1)}, u32[]{:S(2)}, u32[]{:S(2)}) collective-permute-start(bf16[64,5120]{1,0:T(8,128)(2,1)S(1)} %collective-permute-done.6), channel_id=1, source_target_pairs={{0,16},{1,17},{8,24},{9,25},{16,0},{17,1},{24,8},{25,9},{2,18},{3,... | collective-permute-start | bytes 1966088 | tf_op jit(solution)/shard_map/ppermute | solution.py:20
  371.5 28.1 %collective-permute-start.9 = (bf16[64,5120]{1,0:T(8,128)(2,1)S(1)}, bf16[64,5120]{1,0:T(8,128)(2,1)S(1)}, u32[]{:S(2)}, u32[]{:S(2)}) collective-permute-start(bf16[64,5120]{1,0:T(8,128)(2,1)S(1)} %collective-permute-done.8), channel_id=1, source_target_pairs={{0,8},{1,9},{8,0},{9,1},{16,24},{17,25},{24,16},{25,17},{2,10},{3,... | collective-permute-start | bytes 1966088 | tf_op jit(solution)/shard_map/ppermute | solution.py:20
  375.2 37.7 %collective-permute-start.31 = (bf16[64,5120]{1,0:T(8,128)(2,1)}, bf16[64,5120]{1,0:T(8,128)(2,1)S(1)}, u32[]{:S(2)}, u32[]{:S(2)}) collective-permute-start(bf16[64,5120]{1,0:T(8,128)(2,1)} %collective-permute-done.30), channel_id=1, source_target_pairs={{0,16},{1,17},{8,24},{9,25},{16,0},{17,1},{24,8},{25,9},{2,18},{3,... | collective-permute-start | bytes 1966088 | tf_op jit(solution)/shard_map/ppermute | solution.py:20
  375.7 38.0 %collective-permute-start.33 = (bf16[64,5120]{1,0:T(8,128)(2,1)}, bf16[64,5120]{1,0:T(8,128)(2,1)S(1)}, u32[]{:S(2)}, u32[]{:S(2)}) collective-permute-start(bf16[64,5120]{1,0:T(8,128)(2,1)} %collective-permute-done.32), channel_id=1, source_target_pairs={{0,8},{1,9},{8,0},{9,1},{16,24},{17,25},{24,16},{25,17},{2,10},{3,... | collective-permute-start | bytes 1966088 | tf_op jit(solution)/shard_map/ppermute | solution.py:20
  398.8 28.8 %collective-permute-start.23 = (bf16[64,5120]{1,0:T(8,128)(2,1)}, bf16[64,5120]{1,0:T(8,128)(2,1)S(1)}, u32[]{:S(2)}, u32[]{:S(2)}) collective-permute-start(bf16[64,5120]{1,0:T(8,128)(2,1)} %collective-permute-done.22), channel_id=1, source_target_pairs={{0,16},{1,17},{8,24},{9,25},{16,0},{17,1},{24,8},{25,9},{2,18},{3,... | collective-permute-start | bytes 1966088 | tf_op jit(solution)/shard_map/ppermute | solution.py:20
  (68 other events, 1032.4 us)
Sparse Core Ops, SparseCore 0:
  12.2 57.3 all-gather.3
  73.7 53.5 all-gather.5
  137.6 51.0 reduce-scatter.2
  206.6 60.1 all-gather.7
  283.4 51.0 reduce-scatter.4

commit v7 on v5

--- a/solution.py
+++ b/solution.py
@@ -193,24 +193,18 @@
         upstream = jnp.where(position == sections - 1, cotangent[0, step_index], backward_in)
         if step_index == 0:
             upstream_full, backward_normed_full[0] = gathered([upstream, saved_normed[0]])
-            sent = to_partner(jnp.stack([upstream_full, backward_normed_full[0]]), 1)
-            partner_upstream.append(sent[0])
-            partner_normed[0] = sent[1]
             forward_rows, upstream_full = lax.optimization_barrier(
                 ([normed_rows(current)] + saved_normed[1:], upstream_full)
             )
             forward_normed_full, *later = gathered(forward_rows)
             backward_normed_full[1:] = later
-            for later_index, later_full in enumerate(later):
-                partner_normed[later_index + 1] = to_partner(later_full, 0)
+            rows_sent = [upstream_full, backward_normed_full[0]]
         else:
-            upstream, last_result, held = lax.optimization_barrier(
-                (upstream, last_result, (partner_upstream, partner_normed[:step_index], partner_d_projected, partner_mixed))
-            )
-            partner_upstream, normed_done, partner_d_projected, partner_mixed = held
-            partner_normed[:step_index] = normed_done
+            upstream, last_result = lax.optimization_barrier((upstream, last_result))
             upstream_full = gathered([upstream])[0]
-            partner_upstream.append(to_partner(upstream_full, 0))
+            rows_sent = [upstream_full] + ([backward_normed_full[step_index]] if step_index == 1 else [])
+            if step_index == 1:
+                rows_sent += backward_normed_full[2:]
             forward_normed, upstream_full = lax.optimization_barrier(
                 (normed_rows(current), upstream_full)
             )
@@ -221,8 +215,15 @@
         upstream_fulls.append(upstream_full)
         d_projecteds.append(d_projected)
         mixeds.append(mixed)
-        partner_d_projected.append(to_partner(d_projected, 1))
-        partner_mixed.append(to_partner(mixed, 0))
+        rows_back = to_partner(jnp.stack(rows_sent), 1)
+        small_back = to_partner(jnp.concatenate([d_projected, mixed[None]]), 1)
+        partner_upstream.append(rows_back[0])
+        if step_index == 0:
+            partner_normed[0] = rows_back[1]
+        elif step_index == 1:
+            partner_normed[1:] = [rows_back[i] for i in range(1, rows_back.shape[0])]
+        partner_d_projected.append(small_back[:3])
+        partner_mixed.append(small_back[3])
         d_normed_part, forward_normed_full = lax.optimization_barrier(
             (d_normed_part, forward_normed_full)
         )
@@ -240,6 +241,9 @@
         forward_outs.append(forward_out)
         backward_outs.append(backward_out)
         if step_index < last_step:
+            held = (partner_upstream, partner_normed[:1], partner_d_projected, partner_mixed)
+            backward_out, held = lax.optimization_barrier((backward_out, held))
+            partner_upstream, partner_normed[:1], partner_d_projected, partner_mixed = held
             backward_in = lax.ppermute(backward_out, pair_axes, down_pairs)
             forward_in = lax.ppermute(forward_out, pair_axes, up_pairs)
 

time: 368 us -> 383 us (1.041)
  waiting for transfers between devices: 222 us -> 234 us
  starting transfers between devices: 34 us -> 22.7 us
  other arithmetic: 12.9 us -> 19.4 us
  local copies, waits for them, and re-layouts: 25.2 us -> 29.1 us
    ppermute x28 -> x16, waiting for transfers between devices: 44.7 us -> 91.3 us  [flipped(): lax.ppermute(value, axis, [(i, i ^ mask) for i in range(lax.axis_size(axi...]
    reduce_scatter x4, waiting for transfers between devices: 32.2 us -> 14 us  [scattered(): lax.psum_scatter(jnp.stack(blocks), 'tp', scatter_dimension=1, tiled=True)]
    all_gather x4, waiting for transfers between devices: 134 us -> 118 us  [gathered(): full = lax.all_gather(jnp.stack(blocks), 'tp', axis=1, tiled=True)]
    ppermute x28 -> x16, starting transfers between devices: 29.3 us -> 17.3 us  [flipped(): lax.ppermute(value, axis, [(i, i ^ mask) for i in range(lax.axis_size(axi...]
    another operation x0 -> x2, other arithmetic: none -> 6.11 us  [shards(): rows_back = to_partner(jnp.stack(rows_sent), 1)]
    unnamed x96 -> x107, local copies, waits for them, and re-layouts: 10.7 us -> 15.8 us
  transfers between devices with their start and end apart: 38 -> 26, of which waited for: 17 -> 16; matrix products, arithmetic and copies ran while one was open for 22% -> 23% of each run, Pallas kernels for 0% -> 0%
where the time goes in v7:
time: 383 us; the launch traced here: 382 us
  waiting for transfers between devices  234 us (61%)
  matrix products  61.7 us (16%)
  local copies, waits for them, and re-layouts  29.1 us (8%)
  starting transfers between devices  22.7 us (6%)
  other arithmetic  19.4 us (5%)
  between operations  14.8 us (4%)
    all_gather x4, waiting for transfers between devices, gathered(): full = lax.all_gather(jnp.stack(blocks), 'tp', axis=1, tiled=True)  118 us
    ppermute x16, waiting for transfers between devices, flipped(): lax.ppermute(value, axis, [(i, i ^ mask) for i in range(lax.axis_size(axi...  91.3 us
    dot_general x4, matrix products, weight_terms(): jnp.einsum('sd,csn->cdn', normed_full, d_projected, preferred_element_typ...  23.1 us
    ppermute x16, starting transfers between devices, flipped(): lax.ppermute(value, axis, [(i, i ^ mask) for i in range(lax.axis_size(axi...  17.3 us
    unnamed x107, local copies, waits for them, and re-layouts  15.8 us
    reduce_scatter x4, waiting for transfers between devices, scattered(): lax.psum_scatter(jnp.stack(blocks), 'tp', scatter_dimension=1, tiled=True)  14 us
    dot_general x4, matrix products, weight_terms(): jnp.einsum('sn,sd->nd', mixed, upstream_full, preferred_element_type=jnp....  12.6 us
    dot_general x4, matrix products, heads_of(): jnp.einsum('sd,cdn->csn', normed_full, qkv_weight, preferred_element_type...  10 us
  transfers between devices with their start and end apart: 26, of which 16 were waited for; matrix products, arithmetic and copies ran while one was open for 23% of the time, Pallas kernels for 0%

profile of v7, /device:TPU:0, one launch (start us, length us, event | category | flops | bytes accessed | tf_op | source)
XLA Modules:
  0.0 381.9 jit_solution(8873850095463379030)
XLA Ops:
  14.9 53.7 %all-gather.7.cloned.1.call-done = bf16[2,128,5120]{2,1,0:T(8,128)(2,1)} async-done(((bf16[2,32,5120]{2,1,0:T(8,128)(2,1)}), bf16[2,128,5120]{2,1,0:T(8,128)(2,1)}) %all-gather.7.cloned.1.call-update) | async-done | bytes 2621456 | tf_op jit(solution)/shard_map/all_gather | solution.py:54
  72.6 3.5 fusion.78
  80.1 46.1 %all-gather.9.cloned.1.call-done = bf16[2,128,5120]{2,1,0:T(8,128)(2,1)} async-done(((bf16[2,32,5120]{2,1,0:T(8,128)(2,1)}), bf16[2,128,5120]{2,1,0:T(8,128)(2,1)}) %all-gather.9.cloned.1.call-update) | async-done | bytes 2621456 | tf_op jit(solution)/shard_map/all_gather | solution.py:54
  126.2 3.4 fusion.162
  137.8 27.6 %collective-permute-done.5 = bf16[4,64,128]{2,1,0:T(8,128)(2,1)} collective-permute-done((bf16[4,64,128]{2,1,0:T(8,128)(2,1)S(1)}, bf16[4,64,128]{2,1,0:T(8,128)(2,1)}, u32[]{:S(2)}, u32[]{:S(2)}) %collective-permute-start.5) | collective-permute-done | bytes 65568 | tf_op jit(solution)/shard_map/ppermute | solution.py:20
  173.9 3.4 fusion.73
  182.1 17.9 %collective-permute-done.2 = bf16[2,64,5120]{2,1,0:T(8,128)(2,1)} collective-permute-done((bf16[2,64,5120]{2,1,0:T(8,128)(2,1)}, bf16[2,64,5120]{2,1,0:T(8,128)(2,1)}, u32[]{:S(2)}, u32[]{:S(2)}) %collective-permute-start.2) | collective-permute-done | bytes 1310752 | tf_op jit(solution)/shard_map/ppermute | solution.py:20
  205.3 3.9 %reduce-scatter.7.cloned.1.call-done = bf16[1,32,5120]{2,1,0:T(8,128)(2,1)} async-done(((bf16[1,128,5120]{2,1,0:T(8,128)(2,1)}), bf16[1,32,5120]{2,1,0:T(8,128)(2,1)}) %reduce-scatter.7.cloned.1.call-update) | async-done | bytes 327696 | tf_op jit(solution)/shard_map/reduce_scatter | solution.py:59
  210.6 3.5 collective-permute-start
  214.4 4.3 %collective-permute-done = bf16[32,5120]{1,0:T(8,128)(2,1)S(1)} collective-permute-done((bf16[32,5120]{1,0:T(8,128)(2,1)S(1)}, bf16[32,5120]{1,0:T(8,128)(2,1)S(1)}, u32[]{:S(2)}, u32[]{:S(2)}) %collective-permute-start) | collective-permute-done | bytes 327712 | tf_op jit(solution)/shard_map/ppermute | solution.py:248
  221.7 4.3 %fusion.34 = f32[3,128,5120]{2,1,0:T(8,128)} fusion(bf16[1,128,1,128]{3,1,2,0:T(8,128)(2,1)S(1)} %copy-done.35, bf16[1,128,1,128]{3,1,2,0:T(8,128)(2,1)S(1)} %fusion.96, bf16[1,128,1,128]{3,1,2,0:T(8,128)(2,1)S(1)} %fusion.95, bf16[2,128,5120]{2,1,0:T(8,128)(2,1)S(1)} %copy-done.11), kind=kOutput, calls=%fused_computation.57 | convolution fusion | flops 503414784 | bytes 9273344 | tf_op jit(solution)/shard_map/sd,csn->cdn/dot_general | solution.py:127
  226.0 7.0 %collective-permute-done.9 = bf16[32,5120]{1,0:T(8,128)(2,1)S(1)} collective-permute-done((bf16[32,5120]{1,0:T(8,128)(2,1)S(1)}, bf16[32,5120]{1,0:T(8,128)(2,1)S(1)}, u32[]{:S(2)}, u32[]{:S(2)}) %collective-permute-start.9) | collective-permute-done | bytes 327712 | tf_op jit(solution)/shard_map/ppermute | solution.py:247
  242.3 4.3 %fusion.28 = f32[3,128,5120]{2,1,0:T(8,128)} fusion(bf16[3,128,128]{2,1,0:T(8,128)(2,1)S(1)} %slice.199, bf16[128,5120]{1,0:T(8,128)(2,1)S(1)} %copy-done.12), kind=kOutput, calls=%fused_computation.51 | convolution fusion | flops 503316480 | bytes 9273344 | tf_op jit(solution)/shard_map/sd,csn->cdn/dot_general | solution.py:127
  246.6 17.8 %all-gather.11.cloned.1.call-done = bf16[128,5120]{1,0:T(8,128)(2,1)} async-done(((bf16[32,5120]{1,0:T(8,128)(2,1)}), bf16[128,5120]{1,0:T(8,128)(2,1)}) %all-gather.11.cloned.1.call-update) | async-done | bytes 1310736 | tf_op jit(solution)/shard_map/all_gather | solution.py:54
  264.5 3.1 pad_maximum_fusion
  272.5 6.7 %add_convert_fusion.2 = bf16[3,128,5120]{2,1,0:T(8,128)(2,1)} fusion(f32[3,128,5120]{2,1,0:T(8,128)} %fusion.34, bf16[1,128,1,128]{3,1,2,0:T(8,128)(2,1)S(1)} %fusion.102, bf16[1,128,1,128]{3,1,2,0:T(8,128)(2,1)S(1)} %fusion.99, bf16[1,128,1,128]{3,1,2,0:T(8,128)(2,1)S(1)} %fusion.98, bf16[2,128,5120]{2,1,0:T(8,128)(2,1)S(1)} %copy-done.7), kind=kOutput, calls=%fused_computation.2 | convolution fusion | flops 507346944 | bytes 13205504 | tf_op jit(solution)/shard_map/sd,csn->cdn/dot_general | solution.py:127
  281.6 19.3 %collective-permute-done.10 = bf16[4,64,128]{2,1,0:T(8,128)(2,1)} collective-permute-done((bf16[4,64,128]{2,1,0:T(8,128)(2,1)S(1)}, bf16[4,64,128]{2,1,0:T(8,128)(2,1)}, u32[]{:S(2)}, u32[]{:S(2)}) %collective-permute-start.10) | collective-permute-done | bytes 65568 | tf_op jit(solution)/shard_map/ppermute | solution.py:20
  303.0 3.9 %fusion.6 = f32[128,5120]{1,0:T(8,128)} fusion(f32[128,5120]{1,0:T(8,128)} %fusion.140, bf16[128,5120]{1,0:T(8,128)(2,1)S(1)} %copy-done.5, bf16[128,128]{0,1:T(8,128)(2,1)S(1)} %convolution_convert_fusion.4), kind=kOutput, calls=%fused_computation.13 | convolution fusion | flops 169738240 | bytes 6586368 | tf_op jit(solution)/shard_map/sn,sd->nd/dot_general | solution.py:130
  317.1 16.5 %collective-permute-done.15 = bf16[2,64,5120]{2,1,0:T(8,128)(2,1)} collective-permute-done((bf16[2,64,5120]{2,1,0:T(8,128)(2,1)}, bf16[2,64,5120]{2,1,0:T(8,128)(2,1)}, u32[]{:S(2)}, u32[]{:S(2)}) %collective-permute-start.15) | collective-permute-done | bytes 1310752 | tf_op jit(solution)/shard_map/ppermute | solution.py:20
  336.1 5.2 %collective-permute-done.17 = bf16[2,64,5120]{2,1,0:T(8,128)(2,1)S(1)} collective-permute-done((bf16[2,64,5120]{2,1,0:T(8,128)(2,1)}, bf16[2,64,5120]{2,1,0:T(8,128)(2,1)S(1)}, u32[]{:S(2)}, u32[]{:S(2)}) %collective-permute-start.17) | collective-permute-done | bytes 1310752 | tf_op jit(solution)/shard_map/ppermute | solution.py:20
  342.5 7.8 %fusion = bf16[1,1,3,5120,128]{3,4,2,1,0:T(8,128)(2,1)} fusion(f32[3,128,5120]{2,1,0:T(8,128)} %fusion.28, bf16[4,128,128]{2,1,0:T(8,128)(2,1)S(1)} %constant_dynamic-update-slice_fusion.4, bf16[3,128,5120]{2,1,0:T(8,128)(2,1)} %add_convert_fusion.2, bf16[2,128,5120]{2,1,0:T(8,128)(2,1)} %constant_dynamic-update-slice_fusion.6), kind=kOutput, calls=%fused_computation.3 | convolution fusion | flops 515112960 | bytes 17170432 | tf_op jit(solution)/shard_map/sd,csn->cdn/dot_general | solution.py:127
  350.3 6.3 %copy.19 = bf16[1,1,3,5120,128]{4,3,2,1,0:T(8,128)(2,1)} copy(bf16[1,1,3,5120,128]{3,4,2,1,0:T(8,128)(2,1)} %fusion) | data formatting | bytes 7864320
  356.6 4.6 %fusion.9 = bf16[1,1,128,5120]{3,2,1,0:T(8,128)(2,1)} fusion(f32[128,5120]{1,0:T(8,128)} %fusion.6, f32[128,5120]{1,0:T(8,128)} %fusion.169, bf16[2,128,5120]{2,1,0:T(8,128)(2,1)} %constant_dynamic-update-slice_fusion.6, bf16[4,128,128]{2,1,0:T(8,128)(2,1)S(1)} %constant_dynamic-update-slice_fusion.4), kind=kOutput, calls=%fused_computation.18 | convolution fusion | flops 171048960 | bytes 7897088 | tf_op jit(solution)/shard_map/sn,sd->nd/dot_general | solution.py:130
  363.0 10.0 %reduce-scatter.11.cloned.1.call-done = bf16[1,32,5120]{2,1,0:T(8,128)(2,1)} async-done(((bf16[1,128,5120]{2,1,0:T(8,128)(2,1)}), bf16[1,32,5120]{2,1,0:T(8,128)(2,1)}) %reduce-scatter.11.cloned.1.call-update) | async-done | bytes 327696 | tf_op jit(solution)/shard_map/reduce_scatter | solution.py:59
  (226 shorter events, 83.0 us)
Async XLA Ops:
  7.2 61.3 %all-gather.7.cloned.1.call-start = ((), (), s32[]{:S(2)}) async-start(), calls=%async_computation.4 | async-start | bytes 3276800 | tf_op jit(solution)/shard_map/all_gather | solution.py:54
  10.9 115.3 %all-gather.9.cloned.1.call-start = ((), (), s32[]{:S(2)}) async-start(), calls=%async_computation.5 | async-start | bytes 3276800 | tf_op jit(solution)/shard_map/all_gather | solution.py:54
  72.5 108.1 %reduce-scatter.5.cloned.1.call-start = ((), (), s32[]{:S(2)}) async-start(), calls=%async_computation.6 | async-start | bytes 1638400 | tf_op jit(solution)/shard_map/reduce_scatter | solution.py:59
  129.6 79.7 %reduce-scatter.7.cloned.1.call-start = ((), (), s32[]{:S(2)}) async-start(), calls=%async_computation.7 | async-start | bytes 1638400 | tf_op jit(solution)/shard_map/reduce_scatter | solution.py:59
  132.7 37.3 %collective-permute-start.1 = (bf16[2,64,5120]{2,1,0:T(8,128)(2,1)}, bf16[2,64,5120]{2,1,0:T(8,128)(2,1)}, u32[]{:S(2)}, u32[]{:S(2)}) collective-permute-start(bf16[2,64,5120]{2,1,0:T(8,128)(2,1)} %get-tuple-element.55), channel_id=1, source_target_pairs={{0,9},{1,8},{8,1},{9,0},{16,25},{17,24},{24,17},{25,16},{2,11},{3,... | collective-permute-start | bytes 3932168 | tf_op jit(solution)/shard_map/ppermute | solution.py:20
  133.4 39.0 %collective-permute-start.3 = (bf16[2,64,5120]{2,1,0:T(8,128)(2,1)}, bf16[2,64,5120]{2,1,0:T(8,128)(2,1)}, u32[]{:S(2)}, u32[]{:S(2)}) collective-permute-start(bf16[2,64,5120]{2,1,0:T(8,128)(2,1)} %get-tuple-element.54), channel_id=1, source_target_pairs={{0,17},{1,16},{8,25},{9,24},{16,1},{17,0},{24,9},{25,8},{2,19},{3,... | collective-permute-start | bytes 3932168 | tf_op jit(solution)/shard_map/ppermute | solution.py:20
  137.0 28.4 %collective-permute-start.5 = (bf16[4,64,128]{2,1,0:T(8,128)(2,1)S(1)}, bf16[4,64,128]{2,1,0:T(8,128)(2,1)}, u32[]{:S(2)}, u32[]{:S(2)}) collective-permute-start(bf16[4,64,128]{2,1,0:T(8,128)(2,1)S(1)} %get-tuple-element.61), channel_id=1, source_target_pairs={{0,9},{1,8},{8,1},{9,0},{16,25},{17,24},{24,17},{25,16},{2,11},{3,... | collective-permute-start | bytes 196616 | tf_op jit(solution)/shard_map/ppermute | solution.py:20
  137.0 30.5 %collective-permute-start.7 = (bf16[4,64,128]{2,1,0:T(8,128)(2,1)}, bf16[4,64,128]{2,1,0:T(8,128)(2,1)S(1)}, u32[]{:S(2)}, u32[]{:S(2)}) collective-permute-start(bf16[4,64,128]{2,1,0:T(8,128)(2,1)} %get-tuple-element.60), channel_id=1, source_target_pairs={{0,17},{1,16},{8,25},{9,24},{16,1},{17,0},{24,9},{25,8},{2,19},{3,... | collective-permute-start | bytes 196616 | tf_op jit(solution)/shard_map/ppermute | solution.py:20
  165.4 4.5 %collective-permute-start.6 = (bf16[4,64,128]{2,1,0:T(8,128)(2,1)}, bf16[4,64,128]{2,1,0:T(8,128)(2,1)S(1)}, u32[]{:S(2)}, u32[]{:S(2)}) collective-permute-start(bf16[4,64,128]{2,1,0:T(8,128)(2,1)} %collective-permute-done.5), channel_id=1, source_target_pairs={{0,16},{1,17},{8,24},{9,25},{16,0},{17,1},{24,8},{25,9},{2,18},{3,... | collective-permute-start | bytes 196616 | tf_op jit(solution)/shard_map/ppermute | solution.py:20
  169.9 30.0 %collective-permute-start.2 = (bf16[2,64,5120]{2,1,0:T(8,128)(2,1)}, bf16[2,64,5120]{2,1,0:T(8,128)(2,1)}, u32[]{:S(2)}, u32[]{:S(2)}) collective-permute-start(bf16[2,64,5120]{2,1,0:T(8,128)(2,1)} %collective-permute-done.1), channel_id=1, source_target_pairs={{0,16},{1,17},{8,24},{9,25},{16,0},{17,1},{24,8},{25,9},{2,18},{3,... | collective-permute-start | bytes 3932168 | tf_op jit(solution)/shard_map/ppermute | solution.py:20
  172.5 29.7 %collective-permute-start.4 = (bf16[2,64,5120]{2,1,0:T(8,128)(2,1)}, bf16[2,64,5120]{2,1,0:T(8,128)(2,1)}, u32[]{:S(2)}, u32[]{:S(2)}) collective-permute-start(bf16[2,64,5120]{2,1,0:T(8,128)(2,1)} %collective-permute-done.3), channel_id=1, source_target_pairs={{0,8},{1,9},{8,0},{9,1},{16,24},{17,25},{24,16},{25,17},{2,10},{3,... | collective-permute-start | bytes 3932168 | tf_op jit(solution)/shard_map/ppermute | solution.py:20
  180.6 83.8 %all-gather.11.cloned.1.call-start = ((), (), s32[]{:S(2)}) async-start(), calls=%async_computation.10 | async-start | bytes 1638400 | tf_op jit(solution)/shard_map/all_gather | solution.py:54
  210.6 8.1 %collective-permute-start = (bf16[32,5120]{1,0:T(8,128)(2,1)S(1)}, bf16[32,5120]{1,0:T(8,128)(2,1)S(1)}, u32[]{:S(2)}, u32[]{:S(2)}) collective-permute-start(bf16[32,5120]{1,0:T(8,128)(2,1)S(1)} %add_convert_fusion.3), channel_id=1, source_target_pairs={{0,8},{8,16},{9,1},{16,24},{17,9},{25,17},{2,10},{10,18},{11,3},{1... | collective-permute-start | bytes 983048 | tf_op jit(solution)/shard_map/ppermute | solution.py:248
  220.3 12.7 %collective-permute-start.9 = (bf16[32,5120]{1,0:T(8,128)(2,1)S(1)}, bf16[32,5120]{1,0:T(8,128)(2,1)S(1)}, u32[]{:S(2)}, u32[]{:S(2)}) collective-permute-start(bf16[32,5120]{1,0:T(8,128)(2,1)S(1)} %get-tuple-element.30), channel_id=1, source_target_pairs={{1,9},{8,0},{9,17},{16,8},{17,25},{24,16},{3,11},{10,2},{11,19},{1... | collective-permute-start | bytes 983048 | tf_op jit(solution)/shard_map/ppermute | solution.py:247
  233.7 69.2 %all-gather.13.cloned.1.call-start = ((), (), s32[]{:S(2)}) async-start(), calls=%async_computation.11 | async-start | bytes 1638400 | tf_op jit(solution)/shard_map/all_gather | solution.py:54
  264.4 78.0 %reduce-scatter.9.cloned.1.call-start = ((), (), s32[]{:S(2)}) async-start(), calls=%async_computation.8 | async-start | bytes 1638400 | tf_op jit(solution)/shard_map/reduce_scatter | solution.py:59
  268.3 34.1 %collective-permute-start.14 = (bf16[2,64,5120]{2,1,0:T(8,128)(2,1)S(1)}, bf16[2,64,5120]{2,1,0:T(8,128)(2,1)}, u32[]{:S(2)}, u32[]{:S(2)}) collective-permute-start(bf16[2,64,5120]{2,1,0:T(8,128)(2,1)S(1)} %get-tuple-element.49), channel_id=1, source_target_pairs={{0,9},{1,8},{8,1},{9,0},{16,25},{17,24},{24,17},{25,16},{2,11},{3,... | collective-permute-start | bytes 3932168 | tf_op jit(solution)/shard_map/ppermute | solution.py:20
  269.5 37.5 %collective-permute-start.12 = (bf16[4,64,128]{2,1,0:T(8,128)(2,1)S(1)}, bf16[4,64,128]{2,1,0:T(8,128)(2,1)}, u32[]{:S(2)}, u32[]{:S(2)}) collective-permute-start(bf16[4,64,128]{2,1,0:T(8,128)(2,1)S(1)} %get-tuple-element.58), channel_id=1, source_target_pairs={{0,17},{1,16},{8,25},{9,24},{16,1},{17,0},{24,9},{25,8},{2,19},{3,... | collective-permute-start | bytes 196616 | tf_op jit(solution)/shard_map/ppermute | solution.py:20
  271.7 29.2 %collective-permute-start.10 = (bf16[4,64,128]{2,1,0:T(8,128)(2,1)S(1)}, bf16[4,64,128]{2,1,0:T(8,128)(2,1)}, u32[]{:S(2)}, u32[]{:S(2)}) collective-permute-start(bf16[4,64,128]{2,1,0:T(8,128)(2,1)S(1)} %get-tuple-element.59), channel_id=1, source_target_pairs={{0,9},{1,8},{8,1},{9,0},{16,25},{17,24},{24,17},{25,16},{2,11},{3,... | collective-permute-start | bytes 196616 | tf_op jit(solution)/shard_map/ppermute | solution.py:20
  271.7 39.8 %collective-permute-start.16 = (bf16[2,64,5120]{2,1,0:T(8,128)(2,1)}, bf16[2,64,5120]{2,1,0:T(8,128)(2,1)}, u32[]{:S(2)}, u32[]{:S(2)}) collective-permute-start(bf16[2,64,5120]{2,1,0:T(8,128)(2,1)} %get-tuple-element.48), channel_id=1, source_target_pairs={{0,17},{1,16},{8,25},{9,24},{16,1},{17,0},{24,9},{25,8},{2,19},{3,... | collective-permute-start | bytes 3932168 | tf_op jit(solution)/shard_map/ppermute | solution.py:20
  300.9 7.2 %collective-permute-start.11 = (bf16[4,64,128]{2,1,0:T(8,128)(2,1)}, bf16[4,64,128]{2,1,0:T(8,128)(2,1)}, u32[]{:S(2)}, u32[]{:S(2)}) collective-permute-start(bf16[4,64,128]{2,1,0:T(8,128)(2,1)} %collective-permute-done.10), channel_id=1, source_target_pairs={{0,16},{1,17},{8,24},{9,25},{16,0},{17,1},{24,8},{25,9},{2,18},{3,... | collective-permute-start | bytes 196616 | tf_op jit(solution)/shard_map/ppermute | solution.py:20
  302.4 31.2 %collective-permute-start.15 = (bf16[2,64,5120]{2,1,0:T(8,128)(2,1)}, bf16[2,64,5120]{2,1,0:T(8,128)(2,1)}, u32[]{:S(2)}, u32[]{:S(2)}) collective-permute-start(bf16[2,64,5120]{2,1,0:T(8,128)(2,1)} %collective-permute-done.14), channel_id=1, source_target_pairs={{0,16},{1,17},{8,24},{9,25},{16,0},{17,1},{24,8},{25,9},{2,18},{3,... | collective-permute-start | bytes 3932168 | tf_op jit(solution)/shard_map/ppermute | solution.py:20
  303.0 70.1 %reduce-scatter.11.cloned.1.call-start = ((), (), s32[]{:S(2)}) async-start(), calls=%async_computation.9 | async-start | bytes 1638400 | tf_op jit(solution)/shard_map/reduce_scatter | solution.py:59
  311.5 29.8 %collective-permute-start.17 = (bf16[2,64,5120]{2,1,0:T(8,128)(2,1)}, bf16[2,64,5120]{2,1,0:T(8,128)(2,1)S(1)}, u32[]{:S(2)}, u32[]{:S(2)}) collective-permute-start(bf16[2,64,5120]{2,1,0:T(8,128)(2,1)} %collective-permute-done.16), channel_id=1, source_target_pairs={{0,8},{1,9},{8,0},{9,1},{16,24},{17,25},{24,16},{25,17},{2,10},{3,... | collective-permute-start | bytes 3932168 | tf_op jit(solution)/shard_map/ppermute | solution.py:20
  (53 other events, 299.8 us)
Sparse Core Ops, SparseCore 0:
  11.0 57.4 all-gather.6
  72.6 53.5 all-gather.8
  129.7 30.1 reduce-scatter.4
  180.8 28.4 reduce-scatter.6
  233.9 30.5 all-gather.10
  266.4 31.6 all-gather.12
  303.1 30.3 reduce-scatter.8
  342.6 30.4 reduce-scatter.10

commit v8 on v6

--- a/solution.py
+++ b/solution.py
@@ -163,15 +163,8 @@
     else:
         routes = [[1]]
 
-    def to_partner(value, axis):
-        cuts = np.linspace(0, value.shape[axis], len(routes) + 1).astype(int)
-        pieces = []
-        for index, hops in enumerate(routes):
-            piece = lax.slice_in_dim(value, int(cuts[index]), int(cuts[index + 1]), axis=axis)
-            for mask in hops:
-                piece = flipped(piece, pair_axes, mask)
-            pieces.append(piece)
-        return jnp.concatenate(pieces, axis=axis) if len(pieces) > 1 else pieces[0]
+    def to_partner(value):
+        return flipped(value, pair_axes, (1 << bit_count) - 1)
 
     last_step = window_steps - 1
     saved_normed = [normed_rows(saved[0, 0, t]) for t in range(window_steps)]
@@ -187,28 +180,45 @@
     backward_outs = []
     forward_in = carry_acts[0, 0]
     backward_in = grad_in[0, 0]
+    inbox = {}
+    deferred = {}
+    tie_scatter = {}
     for step_index in range(window_steps):
         embedded = embedding(feats[0, step_index], types[0, step_index], type_table)
         current = jnp.where(position == 0, embedded, forward_in)
         upstream = jnp.where(position == sections - 1, cotangent[0, step_index], backward_in)
         if step_index == 0:
             upstream_full, backward_normed_full[0] = gathered([upstream, saved_normed[0]])
+            tie_scatter["first"] = to_partner(jnp.stack([upstream_full, backward_normed_full[0]]))
             forward_rows, upstream_full = lax.optimization_barrier(
                 ([normed_rows(current)] + saved_normed[1:], upstream_full)
             )
             forward_normed_full, *later = gathered(forward_rows)
             backward_normed_full[1:] = later
+            if later:
+                deferred["later"] = jnp.stack(later)
         else:
             upstream_full, forward_normed_full = gathered([upstream, normed_rows(current)])
+            inbox[f"rows{step_index}"] = to_partner(upstream_full)
         d_normed_part, d_projected, mixed = backward_part(
             backward_normed_full[step_index], upstream_full, mask_for(1, step_index + position)
         )
         upstream_fulls.append(upstream_full)
         d_projecteds.append(d_projected)
         mixeds.append(mixed)
+        small = jnp.concatenate([d_projected, mixed[None]])
+        if step_index < last_step:
+            deferred[f"small{step_index}"] = small
+        else:
+            inbox[f"small{step_index}"] = to_partner(small)
         attn_part = forward_part(
             forward_normed_full, mask_for(0, step_index - position + sections - 1)
         )
+        (d_normed_part, attn_part), tie_scatter = lax.optimization_barrier(
+            ((d_normed_part, attn_part), tie_scatter)
+        )
+        inbox.update(tie_scatter)
+        tie_scatter = {}
         d_normed, attn_rows = scattered([d_normed_part, attn_part])
         backward_out = input_grad(saved[0, 0, step_index], upstream, d_normed)
         forward_out = (current.astype(jnp.float32) + attn_rows.astype(jnp.float32)).astype(
@@ -219,18 +229,18 @@
         if step_index < last_step:
             backward_in = lax.ppermute(backward_out, pair_axes, down_pairs)
             forward_in = lax.ppermute(forward_out, pair_axes, up_pairs)
-            held = (upstream_fulls, backward_normed_full, d_projecteds, mixeds)
-            held, backward_in, forward_in = lax.optimization_barrier(
-                (held, backward_in, forward_in)
-            )
-            upstream_fulls, backward_normed_full, d_projecteds, mixeds = held
-            if step_index == 0:
-                for later_index in range(window_steps):
-                    partner_normed[later_index] = to_partner(backward_normed_full[later_index], 0)
-        partner_upstream.append(to_partner(upstream_fulls[step_index], 0))
-        partner_d_projected.append(to_partner(d_projecteds[step_index], 1))
-        partner_mixed.append(to_partner(mixeds[step_index], 0))
-
+            deferred, backward_in, forward_in = lax.optimization_barrier(
+                (deferred, backward_in, forward_in)
+            )
+            tie_scatter = {key: to_partner(value) for key, value in deferred.items()}
+            deferred = {}
+
+    partner_upstream = [inbox["first"][0]] + [inbox[f"rows{t}"] for t in range(1, window_steps)]
+    partner_normed = [inbox["first"][1]] + (
+        [inbox["later"][t] for t in range(window_steps - 1)] if window_steps > 1 else []
+    )
+    partner_d_projected = [inbox[f"small{t}"][:3] for t in range(window_steps)]
+    partner_mixed = [inbox[f"small{t}"][3] for t in range(window_steps)]
     own_qkv, own_out = weight_terms(backward_normed_full, d_projecteds, mixeds, upstream_fulls)
     other_qkv, other_out = weight_terms(
         partner_normed, partner_d_projected, partner_mixed, partner_upstream

time: 441 us -> 344 us (0.78)
  waiting for transfers between devices: 292 us -> 214 us
  starting transfers between devices: 41.2 us -> 13.1 us
  matrix products: 46.6 us -> 58.4 us
  local copies, waits for them, and re-layouts: 23.1 us -> 16.8 us
    ppermute x32 -> x5, waiting for transfers between devices: 100 us -> 6.35 us  [flipped(): lax.ppermute(value, axis, [(i, i ^ mask) for i in range(lax.axis_size(axi...]
    ppermute x32 -> x5, starting transfers between devices: 35 us -> 6.88 us  [flipped(): lax.ppermute(value, axis, [(i, i ^ mask) for i in range(lax.axis_size(axi...]
    reduce_scatter x2, waiting for transfers between devices: 44 us -> 58 us  [scattered(): lax.psum_scatter(jnp.stack(blocks), 'tp', scatter_dimension=1, tiled=True)]
    dot_general x4, matrix products: 6.76 us -> 16.2 us  [weight_terms(): jnp.einsum('sd,csn->cdn', normed_full, d_projected, preferred_element_typ...]
    dot_general x4, matrix products: 4.79 us -> 13.3 us  [weight_terms(): jnp.einsum('sn,sd->nd', mixed, upstream_full, preferred_element_type=jnp....]
    slice x8 -> x1, local copies, waits for them, and re-layouts: 6.6 us -> 1.15 us  [gathered(): return [full[i] for i in range(len(blocks))]]
    unnamed x107 -> x83, local copies, waits for them, and re-layouts: 9.6 us -> 11.9 us
  transfers between devices with their start and end apart: 39 -> 12, of which waited for: 15 -> 8; matrix products, arithmetic and copies ran while one was open for 14% -> 21% of each run, Pallas kernels for 0% -> 0%
where the time goes in v8:
time: 344 us; the launch traced here: 343 us
  waiting for transfers between devices  214 us (62%)
  matrix products  58.4 us (17%)
  other arithmetic  25.7 us (7%)
  local copies, waits for them, and re-layouts  16.8 us (5%)
  between operations  14.4 us (4%)
  starting transfers between devices  13.1 us (4%)
    all_gather x3, waiting for transfers between devices, gathered(): full = lax.all_gather(jnp.stack(blocks), 'tp', axis=1, tiled=True)  146 us
    reduce_scatter x2, waiting for transfers between devices, scattered(): lax.psum_scatter(jnp.stack(blocks), 'tp', scatter_dimension=1, tiled=True)  58 us
    dot_general x4, matrix products, weight_terms(): jnp.einsum('sd,csn->cdn', normed_full, d_projected, preferred_element_typ...  16.2 us
    dot_general x4, matrix products, weight_terms(): jnp.einsum('sn,sd->nd', mixed, upstream_full, preferred_element_type=jnp....  13.3 us
    unnamed x83, local copies, waits for them, and re-layouts  11.9 us
    dot_general x4, matrix products, heads_of(): jnp.einsum('sd,cdn->csn', normed_full, qkv_weight, preferred_element_type...  10.8 us
    ppermute x5, starting transfers between devices, flipped(): lax.ppermute(value, axis, [(i, i ^ mask) for i in range(lax.axis_size(axi...  6.88 us
  transfers between devices with their start and end apart: 12, of which 8 were waited for; matrix products, arithmetic and copies ran while one was open for 21% of the time, Pallas kernels for 0%

profile of v8, /device:TPU:0, one launch (start us, length us, event | category | flops | bytes accessed | tf_op | source)
XLA Modules:
  0.0 342.5 jit_solution(12178344911561519717)
XLA Ops:
  16.1 54.2 %all-gather.4.cloned.1.call-done = bf16[2,128,5120]{2,1,0:T(8,128)(2,1)} async-done(((bf16[2,32,5120]{2,1,0:T(8,128)(2,1)}), bf16[2,128,5120]{2,1,0:T(8,128)(2,1)}) %all-gather.4.cloned.1.call-update) | async-done | bytes 2621456 | tf_op jit(solution)/shard_map/all_gather | solution.py:54
  75.1 3.5 %fusion.65 = bf16[3,128,128]{2,1,0:T(8,128)(2,1)S(1)} fusion(bf16[1,1,3,5120,128]{4,3,2,1,0:T(8,128)(2,1)} %param.16, bf16[2,128,5120]{2,1,0:T(8,128)(2,1)} %all-gather.4.cloned.1.call-done), kind=kOutput, calls=%fused_computation.69 | convolution fusion | flops 503365632 | bytes 5341184 | tf_op jit(solution)/shard_map/sd,cdn->csn/dot_general | solution.py:86
  80.7 2.4 fusion.7
  83.2 43.2 %all-gather.6.cloned.1.call-done = bf16[2,128,5120]{2,1,0:T(8,128)(2,1)} async-done(((bf16[2,32,5120]{2,1,0:T(8,128)(2,1)}), bf16[2,128,5120]{2,1,0:T(8,128)(2,1)}) %all-gather.6.cloned.1.call-update) | async-done | bytes 2621456 | tf_op jit(solution)/shard_map/all_gather | solution.py:54
  126.4 3.4 fusion.62
  130.6 2.5 convolution_convert_fusion.1
  133.8 3.4 %pad_maximum_fusion = bf16[2,128,5120]{2,1,0:T(8,128)(2,1)} fusion(bf16[1,128,5120]{2,1,0:T(8,128)(2,1)} %bitcast.402, bf16[1,128,5120]{2,1,0:T(8,128)(2,1)} %bitcast.403), kind=kLoop, calls=%fused_computation.35 | loop fusion | flops 1310720 | bytes 5242880 | tf_op jit(solution)/shard_map/stack | solution.py:59
  140.3 48.0 %reduce-scatter.3.cloned.1.call-done = bf16[2,32,5120]{2,1,0:T(8,128)(2,1)} async-done(((bf16[2,128,5120]{2,1,0:T(8,128)(2,1)}), bf16[2,32,5120]{2,1,0:T(8,128)(2,1)}) %reduce-scatter.3.cloned.1.call-update) | async-done | bytes 655376 | tf_op jit(solution)/shard_map/reduce_scatter | solution.py:59
  193.5 4.6 %collective-permute-start.2 = (bf16[32,5120]{1,0:T(8,128)(2,1)S(1)}, bf16[32,5120]{1,0:T(8,128)(2,1)S(1)}, u32[]{:S(2)}, u32[]{:S(2)}) collective-permute-start(bf16[32,5120]{1,0:T(8,128)(2,1)S(1)} %get-tuple-element.42), channel_id=1, source_target_pairs={{0,8},{8,16},{9,1},{16,24},{17,9},{25,17},{2,10},{10,18},{11,3},{1... | collective-permute-start | bytes 983048 | tf_op jit(solution)/shard_map/ppermute | solution.py:231
  201.5 3.2 collective-permute-done.1
  209.3 4.7 %fusion.39 = f32[3,128,5120]{2,1,0:T(8,128)} fusion(bf16[2,128,5120]{2,1,0:T(8,128)(2,1)S(1)} %copy-done.20, bf16[1,128,1,128]{3,1,2,0:T(8,128)(2,1)S(1)} %copy-done.31, bf16[1,128,1,128]{3,1,2,0:T(8,128)(2,1)S(1)} %fusion.81, bf16[1,128,1,128]{3,1,2,0:T(8,128)(2,1)S(1)} %fusion.80), kind=kOutput, calls=%fused_computation.57 | convolution fusion | flops 503414784 | bytes 9273344 | tf_op jit(solution)/shard_map/sd,csn->cdn/dot_general | solution.py:127
  215.4 2.5 collective-permute-start.4
  218.0 49.0 %all-gather.8.cloned.1.call-done = bf16[2,128,5120]{2,1,0:T(8,128)(2,1)} async-done(((bf16[2,32,5120]{2,1,0:T(8,128)(2,1)}), bf16[2,128,5120]{2,1,0:T(8,128)(2,1)}) %all-gather.8.cloned.1.call-update) | async-done | bytes 2621456 | tf_op jit(solution)/shard_map/all_gather | solution.py:54
  269.2 3.1 fusion.54
  277.1 3.1 pad_maximum_fusion.1
  286.5 3.3 fusion.6
  289.8 4.5 %add_convert_fusion.2 = bf16[3,128,5120]{2,1,0:T(8,128)(2,1)S(1)} fusion(f32[3,128,5120]{2,1,0:T(8,128)} %fusion.39, bf16[1,128,1,128]{3,1,2,0:T(8,128)(2,1)S(1)} %fusion.87, bf16[1,128,1,128]{3,1,2,0:T(8,128)(2,1)S(1)} %fusion.84, bf16[1,128,1,128]{3,1,2,0:T(8,128)(2,1)S(1)} %fusion.83, bf16[2,128,5120]{2,1,0:T(8,128)(2,1)S(1)} %copy-done.14), kind=kOutput, calls=%fused_computation.2 | convolution fusion | flops 507346944 | bytes 13205504 | tf_op jit(solution)/shard_map/sd,csn->cdn/dot_general | solution.py:127
  294.3 3.4 %fusion.24 = f32[128,5120]{1,0:T(8,128)} fusion(bf16[2,128,5120]{2,1,0:T(8,128)(2,1)} %collective-permute-done, bf16[4,128,128]{2,1,0:T(8,128)(2,1)} %collective-permute-done.4), kind=kOutput, calls=%fused_computation.42 | convolution fusion | flops 167772160 | bytes 3964928 | tf_op jit(solution)/shard_map/sn,sd->nd/dot_general | solution.py:130
  297.8 2.5 fusion.26
  300.3 4.5 %fusion = bf16[1,1,3,5120,128]{3,4,2,1,0:T(8,128)(2,1)} fusion(f32[3,128,5120]{2,1,0:T(8,128)S(1)} %fusion.26, bf16[4,128,128]{2,1,0:T(8,128)(2,1)} %collective-permute-done.4, bf16[3,128,5120]{2,1,0:T(8,128)(2,1)S(1)} %add_convert_fusion.2, bf16[2,128,5120]{2,1,0:T(8,128)(2,1)} %collective-permute-done), kind=kOutput, calls=%fused_computation.3 | convolution fusion | flops 515112960 | bytes 17170432 | tf_op jit(solution)/shard_map/sd,csn->cdn/dot_general | solution.py:127
  304.8 6.3 %copy.23 = bf16[1,1,3,5120,128]{4,3,2,1,0:T(8,128)(2,1)} copy(bf16[1,1,3,5120,128]{3,4,2,1,0:T(8,128)(2,1)} %fusion) | data formatting | bytes 7864320
  311.1 5.7 %collective-permute-done.6 = bf16[128,5120]{1,0:T(8,128)(2,1)} collective-permute-done((bf16[128,5120]{1,0:T(8,128)(2,1)S(1)}, bf16[128,5120]{1,0:T(8,128)(2,1)}, u32[]{:S(2)}, u32[]{:S(2)}) %collective-permute-start.6) | collective-permute-done | bytes 1310752 | tf_op jit(solution)/shard_map/ppermute | solution.py:20
  316.8 4.5 %fusion.9 = bf16[1,1,128,5120]{3,2,1,0:T(8,128)(2,1)} fusion(f32[128,5120]{1,0:T(8,128)} %fusion.6, f32[128,5120]{1,0:T(8,128)} %fusion.24, bf16[128,5120]{1,0:T(8,128)(2,1)} %collective-permute-done.6, bf16[4,128,128]{2,1,0:T(8,128)(2,1)S(1)} %collective-permute-done.5), kind=kOutput, calls=%fused_computation.18 | convolution fusion | flops 171048960 | bytes 7897088 | tf_op jit(solution)/shard_map/sn,sd->nd/dot_general | solution.py:130
  321.3 9.9 %reduce-scatter.5.cloned.1.call-done = bf16[2,32,5120]{2,1,0:T(8,128)(2,1)} async-done(((bf16[2,128,5120]{2,1,0:T(8,128)(2,1)}), bf16[2,32,5120]{2,1,0:T(8,128)(2,1)}) %reduce-scatter.5.cloned.1.call-update) | async-done | bytes 655376 | tf_op jit(solution)/shard_map/reduce_scatter | solution.py:59
  (167 shorter events, 52.5 us)
Async XLA Ops:
  7.2 71.7 %copy-start = (bf16[1,1,128,5120]{3,2,1,0:T(8,128)(2,1)S(1)}, bf16[1,1,128,5120]{3,2,1,0:T(8,128)(2,1)}, u32[]{:S(2)}) copy-start(bf16[1,1,128,5120]{3,2,1,0:T(8,128)(2,1)} %param.17) | copy-start | bytes 3932164
  7.2 5.6 %copy-start.15 = (bf16[64,5120]{1,0:T(8,128)(2,1)S(1)}, bf16[64,5120]{1,0:T(8,128)(2,1)}, u32[]{:S(2)}) copy-start(bf16[64,5120]{1,0:T(8,128)(2,1)} %param.14) | copy-start | bytes 1966084
  7.2 5.6 %copy-start.29 = (bf16[1,1,32,5120]{3,2,1,0:T(8,128)(2,1)S(1)}, bf16[1,1,32,5120]{3,2,1,0:T(8,128)(2,1)}, u32[]{:S(2)}) copy-start(bf16[1,1,32,5120]{3,2,1,0:T(8,128)(2,1)} %param.18) | copy-start | bytes 983044
  7.2 63.1 %all-gather.4.cloned.1.call-start = ((), (), s32[]{:S(2)}) async-start(), calls=%async_computation.2 | async-start | bytes 3276800 | tf_op jit(solution)/shard_map/all_gather | solution.py:54
  12.7 113.7 %all-gather.6.cloned.1.call-start = ((), (), s32[]{:S(2)}) async-start(), calls=%async_computation.3 | async-start | bytes 3276800 | tf_op jit(solution)/shard_map/all_gather | solution.py:54
  16.1 56.7 %copy-start.37 = (s32[1,2,5,128]{3,1,2,0:T(2,128)S(1)}, s32[1,2,5,128]{3,1,2,0:T(2,128)}, u32[]{:S(2)}) copy-start(s32[1,2,5,128]{3,1,2,0:T(2,128)} %param.13) | copy-start | bytes 15364
  72.7 115.6 %reduce-scatter.3.cloned.1.call-start = ((), (), s32[]{:S(2)}) async-start(), calls=%async_computation.4 | async-start | bytes 3276800 | tf_op jit(solution)/shard_map/reduce_scatter | solution.py:59
  73.4 60.3 %collective-permute-start = (bf16[2,128,5120]{2,1,0:T(8,128)(2,1)}, bf16[2,128,5120]{2,1,0:T(8,128)(2,1)}, u32[]{:S(2)}, u32[]{:S(2)}) collective-permute-start(bf16[2,128,5120]{2,1,0:T(8,128)(2,1)} %all-gather.4.cloned.1.call-done), channel_id=1, source_target_pairs={{0,25},{1,24},{8,17},{9,16},{16,9},{17,8},{24,1},{25,0},{2,27},{3,... | collective-permute-start | bytes 7864328 | tf_op jit(solution)/shard_map/ppermute | solution.py:20
  75.1 5.6 %copy-start.2 = (bf16[1,1,3,5120,128]{4,3,2,1,0:T(8,128)(2,1)S(1)}, bf16[1,1,3,5120,128]{4,3,2,1,0:T(8,128)(2,1)}, u32[]{:S(2)}) copy-start(bf16[1,1,3,5120,128]{4,3,2,1,0:T(8,128)(2,1)} %param.16) | copy-start | bytes 11796484
  137.2 129.7 %all-gather.8.cloned.1.call-start = ((), (), s32[]{:S(2)}) async-start(), calls=%async_computation.5 | async-start | bytes 3276800 | tf_op jit(solution)/shard_map/all_gather | solution.py:54
  188.3 12.0 %copy-start.12 = (bf16[2,128,5120]{2,1,0:T(8,128)(2,1)S(1)}, bf16[2,128,5120]{2,1,0:T(8,128)(2,1)}, u32[]{:S(2)}) copy-start(bf16[2,128,5120]{2,1,0:T(8,128)(2,1)} %all-gather.6.cloned.1.call-done) | copy-start | bytes 7864324
  190.0 14.9 %copy-start.22 = (bf16[32,5120]{1,0:T(8,128)(2,1)}, bf16[32,5120]{1,0:T(8,128)(2,1)S(1)}, u32[]{:S(2)}) copy-start(bf16[32,5120]{1,0:T(8,128)(2,1)S(1)} %get-tuple-element.42) | copy-start | bytes 983044
  190.0 14.7 %copy-start.27 = (bf16[32,5120]{1,0:T(8,128)(2,1)S(1)}, bf16[32,5120]{1,0:T(8,128)(2,1)}, u32[]{:S(2)}) copy-start(bf16[32,5120]{1,0:T(8,128)(2,1)} %fusion.11) | copy-start | bytes 983044
  190.7 14.2 %copy-start.17 = (bf16[1,2,32,5120]{3,2,1,0:T(8,128)(2,1)S(1)}, bf16[1,2,32,5120]{3,2,1,0:T(8,128)(2,1)}, u32[]{:S(2)}) copy-start(bf16[1,2,32,5120]{3,2,1,0:T(8,128)(2,1)} %param.21) | copy-start | bytes 1966084
  192.2 12.5 %collective-permute-start.1 = (bf16[32,5120]{1,0:T(8,128)(2,1)S(1)}, bf16[32,5120]{1,0:T(8,128)(2,1)S(1)}, u32[]{:S(2)}, u32[]{:S(2)}) collective-permute-start(bf16[32,5120]{1,0:T(8,128)(2,1)S(1)} %fusion.107), channel_id=1, source_target_pairs={{1,9},{8,0},{9,17},{16,8},{17,25},{24,16},{3,11},{10,2},{11,19},{1... | collective-permute-start | bytes 983048 | tf_op jit(solution)/shard_map/ppermute | solution.py:230
  193.5 11.2 %collective-permute-start.2 = (bf16[32,5120]{1,0:T(8,128)(2,1)S(1)}, bf16[32,5120]{1,0:T(8,128)(2,1)S(1)}, u32[]{:S(2)}, u32[]{:S(2)}) collective-permute-start(bf16[32,5120]{1,0:T(8,128)(2,1)S(1)} %get-tuple-element.42), channel_id=1, source_target_pairs={{0,8},{8,16},{9,1},{16,24},{17,9},{25,17},{2,10},{10,18},{11,3},{1... | collective-permute-start | bytes 983048 | tf_op jit(solution)/shard_map/ppermute | solution.py:231
  206.7 124.6 %reduce-scatter.5.cloned.1.call-start = ((), (), s32[]{:S(2)}) async-start(), calls=%async_computation.6 | async-start | bytes 3276800 | tf_op jit(solution)/shard_map/reduce_scatter | solution.py:59
  215.3 61.8 %collective-permute-start.3 = (bf16[1,128,5120]{2,1,0:T(8,128)(2,1)}, bf16[1,128,5120]{2,1,0:T(8,128)(2,1)}, u32[]{:S(2)}, u32[]{:S(2)}) collective-permute-start(bf16[1,128,5120]{2,1,0:T(8,128)(2,1)} %slice.179), channel_id=1, source_target_pairs={{0,25},{1,24},{8,17},{9,16},{16,9},{17,8},{24,1},{25,0},{2,27},{3,... | collective-permute-start | bytes 3932168 | tf_op jit(solution)/shard_map/ppermute | solution.py:20
  215.4 61.6 %collective-permute-start.4 = (bf16[4,128,128]{2,1,0:T(8,128)(2,1)}, bf16[4,128,128]{2,1,0:T(8,128)(2,1)}, u32[]{:S(2)}, u32[]{:S(2)}) collective-permute-start(bf16[4,128,128]{2,1,0:T(8,128)(2,1)} %pad_maximum_fusion.5), channel_id=1, source_target_pairs={{0,25},{1,24},{8,17},{9,16},{16,9},{17,8},{24,1},{25,0},{2,27},{3,... | collective-permute-start | bytes 393224 | tf_op jit(solution)/shard_map/ppermute | solution.py:20
  282.3 15.5 %collective-permute-start.5 = (bf16[4,128,128]{2,1,0:T(8,128)(2,1)S(1)}, bf16[4,128,128]{2,1,0:T(8,128)(2,1)S(1)}, u32[]{:S(2)}, u32[]{:S(2)}) collective-permute-start(bf16[4,128,128]{2,1,0:T(8,128)(2,1)S(1)} %pad_maximum_fusion.6), channel_id=1, source_target_pairs={{0,25},{1,24},{8,17},{9,16},{16,9},{17,8},{24,1},{25,0},{2,27},{3,... | collective-permute-start | bytes 393224 | tf_op jit(solution)/shard_map/ppermute | solution.py:20
  285.7 31.1 %collective-permute-start.6 = (bf16[128,5120]{1,0:T(8,128)(2,1)S(1)}, bf16[128,5120]{1,0:T(8,128)(2,1)}, u32[]{:S(2)}, u32[]{:S(2)}) collective-permute-start(bf16[128,5120]{1,0:T(8,128)(2,1)S(1)} %slice_bitcast_fusion.2), channel_id=1, source_target_pairs={{0,25},{1,24},{8,17},{9,16},{16,9},{17,8},{24,1},{25,0},{2,27},{3,... | collective-permute-start | bytes 3932168 | tf_op jit(solution)/shard_map/ppermute | solution.py:20
  311.1 21.5 %copy-start.11 = (bf16[32,5120]{1,0:T(8,128)(2,1)S(1)}, bf16[32,5120]{1,0:T(8,128)(2,1)}, u32[]{:S(2)}) copy-start(bf16[32,5120]{1,0:T(8,128)(2,1)} %copy-done.10) | copy-start | bytes 983044
  311.1 21.5 %copy-start.18 = (bf16[1,2,32,5120]{3,2,1,0:T(8,128)(2,1)S(1)}, bf16[1,2,32,5120]{3,2,1,0:T(8,128)(2,1)}, u32[]{:S(2)}) copy-start(bf16[1,2,32,5120]{3,2,1,0:T(8,128)(2,1)} %param.21) | copy-start | bytes 1966084
  321.3 13.7 %copy-start.23 = (bf16[32,5120]{1,0:T(8,128)(2,1)S(1)}, bf16[32,5120]{1,0:T(8,128)(2,1)}, u32[]{:S(2)}) copy-start(bf16[32,5120]{1,0:T(8,128)(2,1)} %copy-done.22) | copy-start | bytes 983044
  (29 other events, 78.6 us)
Sparse Core Ops, SparseCore 0:
  12.9 57.4 all-gather.3
  72.8 53.5 all-gather.5
  137.4 50.8 reduce-scatter.2
  206.8 60.1 all-gather.7
  280.3 50.9 reduce-scatter.4

commit v9 on v8

--- a/solution.py
+++ b/solution.py
@@ -190,13 +190,10 @@
         if step_index == 0:
             upstream_full, backward_normed_full[0] = gathered([upstream, saved_normed[0]])
             tie_scatter["first"] = to_partner(jnp.stack([upstream_full, backward_normed_full[0]]))
-            forward_rows, upstream_full = lax.optimization_barrier(
-                ([normed_rows(current)] + saved_normed[1:], upstream_full)
-            )
-            forward_normed_full, *later = gathered(forward_rows)
-            backward_normed_full[1:] = later
-            if later:
-                deferred["later"] = jnp.stack(later)
+            forward_normed, upstream_full = lax.optimization_barrier(
+                (normed_rows(current), upstream_full)
+            )
+            forward_normed_full = gathered([forward_normed])[0]
         else:
             upstream_full, forward_normed_full = gathered([upstream, normed_rows(current)])
             inbox[f"rows{step_index}"] = to_partner(upstream_full)
@@ -220,6 +217,11 @@
         inbox.update(tie_scatter)
         tie_scatter = {}
         d_normed, attn_rows = scattered([d_normed_part, attn_part])
+        if step_index == 0 and window_steps > 1:
+            later_rows, d_normed = lax.optimization_barrier((saved_normed[1:], d_normed))
+            later = gathered(later_rows)
+            backward_normed_full[1:] = later
+            deferred["later"] = jnp.stack(later)
         backward_out = input_grad(saved[0, 0, step_index], upstream, d_normed)
         forward_out = (current.astype(jnp.float32) + attn_rows.astype(jnp.float32)).astype(
             jnp.bfloat16

time: 344 us -> 358 us (1.041)
  waiting for transfers between devices: 214 us -> 234 us
  matrix products: 58.4 us -> 52.5 us
    ppermute x5, waiting for transfers between devices: 6.35 us -> 33.6 us  [flipped(): lax.ppermute(value, axis, [(i, i ^ mask) for i in range(lax.axis_size(axi...]
    all_gather x3 -> x4, waiting for transfers between devices: 146 us -> 136 us  [gathered(): full = lax.all_gather(jnp.stack(blocks), 'tp', axis=1, tiled=True)]
    dot_general x4, matrix products: 16.2 us -> 9.43 us  [weight_terms(): jnp.einsum('sd,csn->cdn', normed_full, d_projected, preferred_element_typ...]
    ppermute x1, waiting for transfers between devices: 3.16 us -> 8.3 us  [shards(): backward_in = lax.ppermute(backward_out, pair_axes, down_pairs)]
    dot_general x4, matrix products: 13.3 us -> 8.18 us  [weight_terms(): jnp.einsum('sn,sd->nd', mixed, upstream_full, preferred_element_type=jnp....]
    unnamed x83 -> x61, local copies, waits for them, and re-layouts: 11.9 us -> 11.6 us
  transfers between devices with their start and end apart: 12 -> 13, of which waited for: 8 -> 9; matrix products, arithmetic and copies ran while one was open for 21% -> 19% of each run, Pallas kernels for 0% -> 0%
where the time goes in v9:
time: 358 us; the launch traced here: 357 us
  waiting for transfers between devices  234 us (65%)
  matrix products  52.5 us (15%)
  other arithmetic  26.7 us (7%)
  local copies, waits for them, and re-layouts  16.5 us (5%)
  between operations  14.6 us (4%)
  starting transfers between devices  12.2 us (3%)
    all_gather x4, waiting for transfers between devices, gathered(): full = lax.all_gather(jnp.stack(blocks), 'tp', axis=1, tiled=True)  136 us
    reduce_scatter x2, waiting for transfers between devices, scattered(): lax.psum_scatter(jnp.stack(blocks), 'tp', scatter_dimension=1, tiled=True)  56.5 us
    ppermute x5, waiting for transfers between devices, flipped(): lax.ppermute(value, axis, [(i, i ^ mask) for i in range(lax.axis_size(axi...  33.6 us
    dot_general x4, matrix products, heads_of(): jnp.einsum('sd,cdn->csn', normed_full, qkv_weight, preferred_element_type...  13.3 us
    unnamed x61, local copies, waits for them, and re-layouts  11.6 us
    dot_general x4, matrix products, weight_terms(): jnp.einsum('sd,csn->cdn', normed_full, d_projected, preferred_element_typ...  9.43 us
    ppermute x1, waiting for transfers between devices, shards(): backward_in = lax.ppermute(backward_out, pair_axes, down_pairs)  8.3 us
    dot_general x4, matrix products, weight_terms(): jnp.einsum('sn,sd->nd', mixed, upstream_full, preferred_element_type=jnp....  8.18 us
  transfers between devices with their start and end apart: 13, of which 9 were waited for; matrix products, arithmetic and copies ran while one was open for 19% of the time, Pallas kernels for 0%

profile of v9, /device:TPU:0, one launch (start us, length us, event | category | flops | bytes accessed | tf_op | source)
XLA Modules:
  0.0 357.0 jit_solution(8547236212240235511)
XLA Ops:
  15.3 54.2 %all-gather.7.cloned.1.call-done = bf16[2,128,5120]{2,1,0:T(8,128)(2,1)} async-done(((bf16[2,32,5120]{2,1,0:T(8,128)(2,1)}), bf16[2,128,5120]{2,1,0:T(8,128)(2,1)}) %all-gather.7.cloned.1.call-update) | async-done | bytes 2621456 | tf_op jit(solution)/shard_map/all_gather | solution.py:54
  72.7 3.5 fusion.70
  78.4 2.4 fusion.7
  80.8 22.2 %all-gather.11.cloned.1.call-done = bf16[128,5120]{1,0:T(8,128)(2,1)} async-done(((bf16[32,5120]{1,0:T(8,128)(2,1)}), bf16[128,5120]{1,0:T(8,128)(2,1)}) %all-gather.11.cloned.1.call-update) | async-done | bytes 1310736 | tf_op jit(solution)/shard_map/all_gather | solution.py:54
  103.0 3.4 fusion.65
  107.2 2.5 convolution_convert_fusion.1
  109.7 21.7 %collective-permute-done = bf16[2,128,5120]{2,1,0:T(8,128)(2,1)} collective-permute-done((bf16[2,128,5120]{2,1,0:T(8,128)(2,1)}, bf16[2,128,5120]{2,1,0:T(8,128)(2,1)}, u32[]{:S(2)}, u32[]{:S(2)}) %collective-permute-start) | collective-permute-done | bytes 2621472 | tf_op jit(solution)/shard_map/ppermute | solution.py:20
  131.4 3.4 pad_maximum_fusion
  137.9 48.0 %reduce-scatter.3.cloned.1.call-done = bf16[2,32,5120]{2,1,0:T(8,128)(2,1)} async-done(((bf16[2,128,5120]{2,1,0:T(8,128)(2,1)}), bf16[2,32,5120]{2,1,0:T(8,128)(2,1)}) %reduce-scatter.3.cloned.1.call-update) | async-done | bytes 655376 | tf_op jit(solution)/shard_map/reduce_scatter | solution.py:59
  189.7 3.4 collective-permute-start.2
  199.5 8.3 %collective-permute-done.1 = bf16[32,5120]{1,0:T(8,128)(2,1)} collective-permute-done((bf16[32,5120]{1,0:T(8,128)(2,1)S(1)}, bf16[32,5120]{1,0:T(8,128)(2,1)}, u32[]{:S(2)}, u32[]{:S(2)}) %collective-permute-start.1) | collective-permute-done | bytes 327712 | tf_op jit(solution)/shard_map/ppermute | solution.py:232
  207.8 12.1 %all-gather.13.cloned.1.call-done = bf16[128,5120]{1,0:T(8,128)(2,1)} async-done(((bf16[32,5120]{1,0:T(8,128)(2,1)}), bf16[128,5120]{1,0:T(8,128)(2,1)}) %all-gather.13.cloned.1.call-update) | async-done | bytes 1310736 | tf_op jit(solution)/shard_map/all_gather | solution.py:54
  226.4 3.4 fusion.60
  230.0 47.4 %all-gather.9.cloned.1.call-done = bf16[2,128,5120]{2,1,0:T(8,128)(2,1)} async-done(((bf16[2,32,5120]{2,1,0:T(8,128)(2,1)}), bf16[2,128,5120]{2,1,0:T(8,128)(2,1)}) %all-gather.9.cloned.1.call-update) | async-done | bytes 2621456 | tf_op jit(solution)/shard_map/all_gather | solution.py:54
  279.5 3.1 fusion.57
  288.0 2.6 convolution_convert_fusion
  290.6 3.5 pad_maximum_fusion.1
  304.5 3.3 fusion.24
  307.8 2.5 fusion.26
  310.4 4.5 %fusion = bf16[1,1,3,5120,128]{3,4,2,1,0:T(8,128)(2,1)} fusion(f32[3,128,5120]{2,1,0:T(8,128)S(1)} %fusion.26, bf16[4,128,128]{2,1,0:T(8,128)(2,1)} %collective-permute-done.4, bf16[3,128,5120]{2,1,0:T(8,128)(2,1)S(1)} %add_convert_fusion.2, bf16[2,128,5120]{2,1,0:T(8,128)(2,1)} %collective-permute-done), kind=kOutput, calls=%fused_computation.3 | convolution fusion | flops 515112960 | bytes 17170432 | tf_op jit(solution)/shard_map/sd,csn->cdn/dot_general | solution.py:127
  314.9 6.3 %copy.23 = bf16[1,1,3,5120,128]{4,3,2,1,0:T(8,128)(2,1)} copy(bf16[1,1,3,5120,128]{3,4,2,1,0:T(8,128)(2,1)} %fusion) | data formatting | bytes 7864320
  321.1 11.9 %collective-permute-done.6 = bf16[128,5120]{1,0:T(8,128)(2,1)} collective-permute-done((bf16[128,5120]{1,0:T(8,128)(2,1)}, bf16[128,5120]{1,0:T(8,128)(2,1)}, u32[]{:S(2)}, u32[]{:S(2)}) %collective-permute-start.6) | collective-permute-done | bytes 1310752 | tf_op jit(solution)/shard_map/ppermute | solution.py:20
  333.1 3.8 %fusion.9 = bf16[1,1,128,5120]{3,2,1,0:T(8,128)(2,1)} fusion(f32[128,5120]{1,0:T(8,128)S(1)} %fusion.6, f32[128,5120]{1,0:T(8,128)} %fusion.24, bf16[128,5120]{1,0:T(8,128)(2,1)} %collective-permute-done.6, bf16[4,128,128]{2,1,0:T(8,128)(2,1)S(1)} %collective-permute-done.5), kind=kOutput, calls=%fused_computation.18 | convolution fusion | flops 171048960 | bytes 7897088 | tf_op jit(solution)/shard_map/sn,sd->nd/dot_general | solution.py:130
  336.8 8.5 %reduce-scatter.5.cloned.1.call-done = bf16[2,32,5120]{2,1,0:T(8,128)(2,1)} async-done(((bf16[2,128,5120]{2,1,0:T(8,128)(2,1)}), bf16[2,32,5120]{2,1,0:T(8,128)(2,1)}) %reduce-scatter.5.cloned.1.call-update) | async-done | bytes 655376 | tf_op jit(solution)/shard_map/reduce_scatter | solution.py:59
  (147 shorter events, 56.4 us)
Async XLA Ops:
  7.2 69.3 %copy-start = (bf16[1,1,128,5120]{3,2,1,0:T(8,128)(2,1)S(1)}, bf16[1,1,128,5120]{3,2,1,0:T(8,128)(2,1)}, u32[]{:S(2)}) copy-start(bf16[1,1,128,5120]{3,2,1,0:T(8,128)(2,1)} %param.17) | copy-start | bytes 3932164
  7.2 4.9 %copy-start.27 = (s32[1,2,5,128]{3,1,2,0:T(2,128)S(1)}, s32[1,2,5,128]{3,1,2,0:T(2,128)}, u32[]{:S(2)}) copy-start(s32[1,2,5,128]{3,1,2,0:T(2,128)} %param.13) | copy-start | bytes 15364
  7.2 5.5 %copy-start.28 = (s32[1,2,32]{2,1,0:T(2,128)S(1)}, s32[1,2,32]{2,1,0:T(2,128)}, u32[]{:S(2)}) copy-start(s32[1,2,32]{2,1,0:T(2,128)} %param.12) | copy-start | bytes 772
  7.2 5.5 %copy-start.8 = (bf16[64,5120]{1,0:T(8,128)(2,1)S(1)}, bf16[64,5120]{1,0:T(8,128)(2,1)}, u32[]{:S(2)}) copy-start(bf16[64,5120]{1,0:T(8,128)(2,1)} %param.14) | copy-start | bytes 1966084
  7.2 62.3 %all-gather.7.cloned.1.call-start = ((), (), s32[]{:S(2)}) async-start(), calls=%async_computation.2 | async-start | bytes 3276800 | tf_op jit(solution)/shard_map/all_gather | solution.py:54
  9.9 4.3 %copy-start.4 = (bf16[1,1,2,32,5120]{4,3,2,1,0:T(8,128)(2,1)S(1)}, bf16[1,1,2,32,5120]{4,3,2,1,0:T(8,128)(2,1)}, u32[]{:S(2)}) copy-start(bf16[1,1,2,32,5120]{4,3,2,1,0:T(8,128)(2,1)} %param.20) | copy-start | bytes 1966084
  9.9 4.3 %copy-start.16 = (f32[1,1,5120]{2,1,0:T(1,128)S(1)}, f32[1,1,5120]{2,1,0:T(1,128)}, u32[]{:S(2)}) copy-start(f32[1,1,5120]{2,1,0:T(1,128)} %param.15) | copy-start | bytes 61444
  12.0 91.0 %all-gather.11.cloned.1.call-start = ((), (), s32[]{:S(2)}) async-start(), calls=%async_computation.6 | async-start | bytes 1638400 | tf_op jit(solution)/shard_map/all_gather | solution.py:54
  70.9 115.0 %reduce-scatter.3.cloned.1.call-start = ((), (), s32[]{:S(2)}) async-start(), calls=%async_computation.3 | async-start | bytes 3276800 | tf_op jit(solution)/shard_map/reduce_scatter | solution.py:59
  71.0 60.4 %collective-permute-start = (bf16[2,128,5120]{2,1,0:T(8,128)(2,1)}, bf16[2,128,5120]{2,1,0:T(8,128)(2,1)}, u32[]{:S(2)}, u32[]{:S(2)}) collective-permute-start(bf16[2,128,5120]{2,1,0:T(8,128)(2,1)} %all-gather.7.cloned.1.call-done), channel_id=1, source_target_pairs={{0,25},{1,24},{8,17},{9,16},{16,9},{17,8},{24,1},{25,0},{2,27},{3,... | collective-permute-start | bytes 7864328 | tf_op jit(solution)/shard_map/ppermute | solution.py:20
  72.7 5.6 %copy-start.2 = (bf16[1,1,3,5120,128]{4,3,2,1,0:T(8,128)(2,1)S(1)}, bf16[1,1,3,5120,128]{4,3,2,1,0:T(8,128)(2,1)}, u32[]{:S(2)}) copy-start(bf16[1,1,3,5120,128]{4,3,2,1,0:T(8,128)(2,1)} %param.16) | copy-start | bytes 11796484
  134.9 85.0 %all-gather.13.cloned.1.call-start = ((), (), s32[]{:S(2)}) async-start(), calls=%async_computation.7 | async-start | bytes 1638400 | tf_op jit(solution)/shard_map/all_gather | solution.py:54
  187.7 89.7 %all-gather.9.cloned.1.call-start = ((), (), s32[]{:S(2)}) async-start(), calls=%async_computation.4 | async-start | bytes 3276800 | tf_op jit(solution)/shard_map/all_gather | solution.py:54
  189.7 9.0 %collective-permute-start.2 = (bf16[32,5120]{1,0:T(8,128)(2,1)S(1)}, bf16[32,5120]{1,0:T(8,128)(2,1)S(1)}, u32[]{:S(2)}, u32[]{:S(2)}) collective-permute-start(bf16[32,5120]{1,0:T(8,128)(2,1)S(1)} %fusion.120), channel_id=1, source_target_pairs={{0,8},{8,16},{9,1},{16,24},{17,9},{25,17},{2,10},{10,18},{11,3},{1... | collective-permute-start | bytes 983048 | tf_op jit(solution)/shard_map/ppermute | solution.py:233
  195.8 12.0 %collective-permute-start.1 = (bf16[32,5120]{1,0:T(8,128)(2,1)S(1)}, bf16[32,5120]{1,0:T(8,128)(2,1)}, u32[]{:S(2)}, u32[]{:S(2)}) collective-permute-start(bf16[32,5120]{1,0:T(8,128)(2,1)S(1)} %fusion.108), channel_id=1, source_target_pairs={{1,9},{8,0},{9,17},{16,8},{17,25},{24,16},{3,11},{10,2},{11,19},{1... | collective-permute-start | bytes 983048 | tf_op jit(solution)/shard_map/ppermute | solution.py:232
  223.4 121.9 %reduce-scatter.5.cloned.1.call-start = ((), (), s32[]{:S(2)}) async-start(), calls=%async_computation.5 | async-start | bytes 3276800 | tf_op jit(solution)/shard_map/reduce_scatter | solution.py:59
  223.7 67.0 %collective-permute-start.3 = (bf16[1,128,5120]{2,1,0:T(8,128)(2,1)}, bf16[1,128,5120]{2,1,0:T(8,128)(2,1)}, u32[]{:S(2)}, u32[]{:S(2)}) collective-permute-start(bf16[1,128,5120]{2,1,0:T(8,128)(2,1)} %bitcast.381), channel_id=1, source_target_pairs={{0,25},{1,24},{8,17},{9,16},{16,9},{17,8},{24,1},{25,0},{2,27},{3,... | collective-permute-start | bytes 3932168 | tf_op jit(solution)/shard_map/ppermute | solution.py:20
  224.8 65.8 %collective-permute-start.4 = (bf16[4,128,128]{2,1,0:T(8,128)(2,1)}, bf16[4,128,128]{2,1,0:T(8,128)(2,1)}, u32[]{:S(2)}, u32[]{:S(2)}) collective-permute-start(bf16[4,128,128]{2,1,0:T(8,128)(2,1)} %pad_maximum_fusion.4), channel_id=1, source_target_pairs={{0,25},{1,24},{8,17},{9,16},{16,9},{17,8},{24,1},{25,0},{2,27},{3,... | collective-permute-start | bytes 393224 | tf_op jit(solution)/shard_map/ppermute | solution.py:20
  229.7 52.9 %copy-start.17 = (bf16[3,128,128]{2,1,0:T(8,128)(2,1)}, bf16[3,128,128]{2,1,0:T(8,128)(2,1)S(1)}, u32[]{:S(2)}) copy-start(bf16[3,128,128]{2,1,0:T(8,128)(2,1)S(1)} %fusion.60) | copy-start | bytes 294916
  279.5 6.1 %copy-start.3 = (bf16[1,1,3,5120,128]{4,3,2,1,0:T(8,128)(2,1)S(1)}, bf16[1,1,3,5120,128]{4,3,2,1,0:T(8,128)(2,1)}, u32[]{:S(2)}) copy-start(bf16[1,1,3,5120,128]{4,3,2,1,0:T(8,128)(2,1)} %param.16) | copy-start | bytes 11796484
  298.9 9.0 %collective-permute-start.5 = (bf16[4,128,128]{2,1,0:T(8,128)(2,1)S(1)}, bf16[4,128,128]{2,1,0:T(8,128)(2,1)S(1)}, u32[]{:S(2)}, u32[]{:S(2)}) collective-permute-start(bf16[4,128,128]{2,1,0:T(8,128)(2,1)S(1)} %pad_maximum_fusion.5), channel_id=1, source_target_pairs={{0,25},{1,24},{8,17},{9,16},{16,9},{17,8},{24,1},{25,0},{2,27},{3,... | collective-permute-start | bytes 393224 | tf_op jit(solution)/shard_map/ppermute | solution.py:20
  301.8 31.3 %collective-permute-start.6 = (bf16[128,5120]{1,0:T(8,128)(2,1)}, bf16[128,5120]{1,0:T(8,128)(2,1)}, u32[]{:S(2)}, u32[]{:S(2)}) collective-permute-start(bf16[128,5120]{1,0:T(8,128)(2,1)} %slice_bitcast_fusion.2), channel_id=1, source_target_pairs={{0,25},{1,24},{8,17},{9,16},{16,9},{17,8},{24,1},{25,0},{2,27},{3,... | collective-permute-start | bytes 3932168 | tf_op jit(solution)/shard_map/ppermute | solution.py:20
  336.8 11.5 %copy-start.15 = (bf16[32,5120]{1,0:T(8,128)(2,1)S(1)}, bf16[32,5120]{1,0:T(8,128)(2,1)}, u32[]{:S(2)}) copy-start(bf16[32,5120]{1,0:T(8,128)(2,1)} %copy-done.14) | copy-start | bytes 983044
  336.8 12.4 %copy-start.13 = (bf16[32,5120]{1,0:T(8,128)(2,1)S(1)}, bf16[32,5120]{1,0:T(8,128)(2,1)}, u32[]{:S(2)}) copy-start(bf16[32,5120]{1,0:T(8,128)(2,1)} %copy-done.12) | copy-start | bytes 983044
  (19 other events, 32.2 us)
Sparse Core Ops, SparseCore 0:
  12.1 57.3 all-gather.6
  71.7 31.2 all-gather.10
  135.0 50.8 reduce-scatter.2
  187.8 32.0 all-gather.12
  223.6 53.7 all-gather.8
  294.3 51.0 reduce-scatter.4

commit v10 on v9

--- a/solution.py
+++ b/solution.py
@@ -189,7 +189,7 @@
         upstream = jnp.where(position == sections - 1, cotangent[0, step_index], backward_in)
         if step_index == 0:
             upstream_full, backward_normed_full[0] = gathered([upstream, saved_normed[0]])
-            tie_scatter["first"] = to_partner(jnp.stack([upstream_full, backward_normed_full[0]]))
+            first_sent = to_partner(jnp.stack([upstream_full, backward_normed_full[0]]))
             forward_normed, upstream_full = lax.optimization_barrier(
                 (normed_rows(current), upstream_full)
             )
@@ -231,9 +231,15 @@
         if step_index < last_step:
             backward_in = lax.ppermute(backward_out, pair_axes, down_pairs)
             forward_in = lax.ppermute(forward_out, pair_axes, up_pairs)
-            deferred, backward_in, forward_in = lax.optimization_barrier(
-                (deferred, backward_in, forward_in)
-            )
+            if step_index == 0:
+                deferred, first_sent, backward_in, forward_in = lax.optimization_barrier(
+                    (deferred, first_sent, backward_in, forward_in)
+                )
+                inbox["first"] = first_sent
+            else:
+                deferred, backward_in, forward_in = lax.optimization_barrier(
+                    (deferred, backward_in, forward_in)
+                )
             tie_scatter = {key: to_partner(value) for key, value in deferred.items()}
             deferred = {}
 

time: 358 us -> 337 us (0.941)
  waiting for transfers between devices: 234 us -> 212 us
    ppermute x5, waiting for transfers between devices: 33.6 us -> 11.9 us  [flipped(): lax.ppermute(value, axis, [(i, i ^ mask) for i in range(lax.axis_size(axi...]
    all_gather x4, waiting for transfers between devices: 136 us -> 142 us  [gathered(): full = lax.all_gather(jnp.stack(blocks), 'tp', axis=1, tiled=True)]
    ppermute x1, waiting for transfers between devices: 8.3 us -> 2.59 us  [shards(): backward_in = lax.ppermute(backward_out, pair_axes, down_pairs)]
    unnamed x61 -> x63, local copies, waits for them, and re-layouts: 11.6 us -> 11.7 us
  transfers between devices with their start and end apart: 13 -> 13, of which waited for: 9 -> 8; matrix products, arithmetic and copies ran while one was open for 19% -> 19% of each run, Pallas kernels for 0% -> 0%
where the time goes in v10:
time: 337 us; the launch traced here: 336 us
  waiting for transfers between devices  212 us (63%)
  matrix products  52.5 us (16%)
  other arithmetic  26.5 us (8%)
  local copies, waits for them, and re-layouts  16.5 us (5%)
  between operations  14.6 us (4%)
  starting transfers between devices  13.6 us (4%)
    all_gather x4, waiting for transfers between devices, gathered(): full = lax.all_gather(jnp.stack(blocks), 'tp', axis=1, tiled=True)  142 us
    reduce_scatter x2, waiting for transfers between devices, scattered(): lax.psum_scatter(jnp.stack(blocks), 'tp', scatter_dimension=1, tiled=True)  55.9 us
    dot_general x4, matrix products, heads_of(): jnp.einsum('sd,cdn->csn', normed_full, qkv_weight, preferred_element_type...  13.3 us
    ppermute x5, waiting for transfers between devices, flipped(): lax.ppermute(value, axis, [(i, i ^ mask) for i in range(lax.axis_size(axi...  11.9 us
    unnamed x63, local copies, waits for them, and re-layouts  11.7 us
    dot_general x4, matrix products, weight_terms(): jnp.einsum('sd,csn->cdn', normed_full, d_projected, preferred_element_typ...  9.43 us
    dot_general x4, matrix products, weight_terms(): jnp.einsum('sn,sd->nd', mixed, upstream_full, preferred_element_type=jnp....  8.18 us
    another operation x2, other arithmetic, scattered(): jnp.stack(blocks)  6.94 us
  transfers between devices with their start and end apart: 13, of which 8 were waited for; matrix products, arithmetic and copies ran while one was open for 19% of the time, Pallas kernels for 0%

profile of v10, /device:TPU:0, one launch (start us, length us, event | category | flops | bytes accessed | tf_op | source)
XLA Modules:
  0.0 336.0 jit_solution(15347766796887481178)
XLA Ops:
  15.2 54.3 %all-gather.7.cloned.1.call-done = bf16[2,128,5120]{2,1,0:T(8,128)(2,1)} async-done(((bf16[2,32,5120]{2,1,0:T(8,128)(2,1)}), bf16[2,128,5120]{2,1,0:T(8,128)(2,1)}) %all-gather.7.cloned.1.call-update) | async-done | bytes 2621456 | tf_op jit(solution)/shard_map/all_gather | solution.py:54
  71.0 3.5 %fusion.70 = bf16[3,128,128]{2,1,0:T(8,128)(2,1)S(1)} fusion(bf16[1,1,3,5120,128]{4,3,2,1,0:T(8,128)(2,1)} %param.16, bf16[2,128,5120]{2,1,0:T(8,128)(2,1)} %all-gather.7.cloned.1.call-done), kind=kOutput, calls=%fused_computation.69 | convolution fusion | flops 503365632 | bytes 5341184 | tf_op jit(solution)/shard_map/sd,cdn->csn/dot_general | solution.py:86
  76.7 2.4 fusion.7
  79.1 23.9 %all-gather.11.cloned.1.call-done = bf16[128,5120]{1,0:T(8,128)(2,1)} async-done(((bf16[32,5120]{1,0:T(8,128)(2,1)}), bf16[128,5120]{1,0:T(8,128)(2,1)}) %all-gather.11.cloned.1.call-update) | async-done | bytes 1310736 | tf_op jit(solution)/shard_map/all_gather | solution.py:54
  103.0 3.4 fusion.65
  107.2 2.5 convolution_convert_fusion.1
  109.8 3.4 %pad_maximum_fusion = bf16[2,128,5120]{2,1,0:T(8,128)(2,1)} fusion(bf16[1,128,5120]{2,1,0:T(8,128)(2,1)} %bitcast.380, bf16[1,128,5120]{2,1,0:T(8,128)(2,1)} %bitcast.382), kind=kLoop, calls=%fused_computation.35 | loop fusion | flops 1310720 | bytes 5242880 | tf_op jit(solution)/shard_map/stack | solution.py:59
  117.5 47.4 %reduce-scatter.3.cloned.1.call-done = bf16[2,32,5120]{2,1,0:T(8,128)(2,1)} async-done(((bf16[2,128,5120]{2,1,0:T(8,128)(2,1)}), bf16[2,32,5120]{2,1,0:T(8,128)(2,1)}) %reduce-scatter.3.cloned.1.call-update) | async-done | bytes 655376 | tf_op jit(solution)/shard_map/reduce_scatter | solution.py:59
  172.4 5.3 %collective-permute-start.2 = (bf16[32,5120]{1,0:T(8,128)(2,1)S(1)}, bf16[32,5120]{1,0:T(8,128)(2,1)}, u32[]{:S(2)}, u32[]{:S(2)}) collective-permute-start(bf16[32,5120]{1,0:T(8,128)(2,1)S(1)} %fusion.120), channel_id=1, source_target_pairs={{0,8},{8,16},{9,1},{16,24},{17,9},{25,17},{2,10},{10,18},{11,3},{1... | collective-permute-start | bytes 983048 | tf_op jit(solution)/shard_map/ppermute | solution.py:233
  179.4 2.6 collective-permute-done.1
  182.7 16.1 %all-gather.13.cloned.1.call-done = bf16[128,5120]{1,0:T(8,128)(2,1)} async-done(((bf16[32,5120]{1,0:T(8,128)(2,1)}), bf16[128,5120]{1,0:T(8,128)(2,1)}) %all-gather.13.cloned.1.call-update) | async-done | bytes 1310736 | tf_op jit(solution)/shard_map/all_gather | solution.py:54
  205.3 3.4 fusion.60
  208.9 47.4 %all-gather.9.cloned.1.call-done = bf16[2,128,5120]{2,1,0:T(8,128)(2,1)} async-done(((bf16[2,32,5120]{2,1,0:T(8,128)(2,1)}), bf16[2,128,5120]{2,1,0:T(8,128)(2,1)}) %all-gather.9.cloned.1.call-update) | async-done | bytes 2621456 | tf_op jit(solution)/shard_map/all_gather | solution.py:54
  258.4 3.1 fusion.57
  264.5 2.4 fusion.8
  266.9 2.6 convolution_convert_fusion
  269.6 3.5 %pad_maximum_fusion.1 = bf16[2,128,5120]{2,1,0:T(8,128)(2,1)} fusion(bf16[1,128,5120]{2,1,0:T(8,128)(2,1)} %bitcast.379, bf16[1,128,5120]{2,1,0:T(8,128)(2,1)} %bitcast.383), kind=kLoop, calls=%fused_computation.36 | loop fusion | flops 1310720 | bytes 5242880 | tf_op jit(solution)/shard_map/stack | solution.py:59
  283.4 3.3 fusion.24
  286.8 2.5 fusion.26
  289.3 4.5 %fusion = bf16[1,1,3,5120,128]{3,4,2,1,0:T(8,128)(2,1)} fusion(f32[3,128,5120]{2,1,0:T(8,128)S(1)} %fusion.26, bf16[4,128,128]{2,1,0:T(8,128)(2,1)} %collective-permute-done.4, bf16[3,128,5120]{2,1,0:T(8,128)(2,1)S(1)} %add_convert_fusion.2, bf16[2,128,5120]{2,1,0:T(8,128)(2,1)} %collective-permute-done), kind=kOutput, calls=%fused_computation.3 | convolution fusion | flops 515112960 | bytes 17170432 | tf_op jit(solution)/shard_map/sd,csn->cdn/dot_general | solution.py:127
  293.8 6.3 %copy.23 = bf16[1,1,3,5120,128]{4,3,2,1,0:T(8,128)(2,1)} copy(bf16[1,1,3,5120,128]{3,4,2,1,0:T(8,128)(2,1)} %fusion) | data formatting | bytes 7864320
  300.1 11.9 %collective-permute-done.6 = bf16[128,5120]{1,0:T(8,128)(2,1)} collective-permute-done((bf16[128,5120]{1,0:T(8,128)(2,1)}, bf16[128,5120]{1,0:T(8,128)(2,1)}, u32[]{:S(2)}, u32[]{:S(2)}) %collective-permute-start.6) | collective-permute-done | bytes 1310752 | tf_op jit(solution)/shard_map/ppermute | solution.py:20
  312.0 3.8 %fusion.9 = bf16[1,1,128,5120]{3,2,1,0:T(8,128)(2,1)} fusion(f32[128,5120]{1,0:T(8,128)S(1)} %fusion.6, f32[128,5120]{1,0:T(8,128)} %fusion.24, bf16[128,5120]{1,0:T(8,128)(2,1)} %collective-permute-done.6, bf16[4,128,128]{2,1,0:T(8,128)(2,1)S(1)} %collective-permute-done.5), kind=kOutput, calls=%fused_computation.18 | convolution fusion | flops 171048960 | bytes 7897088 | tf_op jit(solution)/shard_map/sn,sd->nd/dot_general | solution.py:130
  315.7 8.5 %reduce-scatter.5.cloned.1.call-done = bf16[2,32,5120]{2,1,0:T(8,128)(2,1)} async-done(((bf16[2,128,5120]{2,1,0:T(8,128)(2,1)}), bf16[2,32,5120]{2,1,0:T(8,128)(2,1)}) %reduce-scatter.5.cloned.1.call-update) | async-done | bytes 655376 | tf_op jit(solution)/shard_map/reduce_scatter | solution.py:59
  (149 shorter events, 53.3 us)
Async XLA Ops:
  7.2 67.6 %copy-start = (bf16[1,1,128,5120]{3,2,1,0:T(8,128)(2,1)S(1)}, bf16[1,1,128,5120]{3,2,1,0:T(8,128)(2,1)}, u32[]{:S(2)}) copy-start(bf16[1,1,128,5120]{3,2,1,0:T(8,128)(2,1)} %param.17) | copy-start | bytes 3932164
  7.2 4.9 %copy-start.28 = (s32[1,2,5,128]{3,1,2,0:T(2,128)S(1)}, s32[1,2,5,128]{3,1,2,0:T(2,128)}, u32[]{:S(2)}) copy-start(s32[1,2,5,128]{3,1,2,0:T(2,128)} %param.13) | copy-start | bytes 15364
  7.2 5.4 %copy-start.29 = (s32[1,2,32]{2,1,0:T(2,128)S(1)}, s32[1,2,32]{2,1,0:T(2,128)}, u32[]{:S(2)}) copy-start(s32[1,2,32]{2,1,0:T(2,128)} %param.12) | copy-start | bytes 772
  7.2 5.4 %copy-start.9 = (bf16[64,5120]{1,0:T(8,128)(2,1)S(1)}, bf16[64,5120]{1,0:T(8,128)(2,1)}, u32[]{:S(2)}) copy-start(bf16[64,5120]{1,0:T(8,128)(2,1)} %param.14) | copy-start | bytes 1966084
  7.2 62.3 %all-gather.7.cloned.1.call-start = ((), (), s32[]{:S(2)}) async-start(), calls=%async_computation.2 | async-start | bytes 3276800 | tf_op jit(solution)/shard_map/all_gather | solution.py:54
  9.9 4.3 %copy-start.4 = (bf16[1,1,2,32,5120]{4,3,2,1,0:T(8,128)(2,1)S(1)}, bf16[1,1,2,32,5120]{4,3,2,1,0:T(8,128)(2,1)}, u32[]{:S(2)}) copy-start(bf16[1,1,2,32,5120]{4,3,2,1,0:T(8,128)(2,1)} %param.20) | copy-start | bytes 1966084
  12.0 91.0 %all-gather.11.cloned.1.call-start = ((), (), s32[]{:S(2)}) async-start(), calls=%async_computation.6 | async-start | bytes 1638400 | tf_op jit(solution)/shard_map/all_gather | solution.py:54
  70.9 93.9 %reduce-scatter.3.cloned.1.call-start = ((), (), s32[]{:S(2)}) async-start(), calls=%async_computation.3 | async-start | bytes 3276800 | tf_op jit(solution)/shard_map/reduce_scatter | solution.py:59
  71.0 5.7 %copy-start.2 = (bf16[1,1,3,5120,128]{4,3,2,1,0:T(8,128)(2,1)S(1)}, bf16[1,1,3,5120,128]{4,3,2,1,0:T(8,128)(2,1)}, u32[]{:S(2)}) copy-start(bf16[1,1,3,5120,128]{4,3,2,1,0:T(8,128)(2,1)} %param.16) | copy-start | bytes 11796484
  113.2 85.6 %all-gather.13.cloned.1.call-start = ((), (), s32[]{:S(2)}) async-start(), calls=%async_computation.7 | async-start | bytes 1638400 | tf_op jit(solution)/shard_map/all_gather | solution.py:54
  115.5 63.9 %collective-permute-start = (bf16[2,128,5120]{2,1,0:T(8,128)(2,1)}, bf16[2,128,5120]{2,1,0:T(8,128)(2,1)}, u32[]{:S(2)}, u32[]{:S(2)}) collective-permute-start(bf16[2,128,5120]{2,1,0:T(8,128)(2,1)} %all-gather.7.cloned.1.call-done), channel_id=1, source_target_pairs={{0,25},{1,24},{8,17},{9,16},{16,9},{17,8},{24,1},{25,0},{2,27},{3,... | collective-permute-start | bytes 7864328 | tf_op jit(solution)/shard_map/ppermute | solution.py:20
  166.6 89.7 %all-gather.9.cloned.1.call-start = ((), (), s32[]{:S(2)}) async-start(), calls=%async_computation.4 | async-start | bytes 3276800 | tf_op jit(solution)/shard_map/all_gather | solution.py:54
  169.3 8.4 %copy-start.15 = (bf16[32,5120]{1,0:T(8,128)(2,1)}, bf16[32,5120]{1,0:T(8,128)(2,1)S(1)}, u32[]{:S(2)}) copy-start(bf16[32,5120]{1,0:T(8,128)(2,1)S(1)} %fusion.108) | copy-start | bytes 983044
  169.4 12.6 %collective-permute-start.1 = (bf16[32,5120]{1,0:T(8,128)(2,1)S(1)}, bf16[32,5120]{1,0:T(8,128)(2,1)S(1)}, u32[]{:S(2)}, u32[]{:S(2)}) collective-permute-start(bf16[32,5120]{1,0:T(8,128)(2,1)S(1)} %fusion.108), channel_id=1, source_target_pairs={{1,9},{8,0},{9,17},{16,8},{17,25},{24,16},{3,11},{10,2},{11,19},{1... | collective-permute-start | bytes 983048 | tf_op jit(solution)/shard_map/ppermute | solution.py:232
  172.4 10.3 %collective-permute-start.2 = (bf16[32,5120]{1,0:T(8,128)(2,1)S(1)}, bf16[32,5120]{1,0:T(8,128)(2,1)}, u32[]{:S(2)}, u32[]{:S(2)}) collective-permute-start(bf16[32,5120]{1,0:T(8,128)(2,1)S(1)} %fusion.120), channel_id=1, source_target_pairs={{0,8},{8,16},{9,1},{16,24},{17,9},{25,17},{2,10},{10,18},{11,3},{1... | collective-permute-start | bytes 983048 | tf_op jit(solution)/shard_map/ppermute | solution.py:233
  202.3 122.0 %reduce-scatter.5.cloned.1.call-start = ((), (), s32[]{:S(2)}) async-start(), calls=%async_computation.5 | async-start | bytes 3276800 | tf_op jit(solution)/shard_map/reduce_scatter | solution.py:59
  202.6 67.0 %collective-permute-start.3 = (bf16[1,128,5120]{2,1,0:T(8,128)(2,1)}, bf16[1,128,5120]{2,1,0:T(8,128)(2,1)}, u32[]{:S(2)}, u32[]{:S(2)}) collective-permute-start(bf16[1,128,5120]{2,1,0:T(8,128)(2,1)} %bitcast.381), channel_id=1, source_target_pairs={{0,25},{1,24},{8,17},{9,16},{16,9},{17,8},{24,1},{25,0},{2,27},{3,... | collective-permute-start | bytes 3932168 | tf_op jit(solution)/shard_map/ppermute | solution.py:20
  203.7 65.8 %collective-permute-start.4 = (bf16[4,128,128]{2,1,0:T(8,128)(2,1)}, bf16[4,128,128]{2,1,0:T(8,128)(2,1)}, u32[]{:S(2)}, u32[]{:S(2)}) collective-permute-start(bf16[4,128,128]{2,1,0:T(8,128)(2,1)} %pad_maximum_fusion.4), channel_id=1, source_target_pairs={{0,25},{1,24},{8,17},{9,16},{16,9},{17,8},{24,1},{25,0},{2,27},{3,... | collective-permute-start | bytes 393224 | tf_op jit(solution)/shard_map/ppermute | solution.py:20
  208.6 52.9 %copy-start.19 = (bf16[3,128,128]{2,1,0:T(8,128)(2,1)}, bf16[3,128,128]{2,1,0:T(8,128)(2,1)S(1)}, u32[]{:S(2)}) copy-start(bf16[3,128,128]{2,1,0:T(8,128)(2,1)S(1)} %fusion.60) | copy-start | bytes 294916
  258.4 6.1 %copy-start.3 = (bf16[1,1,3,5120,128]{4,3,2,1,0:T(8,128)(2,1)S(1)}, bf16[1,1,3,5120,128]{4,3,2,1,0:T(8,128)(2,1)}, u32[]{:S(2)}) copy-start(bf16[1,1,3,5120,128]{4,3,2,1,0:T(8,128)(2,1)} %param.16) | copy-start | bytes 11796484
  277.8 9.0 %collective-permute-start.5 = (bf16[4,128,128]{2,1,0:T(8,128)(2,1)S(1)}, bf16[4,128,128]{2,1,0:T(8,128)(2,1)S(1)}, u32[]{:S(2)}, u32[]{:S(2)}) collective-permute-start(bf16[4,128,128]{2,1,0:T(8,128)(2,1)S(1)} %pad_maximum_fusion.5), channel_id=1, source_target_pairs={{0,25},{1,24},{8,17},{9,16},{16,9},{17,8},{24,1},{25,0},{2,27},{3,... | collective-permute-start | bytes 393224 | tf_op jit(solution)/shard_map/ppermute | solution.py:20
  280.7 31.3 %collective-permute-start.6 = (bf16[128,5120]{1,0:T(8,128)(2,1)}, bf16[128,5120]{1,0:T(8,128)(2,1)}, u32[]{:S(2)}, u32[]{:S(2)}) collective-permute-start(bf16[128,5120]{1,0:T(8,128)(2,1)} %slice_bitcast_fusion.2), channel_id=1, source_target_pairs={{0,25},{1,24},{8,17},{9,16},{16,9},{17,8},{24,1},{25,0},{2,27},{3,... | collective-permute-start | bytes 3932168 | tf_op jit(solution)/shard_map/ppermute | solution.py:20
  315.7 11.6 %copy-start.16 = (bf16[32,5120]{1,0:T(8,128)(2,1)S(1)}, bf16[32,5120]{1,0:T(8,128)(2,1)}, u32[]{:S(2)}) copy-start(bf16[32,5120]{1,0:T(8,128)(2,1)} %copy-done.15) | copy-start | bytes 983044
  315.7 12.5 %copy-start.14 = (bf16[32,5120]{1,0:T(8,128)(2,1)S(1)}, bf16[32,5120]{1,0:T(8,128)(2,1)}, u32[]{:S(2)}) copy-start(bf16[32,5120]{1,0:T(8,128)(2,1)} %copy-done.13) | copy-start | bytes 983044
  (20 other events, 40.2 us)
Sparse Core Ops, SparseCore 0:
  12.1 57.3 all-gather.6
  71.7 31.3 all-gather.10
  113.4 51.4 reduce-scatter.2
  166.7 32.0 all-gather.12
  202.5 53.7 all-gather.8
  273.2 51.0 reduce-scatter.4

commit v11 on v10

--- a/solution.py
+++ b/solution.py
@@ -167,7 +167,7 @@
         return flipped(value, pair_axes, (1 << bit_count) - 1)
 
     last_step = window_steps - 1
-    saved_normed = [normed_rows(saved[0, 0, t]) for t in range(window_steps)]
+    saved_rows = [saved[0, 0, t] for t in range(window_steps)]
     backward_normed_full = [None] * window_steps
     upstream_fulls = []
     d_projecteds = []
@@ -188,7 +188,8 @@
         current = jnp.where(position == 0, embedded, forward_in)
         upstream = jnp.where(position == sections - 1, cotangent[0, step_index], backward_in)
         if step_index == 0:
-            upstream_full, backward_normed_full[0] = gathered([upstream, saved_normed[0]])
+            upstream_full, saved_full = gathered([upstream, saved_rows[0]])
+            backward_normed_full[0] = normed_rows(saved_full)
             first_sent = to_partner(jnp.stack([upstream_full, backward_normed_full[0]]))
             forward_normed, upstream_full = lax.optimization_barrier(
                 (normed_rows(current), upstream_full)
@@ -218,8 +219,8 @@
         tie_scatter = {}
         d_normed, attn_rows = scattered([d_normed_part, attn_part])
         if step_index == 0 and window_steps > 1:
-            later_rows, d_normed = lax.optimization_barrier((saved_normed[1:], d_normed))
-            later = gathered(later_rows)
+            later_rows, d_normed = lax.optimization_barrier((saved_rows[1:], d_normed))
+            later = [normed_rows(rows) for rows in gathered(later_rows)]
             backward_normed_full[1:] = later
             deferred["later"] = jnp.stack(later)
         backward_out = input_grad(saved[0, 0, step_index], upstream, d_normed)

time: 337 us -> 340 us (level)
  other arithmetic: 26.5 us -> 35 us
  matrix products: 52.5 us -> 47.6 us
    reduce_sum x2 -> x5, other arithmetic: 2.63 us -> 6.29 us  [normalize(): mean_square = jnp.mean(values * values, axis=-1, keepdims=True)]
    unnamed x63 -> x53, local copies, waits for them, and re-layouts: 11.7 us -> 10.7 us
  transfers between devices with their start and end apart: 13 -> 13, of which waited for: 8 -> 7; matrix products, arithmetic and copies ran while one was open for 19% -> 21% of each run, Pallas kernels for 0% -> 0%
where the time goes in v11:
time: 340 us; the launch traced here: 339 us
  waiting for transfers between devices  209 us (61%)
  matrix products  47.6 us (14%)
  other arithmetic  35 us (10%)
  local copies, waits for them, and re-layouts  19.3 us (6%)
  between operations  14.5 us (4%)
  starting transfers between devices  13.5 us (4%)
    all_gather x4, waiting for transfers between devices, gathered(): full = lax.all_gather(jnp.stack(blocks), 'tp', axis=1, tiled=True)  145 us
    reduce_scatter x2, waiting for transfers between devices, scattered(): lax.psum_scatter(jnp.stack(blocks), 'tp', scatter_dimension=1, tiled=True)  53.5 us
    unnamed x53, local copies, waits for them, and re-layouts  10.7 us
    dot_general x4, matrix products, heads_of(): jnp.einsum('sd,cdn->csn', normed_full, qkv_weight, preferred_element_type...  10.7 us
    ppermute x5, waiting for transfers between devices, flipped(): lax.ppermute(value, axis, [(i, i ^ mask) for i in range(lax.axis_size(axi...  10.2 us
    dot_general x4, matrix products, weight_terms(): jnp.einsum('sn,sd->nd', mixed, upstream_full, preferred_element_type=jnp....  9.69 us
    dot_general x4, matrix products, weight_terms(): jnp.einsum('sd,csn->cdn', normed_full, d_projected, preferred_element_typ...  9.41 us
    another operation x2, other arithmetic, scattered(): jnp.stack(blocks)  6.92 us
  transfers between devices with their start and end apart: 13, of which 7 were waited for; matrix products, arithmetic and copies ran while one was open for 21% of the time, Pallas kernels for 0%

profile of v11, /device:TPU:0, one launch (start us, length us, event | category | flops | bytes accessed | tf_op | source)
XLA Modules:
  0.0 338.5 jit_solution(16584975055099540035)
XLA Ops:
  14.3 54.5 %all-gather.7.cloned.1.call-done = bf16[2,128,5120]{2,1,0:T(8,128)(2,1)} async-done(((bf16[2,32,5120]{2,1,0:T(8,128)(2,1)}), bf16[2,128,5120]{2,1,0:T(8,128)(2,1)}) %all-gather.7.cloned.1.call-update) | async-done | bytes 2621456 | tf_op jit(solution)/shard_map/all_gather | solution.py:54
  68.8 3.2 fusion.159
  78.8 2.4 fusion.7
  81.3 22.2 %all-gather.11.cloned.1.call-done = bf16[128,5120]{1,0:T(8,128)(2,1)} async-done(((bf16[32,5120]{1,0:T(8,128)(2,1)}), bf16[128,5120]{1,0:T(8,128)(2,1)}) %all-gather.11.cloned.1.call-update) | async-done | bytes 1310736 | tf_op jit(solution)/shard_map/all_gather | solution.py:54
  103.5 3.4 fusion.75
  108.3 2.6 convolution_convert_fusion.1
  110.9 3.4 %pad_maximum_fusion = bf16[2,128,5120]{2,1,0:T(8,128)(2,1)} fusion(bf16[1,128,5120]{2,1,0:T(8,128)(2,1)} %bitcast.368, bf16[1,128,5120]{2,1,0:T(8,128)(2,1)} %bitcast.369), kind=kLoop, calls=%fused_computation.45 | loop fusion | flops 1310720 | bytes 5242880 | tf_op jit(solution)/shard_map/stack | solution.py:59
  116.7 3.1 pad_maximum_fusion.1
  122.2 43.7 %reduce-scatter.3.cloned.1.call-done = bf16[2,32,5120]{2,1,0:T(8,128)(2,1)} async-done(((bf16[2,128,5120]{2,1,0:T(8,128)(2,1)}), bf16[2,32,5120]{2,1,0:T(8,128)(2,1)}) %reduce-scatter.3.cloned.1.call-update) | async-done | bytes 655376 | tf_op jit(solution)/shard_map/reduce_scatter | solution.py:59
  174.4 5.4 %collective-permute-start.2 = (bf16[32,5120]{1,0:T(8,128)(2,1)}, bf16[32,5120]{1,0:T(8,128)(2,1)}, u32[]{:S(2)}, u32[]{:S(2)}) collective-permute-start(bf16[32,5120]{1,0:T(8,128)(2,1)} %fusion.124), channel_id=1, source_target_pairs={{0,8},{8,16},{9,1},{16,24},{17,9},{25,17},{2,10},{10,18},{11,3},{1... | collective-permute-start | bytes 983048 | tf_op jit(solution)/shard_map/ppermute | solution.py:234
  179.8 20.1 %all-gather.13.cloned.1.call-done = bf16[128,5120]{1,0:T(8,128)(2,1)} async-done(((bf16[32,5120]{1,0:T(8,128)(2,1)}), bf16[128,5120]{1,0:T(8,128)(2,1)}) %all-gather.13.cloned.1.call-update) | async-done | bytes 1310736 | tf_op jit(solution)/shard_map/all_gather | solution.py:54
  201.6 2.8 fusion.29
  209.8 3.4 fusion.70
  213.4 48.0 %all-gather.9.cloned.1.call-done = bf16[2,128,5120]{2,1,0:T(8,128)(2,1)} async-done(((bf16[2,32,5120]{2,1,0:T(8,128)(2,1)}), bf16[2,128,5120]{2,1,0:T(8,128)(2,1)}) %all-gather.9.cloned.1.call-update) | async-done | bytes 2621456 | tf_op jit(solution)/shard_map/all_gather | solution.py:54
  263.6 3.1 fusion.67
  267.5 2.4 fusion.8
  271.7 3.5 %pad_maximum_fusion.2 = bf16[2,128,5120]{2,1,0:T(8,128)(2,1)} fusion(bf16[1,128,5120]{2,1,0:T(8,128)(2,1)} %bitcast.367, bf16[1,128,5120]{2,1,0:T(8,128)(2,1)} %bitcast.370), kind=kLoop, calls=%fused_computation.47 | loop fusion | flops 1310720 | bytes 5242880 | tf_op jit(solution)/shard_map/stack | solution.py:59
  285.9 3.3 fusion.30
  289.3 2.5 fusion.32
  291.8 4.4 %fusion = bf16[1,1,3,5120,128]{3,4,2,1,0:T(8,128)(2,1)} fusion(f32[3,128,5120]{2,1,0:T(8,128)S(1)} %fusion.32, bf16[4,128,128]{2,1,0:T(8,128)(2,1)S(1)} %collective-permute-done.4, bf16[3,128,5120]{2,1,0:T(8,128)(2,1)S(1)} %add_convert_fusion.2, bf16[2,128,5120]{2,1,0:T(8,128)(2,1)} %collective-permute-done), kind=kOutput, calls=%fused_computation.3 | convolution fusion | flops 515112960 | bytes 17170432 | tf_op jit(solution)/shard_map/sd,csn->cdn/dot_general | solution.py:127
  296.2 6.4 %copy.23 = bf16[1,1,3,5120,128]{4,3,2,1,0:T(8,128)(2,1)} copy(bf16[1,1,3,5120,128]{3,4,2,1,0:T(8,128)(2,1)} %fusion) | data formatting | bytes 7864320
  302.7 10.2 %collective-permute-done.6 = bf16[128,5120]{1,0:T(8,128)(2,1)} collective-permute-done((bf16[128,5120]{1,0:T(8,128)(2,1)}, bf16[128,5120]{1,0:T(8,128)(2,1)}, u32[]{:S(2)}, u32[]{:S(2)}) %collective-permute-start.6) | collective-permute-done | bytes 1310752 | tf_op jit(solution)/shard_map/ppermute | solution.py:20
  312.9 3.7 %fusion.9 = bf16[1,1,128,5120]{3,2,1,0:T(8,128)(2,1)} fusion(f32[128,5120]{1,0:T(8,128)S(1)} %copy-done.7, f32[128,5120]{1,0:T(8,128)} %fusion.30, bf16[128,5120]{1,0:T(8,128)(2,1)} %collective-permute-done.6, bf16[4,128,128]{2,1,0:T(8,128)(2,1)S(1)} %collective-permute-done.5), kind=kOutput, calls=%fused_computation.18 | convolution fusion | flops 171048960 | bytes 7897088 | tf_op jit(solution)/shard_map/sn,sd->nd/dot_general | solution.py:130
  316.6 9.8 %reduce-scatter.5.cloned.1.call-done = bf16[2,32,5120]{2,1,0:T(8,128)(2,1)} async-done(((bf16[2,128,5120]{2,1,0:T(8,128)(2,1)}), bf16[2,32,5120]{2,1,0:T(8,128)(2,1)}) %reduce-scatter.5.cloned.1.call-update) | async-done | bytes 655376 | tf_op jit(solution)/shard_map/reduce_scatter | solution.py:59
  (143 shorter events, 56.4 us)
Async XLA Ops:
  7.2 69.5 %copy-start = (bf16[1,1,128,5120]{3,2,1,0:T(8,128)(2,1)S(1)}, bf16[1,1,128,5120]{3,2,1,0:T(8,128)(2,1)}, u32[]{:S(2)}) copy-start(bf16[1,1,128,5120]{3,2,1,0:T(8,128)(2,1)} %param.17) | copy-start | bytes 3932164
  7.2 4.2 %copy-start.23 = (s32[1,2,5,128]{3,1,2,0:T(2,128)S(1)}, s32[1,2,5,128]{3,1,2,0:T(2,128)}, u32[]{:S(2)}) copy-start(s32[1,2,5,128]{3,1,2,0:T(2,128)} %param.13) | copy-start | bytes 15364
  7.2 4.7 %copy-start.24 = (s32[1,2,32]{2,1,0:T(2,128)S(1)}, s32[1,2,32]{2,1,0:T(2,128)}, u32[]{:S(2)}) copy-start(s32[1,2,32]{2,1,0:T(2,128)} %param.12) | copy-start | bytes 772
  7.2 4.7 %copy-start.10 = (bf16[64,5120]{1,0:T(8,128)(2,1)S(1)}, bf16[64,5120]{1,0:T(8,128)(2,1)}, u32[]{:S(2)}) copy-start(bf16[64,5120]{1,0:T(8,128)(2,1)} %param.14) | copy-start | bytes 1966084
  7.2 61.6 %all-gather.7.cloned.1.call-start = ((), (), s32[]{:S(2)}) async-start(), calls=%async_computation.2 | async-start | bytes 3276800 | tf_op jit(solution)/shard_map/all_gather | solution.py:54
  9.3 4.2 %copy-start.14 = (f32[1,1,5120]{2,1,0:T(1,128)S(1)}, f32[1,1,5120]{2,1,0:T(1,128)}, u32[]{:S(2)}) copy-start(f32[1,1,5120]{2,1,0:T(1,128)} %param.15) | copy-start | bytes 61444
  11.3 92.2 %all-gather.11.cloned.1.call-start = ((), (), s32[]{:S(2)}) async-start(), calls=%async_computation.6 | async-start | bytes 1638400 | tf_op jit(solution)/shard_map/all_gather | solution.py:54
  72.0 93.9 %reduce-scatter.3.cloned.1.call-start = ((), (), s32[]{:S(2)}) async-start(), calls=%async_computation.3 | async-start | bytes 3276800 | tf_op jit(solution)/shard_map/reduce_scatter | solution.py:59
  81.3 26.2 %copy-start.25 = (s32[128]{0:T(128)S(1)}, s32[128]{0:T(128)}, u32[]{:S(2)}) copy-start(s32[128]{0:T(128)} %get-tuple-element.53) | copy-start | bytes 1540
  114.4 85.5 %all-gather.13.cloned.1.call-start = ((), (), s32[]{:S(2)}) async-start(), calls=%async_computation.7 | async-start | bytes 1638400 | tf_op jit(solution)/shard_map/all_gather | solution.py:54
  119.7 84.6 %collective-permute-start = (bf16[2,128,5120]{2,1,0:T(8,128)(2,1)}, bf16[2,128,5120]{2,1,0:T(8,128)(2,1)}, u32[]{:S(2)}, u32[]{:S(2)}) collective-permute-start(bf16[2,128,5120]{2,1,0:T(8,128)(2,1)} %pad_maximum_fusion.1), channel_id=1, source_target_pairs={{0,25},{1,24},{8,17},{9,16},{16,9},{17,8},{24,1},{25,0},{2,27},{3,... | collective-permute-start | bytes 7864328 | tf_op jit(solution)/shard_map/ppermute | solution.py:20
  167.7 93.7 %all-gather.9.cloned.1.call-start = ((), (), s32[]{:S(2)}) async-start(), calls=%async_computation.4 | async-start | bytes 3276800 | tf_op jit(solution)/shard_map/all_gather | solution.py:54
  171.3 33.0 %collective-permute-start.1 = (bf16[32,5120]{1,0:T(8,128)(2,1)}, bf16[32,5120]{1,0:T(8,128)(2,1)}, u32[]{:S(2)}, u32[]{:S(2)}) collective-permute-start(bf16[32,5120]{1,0:T(8,128)(2,1)} %fusion.112), channel_id=1, source_target_pairs={{1,9},{8,0},{9,17},{16,8},{17,25},{24,16},{3,11},{10,2},{11,19},{1... | collective-permute-start | bytes 983048 | tf_op jit(solution)/shard_map/ppermute | solution.py:233
  174.4 30.3 %copy-start.13 = (bf16[1,2,32,5120]{3,2,1,0:T(8,128)(2,1)S(1)}, bf16[1,2,32,5120]{3,2,1,0:T(8,128)(2,1)}, u32[]{:S(2)}) copy-start(bf16[1,2,32,5120]{3,2,1,0:T(8,128)(2,1)} %param.21) | copy-start | bytes 1966084
  174.4 30.0 %collective-permute-start.2 = (bf16[32,5120]{1,0:T(8,128)(2,1)}, bf16[32,5120]{1,0:T(8,128)(2,1)}, u32[]{:S(2)}, u32[]{:S(2)}) collective-permute-start(bf16[32,5120]{1,0:T(8,128)(2,1)} %fusion.124), channel_id=1, source_target_pairs={{0,8},{8,16},{9,1},{16,24},{17,9},{25,17},{2,10},{10,18},{11,3},{1... | collective-permute-start | bytes 983048 | tf_op jit(solution)/shard_map/ppermute | solution.py:234
  199.9 4.5 %copy-start.15 = (bf16[32,5120]{1,0:T(8,128)(2,1)S(1)}, bf16[32,5120]{1,0:T(8,128)(2,1)}, u32[]{:S(2)}) copy-start(bf16[32,5120]{1,0:T(8,128)(2,1)} %fusion.11) | copy-start | bytes 983044
  206.9 119.5 %reduce-scatter.5.cloned.1.call-start = ((), (), s32[]{:S(2)}) async-start(), calls=%async_computation.5 | async-start | bytes 3276800 | tf_op jit(solution)/shard_map/reduce_scatter | solution.py:59
  207.1 64.6 %collective-permute-start.3 = (bf16[1,128,5120]{2,1,0:T(8,128)(2,1)}, bf16[1,128,5120]{2,1,0:T(8,128)(2,1)}, u32[]{:S(2)}, u32[]{:S(2)}) collective-permute-start(bf16[1,128,5120]{2,1,0:T(8,128)(2,1)} %fusion.29), channel_id=1, source_target_pairs={{0,25},{1,24},{8,17},{9,16},{16,9},{17,8},{24,1},{25,0},{2,27},{3,... | collective-permute-start | bytes 3932168 | tf_op jit(solution)/shard_map/ppermute | solution.py:20
  208.3 63.4 %collective-permute-start.4 = (bf16[4,128,128]{2,1,0:T(8,128)(2,1)}, bf16[4,128,128]{2,1,0:T(8,128)(2,1)S(1)}, u32[]{:S(2)}, u32[]{:S(2)}) collective-permute-start(bf16[4,128,128]{2,1,0:T(8,128)(2,1)} %pad_maximum_fusion.5), channel_id=1, source_target_pairs={{0,25},{1,24},{8,17},{9,16},{16,9},{17,8},{24,1},{25,0},{2,27},{3,... | collective-permute-start | bytes 393224 | tf_op jit(solution)/shard_map/ppermute | solution.py:20
  278.7 10.5 %collective-permute-start.5 = (bf16[4,128,128]{2,1,0:T(8,128)(2,1)S(1)}, bf16[4,128,128]{2,1,0:T(8,128)(2,1)S(1)}, u32[]{:S(2)}, u32[]{:S(2)}) collective-permute-start(bf16[4,128,128]{2,1,0:T(8,128)(2,1)S(1)} %pad_maximum_fusion.6), channel_id=1, source_target_pairs={{0,25},{1,24},{8,17},{9,16},{16,9},{17,8},{24,1},{25,0},{2,27},{3,... | collective-permute-start | bytes 393224 | tf_op jit(solution)/shard_map/ppermute | solution.py:20
  281.6 31.3 %collective-permute-start.6 = (bf16[128,5120]{1,0:T(8,128)(2,1)}, bf16[128,5120]{1,0:T(8,128)(2,1)}, u32[]{:S(2)}, u32[]{:S(2)}) collective-permute-start(bf16[128,5120]{1,0:T(8,128)(2,1)} %slice_bitcast_fusion.2), channel_id=1, source_target_pairs={{0,25},{1,24},{8,17},{9,16},{16,9},{17,8},{24,1},{25,0},{2,27},{3,... | collective-permute-start | bytes 3932168 | tf_op jit(solution)/shard_map/ppermute | solution.py:20
  296.2 16.6 %copy-start.7 = (f32[128,5120]{1,0:T(8,128)S(1)}, f32[128,5120]{1,0:T(8,128)}, u32[]{:S(2)}) copy-start(f32[128,5120]{1,0:T(8,128)} %fusion.6) | copy-start | bytes 7864324
  302.7 23.7 %copy-start.8 = (bf16[1,1,2,32,5120]{4,3,2,1,0:T(8,128)(2,1)S(1)}, bf16[1,1,2,32,5120]{4,3,2,1,0:T(8,128)(2,1)}, u32[]{:S(2)}) copy-start(bf16[1,1,2,32,5120]{4,3,2,1,0:T(8,128)(2,1)} %param.20) | copy-start | bytes 1966084
  327.6 4.1 %copy-start.1 = (bf16[1,1,128,5120]{3,2,1,0:T(8,128)(2,1)S(1)}, bf16[1,1,128,5120]{3,2,1,0:T(8,128)(2,1)}, u32[]{:S(2)}) copy-start(bf16[1,1,128,5120]{3,2,1,0:T(8,128)(2,1)} %param.17) | copy-start | bytes 3932164
  (15 other events, 28.4 us)
Sparse Core Ops, SparseCore 0:
  11.4 57.3 all-gather.6
  72.1 31.2 all-gather.10
  114.5 51.3 reduce-scatter.2
  167.8 32.0 all-gather.12
  207.0 54.3 all-gather.8
  275.3 51.0 reduce-scatter.4

commit v12 on v10

--- a/solution.py
+++ b/solution.py
@@ -95,7 +95,7 @@
             .reshape(seq_len, inner_here)
             .astype(jnp.bfloat16)
         )
-        return jnp.dot(mixed, out_weight, preferred_element_type=jnp.float32).astype(jnp.bfloat16)
+        return mixed
 
     def backward_part(normed_full, upstream_full, seg_mask):
         heads_view = heads_of(normed_full)
@@ -113,10 +113,25 @@
         ).astype(jnp.bfloat16)
         pulled = pull_attend(d_mixed.astype(jnp.float32).reshape(seq_len, heads_here, HD))
         d_projected = jnp.stack(pulled).reshape(3, seq_len, inner_here)
-        d_normed_part = jnp.einsum(
-            "csn,cdn->sd", d_projected, qkv_weight, preferred_element_type=jnp.float32
+        return d_projected, mixed
+
+    qkv_rows = jnp.transpose(qkv_weight, (0, 2, 1)).reshape(3 * inner_here, model_width)
+    block_weight = jnp.concatenate(
+        [
+            jnp.stack([qkv_rows, jnp.zeros_like(qkv_rows)], axis=1),
+            jnp.stack([jnp.zeros_like(out_weight), out_weight], axis=1),
+        ],
+        axis=0,
+    )
+
+    def projected_back(d_projected, forward_mixed):
+        lhs = jnp.concatenate(
+            [jnp.transpose(d_projected, (1, 0, 2)).reshape(seq_len, 3 * inner_here), forward_mixed],
+            axis=1,
+        )
+        return jnp.einsum(
+            "sk,ktd->tsd", lhs, block_weight, preferred_element_type=jnp.float32
         ).astype(jnp.bfloat16)
-        return d_normed_part, d_projected, mixed
 
     def weight_terms(normed_fulls, d_projecteds, mixeds, upstream_fulls):
         qkv_sum = None
@@ -197,7 +212,7 @@
         else:
             upstream_full, forward_normed_full = gathered([upstream, normed_rows(current)])
             inbox[f"rows{step_index}"] = to_partner(upstream_full)
-        d_normed_part, d_projected, mixed = backward_part(
+        d_projected, mixed = backward_part(
             backward_normed_full[step_index], upstream_full, mask_for(1, step_index + position)
         )
         upstream_fulls.append(upstream_full)
@@ -208,15 +223,16 @@
             deferred[f"small{step_index}"] = small
         else:
             inbox[f"small{step_index}"] = to_partner(small)
-        attn_part = forward_part(
+        forward_mixed = forward_part(
             forward_normed_full, mask_for(0, step_index - position + sections - 1)
         )
-        (d_normed_part, attn_part), tie_scatter = lax.optimization_barrier(
-            ((d_normed_part, attn_part), tie_scatter)
+        both_parts, tie_scatter = lax.optimization_barrier(
+            (projected_back(d_projected, forward_mixed), tie_scatter)
         )
         inbox.update(tie_scatter)
         tie_scatter = {}
-        d_normed, attn_rows = scattered([d_normed_part, attn_part])
+        both_rows = lax.psum_scatter(both_parts, "tp", scatter_dimension=1, tiled=True)
+        d_normed, attn_rows = both_rows[0], both_rows[1]
         if step_index == 0 and window_steps > 1:
             later_rows, d_normed = lax.optimization_barrier((saved_normed[1:], d_normed))
             later = gathered(later_rows)

time: 337 us -> 334 us (level)
  local copies, waits for them, and re-layouts: 16.5 us -> 31.6 us
  waiting for transfers between devices: 212 us -> 202 us
  other arithmetic: 26.5 us -> 18.1 us
    all_gather x4, waiting for transfers between devices: 142 us -> 127 us  [gathered(): full = lax.all_gather(jnp.stack(blocks), 'tp', axis=1, tiled=True)]
    another operation x2 -> x0, other arithmetic: 6.94 us -> none  [scattered(): jnp.stack(blocks)]
    unnamed x63 -> x67, local copies, waits for them, and re-layouts: 11.7 us -> 18.1 us
    another operation x0 -> x1, local copies, waits for them, and re-layouts: none -> 6.43 us  [shards(): jnp.stack([qkv_rows, jnp.zeros_like(qkv_rows)], axis=1)]
    dot_general x4 -> x2, matrix products: 9.97 us -> 11.9 us  [projected_back(): jnp.einsum('sk,ktd->tsd', lhs, block_weight, preferred_element_type=jnp.f...]
  transfers between devices with their start and end apart: 13 -> 13, of which waited for: 8 -> 9; matrix products, arithmetic and copies ran while one was open for 19% -> 22% of each run, Pallas kernels for 0% -> 0%
where the time goes in v12:
time: 334 us; the launch traced here: 332 us
  waiting for transfers between devices  202 us (60%)
  matrix products  53 us (16%)
  local copies, waits for them, and re-layouts  31.6 us (9%)
  other arithmetic  18.1 us (5%)
  between operations  14.6 us (4%)
  starting transfers between devices  12.9 us (4%)
    all_gather x4, waiting for transfers between devices, gathered(): full = lax.all_gather(jnp.stack(blocks), 'tp', axis=1, tiled=True)  127 us
    reduce_scatter x2, waiting for transfers between devices, shards(): lax.psum_scatter(both_parts, 'tp', scatter_dimension=1, tiled=True)  57.4 us
    unnamed x67, local copies, waits for them, and re-layouts  18.1 us
    dot_general x4, matrix products, heads_of(): jnp.einsum('sd,cdn->csn', normed_full, qkv_weight, preferred_element_type...  13.3 us
    ppermute x5, waiting for transfers between devices, flipped(): lax.ppermute(value, axis, [(i, i ^ mask) for i in range(lax.axis_size(axi...  12.2 us
    dot_general x2, matrix products, projected_back(): jnp.einsum('sk,ktd->tsd', lhs, block_weight, preferred_element_type=jnp.f...  11.9 us
    dot_general x4, matrix products, weight_terms(): jnp.einsum('sd,csn->cdn', normed_full, d_projected, preferred_element_typ...  9.32 us
    dot_general x4, matrix products, weight_terms(): jnp.einsum('sn,sd->nd', mixed, upstream_full, preferred_element_type=jnp....  8.08 us
  transfers between devices with their start and end apart: 13, of which 9 were waited for; matrix products, arithmetic and copies ran while one was open for 22% of the time, Pallas kernels for 0%

profile of v12, /device:TPU:0, one launch (start us, length us, event | category | flops | bytes accessed | tf_op | source)
XLA Modules:
  0.0 332.4 jit_solution(13303910460964671106)
XLA Ops:
  11.9 6.3 %copy.24 = bf16[1,1,3,5120,128]{3,4,2,1,0:T(8,128)(2,1)} copy(bf16[1,1,3,5120,128]{4,3,2,1,0:T(8,128)(2,1)} %param.16) | data formatting | bytes 7864320 | tf_op args[5]
  18.1 6.4 %copy.25 = bf16[384,1,5120]{0,2,1:T(8,128)(2,1)} copy(bf16[384,1,5120]{2,0,1:T(8,128)(2,1)} %bitcast.380) | data formatting | bytes 7864320 | tf_op jit(solution)/shard_map/stack;reshape | solution.py:121
  29.7 39.6 %all-gather.7.cloned.1.call-done = bf16[2,128,5120]{2,1,0:T(8,128)(2,1)} async-done(((bf16[2,32,5120]{2,1,0:T(8,128)(2,1)}), bf16[2,128,5120]{2,1,0:T(8,128)(2,1)}) %all-gather.7.cloned.1.call-update) | async-done | bytes 2621456 | tf_op jit(solution)/shard_map/all_gather | solution.py:54
  70.8 3.5 %fusion.68 = bf16[3,128,128]{2,1,0:T(8,128)(2,1)S(1)} fusion(bf16[1,1,3,5120,128]{4,3,2,1,0:T(8,128)(2,1)} %param.16, bf16[2,128,5120]{2,1,0:T(8,128)(2,1)} %all-gather.7.cloned.1.call-done), kind=kOutput, calls=%fused_computation.65 | convolution fusion | flops 503365632 | bytes 5341184 | tf_op jit(solution)/shard_map/sd,cdn->csn/dot_general | solution.py:86
  78.0 24.8 %all-gather.11.cloned.1.call-done = bf16[128,5120]{1,0:T(8,128)(2,1)} async-done(((bf16[32,5120]{1,0:T(8,128)(2,1)}), bf16[128,5120]{1,0:T(8,128)(2,1)}) %all-gather.11.cloned.1.call-update) | async-done | bytes 1310736 | tf_op jit(solution)/shard_map/all_gather | solution.py:54
  102.8 3.4 %fusion.63 = bf16[3,128,128]{2,1,0:T(8,128)(2,1)S(1)} fusion(bf16[1,1,3,5120,128]{4,3,2,1,0:T(8,128)(2,1)} %param.16, bf16[128,5120]{1,0:T(8,128)(2,1)} %all-gather.11.cloned.1.call-done), kind=kOutput, calls=%fused_computation.64 | convolution fusion | flops 503365632 | bytes 5341184 | tf_op jit(solution)/shard_map/sd,cdn->csn/dot_general | solution.py:86
  108.7 6.1 %fusion.4 = bf16[2,128,5120]{2,1,0:T(8,128)(2,1)} fusion(bf16[128,1,5120]{0,2,1:T(8,128)(2,1)} %bitcast.383, bf16[384,1,5120]{0,2,1:T(8,128)(2,1)} %copy.25, bf16[128,128]{1,0:T(8,128)(2,1)} %copy.30, bf16[128,384]{1,0:T(8,128)(2,1)S(1)} %copy-done.26), kind=kOutput, calls=%fused_computation.11 | convolution fusion | flops 1385693184 | bytes 7995392 | tf_op jit(solution)/shard_map/sk,ktd->tsd/dot_general | solution.py:132
  115.3 2.0 fusion.14
  118.4 47.9 %reduce-scatter.3.cloned.1.call-done = bf16[2,32,5120]{2,1,0:T(8,128)(2,1)} async-done(((bf16[2,128,5120]{2,1,0:T(8,128)(2,1)}), bf16[2,32,5120]{2,1,0:T(8,128)(2,1)}) %reduce-scatter.3.cloned.1.call-update) | async-done | bytes 655376 | tf_op jit(solution)/shard_map/reduce_scatter | solution.py:234
  171.4 4.6 %collective-permute-start.2 = (bf16[32,5120]{1,0:T(8,128)(2,1)S(1)}, bf16[32,5120]{1,0:T(8,128)(2,1)S(1)}, u32[]{:S(2)}, u32[]{:S(2)}) collective-permute-start(bf16[32,5120]{1,0:T(8,128)(2,1)S(1)} %fusion.121), channel_id=1, source_target_pairs={{0,8},{8,16},{9,1},{16,24},{17,9},{25,17},{2,10},{10,18},{11,3},{1... | collective-permute-start | bytes 983048 | tf_op jit(solution)/shard_map/ppermute | solution.py:249
  177.7 5.5 %collective-permute-done.1 = bf16[32,5120]{1,0:T(8,128)(2,1)S(1)} collective-permute-done((bf16[32,5120]{1,0:T(8,128)(2,1)S(1)}, bf16[32,5120]{1,0:T(8,128)(2,1)S(1)}, u32[]{:S(2)}, u32[]{:S(2)}) %collective-permute-start.1) | collective-permute-done | bytes 327712 | tf_op jit(solution)/shard_map/ppermute | solution.py:248
  184.0 15.8 %all-gather.13.cloned.1.call-done = bf16[128,5120]{1,0:T(8,128)(2,1)} async-done(((bf16[32,5120]{1,0:T(8,128)(2,1)}), bf16[128,5120]{1,0:T(8,128)(2,1)}) %all-gather.13.cloned.1.call-update) | async-done | bytes 1310736 | tf_op jit(solution)/shard_map/all_gather | solution.py:54
  206.2 3.4 %fusion.58 = bf16[3,128,128]{2,1,0:T(8,128)(2,1)S(1)} fusion(bf16[1,1,3,5120,128]{4,3,2,1,0:T(8,128)(2,1)} %param.16, bf16[128,5120]{1,0:T(8,128)(2,1)} %all-gather.13.cloned.1.call-done), kind=kOutput, calls=%fused_computation.63 | convolution fusion | flops 503365632 | bytes 5341184 | tf_op jit(solution)/shard_map/sd,cdn->csn/dot_general | solution.py:86
  209.8 46.5 %all-gather.9.cloned.1.call-done = bf16[2,128,5120]{2,1,0:T(8,128)(2,1)} async-done(((bf16[2,32,5120]{2,1,0:T(8,128)(2,1)}), bf16[2,128,5120]{2,1,0:T(8,128)(2,1)}) %all-gather.9.cloned.1.call-update) | async-done | bytes 2621456 | tf_op jit(solution)/shard_map/all_gather | solution.py:54
  259.3 3.1 fusion.71
  263.1 5.9 %fusion.5 = bf16[2,128,5120]{2,1,0:T(8,128)(2,1)} fusion(bf16[128,1,5120]{0,2,1:T(8,128)(2,1)S(1)} %bitcast.384, bf16[384,1,5120]{0,2,1:T(8,128)(2,1)} %copy.25, bf16[128,128]{1,0:T(8,128)(2,1)S(1)} %copy.35, bf16[128,384]{1,0:T(8,128)(2,1)S(1)} %copy.34), kind=kOutput, calls=%fused_computation.12 | convolution fusion | flops 1385693184 | bytes 7995392 | tf_op jit(solution)/shard_map/sk,ktd->tsd/dot_general | solution.py:132
  272.9 2.1 collective-permute-start.5
  278.7 3.3 %fusion.27 = f32[128,5120]{1,0:T(8,128)} fusion(bf16[2,128,5120]{2,1,0:T(8,128)(2,1)} %collective-permute-done, bf16[4,128,128]{1,2,0:T(8,128)(2,1)S(1)} %collective-permute-done.4), kind=kOutput, calls=%fused_computation.40 | convolution fusion | flops 167772160 | bytes 3964928 | tf_op jit(solution)/shard_map/sn,sd->nd/dot_general | solution.py:145
  282.0 2.5 fusion.29
  284.5 4.5 %fusion.3 = bf16[1,1,3,5120,128]{3,4,2,1,0:T(8,128)(2,1)} fusion(f32[3,128,5120]{2,1,0:T(8,128)S(1)} %fusion.29, bf16[4,128,128]{1,2,0:T(8,128)(2,1)S(1)} %collective-permute-done.4, bf16[3,128,5120]{2,1,0:T(8,128)(2,1)S(1)} %add_convert_fusion.2, bf16[2,128,5120]{2,1,0:T(8,128)(2,1)} %collective-permute-done), kind=kOutput, calls=%fused_computation.10 | convolution fusion | flops 515112960 | bytes 17170432 | tf_op jit(solution)/shard_map/sd,csn->cdn/dot_general | solution.py:142
  289.0 6.3 %copy.37 = bf16[1,1,3,5120,128]{4,3,2,1,0:T(8,128)(2,1)} copy(bf16[1,1,3,5120,128]{3,4,2,1,0:T(8,128)(2,1)} %fusion.3) | data formatting | bytes 7864320
  295.3 12.2 %collective-permute-done.6 = bf16[128,5120]{1,0:T(8,128)(2,1)} collective-permute-done((bf16[128,5120]{1,0:T(8,128)(2,1)}, bf16[128,5120]{1,0:T(8,128)(2,1)}, u32[]{:S(2)}, u32[]{:S(2)}) %collective-permute-start.6) | collective-permute-done | bytes 1310752 | tf_op jit(solution)/shard_map/ppermute | solution.py:20
  307.4 3.7 %fusion.12 = bf16[1,1,128,5120]{3,2,1,0:T(8,128)(2,1)} fusion(f32[128,5120]{1,0:T(8,128)S(1)} %fusion.11, f32[128,5120]{1,0:T(8,128)} %fusion.27, bf16[128,5120]{1,0:T(8,128)(2,1)} %collective-permute-done.6, bf16[4,128,128]{1,2,0:T(8,128)(2,1)S(1)} %collective-permute-done.5), kind=kOutput, calls=%fused_computation.21 | convolution fusion | flops 171048960 | bytes 7897088 | tf_op jit(solution)/shard_map/sn,sd->nd/dot_general | solution.py:145
  311.2 9.5 %reduce-scatter.5.cloned.1.call-done = bf16[2,32,5120]{2,1,0:T(8,128)(2,1)} async-done(((bf16[2,128,5120]{2,1,0:T(8,128)(2,1)}), bf16[2,32,5120]{2,1,0:T(8,128)(2,1)}) %reduce-scatter.5.cloned.1.call-update) | async-done | bytes 655376 | tf_op jit(solution)/shard_map/reduce_scatter | solution.py:234
  (156 shorter events, 48.9 us)
Async XLA Ops:
  7.2 20.0 %copy-start = (bf16[64,5120]{1,0:T(8,128)(2,1)S(1)}, bf16[64,5120]{1,0:T(8,128)(2,1)}, u32[]{:S(2)}) copy-start(bf16[64,5120]{1,0:T(8,128)(2,1)} %param.14) | copy-start | bytes 1966084
  7.2 62.1 %all-gather.7.cloned.1.call-start = ((), (), s32[]{:S(2)}) async-start(), calls=%async_computation.2 | async-start | bytes 3276800 | tf_op jit(solution)/shard_map/all_gather | solution.py:54
  11.8 91.0 %all-gather.11.cloned.1.call-start = ((), (), s32[]{:S(2)}) async-start(), calls=%async_computation.6 | async-start | bytes 1638400 | tf_op jit(solution)/shard_map/all_gather | solution.py:54
  70.8 95.5 %reduce-scatter.3.cloned.1.call-start = ((), (), s32[]{:S(2)}) async-start(), calls=%async_computation.3 | async-start | bytes 3276800 | tf_op jit(solution)/shard_map/reduce_scatter | solution.py:234
  78.0 30.7 %copy-start.26 = (bf16[128,384]{1,0:T(8,128)(2,1)S(1)}, bf16[128,384]{1,0:T(8,128)(2,1)}, u32[]{:S(2)}) copy-start(bf16[128,384]{1,0:T(8,128)(2,1)} %copy.29) | copy-start | bytes 294916
  114.8 85.0 %all-gather.13.cloned.1.call-start = ((), (), s32[]{:S(2)}) async-start(), calls=%async_computation.7 | async-start | bytes 1638400 | tf_op jit(solution)/shard_map/all_gather | solution.py:54
  117.3 59.6 %copy-start.20 = (bf16[3,128,128]{1,2,0:T(8,128)(2,1)S(1)}, bf16[3,128,128]{1,2,0:T(8,128)(2,1)}, u32[]{:S(2)}) copy-start(bf16[3,128,128]{1,2,0:T(8,128)(2,1)} %get-tuple-element.44) | copy-start | bytes 294916
  117.3 60.4 %collective-permute-start = (bf16[2,128,5120]{2,1,0:T(8,128)(2,1)}, bf16[2,128,5120]{2,1,0:T(8,128)(2,1)}, u32[]{:S(2)}, u32[]{:S(2)}) collective-permute-start(bf16[2,128,5120]{2,1,0:T(8,128)(2,1)} %all-gather.7.cloned.1.call-done), channel_id=1, source_target_pairs={{0,25},{1,24},{8,17},{9,16},{16,9},{17,8},{24,1},{25,0},{2,27},{3,... | collective-permute-start | bytes 7864328 | tf_op jit(solution)/shard_map/ppermute | solution.py:20
  167.3 89.1 %all-gather.9.cloned.1.call-start = ((), (), s32[]{:S(2)}) async-start(), calls=%async_computation.4 | async-start | bytes 3276800 | tf_op jit(solution)/shard_map/all_gather | solution.py:54
  168.9 32.1 %copy-start.16 = (bf16[32,5120]{1,0:T(8,128)(2,1)}, bf16[32,5120]{1,0:T(8,128)(2,1)S(1)}, u32[]{:S(2)}) copy-start(bf16[32,5120]{1,0:T(8,128)(2,1)S(1)} %fusion.109) | copy-start | bytes 983044
  168.9 32.1 %copy-start.11 = (bf16[1,2,32,5120]{3,2,1,0:T(8,128)(2,1)S(1)}, bf16[1,2,32,5120]{3,2,1,0:T(8,128)(2,1)}, u32[]{:S(2)}) copy-start(bf16[1,2,32,5120]{3,2,1,0:T(8,128)(2,1)} %param.21) | copy-start | bytes 1966084
  168.9 14.3 %collective-permute-start.1 = (bf16[32,5120]{1,0:T(8,128)(2,1)S(1)}, bf16[32,5120]{1,0:T(8,128)(2,1)S(1)}, u32[]{:S(2)}, u32[]{:S(2)}) collective-permute-start(bf16[32,5120]{1,0:T(8,128)(2,1)S(1)} %fusion.109), channel_id=1, source_target_pairs={{1,9},{8,0},{9,17},{16,8},{17,25},{24,16},{3,11},{10,2},{11,19},{1... | collective-permute-start | bytes 983048 | tf_op jit(solution)/shard_map/ppermute | solution.py:248
  171.4 28.4 %copy-start.13 = (bf16[32,5120]{1,0:T(8,128)(2,1)}, bf16[32,5120]{1,0:T(8,128)(2,1)S(1)}, u32[]{:S(2)}) copy-start(bf16[32,5120]{1,0:T(8,128)(2,1)S(1)} %fusion.121) | copy-start | bytes 983044
  171.4 12.6 %collective-permute-start.2 = (bf16[32,5120]{1,0:T(8,128)(2,1)S(1)}, bf16[32,5120]{1,0:T(8,128)(2,1)S(1)}, u32[]{:S(2)}, u32[]{:S(2)}) collective-permute-start(bf16[32,5120]{1,0:T(8,128)(2,1)S(1)} %fusion.121), channel_id=1, source_target_pairs={{0,8},{8,16},{9,1},{16,24},{17,9},{25,17},{2,10},{10,18},{11,3},{1... | collective-permute-start | bytes 983048 | tf_op jit(solution)/shard_map/ppermute | solution.py:249
  176.9 26.3 %copy-start.23 = (bf16[128,128]{1,0:T(8,128)(2,1)}, bf16[128,128]{1,0:T(8,128)(2,1)S(1)}, u32[]{:S(2)}) copy-start(bf16[128,128]{1,0:T(8,128)(2,1)S(1)} %convolution_convert_fusion.8) | copy-start | bytes 98308
  203.2 53.2 %copy-start.6 = (bf16[1,1,128,5120]{3,2,1,0:T(8,128)(2,1)S(1)}, bf16[1,1,128,5120]{3,2,1,0:T(8,128)(2,1)}, u32[]{:S(2)}) copy-start(bf16[1,1,128,5120]{3,2,1,0:T(8,128)(2,1)} %param.17) | copy-start | bytes 3932164
  203.2 117.4 %reduce-scatter.5.cloned.1.call-start = ((), (), s32[]{:S(2)}) async-start(), calls=%async_computation.5 | async-start | bytes 3276800 | tf_op jit(solution)/shard_map/reduce_scatter | solution.py:234
  203.5 65.5 %collective-permute-start.3 = (bf16[1,128,5120]{2,1,0:T(8,128)(2,1)}, bf16[1,128,5120]{2,1,0:T(8,128)(2,1)}, u32[]{:S(2)}, u32[]{:S(2)}) collective-permute-start(bf16[1,128,5120]{2,1,0:T(8,128)(2,1)} %bitcast.381), channel_id=1, source_target_pairs={{0,25},{1,24},{8,17},{9,16},{16,9},{17,8},{24,1},{25,0},{2,27},{3,... | collective-permute-start | bytes 3932168 | tf_op jit(solution)/shard_map/ppermute | solution.py:20
  204.6 64.4 %collective-permute-start.4 = (bf16[4,128,128]{1,2,0:T(8,128)(2,1)}, bf16[4,128,128]{1,2,0:T(8,128)(2,1)S(1)}, u32[]{:S(2)}, u32[]{:S(2)}) collective-permute-start(bf16[4,128,128]{1,2,0:T(8,128)(2,1)} %pad_maximum_fusion.2), channel_id=1, source_target_pairs={{0,25},{1,24},{8,17},{9,16},{16,9},{17,8},{24,1},{25,0},{2,27},{3,... | collective-permute-start | bytes 393224 | tf_op jit(solution)/shard_map/ppermute | solution.py:20
  272.9 9.1 %collective-permute-start.5 = (bf16[4,128,128]{1,2,0:T(8,128)(2,1)S(1)}, bf16[4,128,128]{1,2,0:T(8,128)(2,1)S(1)}, u32[]{:S(2)}, u32[]{:S(2)}) collective-permute-start(bf16[4,128,128]{1,2,0:T(8,128)(2,1)S(1)} %pad_maximum_fusion.3), channel_id=1, source_target_pairs={{0,25},{1,24},{8,17},{9,16},{16,9},{17,8},{24,1},{25,0},{2,27},{3,... | collective-permute-start | bytes 393224 | tf_op jit(solution)/shard_map/ppermute | solution.py:20
  276.2 31.3 %collective-permute-start.6 = (bf16[128,5120]{1,0:T(8,128)(2,1)}, bf16[128,5120]{1,0:T(8,128)(2,1)}, u32[]{:S(2)}, u32[]{:S(2)}) collective-permute-start(bf16[128,5120]{1,0:T(8,128)(2,1)} %slice_bitcast_fusion.2), channel_id=1, source_target_pairs={{0,25},{1,24},{8,17},{9,16},{16,9},{17,8},{24,1},{25,0},{2,27},{3,... | collective-permute-start | bytes 3932168 | tf_op jit(solution)/shard_map/ppermute | solution.py:20
  295.3 25.4 %copy-start.3 = (bf16[1,1,2,32,5120]{4,3,2,1,0:T(8,128)(2,1)S(1)}, bf16[1,1,2,32,5120]{4,3,2,1,0:T(8,128)(2,1)}, u32[]{:S(2)}) copy-start(bf16[1,1,2,32,5120]{4,3,2,1,0:T(8,128)(2,1)} %param.20) | copy-start | bytes 1966084
  311.1 12.6 %copy-start.17 = (bf16[32,5120]{1,0:T(8,128)(2,1)S(1)}, bf16[32,5120]{1,0:T(8,128)(2,1)}, u32[]{:S(2)}) copy-start(bf16[32,5120]{1,0:T(8,128)(2,1)} %copy-done.16) | copy-start | bytes 983044
  311.1 13.5 %copy-start.14 = (bf16[32,5120]{1,0:T(8,128)(2,1)S(1)}, bf16[32,5120]{1,0:T(8,128)(2,1)}, u32[]{:S(2)}) copy-start(bf16[32,5120]{1,0:T(8,128)(2,1)} %copy-done.13) | copy-start | bytes 983044
  (21 other events, 61.3 us)
Sparse Core Ops, SparseCore 0:
  11.9 57.3 all-gather.6
  71.5 31.3 all-gather.10
  114.9 51.3 reduce-scatter.2
  167.7 32.0 all-gather.12
  203.3 52.9 all-gather.8
  269.1 51.4 reduce-scatter.4

commit v13 on v12

--- a/solution.py
+++ b/solution.py
@@ -116,21 +116,23 @@
         return d_projected, mixed
 
     qkv_rows = jnp.transpose(qkv_weight, (0, 2, 1)).reshape(3 * inner_here, model_width)
-    block_weight = jnp.concatenate(
-        [
-            jnp.stack([qkv_rows, jnp.zeros_like(qkv_rows)], axis=1),
-            jnp.stack([jnp.zeros_like(out_weight), out_weight], axis=1),
-        ],
-        axis=0,
-    )
+    padded_out = jnp.concatenate(
+        [out_weight, jnp.zeros((2 * inner_here, model_width), out_weight.dtype)], axis=0
+    )
+    block_weight = jnp.stack([qkv_rows, padded_out])
 
     def projected_back(d_projected, forward_mixed):
-        lhs = jnp.concatenate(
-            [jnp.transpose(d_projected, (1, 0, 2)).reshape(seq_len, 3 * inner_here), forward_mixed],
-            axis=1,
+        lhs = jnp.stack(
+            [
+                jnp.transpose(d_projected, (1, 0, 2)).reshape(seq_len, 3 * inner_here),
+                jnp.concatenate(
+                    [forward_mixed, jnp.zeros((seq_len, 2 * inner_here), forward_mixed.dtype)],
+                    axis=1,
+                ),
+            ]
         )
         return jnp.einsum(
-            "sk,ktd->tsd", lhs, block_weight, preferred_element_type=jnp.float32
+            "tsk,tkd->tsd", lhs, block_weight, preferred_element_type=jnp.float32
         ).astype(jnp.bfloat16)
 
     def weight_terms(normed_fulls, d_projecteds, mixeds, upstream_fulls):

time: 334 us -> 329 us (0.985)
  local copies, waits for them, and re-layouts: 31.6 us -> 23.6 us
  waiting for transfers between devices: 202 us -> 209 us
  matrix products: 53 us -> 49.1 us
    unnamed x67, local copies, waits for them, and re-layouts: 18.1 us -> 10.2 us
    all_gather x4, waiting for transfers between devices: 127 us -> 134 us  [gathered(): full = lax.all_gather(jnp.stack(blocks), 'tp', axis=1, tiled=True)]
    transpose x0 -> x1, local copies, waits for them, and re-layouts: none -> 6.38 us  [shards(): jnp.transpose(qkv_weight, (0, 2, 1)).reshape(3 * inner_here, model_width)]
    another operation x1 -> x3, local copies, waits for them, and re-layouts: 6.43 us -> 2.37 us  [the longest x1 2.35 us: shards(): block_weight = jnp.stack([qkv_rows, padded_out])]
    dot_general x2, matrix products: 11.9 us -> 8.2 us  [projected_back(): jnp.einsum('tsk,tkd->tsd', lhs, block_weight, preferred_element_type=jnp....]
  transfers between devices with their start and end apart: 13 -> 13, of which waited for: 9 -> 9; matrix products, arithmetic and copies ran while one was open for 22% -> 19% of each run, Pallas kernels for 0% -> 0%
where the time goes in v13:
time: 329 us; the launch traced here: 328 us
  waiting for transfers between devices  209 us (64%)
  matrix products  49.1 us (15%)
  local copies, waits for them, and re-layouts  23.6 us (7%)
  other arithmetic  18.1 us (6%)
  between operations  14.7 us (4%)
  starting transfers between devices  12.9 us (4%)
    all_gather x4, waiting for transfers between devices, gathered(): full = lax.all_gather(jnp.stack(blocks), 'tp', axis=1, tiled=True)  134 us
    reduce_scatter x2, waiting for transfers between devices, shards(): lax.psum_scatter(both_parts, 'tp', scatter_dimension=1, tiled=True)  57.3 us
    dot_general x4, matrix products, heads_of(): jnp.einsum('sd,cdn->csn', normed_full, qkv_weight, preferred_element_type...  13.9 us
    ppermute x5, waiting for transfers between devices, flipped(): lax.ppermute(value, axis, [(i, i ^ mask) for i in range(lax.axis_size(axi...  12 us
    unnamed x67, local copies, waits for them, and re-layouts  10.2 us
    dot_general x4, matrix products, weight_terms(): jnp.einsum('sd,csn->cdn', normed_full, d_projected, preferred_element_typ...  9.31 us
    dot_general x2, matrix products, projected_back(): jnp.einsum('tsk,tkd->tsd', lhs, block_weight, preferred_element_type=jnp....  8.2 us
    dot_general x4, matrix products, weight_terms(): jnp.einsum('sn,sd->nd', mixed, upstream_full, preferred_element_type=jnp....  8.07 us
  transfers between devices with their start and end apart: 13, of which 9 were waited for; matrix products, arithmetic and copies ran while one was open for 19% of the time, Pallas kernels for 0%

profile of v13, /device:TPU:0, one launch (start us, length us, event | category | flops | bytes accessed | tf_op | source)
XLA Modules:
  0.0 327.5 jit_solution(17339304230749823708)
XLA Ops:
  11.9 6.4 %copy.15 = bf16[3,128,5120]{2,1,0:T(8,128)(2,1)} copy(bf16[3,128,5120]{1,2,0:T(8,128)(2,1)} %bitcast.362) | data formatting | bytes 7864320 | tf_op jit(solution)/shard_map/transpose | solution.py:118
  20.8 2.4 pad_bitcast_fusion
  24.2 45.1 %all-gather.7.cloned.1.call-done = bf16[2,128,5120]{2,1,0:T(8,128)(2,1)} async-done(((bf16[2,32,5120]{2,1,0:T(8,128)(2,1)}), bf16[2,128,5120]{2,1,0:T(8,128)(2,1)}) %all-gather.7.cloned.1.call-update) | async-done | bytes 2621456 | tf_op jit(solution)/shard_map/all_gather | solution.py:54
  70.8 3.5 %fusion.60 = bf16[3,128,128]{2,1,0:T(8,128)(2,1)S(1)} fusion(bf16[1,1,3,5120,128]{4,3,2,1,0:T(8,128)(2,1)} %param.16, bf16[2,128,5120]{2,1,0:T(8,128)(2,1)} %all-gather.7.cloned.1.call-done), kind=kOutput, calls=%fused_computation.57 | convolution fusion | flops 503365632 | bytes 5341184 | tf_op jit(solution)/shard_map/sd,cdn->csn/dot_general | solution.py:86
  77.2 25.6 %all-gather.11.cloned.1.call-done = bf16[128,5120]{1,0:T(8,128)(2,1)} async-done(((bf16[32,5120]{1,0:T(8,128)(2,1)}), bf16[128,5120]{1,0:T(8,128)(2,1)}) %all-gather.11.cloned.1.call-update) | async-done | bytes 1310736 | tf_op jit(solution)/shard_map/all_gather | solution.py:54
  102.8 3.5 %fusion.55 = bf16[3,128,128]{2,1,0:T(8,128)(2,1)S(1)} fusion(bf16[1,1,3,5120,128]{4,3,2,1,0:T(8,128)(2,1)} %param.16, bf16[128,5120]{1,0:T(8,128)(2,1)} %all-gather.11.cloned.1.call-done), kind=kOutput, calls=%fused_computation.56 | convolution fusion | flops 503365632 | bytes 5341184 | tf_op jit(solution)/shard_map/sd,cdn->csn/dot_general | solution.py:86
  106.8 5.3 %convolution_convert_fusion.1 = bf16[2,128,5120]{2,1,0:T(8,128)(2,1)} fusion(bf16[1,384,5120]{2,1,0:T(8,128)(2,1)} %pad_bitcast_fusion, bf16[1,384,5120]{2,1,0:T(8,128)(2,1)S(1)} %bitcast.363, bf16[1,128,384]{1,2,0:T(8,128)(2,1)S(1)} %pad_bitcast_fusion.2, bf16[1,128,384]{1,2,0:T(8,128)(2,1)S(1)} %bitcast.376), kind=kOutput, calls=%fused_computation.5 | convolution fusion | flops 1011974144 | bytes 10682368 | tf_op jit(solution)/shard_map/tsk,tkd->tsd/dot_general | solution.py:134
  112.6 2.0 fusion.9
  115.7 47.9 %reduce-scatter.3.cloned.1.call-done = bf16[2,32,5120]{2,1,0:T(8,128)(2,1)} async-done(((bf16[2,128,5120]{2,1,0:T(8,128)(2,1)}), bf16[2,32,5120]{2,1,0:T(8,128)(2,1)}) %reduce-scatter.3.cloned.1.call-update) | async-done | bytes 655376 | tf_op jit(solution)/shard_map/reduce_scatter | solution.py:236
  168.7 4.6 %collective-permute-start.2 = (bf16[32,5120]{1,0:T(8,128)(2,1)S(1)}, bf16[32,5120]{1,0:T(8,128)(2,1)S(1)}, u32[]{:S(2)}, u32[]{:S(2)}) collective-permute-start(bf16[32,5120]{1,0:T(8,128)(2,1)S(1)} %fusion.100), channel_id=1, source_target_pairs={{0,8},{8,16},{9,1},{16,24},{17,9},{25,17},{2,10},{10,18},{11,3},{1... | collective-permute-start | bytes 983048 | tf_op jit(solution)/shard_map/ppermute | solution.py:251
  175.0 5.5 %collective-permute-done.1 = bf16[32,5120]{1,0:T(8,128)(2,1)S(1)} collective-permute-done((bf16[32,5120]{1,0:T(8,128)(2,1)S(1)}, bf16[32,5120]{1,0:T(8,128)(2,1)S(1)}, u32[]{:S(2)}, u32[]{:S(2)}) %collective-permute-start.1) | collective-permute-done | bytes 327712 | tf_op jit(solution)/shard_map/ppermute | solution.py:250
  181.2 16.4 %all-gather.13.cloned.1.call-done = bf16[128,5120]{1,0:T(8,128)(2,1)} async-done(((bf16[32,5120]{1,0:T(8,128)(2,1)}), bf16[128,5120]{1,0:T(8,128)(2,1)}) %all-gather.13.cloned.1.call-update) | async-done | bytes 1310736 | tf_op jit(solution)/shard_map/all_gather | solution.py:54
  204.0 3.4 %fusion.47 = bf16[3,128,128]{2,1,0:T(8,128)(2,1)S(1)} fusion(bf16[1,1,3,5120,128]{4,3,2,1,0:T(8,128)(2,1)} %param.16, bf16[128,5120]{1,0:T(8,128)(2,1)} %all-gather.13.cloned.1.call-done), kind=kOutput, calls=%fused_computation.54 | convolution fusion | flops 503365632 | bytes 5341184 | tf_op jit(solution)/shard_map/sd,cdn->csn/dot_general | solution.py:86
  207.7 47.0 %all-gather.9.cloned.1.call-done = bf16[2,128,5120]{2,1,0:T(8,128)(2,1)} async-done(((bf16[2,32,5120]{2,1,0:T(8,128)(2,1)}), bf16[2,128,5120]{2,1,0:T(8,128)(2,1)}) %all-gather.9.cloned.1.call-update) | async-done | bytes 2621456 | tf_op jit(solution)/shard_map/all_gather | solution.py:54
  254.7 2.0 fusion.78
  256.9 3.5 %fusion.52 = bf16[3,128,128]{2,1,0:T(8,128)(2,1)S(1)} fusion(bf16[1,1,3,5120,128]{4,3,2,1,0:T(8,128)(2,1)} %param.16, bf16[2,128,5120]{2,1,0:T(8,128)(2,1)} %all-gather.9.cloned.1.call-done), kind=kOutput, calls=%fused_computation.55 | convolution fusion | flops 503365632 | bytes 5341184 | tf_op jit(solution)/shard_map/sd,cdn->csn/dot_general | solution.py:86
  261.6 2.9 convolution_convert_fusion
  274.1 3.3 %fusion.20 = f32[128,5120]{1,0:T(8,128)} fusion(bf16[2,128,5120]{2,1,0:T(8,128)(2,1)} %collective-permute-done, bf16[4,128,128]{1,2,0:T(8,128)(2,1)S(1)} %collective-permute-done.4), kind=kOutput, calls=%fused_computation.35 | convolution fusion | flops 167772160 | bytes 3964928 | tf_op jit(solution)/shard_map/sn,sd->nd/dot_general | solution.py:147
  277.4 2.5 fusion.22
  279.9 4.5 %fusion = bf16[1,1,3,5120,128]{3,4,2,1,0:T(8,128)(2,1)} fusion(f32[3,128,5120]{2,1,0:T(8,128)S(1)} %fusion.22, bf16[4,128,128]{1,2,0:T(8,128)(2,1)S(1)} %collective-permute-done.4, bf16[3,128,5120]{2,1,0:T(8,128)(2,1)S(1)} %add_convert_fusion.2, bf16[2,128,5120]{2,1,0:T(8,128)(2,1)} %collective-permute-done), kind=kOutput, calls=%fused_computation.6 | convolution fusion | flops 515112960 | bytes 17170432 | tf_op jit(solution)/shard_map/sd,csn->cdn/dot_general | solution.py:144
  284.4 6.3 %copy.18 = bf16[1,1,3,5120,128]{4,3,2,1,0:T(8,128)(2,1)} copy(bf16[1,1,3,5120,128]{3,4,2,1,0:T(8,128)(2,1)} %fusion) | data formatting | bytes 7864320
  290.7 12.0 %collective-permute-done.6 = bf16[128,5120]{1,0:T(8,128)(2,1)} collective-permute-done((bf16[128,5120]{1,0:T(8,128)(2,1)}, bf16[128,5120]{1,0:T(8,128)(2,1)}, u32[]{:S(2)}, u32[]{:S(2)}) %collective-permute-start.6) | collective-permute-done | bytes 1310752 | tf_op jit(solution)/shard_map/ppermute | solution.py:20
  302.6 3.7 %fusion.7 = bf16[1,1,128,5120]{3,2,1,0:T(8,128)(2,1)} fusion(f32[128,5120]{1,0:T(8,128)S(1)} %fusion.6, f32[128,5120]{1,0:T(8,128)} %fusion.20, bf16[128,5120]{1,0:T(8,128)(2,1)} %collective-permute-done.6, bf16[4,128,128]{1,2,0:T(8,128)(2,1)S(1)} %collective-permute-done.5), kind=kOutput, calls=%fused_computation.15 | convolution fusion | flops 171048960 | bytes 7897088 | tf_op jit(solution)/shard_map/sn,sd->nd/dot_general | solution.py:147
  306.3 9.5 %reduce-scatter.5.cloned.1.call-done = bf16[2,32,5120]{2,1,0:T(8,128)(2,1)} async-done(((bf16[2,128,5120]{2,1,0:T(8,128)(2,1)}), bf16[2,32,5120]{2,1,0:T(8,128)(2,1)}) %reduce-scatter.5.cloned.1.call-update) | async-done | bytes 655376 | tf_op jit(solution)/shard_map/reduce_scatter | solution.py:236
  (155 shorter events, 44.3 us)
Async XLA Ops:
  7.2 12.2 %copy-start = (bf16[64,5120]{1,0:T(8,128)(2,1)S(1)}, bf16[64,5120]{1,0:T(8,128)(2,1)}, u32[]{:S(2)}) copy-start(bf16[64,5120]{1,0:T(8,128)(2,1)} %param.14) | copy-start | bytes 1966084
  7.2 62.1 %all-gather.7.cloned.1.call-start = ((), (), s32[]{:S(2)}) async-start(), calls=%async_computation.2 | async-start | bytes 3276800 | tf_op jit(solution)/shard_map/all_gather | solution.py:54
  11.8 91.0 %all-gather.11.cloned.1.call-start = ((), (), s32[]{:S(2)}) async-start(), calls=%async_computation.6 | async-start | bytes 1638400 | tf_op jit(solution)/shard_map/all_gather | solution.py:54
  70.8 92.8 %reduce-scatter.3.cloned.1.call-start = ((), (), s32[]{:S(2)}) async-start(), calls=%async_computation.3 | async-start | bytes 3276800 | tf_op jit(solution)/shard_map/reduce_scatter | solution.py:236
  112.1 85.6 %all-gather.13.cloned.1.call-start = ((), (), s32[]{:S(2)}) async-start(), calls=%async_computation.7 | async-start | bytes 1638400 | tf_op jit(solution)/shard_map/all_gather | solution.py:54
  114.6 59.6 %copy-start.22 = (bf16[3,128,128]{1,2,0:T(8,128)(2,1)S(1)}, bf16[3,128,128]{1,2,0:T(8,128)(2,1)}, u32[]{:S(2)}) copy-start(bf16[3,128,128]{1,2,0:T(8,128)(2,1)} %get-tuple-element.40) | copy-start | bytes 294916
  114.6 60.4 %collective-permute-start = (bf16[2,128,5120]{2,1,0:T(8,128)(2,1)}, bf16[2,128,5120]{2,1,0:T(8,128)(2,1)}, u32[]{:S(2)}, u32[]{:S(2)}) collective-permute-start(bf16[2,128,5120]{2,1,0:T(8,128)(2,1)} %all-gather.7.cloned.1.call-done), channel_id=1, source_target_pairs={{0,25},{1,24},{8,17},{9,16},{16,9},{17,8},{24,1},{25,0},{2,27},{3,... | collective-permute-start | bytes 7864328 | tf_op jit(solution)/shard_map/ppermute | solution.py:20
  164.6 90.2 %all-gather.9.cloned.1.call-start = ((), (), s32[]{:S(2)}) async-start(), calls=%async_computation.4 | async-start | bytes 3276800 | tf_op jit(solution)/shard_map/all_gather | solution.py:54
  166.2 32.7 %copy-start.17 = (bf16[32,5120]{1,0:T(8,128)(2,1)}, bf16[32,5120]{1,0:T(8,128)(2,1)S(1)}, u32[]{:S(2)}) copy-start(bf16[32,5120]{1,0:T(8,128)(2,1)S(1)} %fusion.88) | copy-start | bytes 983044
  166.2 32.7 %copy-start.13 = (bf16[1,2,32,5120]{3,2,1,0:T(8,128)(2,1)S(1)}, bf16[1,2,32,5120]{3,2,1,0:T(8,128)(2,1)}, u32[]{:S(2)}) copy-start(bf16[1,2,32,5120]{3,2,1,0:T(8,128)(2,1)} %param.21) | copy-start | bytes 1966084
  166.2 14.3 %collective-permute-start.1 = (bf16[32,5120]{1,0:T(8,128)(2,1)S(1)}, bf16[32,5120]{1,0:T(8,128)(2,1)S(1)}, u32[]{:S(2)}, u32[]{:S(2)}) collective-permute-start(bf16[32,5120]{1,0:T(8,128)(2,1)S(1)} %fusion.88), channel_id=1, source_target_pairs={{1,9},{8,0},{9,17},{16,8},{17,25},{24,16},{3,11},{10,2},{11,19},{1... | collective-permute-start | bytes 983048 | tf_op jit(solution)/shard_map/ppermute | solution.py:250
  168.7 29.0 %copy-start.15 = (bf16[32,5120]{1,0:T(8,128)(2,1)}, bf16[32,5120]{1,0:T(8,128)(2,1)S(1)}, u32[]{:S(2)}) copy-start(bf16[32,5120]{1,0:T(8,128)(2,1)S(1)} %fusion.100) | copy-start | bytes 983044
  168.7 12.5 %collective-permute-start.2 = (bf16[32,5120]{1,0:T(8,128)(2,1)S(1)}, bf16[32,5120]{1,0:T(8,128)(2,1)S(1)}, u32[]{:S(2)}, u32[]{:S(2)}) collective-permute-start(bf16[32,5120]{1,0:T(8,128)(2,1)S(1)} %fusion.100), channel_id=1, source_target_pairs={{0,8},{8,16},{9,1},{16,24},{17,9},{25,17},{2,10},{10,18},{11,3},{1... | collective-permute-start | bytes 983048 | tf_op jit(solution)/shard_map/ppermute | solution.py:251
  174.2 26.8 %copy-start.25 = (bf16[128,128]{1,0:T(8,128)(2,1)}, bf16[128,128]{1,0:T(8,128)(2,1)S(1)}, u32[]{:S(2)}) copy-start(bf16[128,128]{1,0:T(8,128)(2,1)S(1)} %convolution_convert_fusion.8) | copy-start | bytes 98308
  198.9 8.6 %copy-start.11 = (bf16[32,5120]{1,0:T(8,128)(2,1)}, bf16[32,5120]{1,0:T(8,128)(2,1)S(1)}, u32[]{:S(2)}) copy-start(bf16[32,5120]{1,0:T(8,128)(2,1)S(1)} %get-tuple-element.35) | copy-start | bytes 983044
  201.1 53.7 %copy-start.9 = (bf16[1,1,128,5120]{3,2,1,0:T(8,128)(2,1)S(1)}, bf16[1,1,128,5120]{3,2,1,0:T(8,128)(2,1)}, u32[]{:S(2)}) copy-start(bf16[1,1,128,5120]{3,2,1,0:T(8,128)(2,1)} %param.17) | copy-start | bytes 3932164
  201.1 114.7 %reduce-scatter.5.cloned.1.call-start = ((), (), s32[]{:S(2)}) async-start(), calls=%async_computation.5 | async-start | bytes 3276800 | tf_op jit(solution)/shard_map/reduce_scatter | solution.py:236
  201.3 63.3 %collective-permute-start.3 = (bf16[1,128,5120]{2,1,0:T(8,128)(2,1)}, bf16[1,128,5120]{2,1,0:T(8,128)(2,1)}, u32[]{:S(2)}, u32[]{:S(2)}) collective-permute-start(bf16[1,128,5120]{2,1,0:T(8,128)(2,1)} %bitcast.366), channel_id=1, source_target_pairs={{0,25},{1,24},{8,17},{9,16},{16,9},{17,8},{24,1},{25,0},{2,27},{3,... | collective-permute-start | bytes 3932168 | tf_op jit(solution)/shard_map/ppermute | solution.py:20
  202.5 62.1 %collective-permute-start.4 = (bf16[4,128,128]{1,2,0:T(8,128)(2,1)}, bf16[4,128,128]{1,2,0:T(8,128)(2,1)S(1)}, u32[]{:S(2)}, u32[]{:S(2)}) collective-permute-start(bf16[4,128,128]{1,2,0:T(8,128)(2,1)} %pad_maximum_fusion.5), channel_id=1, source_target_pairs={{0,25},{1,24},{8,17},{9,16},{16,9},{17,8},{24,1},{25,0},{2,27},{3,... | collective-permute-start | bytes 393224 | tf_op jit(solution)/shard_map/ppermute | solution.py:20
  268.5 8.9 %collective-permute-start.5 = (bf16[4,128,128]{1,2,0:T(8,128)(2,1)S(1)}, bf16[4,128,128]{1,2,0:T(8,128)(2,1)S(1)}, u32[]{:S(2)}, u32[]{:S(2)}) collective-permute-start(bf16[4,128,128]{1,2,0:T(8,128)(2,1)S(1)} %pad_maximum_fusion.6), channel_id=1, source_target_pairs={{0,25},{1,24},{8,17},{9,16},{16,9},{17,8},{24,1},{25,0},{2,27},{3,... | collective-permute-start | bytes 393224 | tf_op jit(solution)/shard_map/ppermute | solution.py:20
  271.4 31.3 %collective-permute-start.6 = (bf16[128,5120]{1,0:T(8,128)(2,1)}, bf16[128,5120]{1,0:T(8,128)(2,1)}, u32[]{:S(2)}, u32[]{:S(2)}) collective-permute-start(bf16[128,5120]{1,0:T(8,128)(2,1)} %slice_bitcast_fusion.2), channel_id=1, source_target_pairs={{0,25},{1,24},{8,17},{9,16},{16,9},{17,8},{24,1},{25,0},{2,27},{3,... | collective-permute-start | bytes 3932168 | tf_op jit(solution)/shard_map/ppermute | solution.py:20
  290.7 25.2 %copy-start.6 = (bf16[1,1,2,32,5120]{4,3,2,1,0:T(8,128)(2,1)S(1)}, bf16[1,1,2,32,5120]{4,3,2,1,0:T(8,128)(2,1)}, u32[]{:S(2)}) copy-start(bf16[1,1,2,32,5120]{4,3,2,1,0:T(8,128)(2,1)} %param.20) | copy-start | bytes 1966084
  306.3 12.6 %copy-start.18 = (bf16[32,5120]{1,0:T(8,128)(2,1)S(1)}, bf16[32,5120]{1,0:T(8,128)(2,1)}, u32[]{:S(2)}) copy-start(bf16[32,5120]{1,0:T(8,128)(2,1)} %copy-done.17) | copy-start | bytes 983044
  306.3 13.5 %copy-start.16 = (bf16[32,5120]{1,0:T(8,128)(2,1)S(1)}, bf16[32,5120]{1,0:T(8,128)(2,1)}, u32[]{:S(2)}) copy-start(bf16[32,5120]{1,0:T(8,128)(2,1)} %copy-done.15) | copy-start | bytes 983044
  (22 other events, 70.7 us)
Sparse Core Ops, SparseCore 0:
  11.9 57.3 all-gather.6
  71.5 31.3 all-gather.10
  112.2 51.3 reduce-scatter.2
  165.5 32.0 all-gather.12
  201.2 53.4 all-gather.8
  264.7 51.0 reduce-scatter.4

commit v14 on v13

--- a/solution.py
+++ b/solution.py
@@ -205,12 +205,10 @@
         current = jnp.where(position == 0, embedded, forward_in)
         upstream = jnp.where(position == sections - 1, cotangent[0, step_index], backward_in)
         if step_index == 0:
-            upstream_full, backward_normed_full[0] = gathered([upstream, saved_normed[0]])
+            upstream_full, backward_normed_full[0], forward_normed_full = gathered(
+                [upstream, saved_normed[0], normed_rows(current)]
+            )
             first_sent = to_partner(jnp.stack([upstream_full, backward_normed_full[0]]))
-            forward_normed, upstream_full = lax.optimization_barrier(
-                (normed_rows(current), upstream_full)
-            )
-            forward_normed_full = gathered([forward_normed])[0]
         else:
             upstream_full, forward_normed_full = gathered([upstream, normed_rows(current)])
             inbox[f"rows{step_index}"] = to_partner(upstream_full)

time: 329 us -> 321 us (0.976)
  other arithmetic: 18.1 us -> 12.3 us
  waiting for transfers between devices: 209 us -> 205 us
    reduce_scatter x2, waiting for transfers between devices: 57.3 us -> 52.4 us  [shards(): lax.psum_scatter(both_parts, 'tp', scatter_dimension=1, tiled=True)]
    another operation x0 -> x1, local copies, waits for them, and re-layouts: none -> 3.47 us  [shards(): first_sent = to_partner(jnp.stack([upstream_full, backward_normed_full[0]]))]
    all_gather x4 -> x3, waiting for transfers between devices: 134 us -> 131 us  [gathered(): full = lax.all_gather(jnp.stack(blocks), 'tp', axis=1, tiled=True)]
    unnamed x67 -> x61, local copies, waits for them, and re-layouts: 10.2 us -> 7.13 us
  transfers between devices with their start and end apart: 13 -> 12, of which waited for: 9 -> 8; matrix products, arithmetic and copies ran while one was open for 19% -> 19% of each run, Pallas kernels for 0% -> 0%
where the time goes in v14:
time: 321 us; the launch traced here: 320 us
  waiting for transfers between devices  205 us (64%)
  matrix products  49 us (15%)
  local copies, waits for them, and re-layouts  24.7 us (8%)
  between operations  14.4 us (4%)
  starting transfers between devices  14.1 us (4%)
  other arithmetic  12.3 us (4%)
    all_gather x3, waiting for transfers between devices, gathered(): full = lax.all_gather(jnp.stack(blocks), 'tp', axis=1, tiled=True)  131 us
    reduce_scatter x2, waiting for transfers between devices, shards(): lax.psum_scatter(both_parts, 'tp', scatter_dimension=1, tiled=True)  52.4 us
    ppermute x5, waiting for transfers between devices, flipped(): lax.ppermute(value, axis, [(i, i ^ mask) for i in range(lax.axis_size(axi...  15.3 us
    dot_general x4, matrix products, heads_of(): jnp.einsum('sd,cdn->csn', normed_full, qkv_weight, preferred_element_type...  12.3 us
    dot_general x4, matrix products, weight_terms(): jnp.einsum('sd,csn->cdn', normed_full, d_projected, preferred_element_typ...  10.7 us
    dot_general x4, matrix products, weight_terms(): jnp.einsum('sn,sd->nd', mixed, upstream_full, preferred_element_type=jnp....  9.49 us
    unnamed x61, local copies, waits for them, and re-layouts  7.13 us
    ppermute x5, starting transfers between devices, flipped(): lax.ppermute(value, axis, [(i, i ^ mask) for i in range(lax.axis_size(axi...  7.09 us
  transfers between devices with their start and end apart: 12, of which 8 were waited for; matrix products, arithmetic and copies ran while one was open for 19% of the time, Pallas kernels for 0%

profile of v14, /device:TPU:0, one launch (start us, length us, event | category | flops | bytes accessed | tf_op | source)
XLA Modules:
  0.0 319.8 jit_solution(11428767402684646129)
XLA Ops:
  13.8 6.3 %copy.15 = bf16[3,128,5120]{2,1,0:T(8,128)(2,1)} copy(bf16[3,128,5120]{1,2,0:T(8,128)(2,1)} %bitcast.371) | data formatting | bytes 7864320 | tf_op jit(solution)/shard_map/transpose | solution.py:118
  20.7 3.7 %pad_bitcast_fusion = bf16[1,384,5120]{2,1,0:T(8,128)(2,1)} fusion(bf16[128,5120]{1,0:T(8,128)(2,1)} %bitcast.373), kind=kLoop, calls=%fused_computation.30 | loop fusion | bytes 5242880 | tf_op jit(solution)/shard_map/stack | solution.py:122
  24.4 68.6 %all-gather.5.cloned.1.call-done = bf16[3,128,5120]{2,1,0:T(8,128)(2,1)} async-done(((bf16[3,32,5120]{2,1,0:T(8,128)(2,1)}), bf16[3,128,5120]{2,1,0:T(8,128)(2,1)}) %all-gather.5.cloned.1.call-update) | async-done | bytes 3932176 | tf_op jit(solution)/shard_map/all_gather | solution.py:54
  93.1 3.5 %fusion.57 = bf16[3,128,128]{2,1,0:T(8,128)(2,1)S(1)} fusion(bf16[1,1,3,5120,128]{4,3,2,1,0:T(8,128)(2,1)} %param.16, bf16[3,128,5120]{2,1,0:T(8,128)(2,1)} %all-gather.5.cloned.1.call-done), kind=kOutput, calls=%fused_computation.59 | convolution fusion | flops 503365632 | bytes 5341184 | tf_op jit(solution)/shard_map/sd,cdn->csn/dot_general | solution.py:86
  99.7 2.3 fusion.54
  102.6 3.0 convolution_convert_fusion.1
  106.9 3.5 %stack.110 = bf16[2,128,5120]{2,1,0:T(8,128)(2,1)} slice(bf16[3,128,5120]{2,1,0:T(8,128)(2,1)} %all-gather.5.cloned.1.call-done), slice={[0:2], [0:128], [0:5120]} | slice | bytes 5242880 | tf_op jit(solution)/shard_map/stack | solution.py:211
  112.1 44.5 %reduce-scatter.3.cloned.1.call-done = bf16[2,32,5120]{2,1,0:T(8,128)(2,1)} async-done(((bf16[2,128,5120]{2,1,0:T(8,128)(2,1)}), bf16[2,32,5120]{2,1,0:T(8,128)(2,1)}) %reduce-scatter.3.cloned.1.call-update) | async-done | bytes 655376 | tf_op jit(solution)/shard_map/reduce_scatter | solution.py:234
  160.5 5.3 %collective-permute-start.2 = (bf16[32,5120]{1,0:T(8,128)(2,1)S(1)}, bf16[32,5120]{1,0:T(8,128)(2,1)}, u32[]{:S(2)}, u32[]{:S(2)}) collective-permute-start(bf16[32,5120]{1,0:T(8,128)(2,1)S(1)} %fusion.98), channel_id=1, source_target_pairs={{0,8},{8,16},{9,1},{16,24},{17,9},{25,17},{2,10},{10,18},{11,3},{1... | collective-permute-start | bytes 983048 | tf_op jit(solution)/shard_map/ppermute | solution.py:249
  167.4 3.3 %collective-permute-done = bf16[2,128,5120]{2,1,0:T(8,128)(2,1)} collective-permute-done((bf16[2,128,5120]{2,1,0:T(8,128)(2,1)}, bf16[2,128,5120]{2,1,0:T(8,128)(2,1)}, u32[]{:S(2)}, u32[]{:S(2)}) %collective-permute-start) | collective-permute-done | bytes 2621472 | tf_op jit(solution)/shard_map/ppermute | solution.py:20
  170.7 6.7 %collective-permute-done.1 = bf16[32,5120]{1,0:T(8,128)(2,1)S(1)} collective-permute-done((bf16[32,5120]{1,0:T(8,128)(2,1)S(1)}, bf16[32,5120]{1,0:T(8,128)(2,1)S(1)}, u32[]{:S(2)}, u32[]{:S(2)}) %collective-permute-start.1) | collective-permute-done | bytes 327712 | tf_op jit(solution)/shard_map/ppermute | solution.py:248
  177.4 13.3 %all-gather.9.cloned.1.call-done = bf16[128,5120]{1,0:T(8,128)(2,1)} async-done(((bf16[32,5120]{1,0:T(8,128)(2,1)}), bf16[128,5120]{1,0:T(8,128)(2,1)}) %all-gather.9.cloned.1.call-update) | async-done | bytes 1310736 | tf_op jit(solution)/shard_map/all_gather | solution.py:54
  195.1 3.0 fusion.46
  198.3 48.9 %all-gather.7.cloned.1.call-done = bf16[2,128,5120]{2,1,0:T(8,128)(2,1)} async-done(((bf16[2,32,5120]{2,1,0:T(8,128)(2,1)}), bf16[2,128,5120]{2,1,0:T(8,128)(2,1)}) %all-gather.7.cloned.1.call-update) | async-done | bytes 2621456 | tf_op jit(solution)/shard_map/all_gather | solution.py:54
  249.4 3.5 %fusion.51 = bf16[3,128,128]{2,1,0:T(8,128)(2,1)S(1)} fusion(bf16[1,1,3,5120,128]{4,3,2,1,0:T(8,128)(2,1)} %param.16, bf16[2,128,5120]{2,1,0:T(8,128)(2,1)} %all-gather.7.cloned.1.call-done), kind=kOutput, calls=%fused_computation.57 | convolution fusion | flops 503365632 | bytes 5341184 | tf_op jit(solution)/shard_map/sd,cdn->csn/dot_general | solution.py:86
  254.2 3.0 convolution_convert_fusion
  259.8 2.6 fusion.31
  268.2 3.4 %fusion.20 = f32[128,5120]{1,0:T(8,128)} fusion(bf16[2,128,5120]{2,1,0:T(8,128)(2,1)} %collective-permute-done, bf16[4,128,128]{1,2,0:T(8,128)(2,1)S(1)} %collective-permute-done.4), kind=kOutput, calls=%fused_computation.36 | convolution fusion | flops 167772160 | bytes 3964928 | tf_op jit(solution)/shard_map/sn,sd->nd/dot_general | solution.py:147
  271.6 2.5 fusion.22
  274.1 4.4 %fusion = bf16[1,1,3,5120,128]{3,4,2,1,0:T(8,128)(2,1)} fusion(f32[3,128,5120]{2,1,0:T(8,128)S(1)} %fusion.22, bf16[4,128,128]{1,2,0:T(8,128)(2,1)S(1)} %collective-permute-done.4, bf16[3,128,5120]{2,1,0:T(8,128)(2,1)S(1)} %add_convert_fusion.2, bf16[2,128,5120]{2,1,0:T(8,128)(2,1)} %collective-permute-done), kind=kOutput, calls=%fused_computation.6 | convolution fusion | flops 515112960 | bytes 17170432 | tf_op jit(solution)/shard_map/sd,csn->cdn/dot_general | solution.py:144
  278.6 6.3 %copy.18 = bf16[1,1,3,5120,128]{4,3,2,1,0:T(8,128)(2,1)} copy(bf16[1,1,3,5120,128]{3,4,2,1,0:T(8,128)(2,1)} %fusion) | data formatting | bytes 7864320
  284.8 11.9 %collective-permute-done.6 = bf16[128,5120]{1,0:T(8,128)(2,1)} collective-permute-done((bf16[128,5120]{1,0:T(8,128)(2,1)}, bf16[128,5120]{1,0:T(8,128)(2,1)}, u32[]{:S(2)}, u32[]{:S(2)}) %collective-permute-start.6) | collective-permute-done | bytes 1310752 | tf_op jit(solution)/shard_map/ppermute | solution.py:20
  296.7 3.8 %fusion.7 = bf16[1,1,128,5120]{3,2,1,0:T(8,128)(2,1)} fusion(f32[128,5120]{1,0:T(8,128)S(1)} %fusion.6, f32[128,5120]{1,0:T(8,128)} %fusion.20, bf16[128,5120]{1,0:T(8,128)(2,1)} %collective-permute-done.6, bf16[4,128,128]{1,2,0:T(8,128)(2,1)S(1)} %collective-permute-done.5), kind=kOutput, calls=%fused_computation.15 | convolution fusion | flops 171048960 | bytes 7897088 | tf_op jit(solution)/shard_map/sn,sd->nd/dot_general | solution.py:147
  300.5 7.9 %reduce-scatter.5.cloned.1.call-done = bf16[2,32,5120]{2,1,0:T(8,128)(2,1)} async-done(((bf16[2,128,5120]{2,1,0:T(8,128)(2,1)}), bf16[2,32,5120]{2,1,0:T(8,128)(2,1)}) %reduce-scatter.5.cloned.1.call-update) | async-done | bytes 655376 | tf_op jit(solution)/shard_map/reduce_scatter | solution.py:234
  (145 shorter events, 40.2 us)
Async XLA Ops:
  7.2 85.8 %all-gather.5.cloned.1.call-start = ((), (), s32[]{:S(2)}) async-start(), calls=%async_computation.2 | async-start | bytes 4915200 | tf_op jit(solution)/shard_map/all_gather | solution.py:54
  13.8 142.8 %reduce-scatter.3.cloned.1.call-start = ((), (), s32[]{:S(2)}) async-start(), calls=%async_computation.3 | async-start | bytes 3276800 | tf_op jit(solution)/shard_map/reduce_scatter | solution.py:234
  13.8 6.3 %copy-start.28 = (s32[1,2,5,128]{3,1,2,0:T(2,128)S(1)}, s32[1,2,5,128]{3,1,2,0:T(2,128)}, u32[]{:S(2)}) copy-start(s32[1,2,5,128]{3,1,2,0:T(2,128)} %param.13) | copy-start | bytes 15364
  93.1 6.7 %copy-start.6 = (bf16[1,1,3,5120,128]{4,3,2,1,0:T(8,128)(2,1)S(1)}, bf16[1,1,3,5120,128]{4,3,2,1,0:T(8,128)(2,1)}, u32[]{:S(2)}) copy-start(bf16[1,1,3,5120,128]{4,3,2,1,0:T(8,128)(2,1)} %param.16) | copy-start | bytes 11796484
  105.6 85.2 %all-gather.9.cloned.1.call-start = ((), (), s32[]{:S(2)}) async-start(), calls=%async_computation.6 | async-start | bytes 1638400 | tf_op jit(solution)/shard_map/all_gather | solution.py:54
  110.4 60.3 %collective-permute-start = (bf16[2,128,5120]{2,1,0:T(8,128)(2,1)}, bf16[2,128,5120]{2,1,0:T(8,128)(2,1)}, u32[]{:S(2)}, u32[]{:S(2)}) collective-permute-start(bf16[2,128,5120]{2,1,0:T(8,128)(2,1)} %stack.110), channel_id=1, source_target_pairs={{0,25},{1,24},{8,17},{9,16},{16,9},{17,8},{24,1},{25,0},{2,27},{3,... | collective-permute-start | bytes 7864328 | tf_op jit(solution)/shard_map/ppermute | solution.py:20
  157.6 89.7 %all-gather.7.cloned.1.call-start = ((), (), s32[]{:S(2)}) async-start(), calls=%async_computation.4 | async-start | bytes 3276800 | tf_op jit(solution)/shard_map/all_gather | solution.py:54
  158.1 32.9 %copy-start.19 = (bf16[32,5120]{1,0:T(8,128)(2,1)}, bf16[32,5120]{1,0:T(8,128)(2,1)S(1)}, u32[]{:S(2)}) copy-start(bf16[32,5120]{1,0:T(8,128)(2,1)S(1)} %fusion.86) | copy-start | bytes 983044
  158.2 19.3 %collective-permute-start.1 = (bf16[32,5120]{1,0:T(8,128)(2,1)S(1)}, bf16[32,5120]{1,0:T(8,128)(2,1)S(1)}, u32[]{:S(2)}, u32[]{:S(2)}) collective-permute-start(bf16[32,5120]{1,0:T(8,128)(2,1)S(1)} %fusion.86), channel_id=1, source_target_pairs={{1,9},{8,0},{9,17},{16,8},{17,25},{24,16},{3,11},{10,2},{11,19},{1... | collective-permute-start | bytes 983048 | tf_op jit(solution)/shard_map/ppermute | solution.py:248
  160.5 30.3 %copy-start.16 = (bf16[32,5120]{1,0:T(8,128)(2,1)}, bf16[32,5120]{1,0:T(8,128)(2,1)S(1)}, u32[]{:S(2)}) copy-start(bf16[32,5120]{1,0:T(8,128)(2,1)S(1)} %fusion.98) | copy-start | bytes 983044
  160.5 16.9 %collective-permute-start.2 = (bf16[32,5120]{1,0:T(8,128)(2,1)S(1)}, bf16[32,5120]{1,0:T(8,128)(2,1)}, u32[]{:S(2)}, u32[]{:S(2)}) collective-permute-start(bf16[32,5120]{1,0:T(8,128)(2,1)S(1)} %fusion.98), channel_id=1, source_target_pairs={{0,8},{8,16},{9,1},{16,24},{17,9},{25,17},{2,10},{10,18},{11,3},{1... | collective-permute-start | bytes 983048 | tf_op jit(solution)/shard_map/ppermute | solution.py:249
  166.7 10.7 %copy-start.25 = (bf16[128,128]{1,0:T(8,128)(2,1)}, bf16[128,128]{1,0:T(8,128)(2,1)S(1)}, u32[]{:S(2)}) copy-start(bf16[128,128]{1,0:T(8,128)(2,1)S(1)} %convolution_convert_fusion.8) | copy-start | bytes 98308
  177.4 14.7 %copy-start.21 = (bf16[32,5120]{1,0:T(8,128)(2,1)}, bf16[32,5120]{1,0:T(8,128)(2,1)S(1)}, u32[]{:S(2)}) copy-start(bf16[32,5120]{1,0:T(8,128)(2,1)S(1)} %collective-permute-done.1) | copy-start | bytes 983044
  191.0 7.1 %copy-start.11 = (bf16[32,5120]{1,0:T(8,128)(2,1)}, bf16[32,5120]{1,0:T(8,128)(2,1)S(1)}, u32[]{:S(2)}) copy-start(bf16[32,5120]{1,0:T(8,128)(2,1)S(1)} %get-tuple-element.31) | copy-start | bytes 983044
  192.2 55.1 %copy-start.15 = (bf16[1,1,128,5120]{3,2,1,0:T(8,128)(2,1)S(1)}, bf16[1,1,128,5120]{3,2,1,0:T(8,128)(2,1)}, u32[]{:S(2)}) copy-start(bf16[1,1,128,5120]{3,2,1,0:T(8,128)(2,1)} %param.17) | copy-start | bytes 3932164
  192.2 116.2 %reduce-scatter.5.cloned.1.call-start = ((), (), s32[]{:S(2)}) async-start(), calls=%async_computation.5 | async-start | bytes 3276800 | tf_op jit(solution)/shard_map/reduce_scatter | solution.py:234
  192.4 64.8 %collective-permute-start.3 = (bf16[1,128,5120]{2,1,0:T(8,128)(2,1)S(1)}, bf16[1,128,5120]{2,1,0:T(8,128)(2,1)}, u32[]{:S(2)}, u32[]{:S(2)}) collective-permute-start(bf16[1,128,5120]{2,1,0:T(8,128)(2,1)S(1)} %bitcast.372), channel_id=1, source_target_pairs={{0,25},{1,24},{8,17},{9,16},{16,9},{17,8},{24,1},{25,0},{2,27},{3,... | collective-permute-start | bytes 3932168 | tf_op jit(solution)/shard_map/ppermute | solution.py:20
  193.6 63.6 %collective-permute-start.4 = (bf16[4,128,128]{1,2,0:T(8,128)(2,1)}, bf16[4,128,128]{1,2,0:T(8,128)(2,1)S(1)}, u32[]{:S(2)}, u32[]{:S(2)}) collective-permute-start(bf16[4,128,128]{1,2,0:T(8,128)(2,1)} %pad_maximum_fusion.5), channel_id=1, source_target_pairs={{0,25},{1,24},{8,17},{9,16},{16,9},{17,8},{24,1},{25,0},{2,27},{3,... | collective-permute-start | bytes 393224 | tf_op jit(solution)/shard_map/ppermute | solution.py:20
  247.3 6.9 %copy-start.5 = (bf16[1,384,5120]{2,1,0:T(8,128)(2,1)S(1)}, bf16[1,384,5120]{2,1,0:T(8,128)(2,1)}, u32[]{:S(2)}) copy-start(bf16[1,384,5120]{2,1,0:T(8,128)(2,1)} %pad_bitcast_fusion) | copy-start | bytes 11796484
  262.7 9.0 %collective-permute-start.5 = (bf16[4,128,128]{1,2,0:T(8,128)(2,1)S(1)}, bf16[4,128,128]{1,2,0:T(8,128)(2,1)S(1)}, u32[]{:S(2)}, u32[]{:S(2)}) collective-permute-start(bf16[4,128,128]{1,2,0:T(8,128)(2,1)S(1)} %pad_maximum_fusion.6), channel_id=1, source_target_pairs={{0,25},{1,24},{8,17},{9,16},{16,9},{17,8},{24,1},{25,0},{2,27},{3,... | collective-permute-start | bytes 393224 | tf_op jit(solution)/shard_map/ppermute | solution.py:20
  265.5 31.2 %collective-permute-start.6 = (bf16[128,5120]{1,0:T(8,128)(2,1)}, bf16[128,5120]{1,0:T(8,128)(2,1)}, u32[]{:S(2)}, u32[]{:S(2)}) collective-permute-start(bf16[128,5120]{1,0:T(8,128)(2,1)} %slice_bitcast_fusion.2), channel_id=1, source_target_pairs={{0,25},{1,24},{8,17},{9,16},{16,9},{17,8},{24,1},{25,0},{2,27},{3,... | collective-permute-start | bytes 3932168 | tf_op jit(solution)/shard_map/ppermute | solution.py:20
  284.8 23.6 %copy-start.8 = (bf16[1,1,2,32,5120]{4,3,2,1,0:T(8,128)(2,1)S(1)}, bf16[1,1,2,32,5120]{4,3,2,1,0:T(8,128)(2,1)}, u32[]{:S(2)}) copy-start(bf16[1,1,2,32,5120]{4,3,2,1,0:T(8,128)(2,1)} %param.20) | copy-start | bytes 1966084
  300.5 11.0 %copy-start.20 = (bf16[32,5120]{1,0:T(8,128)(2,1)S(1)}, bf16[32,5120]{1,0:T(8,128)(2,1)}, u32[]{:S(2)}) copy-start(bf16[32,5120]{1,0:T(8,128)(2,1)} %copy-done.19) | copy-start | bytes 983044
  300.5 11.9 %copy-start.17 = (bf16[32,5120]{1,0:T(8,128)(2,1)S(1)}, bf16[32,5120]{1,0:T(8,128)(2,1)}, u32[]{:S(2)}) copy-start(bf16[32,5120]{1,0:T(8,128)(2,1)} %copy-done.16) | copy-start | bytes 983044
  (18 other events, 64.1 us)
Sparse Core Ops, SparseCore 0:
  13.9 79.1 all-gather.4
  105.7 50.7 reduce-scatter.2
  158.7 32.0 all-gather.8
  192.8 54.4 all-gather.6
  257.4 51.0 reduce-scatter.4

commit v15 on v14

--- a/solution.py
+++ b/solution.py
@@ -88,8 +88,9 @@
         ).astype(jnp.bfloat16)
         return projected.reshape(3, seq_len, heads_here, HD)
 
-    def forward_part(normed_full, seg_mask):
-        heads_view = heads_of(normed_full)
+    def forward_part(normed_full, seg_mask, heads_view=None):
+        if heads_view is None:
+            heads_view = heads_of(normed_full)
         mixed = (
             attend(heads_view[0], heads_view[1], heads_view[2], seg_mask)
             .reshape(seq_len, inner_here)
@@ -97,8 +98,9 @@
         )
         return mixed
 
-    def backward_part(normed_full, upstream_full, seg_mask):
-        heads_view = heads_of(normed_full)
+    def backward_part(normed_full, upstream_full, seg_mask, heads_view=None):
+        if heads_view is None:
+            heads_view = heads_of(normed_full)
         primal, pull_attend = jax.vjp(
             lambda query_part, key_part, value_part: attend(
                 query_part, key_part, value_part, seg_mask
@@ -209,11 +211,22 @@
                 [upstream, saved_normed[0], normed_rows(current)]
             )
             first_sent = to_partner(jnp.stack([upstream_full, backward_normed_full[0]]))
+            paired = jnp.einsum(
+                "tsd,cdn->tcsn",
+                jnp.stack([backward_normed_full[0], forward_normed_full]),
+                qkv_weight,
+                preferred_element_type=jnp.float32,
+            ).astype(jnp.bfloat16)
+            step_heads = [paired[t].reshape(3, seq_len, heads_here, HD) for t in range(2)]
         else:
+            step_heads = [None, None]
             upstream_full, forward_normed_full = gathered([upstream, normed_rows(current)])
             inbox[f"rows{step_index}"] = to_partner(upstream_full)
         d_projected, mixed = backward_part(
-            backward_normed_full[step_index], upstream_full, mask_for(1, step_index + position)
+            backward_normed_full[step_index],
+            upstream_full,
+            mask_for(1, step_index + position),
+            step_heads[0],
         )
         upstream_fulls.append(upstream_full)
         d_projecteds.append(d_projected)
@@ -224,7 +237,7 @@
         else:
             inbox[f"small{step_index}"] = to_partner(small)
         forward_mixed = forward_part(
-            forward_normed_full, mask_for(0, step_index - position + sections - 1)
+            forward_normed_full, mask_for(0, step_index - position + sections - 1), step_heads[1]
         )
         both_parts, tie_scatter = lax.optimization_barrier(
             (projected_back(d_projected, forward_mixed), tie_scatter)

time: 321 us -> 320 us (level)
    dot_general x4 -> x2, matrix products: 12.3 us -> 6.45 us  [heads_of(): jnp.einsum('sd,cdn->csn', normed_full, qkv_weight, preferred_element_type...]
    dot_general x0 -> x1, matrix products: none -> 4.57 us  [shards(): jnp.einsum('tsd,cdn->tcsn', jnp.stack([backward_normed_full[0], forward_n...]
    unnamed x61 -> x59, local copies, waits for them, and re-layouts: 7.13 us -> 7.12 us
where the time goes in v15:
time: 320 us; the launch traced here: 319 us
  waiting for transfers between devices  205 us (64%)
  matrix products  47.8 us (15%)
  local copies, waits for them, and re-layouts  24.6 us (8%)
  between operations  14.4 us (4%)
  starting transfers between devices  14.1 us (4%)
  other arithmetic  12.3 us (4%)
    all_gather x3, waiting for transfers between devices, gathered(): full = lax.all_gather(jnp.stack(blocks), 'tp', axis=1, tiled=True)  131 us
    reduce_scatter x2, waiting for transfers between devices, shards(): lax.psum_scatter(both_parts, 'tp', scatter_dimension=1, tiled=True)  52.4 us
    ppermute x5, waiting for transfers between devices, flipped(): lax.ppermute(value, axis, [(i, i ^ mask) for i in range(lax.axis_size(axi...  15.3 us
    dot_general x4, matrix products, weight_terms(): jnp.einsum('sd,csn->cdn', normed_full, d_projected, preferred_element_typ...  10.7 us
    dot_general x4, matrix products, weight_terms(): jnp.einsum('sn,sd->nd', mixed, upstream_full, preferred_element_type=jnp....  9.49 us
    unnamed x59, local copies, waits for them, and re-layouts  7.12 us
    ppermute x5, starting transfers between devices, flipped(): lax.ppermute(value, axis, [(i, i ^ mask) for i in range(lax.axis_size(axi...  7.08 us
    ppermute x1, waiting for transfers between devices, shards(): backward_in = lax.ppermute(backward_out, pair_axes, down_pairs)  6.69 us
  transfers between devices with their start and end apart: 12, of which 8 were waited for; matrix products, arithmetic and copies ran while one was open for 19% of the time, Pallas kernels for 0%

profile of v15, /device:TPU:0, one launch (start us, length us, event | category | flops | bytes accessed | tf_op | source)
XLA Modules:
  0.0 318.5 jit_solution(18364899609434030031)
XLA Ops:
  13.8 6.3 %copy.15 = bf16[3,128,5120]{2,1,0:T(8,128)(2,1)} copy(bf16[3,128,5120]{1,2,0:T(8,128)(2,1)} %bitcast.361) | data formatting | bytes 7864320 | tf_op jit(solution)/shard_map/transpose | solution.py:120
  20.6 3.7 %pad_bitcast_fusion = bf16[1,384,5120]{2,1,0:T(8,128)(2,1)} fusion(bf16[128,5120]{1,0:T(8,128)(2,1)} %bitcast.363), kind=kLoop, calls=%fused_computation.28 | loop fusion | bytes 5242880 | tf_op jit(solution)/shard_map/stack | solution.py:124
  24.3 68.7 %all-gather.5.cloned.1.call-done = bf16[3,128,5120]{2,1,0:T(8,128)(2,1)} async-done(((bf16[3,32,5120]{2,1,0:T(8,128)(2,1)}), bf16[3,128,5120]{2,1,0:T(8,128)(2,1)}) %all-gather.5.cloned.1.call-update) | async-done | bytes 3932176 | tf_op jit(solution)/shard_map/all_gather | solution.py:54
  93.0 4.6 %fusion.33 = bf16[2,3,128,128]{3,2,1,0:T(8,128)(2,1)S(1)} fusion(bf16[1,1,3,5120,128]{4,3,2,1,0:T(8,128)(2,1)} %param.16, bf16[3,128,5120]{2,1,0:T(8,128)(2,1)} %all-gather.5.cloned.1.call-done), kind=kOutput, calls=%fused_computation.47 | convolution fusion | flops 1006731264 | bytes 6750208 | tf_op jit(solution)/shard_map/tsd,cdn->tcsn/dot_general | solution.py:214
  97.9 2.0 fusion.68
  101.3 3.0 convolution_convert_fusion.1
  105.6 3.5 %stack.115 = bf16[2,128,5120]{2,1,0:T(8,128)(2,1)} slice(bf16[3,128,5120]{2,1,0:T(8,128)(2,1)} %all-gather.5.cloned.1.call-done), slice={[0:2], [0:128], [0:5120]} | slice | bytes 5242880 | tf_op jit(solution)/shard_map/stack | solution.py:213
  110.8 44.5 %reduce-scatter.3.cloned.1.call-done = bf16[2,32,5120]{2,1,0:T(8,128)(2,1)} async-done(((bf16[2,128,5120]{2,1,0:T(8,128)(2,1)}), bf16[2,32,5120]{2,1,0:T(8,128)(2,1)}) %reduce-scatter.3.cloned.1.call-update) | async-done | bytes 655376 | tf_op jit(solution)/shard_map/reduce_scatter | solution.py:247
  159.2 5.3 %collective-permute-start.2 = (bf16[32,5120]{1,0:T(8,128)(2,1)S(1)}, bf16[32,5120]{1,0:T(8,128)(2,1)}, u32[]{:S(2)}, u32[]{:S(2)}) collective-permute-start(bf16[32,5120]{1,0:T(8,128)(2,1)S(1)} %fusion.90), channel_id=1, source_target_pairs={{0,8},{8,16},{9,1},{16,24},{17,9},{25,17},{2,10},{10,18},{11,3},{1... | collective-permute-start | bytes 983048 | tf_op jit(solution)/shard_map/ppermute | solution.py:262
  166.1 3.3 %collective-permute-done = bf16[2,128,5120]{2,1,0:T(8,128)(2,1)} collective-permute-done((bf16[2,128,5120]{2,1,0:T(8,128)(2,1)}, bf16[2,128,5120]{2,1,0:T(8,128)(2,1)}, u32[]{:S(2)}, u32[]{:S(2)}) %collective-permute-start) | collective-permute-done | bytes 2621472 | tf_op jit(solution)/shard_map/ppermute | solution.py:20
  169.4 6.7 %collective-permute-done.1 = bf16[32,5120]{1,0:T(8,128)(2,1)S(1)} collective-permute-done((bf16[32,5120]{1,0:T(8,128)(2,1)S(1)}, bf16[32,5120]{1,0:T(8,128)(2,1)S(1)}, u32[]{:S(2)}, u32[]{:S(2)}) %collective-permute-start.1) | collective-permute-done | bytes 327712 | tf_op jit(solution)/shard_map/ppermute | solution.py:261
  176.1 13.3 %all-gather.9.cloned.1.call-done = bf16[128,5120]{1,0:T(8,128)(2,1)} async-done(((bf16[32,5120]{1,0:T(8,128)(2,1)}), bf16[128,5120]{1,0:T(8,128)(2,1)}) %all-gather.9.cloned.1.call-update) | async-done | bytes 1310736 | tf_op jit(solution)/shard_map/all_gather | solution.py:54
  193.8 3.0 fusion.44
  197.0 48.9 %all-gather.7.cloned.1.call-done = bf16[2,128,5120]{2,1,0:T(8,128)(2,1)} async-done(((bf16[2,32,5120]{2,1,0:T(8,128)(2,1)}), bf16[2,128,5120]{2,1,0:T(8,128)(2,1)}) %all-gather.7.cloned.1.call-update) | async-done | bytes 2621456 | tf_op jit(solution)/shard_map/all_gather | solution.py:54
  248.1 3.5 %fusion.49 = bf16[3,128,128]{2,1,0:T(8,128)(2,1)S(1)} fusion(bf16[1,1,3,5120,128]{4,3,2,1,0:T(8,128)(2,1)} %param.16, bf16[2,128,5120]{2,1,0:T(8,128)(2,1)} %all-gather.7.cloned.1.call-done), kind=kOutput, calls=%fused_computation.55 | convolution fusion | flops 503365632 | bytes 5341184 | tf_op jit(solution)/shard_map/sd,cdn->csn/dot_general | solution.py:86
  252.9 3.0 convolution_convert_fusion
  258.5 2.6 fusion.18
  266.9 3.4 %fusion.19 = f32[128,5120]{1,0:T(8,128)} fusion(bf16[2,128,5120]{2,1,0:T(8,128)(2,1)} %collective-permute-done, bf16[4,128,128]{1,2,0:T(8,128)(2,1)S(1)} %collective-permute-done.4), kind=kOutput, calls=%fused_computation.35 | convolution fusion | flops 167772160 | bytes 3964928 | tf_op jit(solution)/shard_map/sn,sd->nd/dot_general | solution.py:149
  270.3 2.5 fusion.21
  272.8 4.4 %fusion = bf16[1,1,3,5120,128]{3,4,2,1,0:T(8,128)(2,1)} fusion(f32[3,128,5120]{2,1,0:T(8,128)S(1)} %fusion.21, bf16[4,128,128]{1,2,0:T(8,128)(2,1)S(1)} %collective-permute-done.4, bf16[3,128,5120]{2,1,0:T(8,128)(2,1)S(1)} %add_convert_fusion.2, bf16[2,128,5120]{2,1,0:T(8,128)(2,1)} %collective-permute-done), kind=kOutput, calls=%fused_computation.6 | convolution fusion | flops 515112960 | bytes 17170432 | tf_op jit(solution)/shard_map/sd,csn->cdn/dot_general | solution.py:146
  277.3 6.3 %copy.18 = bf16[1,1,3,5120,128]{4,3,2,1,0:T(8,128)(2,1)} copy(bf16[1,1,3,5120,128]{3,4,2,1,0:T(8,128)(2,1)} %fusion) | data formatting | bytes 7864320
  283.5 11.9 %collective-permute-done.6 = bf16[128,5120]{1,0:T(8,128)(2,1)} collective-permute-done((bf16[128,5120]{1,0:T(8,128)(2,1)}, bf16[128,5120]{1,0:T(8,128)(2,1)}, u32[]{:S(2)}, u32[]{:S(2)}) %collective-permute-start.6) | collective-permute-done | bytes 1310752 | tf_op jit(solution)/shard_map/ppermute | solution.py:20
  295.4 3.8 %fusion.7 = bf16[1,1,128,5120]{3,2,1,0:T(8,128)(2,1)} fusion(f32[128,5120]{1,0:T(8,128)S(1)} %fusion.6, f32[128,5120]{1,0:T(8,128)} %fusion.19, bf16[128,5120]{1,0:T(8,128)(2,1)} %collective-permute-done.6, bf16[4,128,128]{1,2,0:T(8,128)(2,1)S(1)} %collective-permute-done.5), kind=kOutput, calls=%fused_computation.15 | convolution fusion | flops 171048960 | bytes 7897088 | tf_op jit(solution)/shard_map/sn,sd->nd/dot_general | solution.py:149
  299.2 7.9 %reduce-scatter.5.cloned.1.call-done = bf16[2,32,5120]{2,1,0:T(8,128)(2,1)} async-done(((bf16[2,128,5120]{2,1,0:T(8,128)(2,1)}), bf16[2,32,5120]{2,1,0:T(8,128)(2,1)}) %reduce-scatter.5.cloned.1.call-update) | async-done | bytes 655376 | tf_op jit(solution)/shard_map/reduce_scatter | solution.py:247
  (142 shorter events, 38.1 us)
Async XLA Ops:
  7.2 85.8 %all-gather.5.cloned.1.call-start = ((), (), s32[]{:S(2)}) async-start(), calls=%async_computation.2 | async-start | bytes 4915200 | tf_op jit(solution)/shard_map/all_gather | solution.py:54
  13.7 141.5 %reduce-scatter.3.cloned.1.call-start = ((), (), s32[]{:S(2)}) async-start(), calls=%async_computation.3 | async-start | bytes 3276800 | tf_op jit(solution)/shard_map/reduce_scatter | solution.py:247
  13.8 6.3 %copy-start.27 = (s32[1,2,5,128]{3,1,2,0:T(2,128)S(1)}, s32[1,2,5,128]{3,1,2,0:T(2,128)}, u32[]{:S(2)}) copy-start(s32[1,2,5,128]{3,1,2,0:T(2,128)} %param.13) | copy-start | bytes 15364
  93.0 8.3 %copy-start.4 = (bf16[1,384,5120]{2,1,0:T(8,128)(2,1)S(1)}, bf16[1,384,5120]{2,1,0:T(8,128)(2,1)}, u32[]{:S(2)}) copy-start(bf16[1,384,5120]{2,1,0:T(8,128)(2,1)} %pad_bitcast_fusion) | copy-start | bytes 11796484
  104.3 85.2 %all-gather.9.cloned.1.call-start = ((), (), s32[]{:S(2)}) async-start(), calls=%async_computation.6 | async-start | bytes 1638400 | tf_op jit(solution)/shard_map/all_gather | solution.py:54
  109.1 60.3 %collective-permute-start = (bf16[2,128,5120]{2,1,0:T(8,128)(2,1)}, bf16[2,128,5120]{2,1,0:T(8,128)(2,1)}, u32[]{:S(2)}, u32[]{:S(2)}) collective-permute-start(bf16[2,128,5120]{2,1,0:T(8,128)(2,1)} %stack.115), channel_id=1, source_target_pairs={{0,25},{1,24},{8,17},{9,16},{16,9},{17,8},{24,1},{25,0},{2,27},{3,... | collective-permute-start | bytes 7864328 | tf_op jit(solution)/shard_map/ppermute | solution.py:20
  156.3 89.7 %all-gather.7.cloned.1.call-start = ((), (), s32[]{:S(2)}) async-start(), calls=%async_computation.4 | async-start | bytes 3276800 | tf_op jit(solution)/shard_map/all_gather | solution.py:54
  156.8 32.9 %copy-start.18 = (bf16[32,5120]{1,0:T(8,128)(2,1)}, bf16[32,5120]{1,0:T(8,128)(2,1)S(1)}, u32[]{:S(2)}) copy-start(bf16[32,5120]{1,0:T(8,128)(2,1)S(1)} %fusion.78) | copy-start | bytes 983044
  156.9 19.3 %collective-permute-start.1 = (bf16[32,5120]{1,0:T(8,128)(2,1)S(1)}, bf16[32,5120]{1,0:T(8,128)(2,1)S(1)}, u32[]{:S(2)}, u32[]{:S(2)}) collective-permute-start(bf16[32,5120]{1,0:T(8,128)(2,1)S(1)} %fusion.78), channel_id=1, source_target_pairs={{1,9},{8,0},{9,17},{16,8},{17,25},{24,16},{3,11},{10,2},{11,19},{1... | collective-permute-start | bytes 983048 | tf_op jit(solution)/shard_map/ppermute | solution.py:261
  159.2 30.3 %copy-start.15 = (bf16[32,5120]{1,0:T(8,128)(2,1)}, bf16[32,5120]{1,0:T(8,128)(2,1)S(1)}, u32[]{:S(2)}) copy-start(bf16[32,5120]{1,0:T(8,128)(2,1)S(1)} %fusion.90) | copy-start | bytes 983044
  159.2 16.9 %collective-permute-start.2 = (bf16[32,5120]{1,0:T(8,128)(2,1)S(1)}, bf16[32,5120]{1,0:T(8,128)(2,1)}, u32[]{:S(2)}, u32[]{:S(2)}) collective-permute-start(bf16[32,5120]{1,0:T(8,128)(2,1)S(1)} %fusion.90), channel_id=1, source_target_pairs={{0,8},{8,16},{9,1},{16,24},{17,9},{25,17},{2,10},{10,18},{11,3},{1... | collective-permute-start | bytes 983048 | tf_op jit(solution)/shard_map/ppermute | solution.py:262
  165.4 10.7 %copy-start.24 = (bf16[128,128]{1,0:T(8,128)(2,1)}, bf16[128,128]{1,0:T(8,128)(2,1)S(1)}, u32[]{:S(2)}) copy-start(bf16[128,128]{1,0:T(8,128)(2,1)S(1)} %convolution_convert_fusion.8) | copy-start | bytes 98308
  176.1 14.7 %copy-start.20 = (bf16[32,5120]{1,0:T(8,128)(2,1)}, bf16[32,5120]{1,0:T(8,128)(2,1)S(1)}, u32[]{:S(2)}) copy-start(bf16[32,5120]{1,0:T(8,128)(2,1)S(1)} %collective-permute-done.1) | copy-start | bytes 983044
  189.7 7.1 %copy-start.10 = (bf16[32,5120]{1,0:T(8,128)(2,1)}, bf16[32,5120]{1,0:T(8,128)(2,1)S(1)}, u32[]{:S(2)}) copy-start(bf16[32,5120]{1,0:T(8,128)(2,1)S(1)} %get-tuple-element.31) | copy-start | bytes 983044
  190.9 55.1 %copy-start.14 = (bf16[1,1,128,5120]{3,2,1,0:T(8,128)(2,1)S(1)}, bf16[1,1,128,5120]{3,2,1,0:T(8,128)(2,1)}, u32[]{:S(2)}) copy-start(bf16[1,1,128,5120]{3,2,1,0:T(8,128)(2,1)} %param.17) | copy-start | bytes 3932164
  190.9 116.2 %reduce-scatter.5.cloned.1.call-start = ((), (), s32[]{:S(2)}) async-start(), calls=%async_computation.5 | async-start | bytes 3276800 | tf_op jit(solution)/shard_map/reduce_scatter | solution.py:247
  191.1 64.8 %collective-permute-start.3 = (bf16[1,128,5120]{2,1,0:T(8,128)(2,1)S(1)}, bf16[1,128,5120]{2,1,0:T(8,128)(2,1)}, u32[]{:S(2)}, u32[]{:S(2)}) collective-permute-start(bf16[1,128,5120]{2,1,0:T(8,128)(2,1)S(1)} %bitcast.362), channel_id=1, source_target_pairs={{0,25},{1,24},{8,17},{9,16},{16,9},{17,8},{24,1},{25,0},{2,27},{3,... | collective-permute-start | bytes 3932168 | tf_op jit(solution)/shard_map/ppermute | solution.py:20
  192.3 63.6 %collective-permute-start.4 = (bf16[4,128,128]{1,2,0:T(8,128)(2,1)}, bf16[4,128,128]{1,2,0:T(8,128)(2,1)S(1)}, u32[]{:S(2)}, u32[]{:S(2)}) collective-permute-start(bf16[4,128,128]{1,2,0:T(8,128)(2,1)} %pad_maximum_fusion.5), channel_id=1, source_target_pairs={{0,25},{1,24},{8,17},{9,16},{16,9},{17,8},{24,1},{25,0},{2,27},{3,... | collective-permute-start | bytes 393224 | tf_op jit(solution)/shard_map/ppermute | solution.py:20
  246.0 6.9 %copy-start.5 = (bf16[1,384,5120]{2,1,0:T(8,128)(2,1)S(1)}, bf16[1,384,5120]{2,1,0:T(8,128)(2,1)}, u32[]{:S(2)}) copy-start(bf16[1,384,5120]{2,1,0:T(8,128)(2,1)} %pad_bitcast_fusion) | copy-start | bytes 11796484
  261.3 9.0 %collective-permute-start.5 = (bf16[4,128,128]{1,2,0:T(8,128)(2,1)S(1)}, bf16[4,128,128]{1,2,0:T(8,128)(2,1)S(1)}, u32[]{:S(2)}, u32[]{:S(2)}) collective-permute-start(bf16[4,128,128]{1,2,0:T(8,128)(2,1)S(1)} %pad_maximum_fusion.6), channel_id=1, source_target_pairs={{0,25},{1,24},{8,17},{9,16},{16,9},{17,8},{24,1},{25,0},{2,27},{3,... | collective-permute-start | bytes 393224 | tf_op jit(solution)/shard_map/ppermute | solution.py:20
  264.2 31.3 %collective-permute-start.6 = (bf16[128,5120]{1,0:T(8,128)(2,1)}, bf16[128,5120]{1,0:T(8,128)(2,1)}, u32[]{:S(2)}, u32[]{:S(2)}) collective-permute-start(bf16[128,5120]{1,0:T(8,128)(2,1)} %slice_bitcast_fusion.6), channel_id=1, source_target_pairs={{0,25},{1,24},{8,17},{9,16},{16,9},{17,8},{24,1},{25,0},{2,27},{3,... | collective-permute-start | bytes 3932168 | tf_op jit(solution)/shard_map/ppermute | solution.py:20
  283.5 23.6 %copy-start.7 = (bf16[1,1,2,32,5120]{4,3,2,1,0:T(8,128)(2,1)S(1)}, bf16[1,1,2,32,5120]{4,3,2,1,0:T(8,128)(2,1)}, u32[]{:S(2)}) copy-start(bf16[1,1,2,32,5120]{4,3,2,1,0:T(8,128)(2,1)} %param.20) | copy-start | bytes 1966084
  299.2 11.0 %copy-start.19 = (bf16[32,5120]{1,0:T(8,128)(2,1)S(1)}, bf16[32,5120]{1,0:T(8,128)(2,1)}, u32[]{:S(2)}) copy-start(bf16[32,5120]{1,0:T(8,128)(2,1)} %copy-done.18) | copy-start | bytes 983044
  299.2 11.9 %copy-start.16 = (bf16[32,5120]{1,0:T(8,128)(2,1)S(1)}, bf16[32,5120]{1,0:T(8,128)(2,1)}, u32[]{:S(2)}) copy-start(bf16[32,5120]{1,0:T(8,128)(2,1)} %copy-done.15) | copy-start | bytes 983044
  (17 other events, 58.8 us)
Sparse Core Ops, SparseCore 0:
  13.8 79.1 all-gather.4
  104.4 50.7 reduce-scatter.2
  157.4 32.0 all-gather.8
  191.5 54.4 all-gather.6
  256.0 51.0 reduce-scatter.4

commit v16 on v15

--- a/solution.py
+++ b/solution.py
@@ -207,10 +207,18 @@
         current = jnp.where(position == 0, embedded, forward_in)
         upstream = jnp.where(position == sections - 1, cotangent[0, step_index], backward_in)
         if step_index == 0:
-            upstream_full, backward_normed_full[0], forward_normed_full = gathered(
-                [upstream, saved_normed[0], normed_rows(current)]
+            first_rows = lax.all_gather(
+                jnp.stack([upstream, saved_normed[0], normed_rows(current)]),
+                "tp",
+                axis=1,
+                tiled=True,
             )
-            first_sent = to_partner(jnp.stack([upstream_full, backward_normed_full[0]]))
+            upstream_full, backward_normed_full[0], forward_normed_full = (
+                first_rows[0],
+                first_rows[1],
+                first_rows[2],
+            )
+            first_sent = to_partner(first_rows)
             paired = jnp.einsum(
                 "tsd,cdn->tcsn",
                 jnp.stack([backward_normed_full[0], forward_normed_full]),

time: 320 us -> 337 us (1.053)
  waiting for transfers between devices: 205 us -> 226 us
  local copies, waits for them, and re-layouts: 24.6 us -> 21.1 us
    all_gather x3 -> x2, waiting for transfers between devices: 131 us -> 54.7 us  [gathered(): full = lax.all_gather(jnp.stack(blocks), 'tp', axis=1, tiled=True)]
    all_gather x0 -> x1, waiting for transfers between devices: none -> 68.8 us  [shards(): lax.all_gather(jnp.stack([upstream, saved_normed[0], normed_rows(current)...]
    ppermute x5, waiting for transfers between devices: 15.3 us -> 40 us  [flipped(): lax.ppermute(value, axis, [(i, i ^ mask) for i in range(lax.axis_size(axi...]
    another operation x1 -> x0, local copies, waits for them, and re-layouts: 3.47 us -> none  [shards(): first_sent = to_partner(jnp.stack([upstream_full, backward_normed_full[0]]))]
    reduce_scatter x2, waiting for transfers between devices: 52.4 us -> 55.8 us  [shards(): lax.psum_scatter(both_parts, 'tp', scatter_dimension=1, tiled=True)]
  transfers between devices with their start and end apart: 12 -> 12, of which waited for: 8 -> 7; matrix products, arithmetic and copies ran while one was open for 19% -> 17% of each run, Pallas kernels for 0% -> 0%
where the time goes in v16:
time: 337 us; the launch traced here: 336 us
  waiting for transfers between devices  226 us (67%)
  matrix products  47.6 us (14%)
  local copies, waits for them, and re-layouts  21.1 us (6%)
  between operations  14.4 us (4%)
  starting transfers between devices  14.1 us (4%)
  other arithmetic  12.3 us (4%)
    all_gather x1, waiting for transfers between devices, shards(): lax.all_gather(jnp.stack([upstream, saved_normed[0], normed_rows(current)...  68.8 us
    reduce_scatter x2, waiting for transfers between devices, shards(): lax.psum_scatter(both_parts, 'tp', scatter_dimension=1, tiled=True)  55.8 us
    all_gather x2, waiting for transfers between devices, gathered(): full = lax.all_gather(jnp.stack(blocks), 'tp', axis=1, tiled=True)  54.7 us
    ppermute x5, waiting for transfers between devices, flipped(): lax.ppermute(value, axis, [(i, i ^ mask) for i in range(lax.axis_size(axi...  40 us
    dot_general x4, matrix products, weight_terms(): jnp.einsum('sd,csn->cdn', normed_full, d_projected, preferred_element_typ...  10.8 us
    dot_general x4, matrix products, weight_terms(): jnp.einsum('sn,sd->nd', mixed, upstream_full, preferred_element_type=jnp....  9.41 us
    unnamed x59, local copies, waits for them, and re-layouts  7.15 us
    ppermute x5, starting transfers between devices, flipped(): lax.ppermute(value, axis, [(i, i ^ mask) for i in range(lax.axis_size(axi...  7.12 us
  transfers between devices with their start and end apart: 12, of which 7 were waited for; matrix products, arithmetic and copies ran while one was open for 17% of the time, Pallas kernels for 0%

profile of v16, /device:TPU:0, one launch (start us, length us, event | category | flops | bytes accessed | tf_op | source)
XLA Modules:
  0.0 335.6 jit_solution(9752184120081034381)
XLA Ops:
  13.8 6.2 %copy.15 = bf16[3,128,5120]{2,1,0:T(8,128)(2,1)} copy(bf16[3,128,5120]{1,2,0:T(8,128)(2,1)} %bitcast.361) | data formatting | bytes 7864320 | tf_op jit(solution)/shard_map/transpose | solution.py:120
  20.6 3.7 %pad_bitcast_fusion = bf16[1,384,5120]{2,1,0:T(8,128)(2,1)} fusion(bf16[128,5120]{1,0:T(8,128)(2,1)} %bitcast.363), kind=kLoop, calls=%fused_computation.28 | loop fusion | bytes 5242880 | tf_op jit(solution)/shard_map/stack | solution.py:124
  24.2 68.8 %all-gather.5.cloned.1.call-done = bf16[3,128,5120]{2,1,0:T(8,128)(2,1)} async-done(((bf16[3,32,5120]{2,1,0:T(8,128)(2,1)}), bf16[3,128,5120]{2,1,0:T(8,128)(2,1)}) %all-gather.5.cloned.1.call-update) | async-done | bytes 3932176 | tf_op jit(solution)/shard_map/all_gather | solution.py:210
  93.0 4.6 %fusion.33 = bf16[2,3,128,128]{3,2,1,0:T(8,128)(2,1)S(1)} fusion(bf16[1,1,3,5120,128]{4,3,2,1,0:T(8,128)(2,1)} %param.16, bf16[3,128,5120]{2,1,0:T(8,128)(2,1)} %all-gather.5.cloned.1.call-done), kind=kOutput, calls=%fused_computation.47 | convolution fusion | flops 1006731264 | bytes 6750208 | tf_op jit(solution)/shard_map/tsd,cdn->tcsn/dot_general | solution.py:222
  97.9 2.0 fusion.68
  101.3 2.9 convolution_convert_fusion.1
  107.3 47.9 %reduce-scatter.3.cloned.1.call-done = bf16[2,32,5120]{2,1,0:T(8,128)(2,1)} async-done(((bf16[2,128,5120]{2,1,0:T(8,128)(2,1)}), bf16[2,32,5120]{2,1,0:T(8,128)(2,1)}) %reduce-scatter.3.cloned.1.call-update) | async-done | bytes 655376 | tf_op jit(solution)/shard_map/reduce_scatter | solution.py:255
  159.2 5.3 %collective-permute-start.2 = (bf16[32,5120]{1,0:T(8,128)(2,1)S(1)}, bf16[32,5120]{1,0:T(8,128)(2,1)}, u32[]{:S(2)}, u32[]{:S(2)}) collective-permute-start(bf16[32,5120]{1,0:T(8,128)(2,1)S(1)} %fusion.90), channel_id=1, source_target_pairs={{0,8},{8,16},{9,1},{16,24},{17,9},{25,17},{2,10},{10,18},{11,3},{1... | collective-permute-start | bytes 983048 | tf_op jit(solution)/shard_map/ppermute | solution.py:270
  166.1 28.0 %collective-permute-done = bf16[3,128,5120]{2,1,0:T(8,128)(2,1)} collective-permute-done((bf16[3,128,5120]{2,1,0:T(8,128)(2,1)}, bf16[3,128,5120]{2,1,0:T(8,128)(2,1)}, u32[]{:S(2)}, u32[]{:S(2)}) %collective-permute-start) | collective-permute-done | bytes 3932192 | tf_op jit(solution)/shard_map/ppermute | solution.py:20
  194.1 6.7 %collective-permute-done.1 = bf16[32,5120]{1,0:T(8,128)(2,1)S(1)} collective-permute-done((bf16[32,5120]{1,0:T(8,128)(2,1)S(1)}, bf16[32,5120]{1,0:T(8,128)(2,1)S(1)}, u32[]{:S(2)}, u32[]{:S(2)}) %collective-permute-start.1) | collective-permute-done | bytes 327712 | tf_op jit(solution)/shard_map/ppermute | solution.py:269
  205.2 3.0 fusion.44
  208.4 54.7 %all-gather.7.cloned.1.call-done = bf16[2,128,5120]{2,1,0:T(8,128)(2,1)} async-done(((bf16[2,32,5120]{2,1,0:T(8,128)(2,1)}), bf16[2,128,5120]{2,1,0:T(8,128)(2,1)}) %all-gather.7.cloned.1.call-update) | async-done | bytes 2621456 | tf_op jit(solution)/shard_map/all_gather | solution.py:54
  263.1 2.0 fusion.67
  265.2 3.5 %fusion.49 = bf16[3,128,128]{2,1,0:T(8,128)(2,1)S(1)} fusion(bf16[1,1,3,5120,128]{4,3,2,1,0:T(8,128)(2,1)} %param.16, bf16[2,128,5120]{2,1,0:T(8,128)(2,1)} %all-gather.7.cloned.1.call-done), kind=kOutput, calls=%fused_computation.55 | convolution fusion | flops 503365632 | bytes 5341184 | tf_op jit(solution)/shard_map/sd,cdn->csn/dot_general | solution.py:86
  270.0 2.9 convolution_convert_fusion
  275.5 2.6 fusion.18
  284.0 3.3 fusion.19
  287.3 2.5 fusion.21
  289.8 4.5 %fusion = bf16[1,1,3,5120,128]{3,4,2,1,0:T(8,128)(2,1)} fusion(f32[3,128,5120]{2,1,0:T(8,128)S(1)} %fusion.21, bf16[4,128,128]{1,2,0:T(8,128)(2,1)S(1)} %collective-permute-done.4, bf16[3,128,5120]{2,1,0:T(8,128)(2,1)S(1)} %add_convert_fusion.2, bf16[3,128,5120]{2,1,0:T(8,128)(2,1)} %collective-permute-done), kind=kOutput, calls=%fused_computation.6 | convolution fusion | flops 515112960 | bytes 17170432 | tf_op jit(solution)/shard_map/sd,csn->cdn/dot_general | solution.py:146
  294.2 6.3 %copy.18 = bf16[1,1,3,5120,128]{4,3,2,1,0:T(8,128)(2,1)} copy(bf16[1,1,3,5120,128]{3,4,2,1,0:T(8,128)(2,1)} %fusion) | data formatting | bytes 7864320
  300.5 12.0 %collective-permute-done.6 = bf16[128,5120]{1,0:T(8,128)(2,1)} collective-permute-done((bf16[128,5120]{1,0:T(8,128)(2,1)}, bf16[128,5120]{1,0:T(8,128)(2,1)}, u32[]{:S(2)}, u32[]{:S(2)}) %collective-permute-start.6) | collective-permute-done | bytes 1310752 | tf_op jit(solution)/shard_map/ppermute | solution.py:20
  312.5 3.8 %fusion.7 = bf16[1,1,128,5120]{3,2,1,0:T(8,128)(2,1)} fusion(f32[128,5120]{1,0:T(8,128)S(1)} %fusion.6, f32[128,5120]{1,0:T(8,128)} %fusion.19, bf16[128,5120]{1,0:T(8,128)(2,1)} %collective-permute-done.6, bf16[4,128,128]{1,2,0:T(8,128)(2,1)S(1)} %collective-permute-done.5), kind=kOutput, calls=%fused_computation.15 | convolution fusion | flops 171048960 | bytes 7897088 | tf_op jit(solution)/shard_map/sn,sd->nd/dot_general | solution.py:149
  316.3 7.9 %reduce-scatter.5.cloned.1.call-done = bf16[2,32,5120]{2,1,0:T(8,128)(2,1)} async-done(((bf16[2,128,5120]{2,1,0:T(8,128)(2,1)}), bf16[2,32,5120]{2,1,0:T(8,128)(2,1)}) %reduce-scatter.5.cloned.1.call-update) | async-done | bytes 655376 | tf_op jit(solution)/shard_map/reduce_scatter | solution.py:255
  325.3 1.9 fusion.92
  (141 shorter events, 34.4 us)
Async XLA Ops:
  7.2 5.4 %copy-start.17 = (bf16[1,1,32,5120]{3,2,1,0:T(8,128)(2,1)S(1)}, bf16[1,1,32,5120]{3,2,1,0:T(8,128)(2,1)}, u32[]{:S(2)}) copy-start(bf16[1,1,32,5120]{3,2,1,0:T(8,128)(2,1)} %param.19) | copy-start | bytes 983044
  7.2 85.8 %all-gather.5.cloned.1.call-start = ((), (), s32[]{:S(2)}) async-start(), calls=%async_computation.2 | async-start | bytes 4915200 | tf_op jit(solution)/shard_map/all_gather | solution.py:210
  13.7 141.5 %reduce-scatter.3.cloned.1.call-start = ((), (), s32[]{:S(2)}) async-start(), calls=%async_computation.3 | async-start | bytes 3276800 | tf_op jit(solution)/shard_map/reduce_scatter | solution.py:255
  13.8 6.2 %copy-start.27 = (s32[1,2,5,128]{3,1,2,0:T(2,128)S(1)}, s32[1,2,5,128]{3,1,2,0:T(2,128)}, u32[]{:S(2)}) copy-start(s32[1,2,5,128]{3,1,2,0:T(2,128)} %param.13) | copy-start | bytes 15364
  93.0 8.3 %copy-start.4 = (bf16[1,384,5120]{2,1,0:T(8,128)(2,1)S(1)}, bf16[1,384,5120]{2,1,0:T(8,128)(2,1)}, u32[]{:S(2)}) copy-start(bf16[1,384,5120]{2,1,0:T(8,128)(2,1)} %pad_bitcast_fusion) | copy-start | bytes 11796484
  104.3 96.5 %all-gather.9.cloned.1.call-start = ((), (), s32[]{:S(2)}) async-start(), calls=%async_computation.6 | async-start | bytes 1638400 | tf_op jit(solution)/shard_map/all_gather | solution.py:54
  105.6 88.5 %collective-permute-start = (bf16[3,128,5120]{2,1,0:T(8,128)(2,1)}, bf16[3,128,5120]{2,1,0:T(8,128)(2,1)}, u32[]{:S(2)}, u32[]{:S(2)}) collective-permute-start(bf16[3,128,5120]{2,1,0:T(8,128)(2,1)} %all-gather.5.cloned.1.call-done), channel_id=1, source_target_pairs={{0,25},{1,24},{8,17},{9,16},{16,9},{17,8},{24,1},{25,0},{2,27},{3,... | collective-permute-start | bytes 11796488 | tf_op jit(solution)/shard_map/ppermute | solution.py:20
  156.2 106.8 %all-gather.7.cloned.1.call-start = ((), (), s32[]{:S(2)}) async-start(), calls=%async_computation.4 | async-start | bytes 3276800 | tf_op jit(solution)/shard_map/all_gather | solution.py:54
  156.8 44.3 %copy-start.18 = (bf16[32,5120]{1,0:T(8,128)(2,1)}, bf16[32,5120]{1,0:T(8,128)(2,1)S(1)}, u32[]{:S(2)}) copy-start(bf16[32,5120]{1,0:T(8,128)(2,1)S(1)} %fusion.78) | copy-start | bytes 983044
  156.8 44.0 %collective-permute-start.1 = (bf16[32,5120]{1,0:T(8,128)(2,1)S(1)}, bf16[32,5120]{1,0:T(8,128)(2,1)S(1)}, u32[]{:S(2)}, u32[]{:S(2)}) collective-permute-start(bf16[32,5120]{1,0:T(8,128)(2,1)S(1)} %fusion.78), channel_id=1, source_target_pairs={{1,9},{8,0},{9,17},{16,8},{17,25},{24,16},{3,11},{10,2},{11,19},{1... | collective-permute-start | bytes 983048 | tf_op jit(solution)/shard_map/ppermute | solution.py:269
  159.2 41.7 %copy-start.15 = (bf16[32,5120]{1,0:T(8,128)(2,1)}, bf16[32,5120]{1,0:T(8,128)(2,1)S(1)}, u32[]{:S(2)}) copy-start(bf16[32,5120]{1,0:T(8,128)(2,1)S(1)} %fusion.90) | copy-start | bytes 983044
  159.2 41.6 %collective-permute-start.2 = (bf16[32,5120]{1,0:T(8,128)(2,1)S(1)}, bf16[32,5120]{1,0:T(8,128)(2,1)}, u32[]{:S(2)}, u32[]{:S(2)}) collective-permute-start(bf16[32,5120]{1,0:T(8,128)(2,1)S(1)} %fusion.90), channel_id=1, source_target_pairs={{0,8},{8,16},{9,1},{16,24},{17,9},{25,17},{2,10},{10,18},{11,3},{1... | collective-permute-start | bytes 983048 | tf_op jit(solution)/shard_map/ppermute | solution.py:270
  165.4 35.4 %copy-start.24 = (bf16[128,128]{1,0:T(8,128)(2,1)}, bf16[128,128]{1,0:T(8,128)(2,1)S(1)}, u32[]{:S(2)}) copy-start(bf16[128,128]{1,0:T(8,128)(2,1)S(1)} %convolution_convert_fusion.8) | copy-start | bytes 98308
  201.1 7.1 %copy-start.10 = (bf16[32,5120]{1,0:T(8,128)(2,1)}, bf16[32,5120]{1,0:T(8,128)(2,1)S(1)}, u32[]{:S(2)}) copy-start(bf16[32,5120]{1,0:T(8,128)(2,1)S(1)} %get-tuple-element.31) | copy-start | bytes 983044
  202.2 60.8 %copy-start.14 = (bf16[1,1,128,5120]{3,2,1,0:T(8,128)(2,1)S(1)}, bf16[1,1,128,5120]{3,2,1,0:T(8,128)(2,1)}, u32[]{:S(2)}) copy-start(bf16[1,1,128,5120]{3,2,1,0:T(8,128)(2,1)} %param.17) | copy-start | bytes 3932164
  202.2 121.9 %reduce-scatter.5.cloned.1.call-start = ((), (), s32[]{:S(2)}) async-start(), calls=%async_computation.5 | async-start | bytes 3276800 | tf_op jit(solution)/shard_map/reduce_scatter | solution.py:255
  202.5 70.4 %collective-permute-start.3 = (bf16[1,128,5120]{2,1,0:T(8,128)(2,1)S(1)}, bf16[1,128,5120]{2,1,0:T(8,128)(2,1)}, u32[]{:S(2)}, u32[]{:S(2)}) collective-permute-start(bf16[1,128,5120]{2,1,0:T(8,128)(2,1)S(1)} %bitcast.362), channel_id=1, source_target_pairs={{0,25},{1,24},{8,17},{9,16},{16,9},{17,8},{24,1},{25,0},{2,27},{3,... | collective-permute-start | bytes 3932168 | tf_op jit(solution)/shard_map/ppermute | solution.py:20
  204.1 68.8 %collective-permute-start.4 = (bf16[4,128,128]{1,2,0:T(8,128)(2,1)}, bf16[4,128,128]{1,2,0:T(8,128)(2,1)S(1)}, u32[]{:S(2)}, u32[]{:S(2)}) collective-permute-start(bf16[4,128,128]{1,2,0:T(8,128)(2,1)} %pad_maximum_fusion.5), channel_id=1, source_target_pairs={{0,25},{1,24},{8,17},{9,16},{16,9},{17,8},{24,1},{25,0},{2,27},{3,... | collective-permute-start | bytes 393224 | tf_op jit(solution)/shard_map/ppermute | solution.py:20
  263.1 6.9 %copy-start.5 = (bf16[1,384,5120]{2,1,0:T(8,128)(2,1)S(1)}, bf16[1,384,5120]{2,1,0:T(8,128)(2,1)}, u32[]{:S(2)}) copy-start(bf16[1,384,5120]{2,1,0:T(8,128)(2,1)} %pad_bitcast_fusion) | copy-start | bytes 11796484
  278.4 8.9 %collective-permute-start.5 = (bf16[4,128,128]{1,2,0:T(8,128)(2,1)S(1)}, bf16[4,128,128]{1,2,0:T(8,128)(2,1)S(1)}, u32[]{:S(2)}, u32[]{:S(2)}) collective-permute-start(bf16[4,128,128]{1,2,0:T(8,128)(2,1)S(1)} %pad_maximum_fusion.6), channel_id=1, source_target_pairs={{0,25},{1,24},{8,17},{9,16},{16,9},{17,8},{24,1},{25,0},{2,27},{3,... | collective-permute-start | bytes 393224 | tf_op jit(solution)/shard_map/ppermute | solution.py:20
  281.2 31.3 %collective-permute-start.6 = (bf16[128,5120]{1,0:T(8,128)(2,1)}, bf16[128,5120]{1,0:T(8,128)(2,1)}, u32[]{:S(2)}, u32[]{:S(2)}) collective-permute-start(bf16[128,5120]{1,0:T(8,128)(2,1)} %slice_bitcast_fusion.6), channel_id=1, source_target_pairs={{0,25},{1,24},{8,17},{9,16},{16,9},{17,8},{24,1},{25,0},{2,27},{3,... | collective-permute-start | bytes 3932168 | tf_op jit(solution)/shard_map/ppermute | solution.py:20
  300.5 23.6 %copy-start.7 = (bf16[1,1,2,32,5120]{4,3,2,1,0:T(8,128)(2,1)S(1)}, bf16[1,1,2,32,5120]{4,3,2,1,0:T(8,128)(2,1)}, u32[]{:S(2)}) copy-start(bf16[1,1,2,32,5120]{4,3,2,1,0:T(8,128)(2,1)} %param.20) | copy-start | bytes 1966084
  316.3 11.0 %copy-start.19 = (bf16[32,5120]{1,0:T(8,128)(2,1)S(1)}, bf16[32,5120]{1,0:T(8,128)(2,1)}, u32[]{:S(2)}) copy-start(bf16[32,5120]{1,0:T(8,128)(2,1)} %copy-done.18) | copy-start | bytes 983044
  316.3 11.9 %copy-start.16 = (bf16[32,5120]{1,0:T(8,128)(2,1)S(1)}, bf16[32,5120]{1,0:T(8,128)(2,1)}, u32[]{:S(2)}) copy-start(bf16[32,5120]{1,0:T(8,128)(2,1)} %copy-done.15) | copy-start | bytes 983044
  (17 other events, 54.9 us)
Sparse Core Ops, SparseCore 0:
  13.8 79.1 all-gather.4
  104.4 50.7 reduce-scatter.2
  157.4 32.0 all-gather.8
  202.4 60.6 all-gather.6
  273.1 51.0 reduce-scatter.4

commit v17 on v15

--- a/solution.py
+++ b/solution.py
@@ -210,7 +210,8 @@
             upstream_full, backward_normed_full[0], forward_normed_full = gathered(
                 [upstream, saved_normed[0], normed_rows(current)]
             )
-            first_sent = to_partner(jnp.stack([upstream_full, backward_normed_full[0]]))
+            first_sent = to_partner(upstream_full)
+            deferred["normed0"] = backward_normed_full[0]
             paired = jnp.einsum(
                 "tsd,cdn->tcsn",
                 jnp.stack([backward_normed_full[0], forward_normed_full]),
@@ -272,8 +273,8 @@
             tie_scatter = {key: to_partner(value) for key, value in deferred.items()}
             deferred = {}
 
-    partner_upstream = [inbox["first"][0]] + [inbox[f"rows{t}"] for t in range(1, window_steps)]
-    partner_normed = [inbox["first"][1]] + (
+    partner_upstream = [inbox["first"]] + [inbox[f"rows{t}"] for t in range(1, window_steps)]
+    partner_normed = [inbox["normed0"]] + (
         [inbox["later"][t] for t in range(window_steps - 1)] if window_steps > 1 else []
     )
     partner_d_projected = [inbox[f"small{t}"][:3] for t in range(window_steps)]

time: 320 us -> 320 us (level)
    all_gather x3, waiting for transfers between devices: 131 us -> 137 us  [gathered(): full = lax.all_gather(jnp.stack(blocks), 'tp', axis=1, tiled=True)]
    another operation x1 -> x0, local copies, waits for them, and re-layouts: 3.47 us -> none  [shards(): first_sent = to_partner(jnp.stack([upstream_full, backward_normed_full[0]]))]
    ppermute x1, waiting for transfers between devices: 6.69 us -> 3.24 us  [shards(): backward_in = lax.ppermute(backward_out, pair_axes, down_pairs)]
    squeeze x1 -> x2, local copies, waits for them, and re-layouts: 1.15 us -> 4.55 us  [gathered(): return [full[i] for i in range(len(blocks))]]
    ppermute x5 -> x6, starting transfers between devices: 7.08 us -> 8.2 us  [flipped(): lax.ppermute(value, axis, [(i, i ^ mask) for i in range(lax.axis_size(axi...]
    ppermute x5 -> x6, waiting for transfers between devices: 15.3 us -> 16.3 us  [flipped(): lax.ppermute(value, axis, [(i, i ^ mask) for i in range(lax.axis_size(axi...]
    unnamed x59 -> x61, local copies, waits for them, and re-layouts: 7.12 us -> 7.1 us
  transfers between devices with their start and end apart: 12 -> 13, of which waited for: 8 -> 8; matrix products, arithmetic and copies ran while one was open for 19% -> 18% of each run, Pallas kernels for 0% -> 0%
where the time goes in v17:
time: 320 us; the launch traced here: 319 us
  waiting for transfers between devices  208 us (65%)
  matrix products  44.7 us (14%)
  local copies, waits for them, and re-layouts  24.6 us (8%)
  starting transfers between devices  15.2 us (5%)
  between operations  14.4 us (4%)
  other arithmetic  12.3 us (4%)
    all_gather x3, waiting for transfers between devices, gathered(): full = lax.all_gather(jnp.stack(blocks), 'tp', axis=1, tiled=True)  137 us
    reduce_scatter x2, waiting for transfers between devices, shards(): lax.psum_scatter(both_parts, 'tp', scatter_dimension=1, tiled=True)  51.5 us
    ppermute x6, waiting for transfers between devices, flipped(): lax.ppermute(value, axis, [(i, i ^ mask) for i in range(lax.axis_size(axi...  16.3 us
    dot_general x4, matrix products, weight_terms(): jnp.einsum('sd,csn->cdn', normed_full, d_projected, preferred_element_typ...  9.61 us
    ppermute x6, starting transfers between devices, flipped(): lax.ppermute(value, axis, [(i, i ^ mask) for i in range(lax.axis_size(axi...  8.2 us
    dot_general x4, matrix products, weight_terms(): jnp.einsum('sn,sd->nd', mixed, upstream_full, preferred_element_type=jnp....  7.19 us
    unnamed x61, local copies, waits for them, and re-layouts  7.1 us
    dot_general x2, matrix products, heads_of(): jnp.einsum('sd,cdn->csn', normed_full, qkv_weight, preferred_element_type...  6.45 us
  transfers between devices with their start and end apart: 13, of which 8 were waited for; matrix products, arithmetic and copies ran while one was open for 18% of the time, Pallas kernels for 0%

profile of v17, /device:TPU:0, one launch (start us, length us, event | category | flops | bytes accessed | tf_op | source)
XLA Modules:
  0.0 318.9 jit_solution(15146844656093826238)
XLA Ops:
  13.8 6.3 %copy.15 = bf16[3,128,5120]{2,1,0:T(8,128)(2,1)} copy(bf16[3,128,5120]{1,2,0:T(8,128)(2,1)} %bitcast.355) | data formatting | bytes 7864320 | tf_op jit(solution)/shard_map/transpose | solution.py:120
  20.7 3.7 %pad_bitcast_fusion = bf16[1,384,5120]{2,1,0:T(8,128)(2,1)} fusion(bf16[128,5120]{1,0:T(8,128)(2,1)} %bitcast.357), kind=kLoop, calls=%fused_computation.28 | loop fusion | bytes 5242880 | tf_op jit(solution)/shard_map/stack | solution.py:124
  24.4 68.6 %all-gather.5.cloned.1.call-done = bf16[3,128,5120]{2,1,0:T(8,128)(2,1)} async-done(((bf16[3,32,5120]{2,1,0:T(8,128)(2,1)}), bf16[3,128,5120]{2,1,0:T(8,128)(2,1)}) %all-gather.5.cloned.1.call-update) | async-done | bytes 3932176 | tf_op jit(solution)/shard_map/all_gather | solution.py:54
  93.0 4.6 %fusion.29 = bf16[2,3,128,128]{3,2,1,0:T(8,128)(2,1)S(1)} fusion(bf16[1,1,3,5120,128]{4,3,2,1,0:T(8,128)(2,1)} %param.16, bf16[3,128,5120]{2,1,0:T(8,128)(2,1)} %all-gather.5.cloned.1.call-done), kind=kOutput, calls=%fused_computation.43 | convolution fusion | flops 1006731264 | bytes 6750208 | tf_op jit(solution)/shard_map/tsd,cdn->tcsn/dot_general | solution.py:215
  97.9 2.0 fusion.62
  101.3 3.0 convolution_convert_fusion.1
  105.7 3.4 %slice_bitcast_fusion.5 = (bf16[128,5120]{1,0:T(8,128)(2,1)}, bf16[128,5120]{1,0:T(8,128)(2,1)}) fusion(bf16[3,128,5120]{2,1,0:T(8,128)(2,1)} %all-gather.5.cloned.1.call-done), kind=kLoop, calls=%fused_computation.32 | loop fusion | bytes 5242880 | tf_op jit(solution)/shard_map/squeeze | solution.py:55
  110.7 44.6 %reduce-scatter.3.cloned.1.call-done = bf16[2,32,5120]{2,1,0:T(8,128)(2,1)} async-done(((bf16[2,128,5120]{2,1,0:T(8,128)(2,1)}), bf16[2,32,5120]{2,1,0:T(8,128)(2,1)}) %reduce-scatter.3.cloned.1.call-update) | async-done | bytes 655376 | tf_op jit(solution)/shard_map/reduce_scatter | solution.py:248
  159.2 5.3 %collective-permute-start.2 = (bf16[32,5120]{1,0:T(8,128)(2,1)S(1)}, bf16[32,5120]{1,0:T(8,128)(2,1)}, u32[]{:S(2)}, u32[]{:S(2)}) collective-permute-start(bf16[32,5120]{1,0:T(8,128)(2,1)S(1)} %fusion.85), channel_id=1, source_target_pairs={{0,8},{8,16},{9,1},{16,24},{17,9},{25,17},{2,10},{10,18},{11,3},{1... | collective-permute-start | bytes 983048 | tf_op jit(solution)/shard_map/ppermute | solution.py:263
  166.1 3.2 %collective-permute-done.1 = bf16[32,5120]{1,0:T(8,128)(2,1)S(1)} collective-permute-done((bf16[32,5120]{1,0:T(8,128)(2,1)S(1)}, bf16[32,5120]{1,0:T(8,128)(2,1)S(1)}, u32[]{:S(2)}, u32[]{:S(2)}) %collective-permute-start.1) | collective-permute-done | bytes 327712 | tf_op jit(solution)/shard_map/ppermute | solution.py:262
  169.4 20.1 %all-gather.9.cloned.1.call-done = bf16[128,5120]{1,0:T(8,128)(2,1)} async-done(((bf16[32,5120]{1,0:T(8,128)(2,1)}), bf16[128,5120]{1,0:T(8,128)(2,1)}) %all-gather.9.cloned.1.call-update) | async-done | bytes 1310736 | tf_op jit(solution)/shard_map/all_gather | solution.py:54
  195.0 3.0 fusion.40
  198.2 47.8 %all-gather.7.cloned.1.call-done = bf16[2,128,5120]{2,1,0:T(8,128)(2,1)} async-done(((bf16[2,32,5120]{2,1,0:T(8,128)(2,1)}), bf16[2,128,5120]{2,1,0:T(8,128)(2,1)}) %all-gather.7.cloned.1.call-update) | async-done | bytes 2621456 | tf_op jit(solution)/shard_map/all_gather | solution.py:54
  246.0 2.4 fusion.63
  248.6 3.5 %fusion.45 = bf16[3,128,128]{2,1,0:T(8,128)(2,1)S(1)} fusion(bf16[1,1,3,5120,128]{4,3,2,1,0:T(8,128)(2,1)} %param.16, bf16[2,128,5120]{2,1,0:T(8,128)(2,1)} %all-gather.7.cloned.1.call-done), kind=kOutput, calls=%fused_computation.51 | convolution fusion | flops 503365632 | bytes 5341184 | tf_op jit(solution)/shard_map/sd,cdn->csn/dot_general | solution.py:86
  253.3 3.0 convolution_convert_fusion
  258.9 2.6 fusion.21
  268.4 2.5 fusion.18
  271.0 3.3 %fusion = bf16[1,1,3,5120,128]{3,4,2,1,0:T(8,128)(2,1)} fusion(f32[3,128,5120]{2,1,0:T(8,128)S(1)} %fusion.18, bf16[4,128,128]{1,2,0:T(8,128)(2,1)S(1)} %collective-permute-done.5, bf16[3,128,5120]{2,1,0:T(8,128)(2,1)S(1)} %add_convert_fusion.2, bf16[128,5120]{1,0:T(8,128)(2,1)S(1)} %copy-done.13), kind=kOutput, calls=%fused_computation.6 | convolution fusion | flops 515112960 | bytes 17170432 | tf_op jit(solution)/shard_map/sd,csn->cdn/dot_general | solution.py:146
  274.2 6.3 %copy.18 = bf16[1,1,3,5120,128]{4,3,2,1,0:T(8,128)(2,1)} copy(bf16[1,1,3,5120,128]{3,4,2,1,0:T(8,128)(2,1)} %fusion) | data formatting | bytes 7864320
  280.5 15.2 %collective-permute-done.7 = bf16[128,5120]{1,0:T(8,128)(2,1)} collective-permute-done((bf16[128,5120]{1,0:T(8,128)(2,1)}, bf16[128,5120]{1,0:T(8,128)(2,1)}, u32[]{:S(2)}, u32[]{:S(2)}) %collective-permute-start.7) | collective-permute-done | bytes 1310752 | tf_op jit(solution)/shard_map/ppermute | solution.py:20
  297.5 3.1 fusion.7
  300.6 6.9 %reduce-scatter.5.cloned.1.call-done = bf16[2,32,5120]{2,1,0:T(8,128)(2,1)} async-done(((bf16[2,128,5120]{2,1,0:T(8,128)(2,1)}), bf16[2,32,5120]{2,1,0:T(8,128)(2,1)}) %reduce-scatter.5.cloned.1.call-update) | async-done | bytes 655376 | tf_op jit(solution)/shard_map/reduce_scatter | solution.py:248
  308.7 1.9 fusion.87
  (146 shorter events, 38.3 us)
Async XLA Ops:
  7.2 85.8 %all-gather.5.cloned.1.call-start = ((), (), s32[]{:S(2)}) async-start(), calls=%async_computation.2 | async-start | bytes 4915200 | tf_op jit(solution)/shard_map/all_gather | solution.py:54
  13.7 141.6 %reduce-scatter.3.cloned.1.call-start = ((), (), s32[]{:S(2)}) async-start(), calls=%async_computation.3 | async-start | bytes 3276800 | tf_op jit(solution)/shard_map/reduce_scatter | solution.py:248
  13.8 6.3 %copy-start.28 = (s32[1,2,5,128]{3,1,2,0:T(2,128)S(1)}, s32[1,2,5,128]{3,1,2,0:T(2,128)}, u32[]{:S(2)}) copy-start(s32[1,2,5,128]{3,1,2,0:T(2,128)} %param.13) | copy-start | bytes 15364
  93.0 8.3 %copy-start.4 = (bf16[1,384,5120]{2,1,0:T(8,128)(2,1)S(1)}, bf16[1,384,5120]{2,1,0:T(8,128)(2,1)}, u32[]{:S(2)}) copy-start(bf16[1,384,5120]{2,1,0:T(8,128)(2,1)} %pad_bitcast_fusion) | copy-start | bytes 11796484
  104.3 85.2 %all-gather.9.cloned.1.call-start = ((), (), s32[]{:S(2)}) async-start(), calls=%async_computation.6 | async-start | bytes 1638400 | tf_op jit(solution)/shard_map/all_gather | solution.py:54
  109.0 57.1 %collective-permute-start = (bf16[128,5120]{1,0:T(8,128)(2,1)}, bf16[128,5120]{1,0:T(8,128)(2,1)}, u32[]{:S(2)}, u32[]{:S(2)}) collective-permute-start(bf16[128,5120]{1,0:T(8,128)(2,1)} %get-tuple-element.36), channel_id=1, source_target_pairs={{0,25},{1,24},{8,17},{9,16},{16,9},{17,8},{24,1},{25,0},{2,27},{3,... | collective-permute-start | bytes 3932168 | tf_op jit(solution)/shard_map/ppermute | solution.py:20
  156.3 89.7 %all-gather.7.cloned.1.call-start = ((), (), s32[]{:S(2)}) async-start(), calls=%async_computation.4 | async-start | bytes 3276800 | tf_op jit(solution)/shard_map/all_gather | solution.py:54
  156.9 32.9 %copy-start.18 = (bf16[32,5120]{1,0:T(8,128)(2,1)}, bf16[32,5120]{1,0:T(8,128)(2,1)S(1)}, u32[]{:S(2)}) copy-start(bf16[32,5120]{1,0:T(8,128)(2,1)S(1)} %fusion.73) | copy-start | bytes 983044
  156.9 12.5 %collective-permute-start.1 = (bf16[32,5120]{1,0:T(8,128)(2,1)S(1)}, bf16[32,5120]{1,0:T(8,128)(2,1)S(1)}, u32[]{:S(2)}, u32[]{:S(2)}) collective-permute-start(bf16[32,5120]{1,0:T(8,128)(2,1)S(1)} %fusion.73), channel_id=1, source_target_pairs={{1,9},{8,0},{9,17},{16,8},{17,25},{24,16},{3,11},{10,2},{11,19},{1... | collective-permute-start | bytes 983048 | tf_op jit(solution)/shard_map/ppermute | solution.py:262
  159.2 30.3 %copy-start.15 = (bf16[32,5120]{1,0:T(8,128)(2,1)}, bf16[32,5120]{1,0:T(8,128)(2,1)S(1)}, u32[]{:S(2)}) copy-start(bf16[32,5120]{1,0:T(8,128)(2,1)S(1)} %fusion.85) | copy-start | bytes 983044
  159.2 10.1 %collective-permute-start.2 = (bf16[32,5120]{1,0:T(8,128)(2,1)S(1)}, bf16[32,5120]{1,0:T(8,128)(2,1)}, u32[]{:S(2)}, u32[]{:S(2)}) collective-permute-start(bf16[32,5120]{1,0:T(8,128)(2,1)S(1)} %fusion.85), channel_id=1, source_target_pairs={{0,8},{8,16},{9,1},{16,24},{17,9},{25,17},{2,10},{10,18},{11,3},{1... | collective-permute-start | bytes 983048 | tf_op jit(solution)/shard_map/ppermute | solution.py:263
  169.4 21.8 %copy-start.20 = (bf16[32,5120]{1,0:T(8,128)(2,1)}, bf16[32,5120]{1,0:T(8,128)(2,1)S(1)}, u32[]{:S(2)}) copy-start(bf16[32,5120]{1,0:T(8,128)(2,1)S(1)} %collective-permute-done.1) | copy-start | bytes 983044
  189.8 8.2 %copy-start.9 = (bf16[32,5120]{1,0:T(8,128)(2,1)}, bf16[32,5120]{1,0:T(8,128)(2,1)S(1)}, u32[]{:S(2)}) copy-start(bf16[32,5120]{1,0:T(8,128)(2,1)S(1)} %get-tuple-element.35) | copy-start | bytes 983044
  190.9 116.6 %reduce-scatter.5.cloned.1.call-start = ((), (), s32[]{:S(2)}) async-start(), calls=%async_computation.5 | async-start | bytes 3276800 | tf_op jit(solution)/shard_map/reduce_scatter | solution.py:248
  191.1 65.1 %collective-permute-start.3 = (bf16[1,128,5120]{2,1,0:T(8,128)(2,1)S(1)}, bf16[1,128,5120]{2,1,0:T(8,128)(2,1)}, u32[]{:S(2)}, u32[]{:S(2)}) collective-permute-start(bf16[1,128,5120]{2,1,0:T(8,128)(2,1)S(1)} %bitcast.356), channel_id=1, source_target_pairs={{0,25},{1,24},{8,17},{9,16},{16,9},{17,8},{24,1},{25,0},{2,27},{3,... | collective-permute-start | bytes 3932168 | tf_op jit(solution)/shard_map/ppermute | solution.py:20
  192.3 64.0 %collective-permute-start.4 = (bf16[128,5120]{1,0:T(8,128)(2,1)}, bf16[128,5120]{1,0:T(8,128)(2,1)S(1)}, u32[]{:S(2)}, u32[]{:S(2)}) collective-permute-start(bf16[128,5120]{1,0:T(8,128)(2,1)} %get-tuple-element.21), channel_id=1, source_target_pairs={{0,25},{1,24},{8,17},{9,16},{16,9},{17,8},{24,1},{25,0},{2,27},{3,... | collective-permute-start | bytes 3932168 | tf_op jit(solution)/shard_map/ppermute | solution.py:20
  193.9 62.4 %collective-permute-start.5 = (bf16[4,128,128]{1,2,0:T(8,128)(2,1)}, bf16[4,128,128]{1,2,0:T(8,128)(2,1)S(1)}, u32[]{:S(2)}, u32[]{:S(2)}) collective-permute-start(bf16[4,128,128]{1,2,0:T(8,128)(2,1)} %pad_maximum_fusion.5), channel_id=1, source_target_pairs={{0,25},{1,24},{8,17},{9,16},{16,9},{17,8},{24,1},{25,0},{2,27},{3,... | collective-permute-start | bytes 393224 | tf_op jit(solution)/shard_map/ppermute | solution.py:20
  246.0 7.3 %copy-start.5 = (bf16[1,384,5120]{2,1,0:T(8,128)(2,1)S(1)}, bf16[1,384,5120]{2,1,0:T(8,128)(2,1)}, u32[]{:S(2)}) copy-start(bf16[1,384,5120]{2,1,0:T(8,128)(2,1)} %pad_bitcast_fusion) | copy-start | bytes 11796484
  256.3 14.7 %copy-start.22 = (bf16[4,128,128]{1,2,0:T(8,128)(2,1)}, bf16[4,128,128]{1,2,0:T(8,128)(2,1)S(1)}, u32[]{:S(2)}) copy-start(bf16[4,128,128]{1,2,0:T(8,128)(2,1)S(1)} %collective-permute-done.5) | copy-start | bytes 393220
  261.7 6.7 %collective-permute-start.6 = (bf16[4,128,128]{1,2,0:T(8,128)(2,1)S(1)}, bf16[4,128,128]{1,2,0:T(8,128)(2,1)S(1)}, u32[]{:S(2)}, u32[]{:S(2)}) collective-permute-start(bf16[4,128,128]{1,2,0:T(8,128)(2,1)S(1)} %pad_maximum_fusion.6), channel_id=1, source_target_pairs={{0,25},{1,24},{8,17},{9,16},{16,9},{17,8},{24,1},{25,0},{2,27},{3,... | collective-permute-start | bytes 393224 | tf_op jit(solution)/shard_map/ppermute | solution.py:20
  264.5 31.2 %collective-permute-start.7 = (bf16[128,5120]{1,0:T(8,128)(2,1)}, bf16[128,5120]{1,0:T(8,128)(2,1)}, u32[]{:S(2)}, u32[]{:S(2)}) collective-permute-start(bf16[128,5120]{1,0:T(8,128)(2,1)} %slice_bitcast_fusion.4), channel_id=1, source_target_pairs={{0,25},{1,24},{8,17},{9,16},{16,9},{17,8},{24,1},{25,0},{2,27},{3,... | collective-permute-start | bytes 3932168 | tf_op jit(solution)/shard_map/ppermute | solution.py:20
  297.5 10.0 %copy-start.7 = (bf16[1,1,2,32,5120]{4,3,2,1,0:T(8,128)(2,1)S(1)}, bf16[1,1,2,32,5120]{4,3,2,1,0:T(8,128)(2,1)}, u32[]{:S(2)}) copy-start(bf16[1,1,2,32,5120]{4,3,2,1,0:T(8,128)(2,1)} %param.20) | copy-start | bytes 1966084
  300.6 10.0 %copy-start.19 = (bf16[32,5120]{1,0:T(8,128)(2,1)S(1)}, bf16[32,5120]{1,0:T(8,128)(2,1)}, u32[]{:S(2)}) copy-start(bf16[32,5120]{1,0:T(8,128)(2,1)} %copy-done.18) | copy-start | bytes 983044
  300.6 10.9 %copy-start.16 = (bf16[32,5120]{1,0:T(8,128)(2,1)S(1)}, bf16[32,5120]{1,0:T(8,128)(2,1)}, u32[]{:S(2)}) copy-start(bf16[32,5120]{1,0:T(8,128)(2,1)} %copy-done.15) | copy-start | bytes 983044
  (19 other events, 67.3 us)
Sparse Core Ops, SparseCore 0:
  13.8 79.1 all-gather.4
  104.4 50.7 reduce-scatter.2
  157.4 32.0 all-gather.8
  191.5 54.4 all-gather.6
  256.4 51.0 reduce-scatter.4
